TPU v7x, 32 devices: a whole 2x2x4 slice. The times are simulated.
32 devices in a mesh: slab: 8 (over z, y), col: 4 (over x, core).
Axes of the slice: x: 2, y: 2, z: 4, core: 2. Of those that a mesh axis runs over, the one named last changes fastest.
Arguments:
- rhs_force: float32 [3, 32, 32, 384], P(None, 'slab', 'col'), may hold values from -33 to 33
- integrity: bfloat16 [61, 32, 32, 384], P(None, 'slab', 'col'), may hold values from 0 to 1
- contact: int32 [32, 32, 384], P('slab', 'col'), may hold values 0 or 1
- coarse_inverse: float32 [768, 768], P(('slab', 'col')), may hold values from 0 to 6, as said below
Outputs:
- displacement: float32 [3, 32, 32, 384], P(None, 'slab', 'col')
- residual: float32 [3, 32, 32, 384], P(None, 'slab', 'col')
Inputs may be any that keep to these rules, and one draw needn't show every extreme that they name: `coarse_inverse`: symmetric and positive definite, with no negative entry.
All inputs are finite; a program needn't handle non-finite values. No bound on the sum of `contact` on one device may be relied on, other than what follows from the above.
Results may differ from a plain program's by a relative error of at most 0.0007.
Values may be sent and summed in bfloat16 or wider, within the bound.
No kernel may reach another device: no remote copies, remote signals or barrier semaphores. Data moves between devices by JAX's collectives and lax.ppermute only.
A program may use at most 128 MiB of HBM per device.

v0:
```python
import jax
import jax.numpy as jnp
import numpy as np
from jax import lax
from jax.sharding import PartitionSpec as P

ITERS = 2


STIFFNESS = 0.6
PENALTY = 2.0
FOUNDATION = 1.0


def with_halo(x, sides, width):
    for axis, dim in sides:
        count, length = (lax.axis_size(axis), x.shape[dim])
        up = [(i, (i + 1) % count) for i in range(count - 1)]
        down = [(j, i) for i, j in up]
        last = lax.slice_in_dim(x, length - width, length, axis=dim)
        first = lax.slice_in_dim(x, 0, width, axis=dim)
        before = lax.ppermute(last, axis, up)
        after = lax.ppermute(first, axis, down)
        x = jnp.concatenate([before, x, after], axis=dim)
    return x


def bond_list():
    listed = []
    for shift_x in range(-3, 4):
        for shift_y in range(-3, 4):
            for shift_z in range(-3, 4):
                radius = shift_x * shift_x + shift_y * shift_y + shift_z * shift_z
                if 0 < radius <= 9 and (shift_x, shift_y, shift_z) > (0, 0, 0):
                    listed.append((shift_x, shift_y, shift_z))
    return listed


def bond_tables():
    offsets = np.array(bond_list(), dtype=np.int32)
    lengths = np.sqrt(np.sum(offsets * offsets, axis=1).astype(np.float32)).astype(np.float32)
    unit_dirs = (offsets.astype(np.float32) / lengths[:, None]).astype(np.float32)
    weights = (np.float32(STIFFNESS) / lengths).astype(np.float32)
    nearest = (lengths < 1.5).astype(np.float32)
    return (offsets, unit_dirs, weights, nearest)


def rim_mask(count, whole, position):
    places = position * count + jnp.arange(count + 6, dtype=jnp.int32) - 3
    return ((places >= 0) & (places < whole)).astype(jnp.float32)


def window(array, shift_x, shift_y, shift_z, extent):
    return array[
        ...,
        3 + shift_x : 3 + shift_x + extent[0],
        3 + shift_y : 3 + shift_y + extent[1],
        3 + shift_z : 3 + shift_z + extent[2],
    ]


def pad_depth(array):
    return jnp.pad(array, [(0, 0)] * (array.ndim - 1) + [(3, 3)])


def on_device(rhs_force, integrity, contact, coarse_inverse):
    components, cells_x, cells_y, depth = rhs_force.shape
    bond_count = integrity.shape[0]
    aggregates = coarse_inverse.shape[0] // 3
    agg_depth = depth // aggregates
    agg_cells = cells_x * cells_y * agg_depth
    extent = (cells_x, cells_y, depth)
    offsets, unit_dirs, weights, nearest = bond_tables()
    slab_mask = rim_mask(cells_x, cells_x * lax.axis_size("slab"), lax.axis_index("slab"))
    col_mask = rim_mask(cells_y, cells_y * lax.axis_size("col"), lax.axis_index("col"))
    depth_mask = rim_mask(depth, depth, jnp.zeros((), jnp.int32))
    inside_pad = slab_mask[:, None, None] * col_mask[None, :, None] * depth_mask[None, None, :]

    def bond_shift(bond_index):
        return [int(entry) for entry in offsets[bond_index]]

    def heading_of(bond_index):
        return [float(unit_dirs[bond_index, component]) for component in range(3)]

    def rimmed(vector):
        return pad_depth(with_halo(vector, (("slab", 1), ("col", 2)), 3))

    stacked = jnp.concatenate([integrity, contact.astype(jnp.bfloat16)[None]], axis=0)
    spread = pad_depth(with_halo(stacked, (("slab", 1), ("col", 2)), 3))
    contact_pad = spread[bond_count].astype(jnp.float32)
    near_contact = window(contact_pad, 0, 0, 0, extent)

    def bond_pair(bond_index):
        shift_x, shift_y, shift_z = bond_shift(bond_index)
        weight = float(weights[bond_index])
        level_pad = spread[bond_index]
        intact = window(level_pad, 0, 0, 0, extent).astype(jnp.float32)
        prior = window(level_pad, -shift_x, -shift_y, -shift_z, extent).astype(jnp.float32)
        forward = weight * intact
        backward = weight * prior
        if nearest[bond_index] > 0.5:
            forward = forward + PENALTY * near_contact * window(
                contact_pad, shift_x, shift_y, shift_z, extent
            ) * (1.0 - intact)
            backward = backward + PENALTY * window(
                contact_pad, -shift_x, -shift_y, -shift_z, extent
            ) * near_contact * (1.0 - prior)
        forward = window(inside_pad, shift_x, shift_y, shift_z, extent) * forward
        return (forward, backward)

    diag_list = [jnp.full(extent, FOUNDATION, jnp.float32) for component in range(3)]
    for bond_index in range(bond_count):
        forward, backward = bond_pair(bond_index)
        heading = heading_of(bond_index)
        both_ends = forward + backward
        for component in range(3):
            diag_list[component] = (
                diag_list[component] + heading[component] * heading[component] * both_ends
            )
    diagonal = jnp.stack(diag_list)

    def operator(vector):
        padded = rimmed(vector)
        summed = [FOUNDATION * vector[component] for component in range(3)]
        for bond_index in range(bond_count):
            shift_x, shift_y, shift_z = bond_shift(bond_index)
            forward, backward = bond_pair(bond_index)
            heading = heading_of(bond_index)
            ahead_part = heading[0] * (
                vector[0] - window(padded[0], shift_x, shift_y, shift_z, extent)
            )
            behind_part = heading[0] * (
                vector[0] - window(padded[0], -shift_x, -shift_y, -shift_z, extent)
            )
            for component in range(1, 3):
                ahead_part = ahead_part + heading[component] * (
                    vector[component] - window(padded[component], shift_x, shift_y, shift_z, extent)
                )
                behind_part = behind_part + heading[component] * (
                    vector[component]
                    - window(padded[component], -shift_x, -shift_y, -shift_z, extent)
                )
            stretch = forward * ahead_part + backward * behind_part
            for component in range(3):
                summed[component] = summed[component] + heading[component] * stretch
        return jnp.stack(summed)

    def local_means(vector):
        blocks = vector.reshape(3, cells_x * cells_y, aggregates, agg_depth)
        return (jnp.sum(blocks, axis=(1, 3)) / agg_cells).T.reshape(3 * aggregates)

    def gathered(vector):
        return lax.all_gather(local_means(vector), ("slab", "col"), axis=0, tiled=True)

    def precondition(vector, coarse):
        solved = jnp.dot(coarse_inverse, coarse, precision=lax.Precision.HIGHEST)
        spread_back = solved.reshape(aggregates, 3).T[:, None, :, None]
        scaled = (vector / diagonal).reshape(
            3, cells_x * cells_y, aggregates, agg_depth
        ) + spread_back
        return scaled.reshape(vector.shape)

    displacement = jnp.zeros_like(rhs_force)
    residual = rhs_force

    def rz_total(left_vec, right_vec):
        return lax.psum(jnp.sum(left_vec * right_vec), ("slab", "col"))

    direction = precondition(residual, gathered(residual))
    rz_now = rz_total(residual, direction)
    for iteration in range(ITERS):
        image_vec = operator(direction)
        step_size = rz_now / lax.psum(jnp.sum(direction * image_vec), ("slab", "col"))
        displacement = displacement + step_size * direction
        residual = residual - step_size * image_vec
        if iteration + 1 < ITERS:
            precond_r = precondition(residual, gathered(residual))
            fresh_rz = rz_total(residual, precond_r)
            direction = precond_r + fresh_rz / rz_now * direction
            rz_now = fresh_rz
    return (displacement, residual)


def solution(mesh):
    return jax.shard_map(
        on_device,
        mesh=mesh,
        in_specs=(
            P(None, "slab", "col", None),
            P(None, "slab", "col", None),
            P("slab", "col", None),
            P(("slab", "col"), None),
        ),
        out_specs=(P(None, "slab", "col", None), P(None, "slab", "col", None)),
        check_vma=False,
    )
```

profile of v0, /device:TPU:0, one launch (start us, length us, event | category | flops | bytes accessed | tf_op | source)
XLA Modules:
  0.0 417.7 jit_solution(580272318926781936)
XLA Ops:
  1.6 1.9 fusion.8
  3.4 4.9 %collective-permute-start = (bf16[62,3,8,384]{3,2,1,0:T(8,128)(2,1)S(1)}, bf16[62,3,8,384]{3,2,1,0:T(8,128)(2,1)S(1)}, u32[]{:S(2)}, u32[]{:S(2)}) collective-permute-start(bf16[62,3,8,384]{3,2,1,0:T(8,128)(2,1)S(1)} %get-tuple-element.218), channel_id=1, source_target_pairs={{0,4},{4,8},{8,12},{12,16},{16,20},{20,24},{24,28},{1,5},{5,9},{9,... | collective-permute-start | bytes 3428360 | tf_op jit(solution)/shard_map/ppermute | solution.py:22
  9.7 47.5 %collective-permute-done = bf16[62,3,8,384]{3,2,1,0:T(8,128)(2,1)S(1)} collective-permute-done((bf16[62,3,8,384]{3,2,1,0:T(8,128)(2,1)S(1)}, bf16[62,3,8,384]{3,2,1,0:T(8,128)(2,1)S(1)}, u32[]{:S(2)}, u32[]{:S(2)}) %collective-permute-start) | collective-permute-done | bytes 1142816 | tf_op jit(solution)/shard_map/ppermute | solution.py:22
  61.9 2.4 collective-permute-start.2
  67.7 55.2 %all-reduce.3 = f32[768]{0:T(1024)S(1)} all-reduce(f32[768]{0:T(1024)S(1)} %dynamic-update-slice), channel_id=1, replica_groups=mesh['slab'=8,'col'=4] {'slab','col'}, use_global_device_ids=true, to_apply=%add.3 | all-reduce | flops 768 | bytes 6144
  123.6 2.7 copy.86
  126.3 2.6 copy.87
  129.0 32.2 %select_maximum_fusion = bf16[62,10,14,390]{3,2,1,0:T(8,128)(2,1)S(1)} fusion(bf16[62,10,3,384]{3,2,1,0:T(4,128)(2,1)S(1)} %copy.87, bf16[62,10,3,384]{3,2,1,0:T(4,128)(2,1)S(1)} %copy.86, bf16[62,3,8,384]{3,2,1,0:T(8,128)(2,1)S(1)} %copy-done.3, bf16[62,3,8,384]{3,2,1,0:T(8,128)(2,1)S(1)} %collective-permute-done, ...), kind=kLoop, calls=%fused_computation.3 | loop fusion | flops 71089200 | bytes 13436640 | tf_op jit(solution)/shard_map/concatenate | solution.py:24
  164.8 4.7 %add_bitcast_fusion.8 = (f32[1,4,8,384]{3,2,1,0:T(8,128)S(1)}, f32[4,8,384]{2,1,0:T(8,128)S(1)}, f32[4,8,384]{2,1,0:T(8,128)S(1)}, f32[4,8,384]{2,1,0:T(8,128)S(...) fusion(bf16[10,14,390]{2,1,0:T(8,128)(2,1)} %get-tuple-element., ...), kind=kLoop, calls=%fused_computation.2524 | loop fusion | flops 6967296 | bytes 7913472 | tf_op jit(solution)/shard_map/stack | solution.py:120
  169.5 3.4 add_bitcast_fusion.7
  173.3 3.8 add_bitcast_fusion.6
  177.8 4.8 %collective-permute-start.4 = (f32[3,3,8,384]{3,2,1,0:T(8,128)}, f32[3,3,8,384]{3,2,1,0:T(8,128)}, u32[]{:S(2)}, u32[]{:S(2)}) collective-permute-start(f32[3,3,8,384]{3,2,1,0:T(8,128)} %get-tuple-element.235), channel_id=1, source_target_pairs={{0,4},{4,8},{8,12},{12,16},{16,20},{20,24},{24,28},{1,5},{5,9},{9,... | collective-permute-start | bytes 331784 | tf_op jit(solution)/shard_map/ppermute | solution.py:22
  184.6 5.0 %collective-permute-done.5 = f32[3,3,8,384]{3,2,1,0:T(8,128)} collective-permute-done((f32[3,3,8,384]{3,2,1,0:T(8,128)}, f32[3,3,8,384]{3,2,1,0:T(8,128)}, u32[]{:S(2)}, u32[]{:S(2)}) %collective-permute-start.5) | collective-permute-done | bytes 110624 | tf_op jit(solution)/shard_map/ppermute | solution.py:23
  191.4 2.0 collective-permute-start.6
  195.0 3.6 collective-permute-done.7
  200.5 12.8 %add_bitcast_fusion.5 = (f32[1,4,8,384]{3,2,1,0:T(8,128)S(1)}, f32[4,8,384]{2,1,0:T(8,128)S(1)}, f32[4,8,384]{2,1,0:T(8,128)S(1)}, f32[4,8,384]{2,1,0:T(8,128)S(...) fusion(f32[4,8,384]{2,1,0:T(8,128)S(1)} %squeeze.207, ...), kind=kLoop, calls=%fused_computation.2521 | loop fusion | flops 18382848 | bytes 27181056 | tf_op jit(solution)/shard_map/stack | solution.py:146
  214.6 41.4 %all-reduce.5 = (f32[]{:T(128)}, f32[]{:T(128)}) all-reduce(f32[]{:T(128)} %get-tuple-element.3, f32[]{:T(128)} %get-tuple-element.2), channel_id=1, replica_groups=mesh['slab'=8,'col'=4] {'slab','col'}, use_global_device_ids=true, to_apply=%region_3.4 | all-reduce | flops 2 | bytes 16 | tf_op jit(solution)/shard_map/psum | solution.py:167
  258.0 40.8 %all-reduce.4 = f32[768]{0:T(1024)S(1)} all-reduce(f32[768]{0:T(1024)S(1)} %dynamic-update-slice.1), channel_id=1, replica_groups=mesh['slab'=8,'col'=4] {'slab','col'}, use_global_device_ids=true, to_apply=%add.4 | all-reduce | flops 768 | bytes 6144
  299.9 39.6 %psum.30 = f32[]{:T(128)} all-reduce(f32[]{:T(128)} %multiply_reduce_fusion.1), channel_id=1, replica_groups=mesh['slab'=8,'col'=4] {'slab','col'}, use_global_device_ids=true, to_apply=%region_9.10 | all-reduce | flops 1 | bytes 8 | tf_op jit(solution)/shard_map/psum | solution.py:167
  340.9 4.4 %collective-permute-start.8 = (f32[3,3,8,384]{3,2,1,0:T(8,128)S(1)}, f32[3,3,8,384]{3,2,1,0:T(8,128)S(1)}, u32[]{:S(2)}, u32[]{:S(2)}) collective-permute-start(f32[3,3,8,384]{3,2,1,0:T(8,128)S(1)} %get-tuple-element.233), channel_id=1, source_target_pairs={{0,4},{4,8},{8,12},{12,16},{16,20},{20,24},{24,28},{1,5},{5,9},{9,... | collective-permute-start | bytes 331784 | tf_op jit(solution)/shard_map/ppermute | solution.py:22
  347.6 4.3 %collective-permute-done.9 = f32[3,3,8,384]{3,2,1,0:T(8,128)S(1)} collective-permute-done((f32[3,3,8,384]{3,2,1,0:T(8,128)S(1)}, f32[3,3,8,384]{3,2,1,0:T(8,128)S(1)}, u32[]{:S(2)}, u32[]{:S(2)}) %collective-permute-start.9) | collective-permute-done | bytes 110624 | tf_op jit(solution)/shard_map/ppermute | solution.py:23
  354.6 2.9 collective-permute-done.11
  358.2 12.6 %add_bitcast_fusion.2 = (f32[1,4,8,384]{3,2,1,0:T(8,128)S(1)}, f32[4,8,384]{2,1,0:T(8,128)S(1)}, f32[4,8,384]{2,1,0:T(8,128)S(1)}, f32[4,8,384]{2,1,0:T(8,128)S(...) fusion(f32[3,4,8,384]{3,2,1,0:T(8,128)S(1)} %multiply_add_fusio, ...), kind=kLoop, calls=%fused_computation.2518 | loop fusion | flops 18382848 | bytes 27181056 | tf_op jit(solution)/shard_map/stack | solution.py:146
  372.1 43.5 %psum.31 = f32[]{:T(128)} all-reduce(f32[]{:T(128)} %multiply_reduce_fusion), channel_id=1, replica_groups=mesh['slab'=8,'col'=4] {'slab','col'}, use_global_device_ids=true, to_apply=%region_11.12 | all-reduce | flops 1 | bytes 8 | tf_op jit(solution)/shard_map/psum | solution.py:173
  (174 shorter events, 33.2 us)
Async XLA Ops:
  0.6 122.2 %copy-start = (f32[24,768]{1,0:T(8,128)S(1)}, f32[24,768]{1,0:T(8,128)}, u32[]{:S(2)}) copy-start(f32[24,768]{1,0:T(8,128)} %param.7) | copy-start | bytes 221188
  0.6 57.6 %copy-start.1 = (bf16[61,4,8,384]{3,2,1,0:T(8,128)(2,1)S(1)}, bf16[61,4,8,384]{3,2,1,0:T(8,128)(2,1)}, u32[]{:S(2)}) copy-start(bf16[61,4,8,384]{3,2,1,0:T(8,128)(2,1)} %param.5) | copy-start | bytes 4497412
  3.4 53.8 %collective-permute-start = (bf16[62,3,8,384]{3,2,1,0:T(8,128)(2,1)S(1)}, bf16[62,3,8,384]{3,2,1,0:T(8,128)(2,1)S(1)}, u32[]{:S(2)}, u32[]{:S(2)}) collective-permute-start(bf16[62,3,8,384]{3,2,1,0:T(8,128)(2,1)S(1)} %get-tuple-element.218), channel_id=1, source_target_pairs={{0,4},{4,8},{8,12},{12,16},{16,20},{20,24},{24,28},{1,5},{5,9},{9,... | collective-permute-start | bytes 3428360 | tf_op jit(solution)/shard_map/ppermute | solution.py:22
  8.4 48.8 %collective-permute-start.1 = (bf16[62,3,8,384]{3,2,1,0:T(8,128)(2,1)S(1)}, bf16[62,3,8,384]{3,2,1,0:T(8,128)(2,1)S(1)}, u32[]{:S(2)}, u32[]{:S(2)}) collective-permute-start(bf16[62,3,8,384]{3,2,1,0:T(8,128)(2,1)S(1)} %get-tuple-element.219), channel_id=1, source_target_pairs={{4,0},{8,4},{12,8},{16,12},{20,16},{24,20},{28,24},{5,1},{9,5},{13... | collective-permute-start | bytes 3428360 | tf_op jit(solution)/shard_map/ppermute | solution.py:23
  61.9 61.7 %collective-permute-start.2 = (bf16[62,10,3,384]{3,0,2,1:T(8,128)(2,1)}, bf16[62,10,3,384]{3,0,2,1:T(8,128)(2,1)}, u32[]{:S(2)}, u32[]{:S(2)}) collective-permute-start(bf16[62,10,3,384]{3,0,2,1:T(8,128)(2,1)} %copy.84), channel_id=1, source_target_pairs={{0,1},{1,2},{2,3},{4,5},{5,6},{6,7},{8,9},{9,10},{10,11},{12,13},{... | collective-permute-start | bytes 4285448 | tf_op jit(solution)/shard_map/ppermute | solution.py:22
  65.8 60.5 %collective-permute-start.3 = (bf16[62,10,3,384]{3,0,2,1:T(8,128)(2,1)}, bf16[62,10,3,384]{3,0,2,1:T(8,128)(2,1)}, u32[]{:S(2)}, u32[]{:S(2)}) collective-permute-start(bf16[62,10,3,384]{3,0,2,1:T(8,128)(2,1)} %copy.85), channel_id=1, source_target_pairs={{1,0},{2,1},{3,2},{5,4},{6,5},{7,6},{9,8},{10,9},{11,10},{13,12},{... | collective-permute-start | bytes 4285448 | tf_op jit(solution)/shard_map/ppermute | solution.py:23
  161.5 11.3 %copy-start.5 = (bf16[10,14,390]{2,1,0:T(8,128)(2,1)}, bf16[10,14,390]{2,1,0:T(8,128)(2,1)S(1)}, u32[]{:S(2)}) copy-start(bf16[10,14,390]{2,1,0:T(8,128)(2,1)S(1)} %get-tuple-element.161) | copy-start | bytes 327604
  161.6 11.3 %copy-start.6 = (bf16[10,14,390]{2,1,0:T(8,128)(2,1)}, bf16[10,14,390]{2,1,0:T(8,128)(2,1)S(1)}, u32[]{:S(2)}) copy-start(bf16[10,14,390]{2,1,0:T(8,128)(2,1)S(1)} %get-tuple-element.162) | copy-start | bytes 327604
  161.6 11.3 %copy-start.7 = (bf16[10,14,390]{2,1,0:T(8,128)(2,1)}, bf16[10,14,390]{2,1,0:T(8,128)(2,1)S(1)}, u32[]{:S(2)}) copy-start(bf16[10,14,390]{2,1,0:T(8,128)(2,1)S(1)} %get-tuple-element.163) | copy-start | bytes 327604
  161.6 11.3 %copy-start.8 = (bf16[10,14,390]{2,1,0:T(8,128)(2,1)}, bf16[10,14,390]{2,1,0:T(8,128)(2,1)S(1)}, u32[]{:S(2)}) copy-start(bf16[10,14,390]{2,1,0:T(8,128)(2,1)S(1)} %get-tuple-element.164) | copy-start | bytes 327604
  161.6 11.3 %copy-start.9 = (bf16[10,14,390]{2,1,0:T(8,128)(2,1)}, bf16[10,14,390]{2,1,0:T(8,128)(2,1)S(1)}, u32[]{:S(2)}) copy-start(bf16[10,14,390]{2,1,0:T(8,128)(2,1)S(1)} %get-tuple-element.165) | copy-start | bytes 327604
  161.6 11.3 %copy-start.10 = (bf16[10,14,390]{2,1,0:T(8,128)(2,1)}, bf16[10,14,390]{2,1,0:T(8,128)(2,1)S(1)}, u32[]{:S(2)}) copy-start(bf16[10,14,390]{2,1,0:T(8,128)(2,1)S(1)} %get-tuple-element.166) | copy-start | bytes 327604
  161.6 11.3 %copy-start.11 = (bf16[10,14,390]{2,1,0:T(8,128)(2,1)}, bf16[10,14,390]{2,1,0:T(8,128)(2,1)S(1)}, u32[]{:S(2)}) copy-start(bf16[10,14,390]{2,1,0:T(8,128)(2,1)S(1)} %get-tuple-element.167) | copy-start | bytes 327604
  161.6 11.3 %copy-start.12 = (bf16[10,14,390]{2,1,0:T(8,128)(2,1)}, bf16[10,14,390]{2,1,0:T(8,128)(2,1)S(1)}, u32[]{:S(2)}) copy-start(bf16[10,14,390]{2,1,0:T(8,128)(2,1)S(1)} %get-tuple-element.168) | copy-start | bytes 327604
  161.6 11.3 %copy-start.13 = (bf16[10,14,390]{2,1,0:T(8,128)(2,1)}, bf16[10,14,390]{2,1,0:T(8,128)(2,1)S(1)}, u32[]{:S(2)}) copy-start(bf16[10,14,390]{2,1,0:T(8,128)(2,1)S(1)} %get-tuple-element.169) | copy-start | bytes 327604
  177.8 6.8 %collective-permute-start.4 = (f32[3,3,8,384]{3,2,1,0:T(8,128)}, f32[3,3,8,384]{3,2,1,0:T(8,128)}, u32[]{:S(2)}, u32[]{:S(2)}) collective-permute-start(f32[3,3,8,384]{3,2,1,0:T(8,128)} %get-tuple-element.235), channel_id=1, source_target_pairs={{0,4},{4,8},{8,12},{12,16},{16,20},{20,24},{24,28},{1,5},{5,9},{9,... | collective-permute-start | bytes 331784 | tf_op jit(solution)/shard_map/ppermute | solution.py:22
  182.7 6.9 %collective-permute-start.5 = (f32[3,3,8,384]{3,2,1,0:T(8,128)}, f32[3,3,8,384]{3,2,1,0:T(8,128)}, u32[]{:S(2)}, u32[]{:S(2)}) collective-permute-start(f32[3,3,8,384]{3,2,1,0:T(8,128)} %get-tuple-element.236), channel_id=1, source_target_pairs={{4,0},{8,4},{12,8},{16,12},{20,16},{24,20},{28,24},{5,1},{9,5},{13... | collective-permute-start | bytes 331784 | tf_op jit(solution)/shard_map/ppermute | solution.py:23
  191.4 3.6 collective-permute-start.6
  193.4 5.2 %collective-permute-start.7 = (f32[3,10,3,384]{3,2,1,0:T(4,128)}, f32[3,10,3,384]{3,2,1,0:T(4,128)}, u32[]{:S(2)}, u32[]{:S(2)}) collective-permute-start(f32[3,10,3,384]{3,2,1,0:T(4,128)} %get-tuple-element.232), channel_id=1, source_target_pairs={{1,0},{2,1},{3,2},{5,4},{6,5},{7,6},{9,8},{10,9},{11,10},{13,12},{... | collective-permute-start | bytes 414728 | tf_op jit(solution)/shard_map/ppermute | solution.py:23
  213.3 86.0 %copy-start.45 = (f32[1,4,8,384]{3,2,1,0:T(8,128)S(1)}, f32[1,4,8,384]{3,2,1,0:T(8,128)}, u32[]{:S(2)}) copy-start(f32[1,4,8,384]{3,2,1,0:T(8,128)} %copy-done.44) | copy-start | bytes 147460
  340.9 6.7 %collective-permute-start.8 = (f32[3,3,8,384]{3,2,1,0:T(8,128)S(1)}, f32[3,3,8,384]{3,2,1,0:T(8,128)S(1)}, u32[]{:S(2)}, u32[]{:S(2)}) collective-permute-start(f32[3,3,8,384]{3,2,1,0:T(8,128)S(1)} %get-tuple-element.233), channel_id=1, source_target_pairs={{0,4},{4,8},{8,12},{12,16},{16,20},{20,24},{24,28},{1,5},{5,9},{9,... | collective-permute-start | bytes 331784 | tf_op jit(solution)/shard_map/ppermute | solution.py:22
  345.3 6.6 %collective-permute-start.9 = (f32[3,3,8,384]{3,2,1,0:T(8,128)S(1)}, f32[3,3,8,384]{3,2,1,0:T(8,128)S(1)}, u32[]{:S(2)}, u32[]{:S(2)}) collective-permute-start(f32[3,3,8,384]{3,2,1,0:T(8,128)S(1)} %get-tuple-element.234), channel_id=1, source_target_pairs={{4,0},{8,4},{12,8},{16,12},{20,16},{24,20},{28,24},{5,1},{9,5},{13... | collective-permute-start | bytes 331784 | tf_op jit(solution)/shard_map/ppermute | solution.py:23
  352.0 2.6 collective-permute-start.10
  353.3 4.2 collective-permute-start.11
  (34 other events, 333.8 us)
where the time goes:
time: 419 us; the launch traced here: 418 us
  blocking collectives  220 us (53%)
  other arithmetic  82.3 us (20%)
  waiting for transfers between devices  64.7 us (15%)
  starting transfers between devices  27.5 us (7%)
  local copies, waits for them, and re-layouts  16.8 us (4%)
  between operations  5.72 us (1%)
    unnamed x2, blocking collectives  95.9 us
    psum x2, blocking collectives, rz_total(): return lax.psum(jnp.sum(left_vec * right_vec), ('slab', 'col'))  80.9 us
    ppermute x6, waiting for transfers between devices, with_halo(): before = lax.ppermute(last, axis, up)  49 us
    psum x1, blocking collectives, on_device(): lax.psum(jnp.sum(direction * image_vec), ('slab', 'col'))  43.5 us
    concatenate x6, other arithmetic, with_halo(): x = jnp.concatenate([before, x, after], axis=dim)  36.5 us
    another operation x6, other arithmetic, operator(): return jnp.stack(summed)  26.7 us
    ppermute x6, starting transfers between devices, with_halo(): before = lax.ppermute(last, axis, up)  19.8 us
    ppermute x6, waiting for transfers between devices, with_halo(): after = lax.ppermute(first, axis, down)  15.8 us
  transfers between devices with their start and end apart: 12, of which 7 were waited for; matrix products, arithmetic and copies ran while one was open for 1% of the time, Pallas kernels for 0%

commit v1 on v0

--- a/solution.py
+++ b/solution.py
@@ -12,17 +12,28 @@
 FOUNDATION = 1.0
 
 
-def with_halo(x, sides, width):
+def with_halo(x, sides, width, low=True, high=True):
     for axis, dim in sides:
         count, length = (lax.axis_size(axis), x.shape[dim])
         up = [(i, (i + 1) % count) for i in range(count - 1)]
         down = [(j, i) for i, j in up]
         last = lax.slice_in_dim(x, length - width, length, axis=dim)
         first = lax.slice_in_dim(x, 0, width, axis=dim)
-        before = lax.ppermute(last, axis, up)
-        after = lax.ppermute(first, axis, down)
-        x = jnp.concatenate([before, x, after], axis=dim)
+        parts = [x]
+        if low:
+            parts.insert(0, lax.ppermute(last, axis, up))
+        if high:
+            parts.append(lax.ppermute(first, axis, down))
+        x = jnp.concatenate(parts, axis=dim)
     return x
+
+
+def device_rows(vector, axes):
+    count = 1
+    for axis in axes:
+        count = count * lax.axis_size(axis)
+    tiled = jnp.broadcast_to(vector[None], (count,) + vector.shape)
+    return lax.all_to_all(tiled, axes, 0, 0, tiled=True)
 
 
 def bond_list():
@@ -85,15 +96,17 @@
     def rimmed(vector):
         return pad_depth(with_halo(vector, (("slab", 1), ("col", 2)), 3))
 
-    stacked = jnp.concatenate([integrity, contact.astype(jnp.bfloat16)[None]], axis=0)
-    spread = pad_depth(with_halo(stacked, (("slab", 1), ("col", 2)), 3))
-    contact_pad = spread[bond_count].astype(jnp.float32)
+    lower_x = with_halo(integrity, (("slab", 1),), 3, high=False)
+    spread = pad_depth(with_halo(lower_x, (("col", 2),), 3))
+    contact_pad = pad_depth(
+        with_halo(contact.astype(jnp.bfloat16), (("slab", 0), ("col", 1)), 3)
+    ).astype(jnp.float32)
     near_contact = window(contact_pad, 0, 0, 0, extent)
 
     def bond_pair(bond_index):
         shift_x, shift_y, shift_z = bond_shift(bond_index)
         weight = float(weights[bond_index])
-        level_pad = spread[bond_index]
+        level_pad = jnp.pad(spread[bond_index], ((0, 3), (0, 0), (0, 0)))
         intact = window(level_pad, 0, 0, 0, extent).astype(jnp.float32)
         prior = window(level_pad, -shift_x, -shift_y, -shift_z, extent).astype(jnp.float32)
         forward = weight * intact
@@ -149,9 +162,6 @@
         blocks = vector.reshape(3, cells_x * cells_y, aggregates, agg_depth)
         return (jnp.sum(blocks, axis=(1, 3)) / agg_cells).T.reshape(3 * aggregates)
 
-    def gathered(vector):
-        return lax.all_gather(local_means(vector), ("slab", "col"), axis=0, tiled=True)
-
     def precondition(vector, coarse):
         solved = jnp.dot(coarse_inverse, coarse, precision=lax.Precision.HIGHEST)
         spread_back = solved.reshape(aggregates, 3).T[:, None, :, None]
@@ -160,24 +170,49 @@
         ) + spread_back
         return scaled.reshape(vector.shape)
 
-    displacement = jnp.zeros_like(rhs_force)
+    every = ("slab", "col")
+
+    def total(vector):
+        return jnp.sum(device_rows(vector, every), axis=0)
+
     residual = rhs_force
-
-    def rz_total(left_vec, right_vec):
-        return lax.psum(jnp.sum(left_vec * right_vec), ("slab", "col"))
-
-    direction = precondition(residual, gathered(residual))
-    rz_now = rz_total(residual, direction)
-    for iteration in range(ITERS):
+    coarse_now = device_rows(local_means(residual), every).reshape(-1)
+    direction = precondition(residual, coarse_now)
+    image_vec = operator(direction)
+    sums = device_rows(
+        jnp.concatenate(
+            [
+                jnp.stack([jnp.sum(residual * direction), jnp.sum(direction * image_vec)]),
+                local_means(image_vec),
+            ]
+        ),
+        every,
+    )
+    rz_now = jnp.sum(sums[:, 0])
+    step_size = rz_now / jnp.sum(sums[:, 1])
+    image_means = sums[:, 2:].reshape(-1)
+    displacement = step_size * direction
+    residual = residual - step_size * image_vec
+    for iteration in range(1, ITERS):
+        coarse_now = coarse_now - step_size * image_means
+        precond_r = precondition(residual, coarse_now)
+        fresh_rz = total(jnp.sum(residual * precond_r)[None])[0]
+        direction = precond_r + fresh_rz / rz_now * direction
+        rz_now = fresh_rz
         image_vec = operator(direction)
-        step_size = rz_now / lax.psum(jnp.sum(direction * image_vec), ("slab", "col"))
+        if iteration + 1 < ITERS:
+            sums = device_rows(
+                jnp.concatenate(
+                    [jnp.sum(direction * image_vec)[None], local_means(image_vec)]
+                ),
+                every,
+            )
+            step_size = rz_now / jnp.sum(sums[:, 0])
+            image_means = sums[:, 1:].reshape(-1)
+        else:
+            step_size = rz_now / total(jnp.sum(direction * image_vec)[None])[0]
         displacement = displacement + step_size * direction
         residual = residual - step_size * image_vec
-        if iteration + 1 < ITERS:
-            precond_r = precondition(residual, gathered(residual))
-            fresh_rz = rz_total(residual, precond_r)
-            direction = precond_r + fresh_rz / rz_now * direction
-            rz_now = fresh_rz
     return (displacement, residual)
 
 

time: 419 us -> 200 us (0.48)
  blocking collectives: 220 us -> 43.2 us
  waiting for transfers between devices: 64.7 us -> 17.2 us
  starting transfers between devices: 27.5 us -> 51.2 us
  other arithmetic: 82.3 us -> 59.1 us
  local copies, waits for them, and re-layouts: 16.8 us -> 21.6 us
    psum x3 -> x0, blocking collectives: 124 us -> none  [the longest x2 80.9 us: rz_total(): return lax.psum(jnp.sum(left_vec * right_vec), ('slab', 'col'))]
    unnamed x2 -> x0, blocking collectives: 95.9 us -> none
    ppermute x12 -> x15, waiting for transfers between devices: 64.7 us -> 17.2 us  [the longest x8 15.6 us: with_halo(): parts.insert(0, lax.ppermute(last, axis, up))]
    all_to_all x0 -> x3, blocking collectives: none -> 43.2 us  [device_rows(): return lax.all_to_all(tiled, axes, 0, 0, tiled=True)]
    concatenate x7, other arithmetic: 38.4 us -> 13.6 us  [the longest x6 12.2 us: with_halo(): x = jnp.concatenate(parts, axis=dim)]
    ppermute x12 -> x15, starting transfers between devices: 27.5 us -> 47.3 us  [the longest x8 38.3 us: with_halo(): parts.insert(0, lax.ppermute(last, axis, up))]
    another operation x6 -> x3, other arithmetic: 26.7 us -> 12.5 us  [operator(): return jnp.stack(summed)]
    add x0 -> x3, other arithmetic: none -> 13.4 us  [operator(): summed[component] = summed[component] + heading[component] * stretch]
  transfers between devices with their start and end apart: 12 -> 16, of which waited for: 7 -> 7; matrix products, arithmetic and copies ran while one was open for 1% -> 7% of each run, Pallas kernels for 0% -> 0%
where the time goes in v1:
time: 200 us; the launch traced here: 199 us
  other arithmetic  59.1 us (30%)
  starting transfers between devices  51.2 us (26%)
  blocking collectives  43.2 us (22%)
  local copies, waits for them, and re-layouts  21.6 us (11%)
  waiting for transfers between devices  17.2 us (9%)
  between operations  5.95 us (3%)
    all_to_all x3, blocking collectives, device_rows(): return lax.all_to_all(tiled, axes, 0, 0, tiled=True)  43.2 us
    ppermute x8, starting transfers between devices, with_halo(): parts.insert(0, lax.ppermute(last, axis, up))  38.3 us
    ppermute x8, waiting for transfers between devices, with_halo(): parts.insert(0, lax.ppermute(last, axis, up))  15.6 us
    add x3, other arithmetic, operator(): summed[component] = summed[component] + heading[component] * stretch  13.4 us
    another operation x3, other arithmetic, operator(): return jnp.stack(summed)  12.5 us
    concatenate x6, other arithmetic, with_halo(): x = jnp.concatenate(parts, axis=dim)  12.2 us
    another operation x3, other arithmetic, on_device(): diagonal = jnp.stack(diag_list)  9.24 us
    ppermute x7, starting transfers between devices, with_halo(): parts.append(lax.ppermute(first, axis, down))  9.02 us
  transfers between devices with their start and end apart: 16, of which 7 were waited for; matrix products, arithmetic and copies ran while one was open for 7% of the time, Pallas kernels for 0%

profile of v1, /device:TPU:0, one launch (start us, length us, event | category | flops | bytes accessed | tf_op | source)
XLA Modules:
  0.0 198.6 jit_solution(1029844956520236637)
XLA Ops:
  2.0 5.9 %collective-permute-start = (bf16[61,3,8,384]{3,2,1,0:T(8,128)(2,1)S(1)}, bf16[61,3,8,384]{3,2,1,0:T(8,128)(2,1)}, u32[]{:S(2)}, u32[]{:S(2)}) collective-permute-start(bf16[61,3,8,384]{3,2,1,0:T(8,128)(2,1)S(1)} %slice.2176), channel_id=1, source_target_pairs={{0,4},{4,8},{8,12},{12,16},{16,20},{20,24},{24,28},{1,5},{5,9},{9,... | collective-permute-start | bytes 3373064 | tf_op jit(solution)/shard_map/ppermute | solution.py:24
  9.8 3.9 %all-to-all-start = ((f32[32,1,24]{2,1,0:T(1,128)}), f32[32,1,24]{2,1,0:T(1,128)S(1)}, u32[]{:S(2)}, u32[]{:S(2)}) async-start(f32[32,1,24]{2,1,0:T(1,128)} %broadcast_in_dim.11), calls=%async_computation | async-start | bytes 32768 | tf_op jit(solution)/shard_map/all_to_all | solution.py:36
  15.8 4.5 %collective-permute-start.3 = (bf16[3,8,384]{2,1,0:T(8,128)(2,1)S(1)}, bf16[3,8,384]{2,1,0:T(8,128)(2,1)S(1)}, u32[]{:S(2)}, u32[]{:S(2)}) collective-permute-start(bf16[3,8,384]{2,1,0:T(8,128)(2,1)S(1)} %get-tuple-element.236), channel_id=1, source_target_pairs={{0,4},{4,8},{8,12},{12,16},{16,20},{20,24},{24,28},{1,5},{5,9},{9,... | collective-permute-start | bytes 55304 | tf_op jit(solution)/shard_map/ppermute | solution.py:24
  20.5 11.2 %collective-permute-done = bf16[61,3,8,384]{3,2,1,0:T(8,128)(2,1)} collective-permute-done((bf16[61,3,8,384]{3,2,1,0:T(8,128)(2,1)S(1)}, bf16[61,3,8,384]{3,2,1,0:T(8,128)(2,1)}, u32[]{:S(2)}, u32[]{:S(2)}) %collective-permute-start) | collective-permute-done | bytes 1124384 | tf_op jit(solution)/shard_map/ppermute | solution.py:24
  33.0 1.7 constant_dynamic-update-slice_fusion
  39.2 4.0 %collective-permute-start.1 = (bf16[61,7,3,384]{3,0,2,1:T(8,128)(2,1)}, bf16[61,7,3,384]{3,0,2,1:T(8,128)(2,1)}, u32[]{:S(2)}, u32[]{:S(2)}) collective-permute-start(bf16[61,7,3,384]{3,0,2,1:T(8,128)(2,1)} %copy.82), channel_id=1, source_target_pairs={{0,1},{1,2},{2,3},{4,5},{5,6},{6,7},{8,9},{9,10},{10,11},{12,13},{... | collective-permute-start | bytes 2951432 | tf_op jit(solution)/shard_map/ppermute | solution.py:24
  46.1 3.0 %collective-permute-start.5 = (bf16[10,3,384]{2,1,0:T(4,128)(2,1)S(1)}, bf16[10,3,384]{2,1,0:T(4,128)(2,1)S(1)}, u32[]{:S(2)}, u32[]{:S(2)}) collective-permute-start(bf16[10,3,384]{2,1,0:T(4,128)(2,1)S(1)} %get-tuple-element.234), channel_id=1, source_target_pairs={{0,1},{1,2},{2,3},{4,5},{5,6},{6,7},{8,9},{9,10},{10,11},{12,13},{... | collective-permute-start | bytes 69128 | tf_op jit(solution)/shard_map/ppermute | solution.py:24
  50.2 2.1 %copy.85 = bf16[61,7,3,384]{3,2,1,0:T(4,128)(2,1)S(1)} copy(bf16[61,7,3,384]{3,0,2,1:T(8,128)(2,1)} %collective-permute-done.2) | data formatting | bytes 1967616 | tf_op jit(solution)/shard_map/ppermute | solution.py:26
  52.2 2.1 %copy.84 = bf16[61,7,3,384]{3,2,1,0:T(4,128)(2,1)S(1)} copy(bf16[61,7,3,384]{3,0,2,1:T(8,128)(2,1)} %collective-permute-done.1) | data formatting | bytes 1967616 | tf_op jit(solution)/shard_map/ppermute | solution.py:24
  54.3 9.8 %fusion.5 = bf16[61,7,14,390]{3,2,1,0:T(8,128)(2,1)S(1)} fusion(bf16[61,7,3,384]{3,2,1,0:T(4,128)(2,1)S(1)} %copy.85, bf16[61,7,8,384]{3,2,1,0:T(8,128)(2,1)S(1)} %constant_dynamic-update-slice_fusion, bf16[61,7,3,384]{3,2,1,0:T(4,128)(2,1)S(1)} %copy.84), kind=kLoop, calls=%fused_computation.7 | loop fusion | flops 27977040 | bytes 9253944 | tf_op jit(solution)/shard_map/concatenate | solution.py:27
  65.1 3.7 %add_bitcast_fusion.5 = (f32[1,4,8,384]{3,2,1,0:T(8,128)S(1)}, f32[4,8,384]{2,1,0:T(8,128)S(1)}, f32[4,8,384]{2,1,0:T(8,128)S(1)}, f32[4,8,384]{2,1,0:T(8,128)S(...) fusion(bf16[7,14,390]{2,1,0:T(8,128)(2,1)S(1)} %get-tuple-eleme, ...), kind=kLoop, calls=%fused_computation.2528 | loop fusion | flops 6967296 | bytes 7913472 | tf_op jit(solution)/shard_map/stack | solution.py:133
  68.8 2.3 %add_bitcast_fusion.4 = f32[1,4,8,384]{3,2,1,0:T(8,128)S(1)} fusion(f32[4,8,384]{2,1,0:T(8,128)S(1)} %get-tuple-element.135, bf16[7,14,390]{2,1,0:T(8,128)(2,1)S(1)} %get-tuple-element.212, bf16[7,14,390]{2,1,0:T(8,128)(2,1)S(1)} %get-tuple-element.207, bf16[7,14,390]{2,1,0:T(8,128)(2,1)S(1)} %get-tuple-element.206, ...), kind=kLoop, calls=%fused_computation.2527 | loop fusion | flops 5173248 | bytes 5799936 | tf_op jit(solution)/shard_map/stack | solution.py:133
  71.4 3.3 %add_bitcast_fusion.3 = f32[1,4,8,384]{3,2,1,0:T(8,128)S(1)} fusion(f32[4,8,384]{2,1,0:T(8,128)} %get-tuple-element.153, f32[4,8,384]{2,1,0:T(8,128)} %get-tuple-element.152, bf16[7,14,390]{2,1,0:T(8,128)(2,1)S(1)} %get-tuple-element.213, bf16[7,14,390]{2,1,0:T(8,128)(2,1)S(1)} %get-tuple-element.211, bf16[7,14,390]{2,1,0:T(8,128)(2,1)S(1)} %get-tuple-element.212, ...), kind=kLoop, calls=%fused_computation.2526 | loop fusion | flops 5406720 | bytes 6045696 | tf_op jit(solution)/shard_map/stack | solution.py:133
  77.9 5.1 %collective-permute-start.7 = (f32[3,3,8,384]{3,2,1,0:T(8,128)S(1)}, f32[3,3,8,384]{3,2,1,0:T(8,128)S(1)}, u32[]{:S(2)}, u32[]{:S(2)}) collective-permute-start(f32[3,3,8,384]{3,2,1,0:T(8,128)S(1)} %get-tuple-element.232), channel_id=1, source_target_pairs={{0,4},{4,8},{8,12},{12,16},{16,20},{20,24},{24,28},{1,5},{5,9},{9,... | collective-permute-start | bytes 331784 | tf_op jit(solution)/shard_map/ppermute | solution.py:24
  83.8 1.6 collective-permute-done.7
  87.6 8.1 %collective-permute-start.9 = (f32[3,10,3,384]{3,2,1,0:T(4,128)}, f32[3,10,3,384]{3,2,1,0:T(4,128)}, u32[]{:S(2)}, u32[]{:S(2)}) collective-permute-start(f32[3,10,3,384]{3,2,1,0:T(4,128)} %get-tuple-element.228), channel_id=1, source_target_pairs={{0,1},{1,2},{2,3},{4,5},{5,6},{6,7},{8,9},{9,10},{10,11},{12,13},{... | collective-permute-start | bytes 414728 | tf_op jit(solution)/shard_map/ppermute | solution.py:24
  96.7 1.8 select_maximum_fusion.4
  98.5 11.9 %add_add_fusion.2 = (f32[4,8,384]{2,1,0:T(8,128)S(1)}, f32[4,8,384]{2,1,0:T(8,128)S(1)}, f32[4,8,384]{2,1,0:T(8,128)S(1)}, f32[4,8,384]{2,1,0:T(8,128)S(1)}, f32...) fusion(f32[4,8,384]{2,1,0:T(8,128)S(1)} %copy-done.50, ...), kind=kLoop, calls=%fused_computation.2525 | loop fusion | flops 18382848 | bytes 27181056 | tf_op jit(solution)/shard_map/add | solution.py:158
  117.6 20.3 %all_to_all.27 = f32[32,1,26]{2,1,0:T(1,128)S(1)} all-to-all(f32[32,1,26]{2,1,0:T(1,128)S(1)} %broadcast_in_dim.12), channel_id=1, replica_groups=mesh['slab'=8,'col'=4] {'slab','col'}, dimensions={0} | all-to-all | bytes 6656 | tf_op jit(solution)/shard_map/all_to_all | solution.py:36
  142.7 8.8 %all_to_all.28 = f32[32,1,1]{2,1,0:T(1,128)S(1)} all-to-all(f32[32,1,1]{2,1,0:T(1,128)S(1)} %broadcast_in_dim.13), channel_id=1, replica_groups=mesh['slab'=8,'col'=4] {'slab','col'}, dimensions={0} | all-to-all | bytes 256 | tf_op jit(solution)/shard_map/all_to_all | solution.py:36
  154.9 4.6 %collective-permute-start.11 = (f32[3,3,8,384]{3,2,1,0:T(8,128)S(1)}, f32[3,3,8,384]{3,2,1,0:T(8,128)S(1)}, u32[]{:S(2)}, u32[]{:S(2)}) collective-permute-start(f32[3,3,8,384]{3,2,1,0:T(8,128)S(1)} %get-tuple-element.230), channel_id=1, source_target_pairs={{0,4},{4,8},{8,12},{12,16},{16,20},{20,24},{24,28},{1,5},{5,9},{9,... | collective-permute-start | bytes 331784 | tf_op jit(solution)/shard_map/ppermute | solution.py:24
  163.2 3.0 %collective-permute-start.13 = (f32[3,10,3,384]{3,2,1,0:T(4,128)S(1)}, f32[3,10,3,384]{3,2,1,0:T(4,128)S(1)}, u32[]{:S(2)}, u32[]{:S(2)}) collective-permute-start(f32[3,10,3,384]{3,2,1,0:T(4,128)S(1)} %get-tuple-element.226), channel_id=1, source_target_pairs={{0,1},{1,2},{2,3},{4,5},{5,6},{6,7},{8,9},{9,10},{10,11},{12,13},{... | collective-permute-start | bytes 414728 | tf_op jit(solution)/shard_map/ppermute | solution.py:24
  168.0 11.8 %add_bitcast_fusion.2 = (f32[1,4,8,384]{3,2,1,0:T(8,128)S(1)}, f32[4,8,384]{2,1,0:T(8,128)S(1)}, f32[4,8,384]{2,1,0:T(8,128)S(1)}, f32[4,8,384]{2,1,0:T(8,128)S(...) fusion(f32[3,4,8,384]{3,2,1,0:T(8,128)S(1)} %multiply_add_fusio, ...), kind=kLoop, calls=%fused_computation.2522 | loop fusion | flops 18382848 | bytes 27181056 | tf_op jit(solution)/shard_map/stack | solution.py:159
  181.8 14.1 %all_to_all.29 = f32[32,1,1]{2,1,0:T(1,128)S(1)} all-to-all(f32[32,1,1]{2,1,0:T(1,128)S(1)} %broadcast_in_dim.14), channel_id=1, replica_groups=mesh['slab'=8,'col'=4] {'slab','col'}, dimensions={0} | all-to-all | bytes 256 | tf_op jit(solution)/shard_map/all_to_all | solution.py:36
  (205 shorter events, 44.2 us)
Async XLA Ops:
  2.0 29.7 %collective-permute-start = (bf16[61,3,8,384]{3,2,1,0:T(8,128)(2,1)S(1)}, bf16[61,3,8,384]{3,2,1,0:T(8,128)(2,1)}, u32[]{:S(2)}, u32[]{:S(2)}) collective-permute-start(bf16[61,3,8,384]{3,2,1,0:T(8,128)(2,1)S(1)} %slice.2176), channel_id=1, source_target_pairs={{0,4},{4,8},{8,12},{12,16},{16,20},{20,24},{24,28},{1,5},{5,9},{9,... | collective-permute-start | bytes 3373064 | tf_op jit(solution)/shard_map/ppermute | solution.py:24
  9.8 33.6 %all-to-all-start = ((f32[32,1,24]{2,1,0:T(1,128)}), f32[32,1,24]{2,1,0:T(1,128)S(1)}, u32[]{:S(2)}, u32[]{:S(2)}) async-start(f32[32,1,24]{2,1,0:T(1,128)} %broadcast_in_dim.11), calls=%async_computation | async-start | bytes 32768 | tf_op jit(solution)/shard_map/all_to_all | solution.py:36
  14.5 30.2 %collective-permute-start.4 = (bf16[3,8,384]{2,1,0:T(8,128)(2,1)S(1)}, bf16[3,8,384]{2,1,0:T(8,128)(2,1)S(1)}, u32[]{:S(2)}, u32[]{:S(2)}) collective-permute-start(bf16[3,8,384]{2,1,0:T(8,128)(2,1)S(1)} %get-tuple-element.237), channel_id=1, source_target_pairs={{4,0},{8,4},{12,8},{16,12},{20,16},{24,20},{28,24},{5,1},{9,5},{13... | collective-permute-start | bytes 55304 | tf_op jit(solution)/shard_map/ppermute | solution.py:26
  15.8 28.9 %collective-permute-start.3 = (bf16[3,8,384]{2,1,0:T(8,128)(2,1)S(1)}, bf16[3,8,384]{2,1,0:T(8,128)(2,1)S(1)}, u32[]{:S(2)}, u32[]{:S(2)}) collective-permute-start(bf16[3,8,384]{2,1,0:T(8,128)(2,1)S(1)} %get-tuple-element.236), channel_id=1, source_target_pairs={{0,4},{4,8},{8,12},{12,16},{16,20},{20,24},{24,28},{1,5},{5,9},{9,... | collective-permute-start | bytes 55304 | tf_op jit(solution)/shard_map/ppermute | solution.py:24
  36.8 13.4 %collective-permute-start.2 = (bf16[61,7,3,384]{3,0,2,1:T(8,128)(2,1)}, bf16[61,7,3,384]{3,0,2,1:T(8,128)(2,1)}, u32[]{:S(2)}, u32[]{:S(2)}) collective-permute-start(bf16[61,7,3,384]{3,0,2,1:T(8,128)(2,1)} %copy.83), channel_id=1, source_target_pairs={{1,0},{2,1},{3,2},{5,4},{6,5},{7,6},{9,8},{10,9},{11,10},{13,12},{... | collective-permute-start | bytes 2951432 | tf_op jit(solution)/shard_map/ppermute | solution.py:26
  39.2 13.0 %collective-permute-start.1 = (bf16[61,7,3,384]{3,0,2,1:T(8,128)(2,1)}, bf16[61,7,3,384]{3,0,2,1:T(8,128)(2,1)}, u32[]{:S(2)}, u32[]{:S(2)}) collective-permute-start(bf16[61,7,3,384]{3,0,2,1:T(8,128)(2,1)} %copy.82), channel_id=1, source_target_pairs={{0,1},{1,2},{2,3},{4,5},{5,6},{6,7},{8,9},{9,10},{10,11},{12,13},{... | collective-permute-start | bytes 2951432 | tf_op jit(solution)/shard_map/ppermute | solution.py:24
  43.4 20.7 %copy-start.45 = (f32[8,3,768]{2,1,0:T(4,128)}, f32[8,3,768]{2,1,0:T(4,128)S(1)}, u32[]{:S(2)}) copy-start(f32[8,3,768]{2,1,0:T(4,128)S(1)} %dot_general.8) | copy-start | bytes 221188
  44.8 4.8 %collective-permute-start.6 = (bf16[10,3,384]{2,1,0:T(4,128)(2,1)S(1)}, bf16[10,3,384]{2,1,0:T(4,128)(2,1)S(1)}, u32[]{:S(2)}, u32[]{:S(2)}) collective-permute-start(bf16[10,3,384]{2,1,0:T(4,128)(2,1)S(1)} %get-tuple-element.235), channel_id=1, source_target_pairs={{1,0},{2,1},{3,2},{5,4},{6,5},{7,6},{9,8},{10,9},{11,10},{13,12},{... | collective-permute-start | bytes 69128 | tf_op jit(solution)/shard_map/ppermute | solution.py:26
  46.1 3.9 %collective-permute-start.5 = (bf16[10,3,384]{2,1,0:T(4,128)(2,1)S(1)}, bf16[10,3,384]{2,1,0:T(4,128)(2,1)S(1)}, u32[]{:S(2)}, u32[]{:S(2)}) collective-permute-start(bf16[10,3,384]{2,1,0:T(4,128)(2,1)S(1)} %get-tuple-element.234), channel_id=1, source_target_pairs={{0,1},{1,2},{2,3},{4,5},{5,6},{6,7},{8,9},{9,10},{10,11},{12,13},{... | collective-permute-start | bytes 69128 | tf_op jit(solution)/shard_map/ppermute | solution.py:24
  76.6 7.2 %collective-permute-start.8 = (f32[3,3,8,384]{3,2,1,0:T(8,128)S(1)}, f32[3,3,8,384]{3,2,1,0:T(8,128)S(1)}, u32[]{:S(2)}, u32[]{:S(2)}) collective-permute-start(f32[3,3,8,384]{3,2,1,0:T(8,128)S(1)} %get-tuple-element.233), channel_id=1, source_target_pairs={{4,0},{8,4},{12,8},{16,12},{20,16},{24,20},{28,24},{5,1},{9,5},{13... | collective-permute-start | bytes 331784 | tf_op jit(solution)/shard_map/ppermute | solution.py:26
  77.9 7.5 %collective-permute-start.7 = (f32[3,3,8,384]{3,2,1,0:T(8,128)S(1)}, f32[3,3,8,384]{3,2,1,0:T(8,128)S(1)}, u32[]{:S(2)}, u32[]{:S(2)}) collective-permute-start(f32[3,3,8,384]{3,2,1,0:T(8,128)S(1)} %get-tuple-element.232), channel_id=1, source_target_pairs={{0,4},{4,8},{8,12},{12,16},{16,20},{20,24},{24,28},{1,5},{5,9},{9,... | collective-permute-start | bytes 331784 | tf_op jit(solution)/shard_map/ppermute | solution.py:24
  83.8 11.9 %copy-start.47 = (f32[3,3,8,384]{3,2,1,0:T(8,128)}, f32[3,3,8,384]{3,2,1,0:T(8,128)S(1)}, u32[]{:S(2)}) copy-start(f32[3,3,8,384]{3,2,1,0:T(8,128)S(1)} %collective-permute-done.8) | copy-start | bytes 331780
  85.4 10.3 %copy-start.48 = (f32[3,3,8,384]{3,2,1,0:T(8,128)}, f32[3,3,8,384]{3,2,1,0:T(8,128)S(1)}, u32[]{:S(2)}) copy-start(f32[3,3,8,384]{3,2,1,0:T(8,128)S(1)} %collective-permute-done.7) | copy-start | bytes 331780
  86.3 10.3 %collective-permute-start.10 = (f32[3,10,3,384]{3,2,1,0:T(4,128)}, f32[3,10,3,384]{3,2,1,0:T(4,128)}, u32[]{:S(2)}, u32[]{:S(2)}) collective-permute-start(f32[3,10,3,384]{3,2,1,0:T(4,128)} %get-tuple-element.229), channel_id=1, source_target_pairs={{1,0},{2,1},{3,2},{5,4},{6,5},{7,6},{9,8},{10,9},{11,10},{13,12},{... | collective-permute-start | bytes 414728 | tf_op jit(solution)/shard_map/ppermute | solution.py:26
  87.6 9.1 %collective-permute-start.9 = (f32[3,10,3,384]{3,2,1,0:T(4,128)}, f32[3,10,3,384]{3,2,1,0:T(4,128)}, u32[]{:S(2)}, u32[]{:S(2)}) collective-permute-start(f32[3,10,3,384]{3,2,1,0:T(4,128)} %get-tuple-element.228), channel_id=1, source_target_pairs={{0,1},{1,2},{2,3},{4,5},{5,6},{6,7},{8,9},{9,10},{10,11},{12,13},{... | collective-permute-start | bytes 414728 | tf_op jit(solution)/shard_map/ppermute | solution.py:24
  96.6 13.7 %copy-start.49 = (f32[4,8,384]{2,1,0:T(8,128)}, f32[4,8,384]{2,1,0:T(8,128)S(1)}, u32[]{:S(2)}) copy-start(f32[4,8,384]{2,1,0:T(8,128)S(1)} %squeeze.209) | copy-start | bytes 147460
  110.4 29.7 %copy-start.46 = (f32[8,3,768]{2,1,0:T(4,128)S(1)}, f32[8,3,768]{2,1,0:T(4,128)}, u32[]{:S(2)}) copy-start(f32[8,3,768]{2,1,0:T(4,128)} %copy-done.45) | copy-start | bytes 221188
  110.4 30.2 %copy-start.39 = (f32[1,4,8,384]{3,2,1,0:T(8,128)S(1)}, f32[1,4,8,384]{3,2,1,0:T(8,128)}, u32[]{:S(2)}) copy-start(f32[1,4,8,384]{3,2,1,0:T(8,128)} %copy-done.38) | copy-start | bytes 147460
  110.4 30.2 %copy-start.41 = (f32[1,4,8,384]{3,2,1,0:T(8,128)S(1)}, f32[1,4,8,384]{3,2,1,0:T(8,128)}, u32[]{:S(2)}) copy-start(f32[1,4,8,384]{3,2,1,0:T(8,128)} %copy-done.40) | copy-start | bytes 147460
  110.4 30.2 %copy-start.43 = (f32[1,4,8,384]{3,2,1,0:T(8,128)S(1)}, f32[1,4,8,384]{3,2,1,0:T(8,128)}, u32[]{:S(2)}) copy-start(f32[1,4,8,384]{3,2,1,0:T(8,128)} %copy-done.42) | copy-start | bytes 147460
  153.6 6.7 %collective-permute-start.12 = (f32[3,3,8,384]{3,2,1,0:T(8,128)S(1)}, f32[3,3,8,384]{3,2,1,0:T(8,128)S(1)}, u32[]{:S(2)}, u32[]{:S(2)}) collective-permute-start(f32[3,3,8,384]{3,2,1,0:T(8,128)S(1)} %get-tuple-element.231), channel_id=1, source_target_pairs={{4,0},{8,4},{12,8},{16,12},{20,16},{24,20},{28,24},{5,1},{9,5},{13... | collective-permute-start | bytes 331784 | tf_op jit(solution)/shard_map/ppermute | solution.py:26
  154.9 6.9 %collective-permute-start.11 = (f32[3,3,8,384]{3,2,1,0:T(8,128)S(1)}, f32[3,3,8,384]{3,2,1,0:T(8,128)S(1)}, u32[]{:S(2)}, u32[]{:S(2)}) collective-permute-start(f32[3,3,8,384]{3,2,1,0:T(8,128)S(1)} %get-tuple-element.230), channel_id=1, source_target_pairs={{0,4},{4,8},{8,12},{12,16},{16,20},{20,24},{24,28},{1,5},{5,9},{9,... | collective-permute-start | bytes 331784 | tf_op jit(solution)/shard_map/ppermute | solution.py:24
  161.9 4.4 %collective-permute-start.14 = (f32[3,10,3,384]{3,2,1,0:T(4,128)S(1)}, f32[3,10,3,384]{3,2,1,0:T(4,128)S(1)}, u32[]{:S(2)}, u32[]{:S(2)}) collective-permute-start(f32[3,10,3,384]{3,2,1,0:T(4,128)S(1)} %get-tuple-element.227), channel_id=1, source_target_pairs={{1,0},{2,1},{3,2},{5,4},{6,5},{7,6},{9,8},{10,9},{11,10},{13,12},{... | collective-permute-start | bytes 414728 | tf_op jit(solution)/shard_map/ppermute | solution.py:26
  163.2 4.1 %collective-permute-start.13 = (f32[3,10,3,384]{3,2,1,0:T(4,128)S(1)}, f32[3,10,3,384]{3,2,1,0:T(4,128)S(1)}, u32[]{:S(2)}, u32[]{:S(2)}) collective-permute-start(f32[3,10,3,384]{3,2,1,0:T(4,128)S(1)} %get-tuple-element.226), channel_id=1, source_target_pairs={{0,1},{1,2},{2,3},{4,5},{5,6},{6,7},{8,9},{9,10},{10,11},{12,13},{... | collective-permute-start | bytes 414728 | tf_op jit(solution)/shard_map/ppermute | solution.py:24
  (44 other events, 271.7 us)

commit v2 on v1

--- a/solution.py
+++ b/solution.py
@@ -172,9 +172,6 @@
 
     every = ("slab", "col")
 
-    def total(vector):
-        return jnp.sum(device_rows(vector, every), axis=0)
-
     residual = rhs_force
     coarse_now = device_rows(local_means(residual), every).reshape(-1)
     direction = precondition(residual, coarse_now)
@@ -189,28 +186,42 @@
         every,
     )
     rz_now = jnp.sum(sums[:, 0])
-    step_size = rz_now / jnp.sum(sums[:, 1])
+    curvature = jnp.sum(sums[:, 1])
+    step_size = rz_now / curvature
     image_means = sums[:, 2:].reshape(-1)
     displacement = step_size * direction
     residual = residual - step_size * image_vec
     for iteration in range(1, ITERS):
+        more = iteration + 1 < ITERS
         coarse_now = coarse_now - step_size * image_means
         precond_r = precondition(residual, coarse_now)
-        fresh_rz = total(jnp.sum(residual * precond_r)[None])[0]
-        direction = precond_r + fresh_rz / rz_now * direction
+        image_z = operator(precond_r)
+        parts = [
+            jnp.stack(
+                [
+                    jnp.sum(residual * precond_r),
+                    jnp.sum(precond_r * image_z),
+                    jnp.sum(precond_r * image_vec),
+                    jnp.sum(direction * image_z),
+                ]
+            )
+        ]
+        if more:
+            parts.append(local_means(image_z))
+        sums = device_rows(jnp.concatenate(parts), every)
+        fresh_rz = jnp.sum(sums[:, 0])
+        ratio = fresh_rz / rz_now
+        curvature = (
+            jnp.sum(sums[:, 1])
+            + ratio * (jnp.sum(sums[:, 2]) + jnp.sum(sums[:, 3]))
+            + ratio * ratio * curvature
+        )
         rz_now = fresh_rz
-        image_vec = operator(direction)
-        if iteration + 1 < ITERS:
-            sums = device_rows(
-                jnp.concatenate(
-                    [jnp.sum(direction * image_vec)[None], local_means(image_vec)]
-                ),
-                every,
-            )
-            step_size = rz_now / jnp.sum(sums[:, 0])
-            image_means = sums[:, 1:].reshape(-1)
-        else:
-            step_size = rz_now / total(jnp.sum(direction * image_vec)[None])[0]
+        direction = precond_r + ratio * direction
+        image_vec = image_z + ratio * image_vec
+        step_size = rz_now / curvature
+        if more:
+            image_means = sums[:, 4:].reshape(-1) + ratio * image_means
         displacement = displacement + step_size * direction
         residual = residual - step_size * image_vec
     return (displacement, residual)

time: 200 us -> 197 us (0.985)
  blocking collectives: 43.2 us -> 34 us
  other arithmetic: 59.1 us -> 63.4 us
    all_to_all x3 -> x2, blocking collectives: 43.2 us -> 34 us  [device_rows(): return lax.all_to_all(tiled, axes, 0, 0, tiled=True)]
    another operation x0 -> x1, other arithmetic: none -> 2.58 us  [on_device(): jnp.stack([jnp.sum(residual * precond_r), jnp.sum(precond_r * image_z), j...]
    add x2 -> x4, other arithmetic: 0.79 us -> 3.27 us  [precondition(): (vector / diagonal).reshape(3, cells_x * cells_y, aggregates, agg_depth)]
    reduce_sum x5 -> x3, other arithmetic: 4.04 us -> 2.09 us  [the longest x1 0.76 us: on_device(): curvature = jnp.sum(sums[:, 1])]
  transfers between devices with their start and end apart: 16 -> 16, of which waited for: 7 -> 6; matrix products, arithmetic and copies ran while one was open for 7% -> 8% of each run, Pallas kernels for 0% -> 0%
where the time goes in v2:
time: 197 us; the launch traced here: 195 us
  other arithmetic  63.4 us (32%)
  starting transfers between devices  51.8 us (26%)
  blocking collectives  34 us (17%)
  local copies, waits for them, and re-layouts  21.8 us (11%)
  waiting for transfers between devices  16.1 us (8%)
  between operations  7.59 us (4%)
    ppermute x8, starting transfers between devices, with_halo(): parts.insert(0, lax.ppermute(last, axis, up))  38.7 us
    all_to_all x2, blocking collectives, device_rows(): return lax.all_to_all(tiled, axes, 0, 0, tiled=True)  34 us
    ppermute x8, waiting for transfers between devices, with_halo(): parts.insert(0, lax.ppermute(last, axis, up))  14.6 us
    concatenate x6, other arithmetic, with_halo(): x = jnp.concatenate(parts, axis=dim)  13.3 us
    another operation x3, other arithmetic, operator(): return jnp.stack(summed)  12.7 us
    add x3, other arithmetic, operator(): summed[component] = summed[component] + heading[component] * stretch  12.5 us
    another operation x3, other arithmetic, on_device(): diagonal = jnp.stack(diag_list)  11 us
    ppermute x7, starting transfers between devices, with_halo(): parts.append(lax.ppermute(first, axis, down))  9.23 us
  transfers between devices with their start and end apart: 16, of which 6 were waited for; matrix products, arithmetic and copies ran while one was open for 8% of the time, Pallas kernels for 0%

profile of v2, /device:TPU:0, one launch (start us, length us, event | category | flops | bytes accessed | tf_op | source)
XLA Modules:
  0.0 195.1 jit_solution(9426635662257751885)
XLA Ops:
  2.0 5.9 %collective-permute-start = (bf16[61,3,8,384]{3,2,1,0:T(8,128)(2,1)S(1)}, bf16[61,3,8,384]{3,2,1,0:T(8,128)(2,1)}, u32[]{:S(2)}, u32[]{:S(2)}) collective-permute-start(bf16[61,3,8,384]{3,2,1,0:T(8,128)(2,1)S(1)} %slice.2187), channel_id=1, source_target_pairs={{0,4},{4,8},{8,12},{12,16},{16,20},{20,24},{24,28},{1,5},{5,9},{9,... | collective-permute-start | bytes 3373064 | tf_op jit(solution)/shard_map/ppermute | solution.py:24
  9.8 3.9 %all-to-all-start = ((f32[32,1,24]{2,1,0:T(1,128)}), f32[32,1,24]{2,1,0:T(1,128)S(1)}, u32[]{:S(2)}, u32[]{:S(2)}) async-start(f32[32,1,24]{2,1,0:T(1,128)} %broadcast_in_dim.9), calls=%async_computation | async-start | bytes 32768 | tf_op jit(solution)/shard_map/all_to_all | solution.py:36
  15.8 4.5 %collective-permute-start.3 = (bf16[3,8,384]{2,1,0:T(8,128)(2,1)S(1)}, bf16[3,8,384]{2,1,0:T(8,128)(2,1)S(1)}, u32[]{:S(2)}, u32[]{:S(2)}) collective-permute-start(bf16[3,8,384]{2,1,0:T(8,128)(2,1)S(1)} %get-tuple-element.247), channel_id=1, source_target_pairs={{0,4},{4,8},{8,12},{12,16},{16,20},{20,24},{24,28},{1,5},{5,9},{9,... | collective-permute-start | bytes 55304 | tf_op jit(solution)/shard_map/ppermute | solution.py:24
  20.5 11.2 %collective-permute-done = bf16[61,3,8,384]{3,2,1,0:T(8,128)(2,1)} collective-permute-done((bf16[61,3,8,384]{3,2,1,0:T(8,128)(2,1)S(1)}, bf16[61,3,8,384]{3,2,1,0:T(8,128)(2,1)}, u32[]{:S(2)}, u32[]{:S(2)}) %collective-permute-start) | collective-permute-done | bytes 1124384 | tf_op jit(solution)/shard_map/ppermute | solution.py:24
  33.0 1.7 constant_dynamic-update-slice_fusion
  39.2 4.0 %collective-permute-start.1 = (bf16[61,7,3,384]{3,0,2,1:T(8,128)(2,1)}, bf16[61,7,3,384]{3,0,2,1:T(8,128)(2,1)}, u32[]{:S(2)}, u32[]{:S(2)}) collective-permute-start(bf16[61,7,3,384]{3,0,2,1:T(8,128)(2,1)} %copy.78), channel_id=1, source_target_pairs={{0,1},{1,2},{2,3},{4,5},{5,6},{6,7},{8,9},{9,10},{10,11},{12,13},{... | collective-permute-start | bytes 2951432 | tf_op jit(solution)/shard_map/ppermute | solution.py:24
  46.1 3.0 %collective-permute-start.5 = (bf16[10,3,384]{2,1,0:T(4,128)(2,1)S(1)}, bf16[10,3,384]{2,1,0:T(4,128)(2,1)S(1)}, u32[]{:S(2)}, u32[]{:S(2)}) collective-permute-start(bf16[10,3,384]{2,1,0:T(4,128)(2,1)S(1)} %get-tuple-element.245), channel_id=1, source_target_pairs={{0,1},{1,2},{2,3},{4,5},{5,6},{6,7},{8,9},{9,10},{10,11},{12,13},{... | collective-permute-start | bytes 69128 | tf_op jit(solution)/shard_map/ppermute | solution.py:24
  50.2 2.1 %copy.81 = bf16[61,7,3,384]{3,2,1,0:T(4,128)(2,1)S(1)} copy(bf16[61,7,3,384]{3,0,2,1:T(8,128)(2,1)} %collective-permute-done.2) | data formatting | bytes 1967616 | tf_op jit(solution)/shard_map/ppermute | solution.py:26
  52.3 2.1 %copy.80 = bf16[61,7,3,384]{3,2,1,0:T(4,128)(2,1)S(1)} copy(bf16[61,7,3,384]{3,0,2,1:T(8,128)(2,1)} %collective-permute-done.1) | data formatting | bytes 1967616 | tf_op jit(solution)/shard_map/ppermute | solution.py:24
  54.3 9.8 %fusion.5 = bf16[61,7,14,390]{3,2,1,0:T(8,128)(2,1)S(1)} fusion(bf16[61,7,3,384]{3,2,1,0:T(4,128)(2,1)S(1)} %copy.81, bf16[61,7,8,384]{3,2,1,0:T(8,128)(2,1)S(1)} %constant_dynamic-update-slice_fusion, bf16[61,7,3,384]{3,2,1,0:T(4,128)(2,1)S(1)} %copy.80), kind=kLoop, calls=%fused_computation.7 | loop fusion | flops 27977040 | bytes 9253944 | tf_op jit(solution)/shard_map/concatenate | solution.py:27
  65.8 4.7 %add_bitcast_fusion.5 = (f32[1,4,8,384]{3,2,1,0:T(8,128)}, f32[4,8,384]{2,1,0:T(8,128)S(1)}, f32[4,8,384]{2,1,0:T(8,128)S(1)}, f32[4,8,384]{2,1,0:T(8,128)S(1)},...) fusion(bf16[7,14,390]{2,1,0:T(8,128)(2,1)S(1)} %get-tuple-eleme, ...), kind=kLoop, calls=%fused_computation.2528 | loop fusion | flops 6967296 | bytes 7913472 | tf_op jit(solution)/shard_map/stack | solution.py:133
  70.5 2.9 %add_bitcast_fusion.4 = f32[1,4,8,384]{3,2,1,0:T(8,128)} fusion(f32[4,8,384]{2,1,0:T(8,128)S(1)} %get-tuple-element.143, bf16[7,14,390]{2,1,0:T(8,128)(2,1)S(1)} %get-tuple-element.220, bf16[7,14,390]{2,1,0:T(8,128)(2,1)S(1)} %get-tuple-element.215, bf16[7,14,390]{2,1,0:T(8,128)(2,1)S(1)} %get-tuple-element.214, ...), kind=kLoop, calls=%fused_computation.2527 | loop fusion | flops 5173248 | bytes 5799936 | tf_op jit(solution)/shard_map/stack | solution.py:133
  73.7 3.4 %add_bitcast_fusion.3 = f32[1,4,8,384]{3,2,1,0:T(8,128)S(1)} fusion(f32[4,8,384]{2,1,0:T(8,128)} %get-tuple-element.161, f32[4,8,384]{2,1,0:T(8,128)S(1)} %get-tuple-element.160, bf16[7,14,390]{2,1,0:T(8,128)(2,1)} %get-tuple-element.221, bf16[7,14,390]{2,1,0:T(8,128)(2,1)S(1)} %get-tuple-element.219, bf16[7,14,390]{2,1,0:T(8,128)(2,1)S(1)} %get-tuple-element.220, ...), kind=kLoop, calls=%fused_computation.2526 | loop fusion | flops 5406720 | bytes 6045696 | tf_op jit(solution)/shard_map/stack | solution.py:133
  81.0 5.1 %collective-permute-start.7 = (f32[3,3,8,384]{3,2,1,0:T(8,128)S(1)}, f32[3,3,8,384]{3,2,1,0:T(8,128)S(1)}, u32[]{:S(2)}, u32[]{:S(2)}) collective-permute-start(f32[3,3,8,384]{3,2,1,0:T(8,128)S(1)} %get-tuple-element.243), channel_id=1, source_target_pairs={{0,4},{4,8},{8,12},{12,16},{16,20},{20,24},{24,28},{1,5},{5,9},{9,... | collective-permute-start | bytes 331784 | tf_op jit(solution)/shard_map/ppermute | solution.py:24
  90.9 7.8 %collective-permute-start.9 = (f32[3,10,3,384]{3,2,1,0:T(4,128)}, f32[3,10,3,384]{3,2,1,0:T(4,128)}, u32[]{:S(2)}, u32[]{:S(2)}) collective-permute-start(f32[3,10,3,384]{3,2,1,0:T(4,128)} %get-tuple-element.239), channel_id=1, source_target_pairs={{0,1},{1,2},{2,3},{4,5},{5,6},{6,7},{8,9},{9,10},{10,11},{12,13},{... | collective-permute-start | bytes 414728 | tf_op jit(solution)/shard_map/ppermute | solution.py:24
  99.8 1.8 select_maximum_fusion.4
  101.7 11.9 %add_add_fusion.2 = (f32[4,8,384]{2,1,0:T(8,128)S(1)}, f32[4,8,384]{2,1,0:T(8,128)S(1)}, f32[4,8,384]{2,1,0:T(8,128)S(1)}, f32[4,8,384]{2,1,0:T(8,128)S(1)}, f32...) fusion(f32[4,8,384]{2,1,0:T(8,128)S(1)} %copy-done.48, ...), kind=kLoop, calls=%fused_computation.2525 | loop fusion | flops 18382848 | bytes 27181056 | tf_op jit(solution)/shard_map/add | solution.py:158
  116.9 20.3 %all_to_all.24 = f32[32,1,26]{2,1,0:T(1,128)S(1)} all-to-all(f32[32,1,26]{2,1,0:T(1,128)S(1)} %broadcast_in_dim.10), channel_id=1, replica_groups=mesh['slab'=8,'col'=4] {'slab','col'}, dimensions={0} | all-to-all | bytes 6656 | tf_op jit(solution)/shard_map/all_to_all | solution.py:36
  143.8 4.6 %collective-permute-start.11 = (f32[3,3,8,384]{3,2,1,0:T(8,128)S(1)}, f32[3,3,8,384]{3,2,1,0:T(8,128)S(1)}, u32[]{:S(2)}, u32[]{:S(2)}) collective-permute-start(f32[3,3,8,384]{3,2,1,0:T(8,128)S(1)} %get-tuple-element.241), channel_id=1, source_target_pairs={{0,4},{4,8},{8,12},{12,16},{16,20},{20,24},{24,28},{1,5},{5,9},{9,... | collective-permute-start | bytes 331784 | tf_op jit(solution)/shard_map/ppermute | solution.py:24
  152.8 3.7 %collective-permute-start.13 = (f32[3,10,3,384]{3,2,1,0:T(4,128)}, f32[3,10,3,384]{3,2,1,0:T(4,128)}, u32[]{:S(2)}, u32[]{:S(2)}) collective-permute-start(f32[3,10,3,384]{3,2,1,0:T(4,128)} %get-tuple-element.237), channel_id=1, source_target_pairs={{0,1},{1,2},{2,3},{4,5},{5,6},{6,7},{8,9},{9,10},{10,11},{12,13},{... | collective-permute-start | bytes 414728 | tf_op jit(solution)/shard_map/ppermute | solution.py:24
  157.6 1.8 select_maximum_fusion
  159.4 12.1 %add_bitcast_fusion.2 = (f32[1,4,8,384]{3,2,1,0:T(8,128)S(1)}, f32[4,8,384]{2,1,0:T(8,128)S(1)}, f32[4,8,384]{2,1,0:T(8,128)S(1)}, f32[4,8,384]{2,1,0:T(8,128)S(...) fusion(f32[4,8,384]{2,1,0:T(8,128)S(1)} %copy-done.47, ...), kind=kLoop, calls=%fused_computation.2522 | loop fusion | flops 18382848 | bytes 27181056 | tf_op jit(solution)/shard_map/stack | solution.py:159
  172.9 2.6 %pad_maximum_fusion.7 = f32[4]{0:T(128)S(1)} fusion(f32[1]{0:T(128)} %bitcast.91, f32[1]{0:T(128)} %bitcast.90, f32[1]{0:T(128)} %bitcast.89, f32[1]{0:T(128)} %bitcast.81), kind=kLoop, calls=%fused_computation.2651 | loop fusion | flops 12 | bytes 32 | tf_op jit(solution)/shard_map/stack | solution.py:200
  175.4 13.8 %all_to_all.25 = f32[32,1,4]{2,1,0:T(1,128)S(1)} all-to-all(f32[32,1,4]{2,1,0:T(1,128)S(1)} %broadcast_in_dim.11), channel_id=1, replica_groups=mesh['slab'=8,'col'=4] {'slab','col'}, dimensions={0} | all-to-all | bytes 1024 | tf_op jit(solution)/shard_map/all_to_all | solution.py:36
  (205 shorter events, 43.1 us)
Async XLA Ops:
  2.0 29.7 %collective-permute-start = (bf16[61,3,8,384]{3,2,1,0:T(8,128)(2,1)S(1)}, bf16[61,3,8,384]{3,2,1,0:T(8,128)(2,1)}, u32[]{:S(2)}, u32[]{:S(2)}) collective-permute-start(bf16[61,3,8,384]{3,2,1,0:T(8,128)(2,1)S(1)} %slice.2187), channel_id=1, source_target_pairs={{0,4},{4,8},{8,12},{12,16},{16,20},{20,24},{24,28},{1,5},{5,9},{9,... | collective-permute-start | bytes 3373064 | tf_op jit(solution)/shard_map/ppermute | solution.py:24
  9.8 33.6 %all-to-all-start = ((f32[32,1,24]{2,1,0:T(1,128)}), f32[32,1,24]{2,1,0:T(1,128)S(1)}, u32[]{:S(2)}, u32[]{:S(2)}) async-start(f32[32,1,24]{2,1,0:T(1,128)} %broadcast_in_dim.9), calls=%async_computation | async-start | bytes 32768 | tf_op jit(solution)/shard_map/all_to_all | solution.py:36
  14.5 30.2 %collective-permute-start.4 = (bf16[3,8,384]{2,1,0:T(8,128)(2,1)S(1)}, bf16[3,8,384]{2,1,0:T(8,128)(2,1)S(1)}, u32[]{:S(2)}, u32[]{:S(2)}) collective-permute-start(bf16[3,8,384]{2,1,0:T(8,128)(2,1)S(1)} %get-tuple-element.248), channel_id=1, source_target_pairs={{4,0},{8,4},{12,8},{16,12},{20,16},{24,20},{28,24},{5,1},{9,5},{13... | collective-permute-start | bytes 55304 | tf_op jit(solution)/shard_map/ppermute | solution.py:26
  15.8 28.9 %collective-permute-start.3 = (bf16[3,8,384]{2,1,0:T(8,128)(2,1)S(1)}, bf16[3,8,384]{2,1,0:T(8,128)(2,1)S(1)}, u32[]{:S(2)}, u32[]{:S(2)}) collective-permute-start(bf16[3,8,384]{2,1,0:T(8,128)(2,1)S(1)} %get-tuple-element.247), channel_id=1, source_target_pairs={{0,4},{4,8},{8,12},{12,16},{16,20},{20,24},{24,28},{1,5},{5,9},{9,... | collective-permute-start | bytes 55304 | tf_op jit(solution)/shard_map/ppermute | solution.py:24
  36.8 13.4 %collective-permute-start.2 = (bf16[61,7,3,384]{3,0,2,1:T(8,128)(2,1)}, bf16[61,7,3,384]{3,0,2,1:T(8,128)(2,1)}, u32[]{:S(2)}, u32[]{:S(2)}) collective-permute-start(bf16[61,7,3,384]{3,0,2,1:T(8,128)(2,1)} %copy.79), channel_id=1, source_target_pairs={{1,0},{2,1},{3,2},{5,4},{6,5},{7,6},{9,8},{10,9},{11,10},{13,12},{... | collective-permute-start | bytes 2951432 | tf_op jit(solution)/shard_map/ppermute | solution.py:26
  39.2 13.0 %collective-permute-start.1 = (bf16[61,7,3,384]{3,0,2,1:T(8,128)(2,1)}, bf16[61,7,3,384]{3,0,2,1:T(8,128)(2,1)}, u32[]{:S(2)}, u32[]{:S(2)}) collective-permute-start(bf16[61,7,3,384]{3,0,2,1:T(8,128)(2,1)} %copy.78), channel_id=1, source_target_pairs={{0,1},{1,2},{2,3},{4,5},{5,6},{6,7},{8,9},{9,10},{10,11},{12,13},{... | collective-permute-start | bytes 2951432 | tf_op jit(solution)/shard_map/ppermute | solution.py:24
  43.4 20.7 %copy-start.40 = (f32[8,3,768]{2,1,0:T(4,128)}, f32[8,3,768]{2,1,0:T(4,128)S(1)}, u32[]{:S(2)}) copy-start(f32[8,3,768]{2,1,0:T(4,128)S(1)} %dot_general.8) | copy-start | bytes 221188
  44.8 4.8 %collective-permute-start.6 = (bf16[10,3,384]{2,1,0:T(4,128)(2,1)S(1)}, bf16[10,3,384]{2,1,0:T(4,128)(2,1)S(1)}, u32[]{:S(2)}, u32[]{:S(2)}) collective-permute-start(bf16[10,3,384]{2,1,0:T(4,128)(2,1)S(1)} %get-tuple-element.246), channel_id=1, source_target_pairs={{1,0},{2,1},{3,2},{5,4},{6,5},{7,6},{9,8},{10,9},{11,10},{13,12},{... | collective-permute-start | bytes 69128 | tf_op jit(solution)/shard_map/ppermute | solution.py:26
  46.1 3.9 %collective-permute-start.5 = (bf16[10,3,384]{2,1,0:T(4,128)(2,1)S(1)}, bf16[10,3,384]{2,1,0:T(4,128)(2,1)S(1)}, u32[]{:S(2)}, u32[]{:S(2)}) collective-permute-start(bf16[10,3,384]{2,1,0:T(4,128)(2,1)S(1)} %get-tuple-element.245), channel_id=1, source_target_pairs={{0,1},{1,2},{2,3},{4,5},{5,6},{6,7},{8,9},{9,10},{10,11},{12,13},{... | collective-permute-start | bytes 69128 | tf_op jit(solution)/shard_map/ppermute | solution.py:24
  64.8 8.5 %copy-start.39 = (bf16[7,14,390]{2,1,0:T(8,128)(2,1)}, bf16[7,14,390]{2,1,0:T(8,128)(2,1)S(1)}, u32[]{:S(2)}) copy-start(bf16[7,14,390]{2,1,0:T(8,128)(2,1)S(1)} %get-tuple-element.219) | copy-start | bytes 229324
  65.0 36.6 %copy-start.1 = (bf16[7,14,390]{2,1,0:T(8,128)(2,1)}, bf16[7,14,390]{2,1,0:T(8,128)(2,1)S(1)}, u32[]{:S(2)}) copy-start(bf16[7,14,390]{2,1,0:T(8,128)(2,1)S(1)} %get-tuple-element.211) | copy-start | bytes 229324
  65.0 36.6 %copy-start.2 = (bf16[7,14,390]{2,1,0:T(8,128)(2,1)}, bf16[7,14,390]{2,1,0:T(8,128)(2,1)S(1)}, u32[]{:S(2)}) copy-start(bf16[7,14,390]{2,1,0:T(8,128)(2,1)S(1)} %get-tuple-element.212) | copy-start | bytes 229324
  77.1 24.5 %copy-start.42 = (f32[1,4,8,384]{3,2,1,0:T(8,128)}, f32[1,4,8,384]{3,2,1,0:T(8,128)S(1)}, u32[]{:S(2)}) copy-start(f32[1,4,8,384]{3,2,1,0:T(8,128)S(1)} %add_bitcast_fusion.3) | copy-start | bytes 147460
  79.7 7.2 %collective-permute-start.8 = (f32[3,3,8,384]{3,2,1,0:T(8,128)S(1)}, f32[3,3,8,384]{3,2,1,0:T(8,128)S(1)}, u32[]{:S(2)}, u32[]{:S(2)}) collective-permute-start(f32[3,3,8,384]{3,2,1,0:T(8,128)S(1)} %get-tuple-element.244), channel_id=1, source_target_pairs={{4,0},{8,4},{12,8},{16,12},{20,16},{24,20},{28,24},{5,1},{9,5},{13... | collective-permute-start | bytes 331784 | tf_op jit(solution)/shard_map/ppermute | solution.py:26
  81.0 7.5 %collective-permute-start.7 = (f32[3,3,8,384]{3,2,1,0:T(8,128)S(1)}, f32[3,3,8,384]{3,2,1,0:T(8,128)S(1)}, u32[]{:S(2)}, u32[]{:S(2)}) collective-permute-start(f32[3,3,8,384]{3,2,1,0:T(8,128)S(1)} %get-tuple-element.243), channel_id=1, source_target_pairs={{0,4},{4,8},{8,12},{12,16},{16,20},{20,24},{24,28},{1,5},{5,9},{9,... | collective-permute-start | bytes 331784 | tf_op jit(solution)/shard_map/ppermute | solution.py:24
  87.0 11.8 %copy-start.43 = (f32[3,3,8,384]{3,2,1,0:T(8,128)}, f32[3,3,8,384]{3,2,1,0:T(8,128)S(1)}, u32[]{:S(2)}) copy-start(f32[3,3,8,384]{3,2,1,0:T(8,128)S(1)} %collective-permute-done.8) | copy-start | bytes 331780
  88.6 10.2 %copy-start.45 = (f32[3,3,8,384]{3,2,1,0:T(8,128)}, f32[3,3,8,384]{3,2,1,0:T(8,128)S(1)}, u32[]{:S(2)}) copy-start(f32[3,3,8,384]{3,2,1,0:T(8,128)S(1)} %collective-permute-done.7) | copy-start | bytes 331780
  89.4 10.3 %collective-permute-start.10 = (f32[3,10,3,384]{3,2,1,0:T(4,128)}, f32[3,10,3,384]{3,2,1,0:T(4,128)}, u32[]{:S(2)}, u32[]{:S(2)}) collective-permute-start(f32[3,10,3,384]{3,2,1,0:T(4,128)} %get-tuple-element.240), channel_id=1, source_target_pairs={{1,0},{2,1},{3,2},{5,4},{6,5},{7,6},{9,8},{10,9},{11,10},{13,12},{... | collective-permute-start | bytes 414728 | tf_op jit(solution)/shard_map/ppermute | solution.py:26
  90.9 8.8 %collective-permute-start.9 = (f32[3,10,3,384]{3,2,1,0:T(4,128)}, f32[3,10,3,384]{3,2,1,0:T(4,128)}, u32[]{:S(2)}, u32[]{:S(2)}) collective-permute-start(f32[3,10,3,384]{3,2,1,0:T(4,128)} %get-tuple-element.239), channel_id=1, source_target_pairs={{0,1},{1,2},{2,3},{4,5},{5,6},{6,7},{8,9},{9,10},{10,11},{12,13},{... | collective-permute-start | bytes 414728 | tf_op jit(solution)/shard_map/ppermute | solution.py:24
  113.5 25.9 %copy-start.41 = (f32[8,3,768]{2,1,0:T(4,128)S(1)}, f32[8,3,768]{2,1,0:T(4,128)}, u32[]{:S(2)}) copy-start(f32[8,3,768]{2,1,0:T(4,128)} %copy-done.40) | copy-start | bytes 221188
  142.5 6.7 %collective-permute-start.12 = (f32[3,3,8,384]{3,2,1,0:T(8,128)S(1)}, f32[3,3,8,384]{3,2,1,0:T(8,128)S(1)}, u32[]{:S(2)}, u32[]{:S(2)}) collective-permute-start(f32[3,3,8,384]{3,2,1,0:T(8,128)S(1)} %get-tuple-element.242), channel_id=1, source_target_pairs={{4,0},{8,4},{12,8},{16,12},{20,16},{24,20},{28,24},{5,1},{9,5},{13... | collective-permute-start | bytes 331784 | tf_op jit(solution)/shard_map/ppermute | solution.py:26
  143.8 6.9 %collective-permute-start.11 = (f32[3,3,8,384]{3,2,1,0:T(8,128)S(1)}, f32[3,3,8,384]{3,2,1,0:T(8,128)S(1)}, u32[]{:S(2)}, u32[]{:S(2)}) collective-permute-start(f32[3,3,8,384]{3,2,1,0:T(8,128)S(1)} %get-tuple-element.241), channel_id=1, source_target_pairs={{0,4},{4,8},{8,12},{12,16},{16,20},{20,24},{24,28},{1,5},{5,9},{9,... | collective-permute-start | bytes 331784 | tf_op jit(solution)/shard_map/ppermute | solution.py:24
  151.5 6.0 %collective-permute-start.14 = (f32[3,10,3,384]{3,2,1,0:T(4,128)}, f32[3,10,3,384]{3,2,1,0:T(4,128)}, u32[]{:S(2)}, u32[]{:S(2)}) collective-permute-start(f32[3,10,3,384]{3,2,1,0:T(4,128)} %get-tuple-element.238), channel_id=1, source_target_pairs={{1,0},{2,1},{3,2},{5,4},{6,5},{7,6},{9,8},{10,9},{11,10},{13,12},{... | collective-permute-start | bytes 414728 | tf_op jit(solution)/shard_map/ppermute | solution.py:26
  152.8 4.7 %collective-permute-start.13 = (f32[3,10,3,384]{3,2,1,0:T(4,128)}, f32[3,10,3,384]{3,2,1,0:T(4,128)}, u32[]{:S(2)}, u32[]{:S(2)}) collective-permute-start(f32[3,10,3,384]{3,2,1,0:T(4,128)} %get-tuple-element.237), channel_id=1, source_target_pairs={{0,1},{1,2},{2,3},{4,5},{5,6},{6,7},{8,9},{9,10},{10,11},{12,13},{... | collective-permute-start | bytes 414728 | tf_op jit(solution)/shard_map/ppermute | solution.py:24
  (42 other events, 318.3 us)

commit v3 on v2

--- a/solution.py
+++ b/solution.py
@@ -28,6 +28,42 @@
     return x
 
 
+def neighbourhood(x, x_dim, y_dim, width, blocks):
+    slabs, cols = (lax.axis_size("slab"), lax.axis_size("col"))
+    lengths = {x_dim: x.shape[x_dim], y_dim: x.shape[y_dim]}
+
+    def side(array, dim, offset):
+        if offset < 0:
+            return lax.slice_in_dim(array, lengths[dim] - width, lengths[dim], axis=dim)
+        if offset > 0:
+            return lax.slice_in_dim(array, 0, width, axis=dim)
+        return array
+
+    grid = {(0, 0): x}
+    for off_x, off_y in blocks:
+        piece = side(side(x, x_dim, off_x), y_dim, off_y)
+        pairs = [
+            (s * cols + c, (s - off_x) * cols + (c - off_y))
+            for s in range(slabs)
+            for c in range(cols)
+            if 0 <= s - off_x < slabs and 0 <= c - off_y < cols
+        ]
+        grid[(off_x, off_y)] = lax.ppermute(piece, ("slab", "col"), pairs)
+    rows = []
+    for off_x in (-1, 0, 1):
+        cells = []
+        for off_y in (-1, 0, 1):
+            if (off_x, off_y) in grid:
+                cells.append(grid[(off_x, off_y)])
+            else:
+                shape = list(x.shape)
+                shape[x_dim] = width if off_x else lengths[x_dim]
+                shape[y_dim] = width if off_y else lengths[y_dim]
+                cells.append(jnp.zeros(shape, x.dtype))
+        rows.append(jnp.concatenate(cells, axis=y_dim))
+    return jnp.concatenate(rows, axis=x_dim)
+
+
 def device_rows(vector, axes):
     count = 1
     for axis in axes:
@@ -93,20 +129,25 @@
     def heading_of(bond_index):
         return [float(unit_dirs[bond_index, component]) for component in range(3)]
 
+    every_side = [(a, b) for a in (-1, 0, 1) for b in (-1, 0, 1) if (a, b) != (0, 0)]
+    lower_sides = [(-1, -1), (-1, 0), (-1, 1), (0, -1), (0, 1)]
+
     def rimmed(vector):
-        return pad_depth(with_halo(vector, (("slab", 1), ("col", 2)), 3))
-
-    lower_x = with_halo(integrity, (("slab", 1),), 3, high=False)
-    spread = pad_depth(with_halo(lower_x, (("col", 2),), 3))
-    contact_pad = pad_depth(
-        with_halo(contact.astype(jnp.bfloat16), (("slab", 0), ("col", 1)), 3)
+        return pad_depth(neighbourhood(vector, 1, 2, 3, every_side))
+
+    contact_flags = contact.astype(jnp.bfloat16)
+    stacked = jnp.concatenate([integrity, contact_flags[None]], axis=0)
+    spread = pad_depth(neighbourhood(stacked, 1, 2, 3, lower_sides))
+    upper_contact = neighbourhood(contact_flags, 0, 1, 3, [(1, -1), (1, 0), (1, 1)])
+    contact_pad = jnp.concatenate(
+        [spread[bond_count][: cells_x + 3], pad_depth(upper_contact[cells_x + 3 :])], axis=0
     ).astype(jnp.float32)
     near_contact = window(contact_pad, 0, 0, 0, extent)
 
     def bond_pair(bond_index):
         shift_x, shift_y, shift_z = bond_shift(bond_index)
         weight = float(weights[bond_index])
-        level_pad = jnp.pad(spread[bond_index], ((0, 3), (0, 0), (0, 0)))
+        level_pad = spread[bond_index]
         intact = window(level_pad, 0, 0, 0, extent).astype(jnp.float32)
         prior = window(level_pad, -shift_x, -shift_y, -shift_z, extent).astype(jnp.float32)
         forward = weight * intact

time: 197 us -> 226 us (1.15)
  starting transfers between devices: 51.8 us -> 83.2 us
  waiting for transfers between devices: 16.1 us -> 5.37 us
  other arithmetic: 63.4 us -> 71.3 us
  local copies, waits for them, and re-layouts: 21.8 us -> 26.7 us
  blocking collectives: 34 us -> 29.4 us
    ppermute x15 -> x24, starting transfers between devices: 48 us -> 73.4 us  [neighbourhood(): grid[off_x, off_y] = lax.ppermute(piece, ('slab', 'col'), pairs)]
    ppermute x15 -> x24, waiting for transfers between devices: 16.1 us -> 5.37 us  [neighbourhood(): grid[off_x, off_y] = lax.ppermute(piece, ('slab', 'col'), pairs)]
    squeeze x4, local copies, waits for them, and re-layouts: 1.24 us -> 7.16 us  [bond_pair(): level_pad = spread[bond_index]]
    all_to_all x1, starting transfers between devices: 3.86 us -> 9.72 us  [device_rows(): return lax.all_to_all(tiled, axes, 0, 0, tiled=True)]
    all_to_all x2, blocking collectives: 34 us -> 29.4 us  [device_rows(): return lax.all_to_all(tiled, axes, 0, 0, tiled=True)]
    concatenate x6 -> x7, other arithmetic: 13.3 us -> 16.8 us  [the longest x3 11.2 us: neighbourhood(): return jnp.concatenate(rows, axis=x_dim)]
    slice x10 -> x13, local copies, waits for them, and re-layouts: 6.28 us -> 7.26 us  [the longest x9 5.26 us: side(): return lax.slice_in_dim(array, lengths[dim] - width, lengths[dim], axis=dim)]
  transfers between devices with their start and end apart: 16 -> 25, of which waited for: 6 -> 4; matrix products, arithmetic and copies ran while one was open for 8% -> 10% of each run, Pallas kernels for 0% -> 0%
where the time goes in v3:
time: 226 us; the launch traced here: 224 us
  starting transfers between devices  83.2 us (37%)
  other arithmetic  71.3 us (32%)
  blocking collectives  29.4 us (13%)
  local copies, waits for them, and re-layouts  26.7 us (12%)
  between operations  7.57 us (3%)
  waiting for transfers between devices  5.37 us (2%)
    ppermute x24, starting transfers between devices, neighbourhood(): grid[off_x, off_y] = lax.ppermute(piece, ('slab', 'col'), pairs)  73.4 us
    all_to_all x2, blocking collectives, device_rows(): return lax.all_to_all(tiled, axes, 0, 0, tiled=True)  29.4 us
    another operation x3, other arithmetic, operator(): return jnp.stack(summed)  13.2 us
    another operation x3, other arithmetic, on_device(): diagonal = jnp.stack(diag_list)  13 us
    add x3, other arithmetic, operator(): summed[component] = summed[component] + heading[component] * stretch  12.9 us
    concatenate x3, other arithmetic, neighbourhood(): return jnp.concatenate(rows, axis=x_dim)  11.2 us
    all_to_all x1, starting transfers between devices, device_rows(): return lax.all_to_all(tiled, axes, 0, 0, tiled=True)  9.72 us
    squeeze x4, local copies, waits for them, and re-layouts, bond_pair(): level_pad = spread[bond_index]  7.16 us
  transfers between devices with their start and end apart: 25, of which 4 were waited for; matrix products, arithmetic and copies ran while one was open for 10% of the time, Pallas kernels for 0%

profile of v3, /device:TPU:0, one launch (start us, length us, event | category | flops | bytes accessed | tf_op | source)
XLA Modules:
  0.0 223.8 jit_solution(728659359008332675)
XLA Ops:
  1.6 2.4 %fusion.6 = (bf16[62,4,3,384]{3,2,1,0:T(4,128)(2,1)S(1)}, bf16[62,4,3,384]{3,2,1,0:T(4,128)(2,1)S(1)}) fusion(bf16[61,4,8,384]{3,2,1,0:T(8,128)(2,1)} %param.5, bf16[1,4,8,384]{3,2,1,0:T(8,128)(2,1)S(1)} %convert_bitcast_fusion), kind=kLoop, calls=%fused_computation.90 | loop fusion | flops 2285568 | bytes 2666496 | tf_op jit(solution)/shard_map/concatenate | solution.py:139
  4.3 3.2 %collective-permute-start.3 = (bf16[62,4,3,384]{3,1,2,0:T(4,128)(2,1)S(1)}, bf16[62,4,3,384]{3,1,2,0:T(4,128)(2,1)}, u32[]{:S(2)}, u32[]{:S(2)}) collective-permute-start(bf16[62,4,3,384]{3,1,2,0:T(4,128)(2,1)S(1)} %copy.91), channel_id=1, source_target_pairs={{0,1},{1,2},{2,3},{4,5},{5,6},{6,7},{8,9},{9,10},{10,11},{12,13},{... | collective-permute-start | bytes 1714184 | tf_op jit(solution)/shard_map/ppermute | solution.py:51
  7.4 2.4 %fusion = bf16[62,3,8,384]{3,2,1,0:T(8,128)(2,1)} fusion(bf16[1,4,8,384]{3,2,1,0:T(8,128)(2,1)S(1)} %convert_bitcast_fusion, bf16[61,4,8,384]{3,2,1,0:T(8,128)(2,1)} %param.5), kind=kLoop, calls=%fused_computation.69 | loop fusion | flops 571392 | bytes 2666496 | tf_op jit(solution)/shard_map/concatenate | solution.py:139
  9.9 5.3 %collective-permute-start.1 = (bf16[62,3,8,384]{3,2,1,0:T(8,128)(2,1)}, bf16[62,3,8,384]{3,2,1,0:T(8,128)(2,1)}, u32[]{:S(2)}, u32[]{:S(2)}) collective-permute-start(bf16[62,3,8,384]{3,2,1,0:T(8,128)(2,1)} %fusion), channel_id=1, source_target_pairs={{0,4},{1,5},{2,6},{3,7},{4,8},{5,9},{6,10},{7,11},{8,12},{9,13},{1... | collective-permute-start | bytes 3428360 | tf_op jit(solution)/shard_map/ppermute | solution.py:51
  21.1 9.7 %all-to-all-start = ((f32[32,1,24]{2,1,0:T(1,128)}), f32[32,1,24]{2,1,0:T(1,128)S(1)}, u32[]{:S(2)}, u32[]{:S(2)}) async-start(f32[32,1,24]{2,1,0:T(1,128)} %broadcast_in_dim.15), calls=%async_computation | async-start | bytes 32768 | tf_op jit(solution)/shard_map/all_to_all | solution.py:72
  35.7 5.2 %collective-permute-start = (bf16[62,3,3,384]{3,0,2,1:T(8,128)(2,1)}, bf16[62,3,3,384]{3,0,2,1:T(8,128)(2,1)}, u32[]{:S(2)}, u32[]{:S(2)}) collective-permute-start(bf16[62,3,3,384]{3,0,2,1:T(8,128)(2,1)} %copy.87), channel_id=1, source_target_pairs={{0,5},{1,6},{2,7},{4,9},{5,10},{6,11},{8,13},{9,14},{10,15},{12,17... | collective-permute-start | bytes 1285640 | tf_op jit(solution)/shard_map/ppermute | solution.py:51
  44.9 2.4 %collective-permute-done = bf16[62,3,3,384]{3,0,2,1:T(8,128)(2,1)} collective-permute-done((bf16[62,3,3,384]{3,0,2,1:T(8,128)(2,1)}, bf16[62,3,3,384]{3,0,2,1:T(8,128)(2,1)}, u32[]{:S(2)}, u32[]{:S(2)}) %collective-permute-start) | collective-permute-done | bytes 428576 | tf_op jit(solution)/shard_map/ppermute | solution.py:51
  51.9 7.7 %maximum_maximum_fusion = bf16[62,10,14,384]{3,2,1,0:T(8,128)(2,1)S(1)} fusion(bf16[62,3,3,384]{3,2,1,0:T(4,128)(2,1)S(1)} %broadcast.239, bf16[62,4,3,384]{3,2,1,0:T(4,128)(2,1)S(1)} %copy.94, bf16[1,4,8,384]{3,2,1,0:T(8,128)(2,1)S(1)} %convert_bitcast_fusion, bf16[61,4,8,384]{3,2,1,0:T(8,128)(2,1)S(1)} %copy-done, bf16[62,4,3,384]{3,2,1,0:T(4,128)(2,1)S(1)} %copy.93, ...), kind=kLoop, calls=%fused_computation.62 | loop fusion | flops 66662400 | bytes 11761432 | tf_op jit(solution)/shard_map/concatenate | solution.py:64
  62.0 2.3 %fusion.40 = (bf16[10,14,390]{2,1,0:T(8,128)(2,1)S(1)}, bf16[10,14,390]{2,1,0:T(8,128)(2,1)S(1)}, bf16[10,14,390]{2,1,0:T(8,128)(2,1)S(1)}, bf16[10,14,390]{2,1,...) fusion(bf16[62,10,14,384]{3,2,1,0:T(8,128)(2,1)S(1)} %maximum_m, ...), kind=kLoop, calls=%fused_computation.134 | loop fusion | bytes 8741040 | tf_op jit(solution)/shard_map/squeeze | solution.py:150
  64.4 2.3 %fusion.69 = (bf16[10,14,390]{2,1,0:T(8,128)(2,1)S(1)}, bf16[10,14,390]{2,1,0:T(8,128)(2,1)S(1)}, bf16[10,14,390]{2,1,0:T(8,128)(2,1)S(1)}, bf16[10,14,390]{2,1,...) fusion(bf16[62,10,14,384]{3,2,1,0:T(8,128)(2,1)S(1)} %maximum_m, ...), kind=kLoop, calls=%fused_computation.163 | loop fusion | bytes 8741040 | tf_op jit(solution)/shard_map/squeeze | solution.py:150
  67.3 5.1 %add_bitcast_fusion.5 = (f32[1,4,8,384]{3,2,1,0:T(8,128)}, f32[4,8,384]{2,1,0:T(8,128)S(1)}, f32[4,8,384]{2,1,0:T(8,128)S(1)}, f32[4,8,384]{2,1,0:T(8,128)S(1)},...) fusion(bf16[10,14,390]{2,1,0:T(8,128)(2,1)S(1)} %get-tuple-elem, ...), kind=kLoop, calls=%fused_computation.2599 | loop fusion | flops 6967296 | bytes 7913472 | tf_op jit(solution)/shard_map/stack | solution.py:174
  72.4 4.1 %add_bitcast_fusion.4 = f32[1,4,8,384]{3,2,1,0:T(8,128)} fusion(f32[4,8,384]{2,1,0:T(8,128)S(1)} %get-tuple-element.143, bf16[10,14,390]{2,1,0:T(8,128)(2,1)S(1)} %get-tuple-element.165, bf16[10,14,390]{2,1,0:T(8,128)(2,1)S(1)} %get-tuple-element.169, bf16[10,14,390]{2,1,0:T(8,128)(2,1)S(1)} %get-tuple-element.170, ...), kind=kLoop, calls=%fused_computation.2598 | loop fusion | flops 5173248 | bytes 5799936 | tf_op jit(solution)/shard_map/stack | solution.py:174
  76.8 3.9 %add_bitcast_fusion.3 = f32[1,4,8,384]{3,2,1,0:T(8,128)S(1)} fusion(f32[4,8,384]{2,1,0:T(8,128)} %get-tuple-element.161, f32[4,8,384]{2,1,0:T(8,128)S(1)} %get-tuple-element.160, bf16[10,14,390]{2,1,0:T(8,128)(2,1)} %get-tuple-element.164, bf16[10,14,390]{2,1,0:T(8,128)(2,1)} %get-tuple-element.163, bf16[10,14,390]{2,1,0:T(8,128)(2,1)S(1)} %get-tuple-element.165, ...), kind=kLoop, calls=%fused_computation.2597 | loop fusion | flops 5406720 | bytes 6045696 | tf_op jit(solution)/shard_map/stack | solution.py:174
  84.9 12.7 %collective-permute-start.9 = (f32[3,3,8,384]{3,2,1,0:T(8,128)}, f32[3,3,8,384]{3,2,1,0:T(8,128)}, u32[]{:S(2)}, u32[]{:S(2)}) collective-permute-start(f32[3,3,8,384]{3,2,1,0:T(8,128)} %get-tuple-element.251), channel_id=1, source_target_pairs={{0,4},{1,5},{2,6},{3,7},{4,8},{5,9},{6,10},{7,11},{8,12},{9,13},{1... | collective-permute-start | bytes 331784 | tf_op jit(solution)/shard_map/ppermute | solution.py:51
  103.9 12.3 %collective-permute-start.8 = (f32[3,3,3,384]{3,2,1,0:T(4,128)}, f32[3,3,3,384]{3,2,1,0:T(4,128)}, u32[]{:S(2)}, u32[]{:S(2)}) collective-permute-start(f32[3,3,3,384]{3,2,1,0:T(4,128)} %get-tuple-element.247), channel_id=1, source_target_pairs={{0,5},{1,6},{2,7},{4,9},{5,10},{6,11},{8,13},{9,14},{10,15},{12,17... | collective-permute-start | bytes 124424 | tf_op jit(solution)/shard_map/ppermute | solution.py:51
  116.2 3.4 %collective-permute-start.11 = (f32[3,4,3,384]{3,2,1,0:T(4,128)}, f32[3,4,3,384]{3,2,1,0:T(4,128)}, u32[]{:S(2)}, u32[]{:S(2)}) collective-permute-start(f32[3,4,3,384]{3,2,1,0:T(4,128)} %get-tuple-element.253), channel_id=1, source_target_pairs={{0,1},{1,2},{2,3},{4,5},{5,6},{6,7},{8,9},{9,10},{10,11},{12,13},{... | collective-permute-start | bytes 165896 | tf_op jit(solution)/shard_map/ppermute | solution.py:51
  125.0 12.3 %add_add_fusion.2 = (f32[4,8,384]{2,1,0:T(8,128)S(1)}, f32[4,8,384]{2,1,0:T(8,128)S(1)}, f32[4,8,384]{2,1,0:T(8,128)S(1)}, f32[4,8,384]{2,1,0:T(8,128)S(1)}, f32...) fusion(f32[4,8,384]{2,1,0:T(8,128)} %squeeze.207, ...), kind=kLoop, calls=%fused_computation.2596 | loop fusion | flops 18382848 | bytes 27181056 | tf_op jit(solution)/shard_map/add | solution.py:199
  140.6 14.2 %all_to_all.24 = f32[32,1,26]{2,1,0:T(1,128)S(1)} all-to-all(f32[32,1,26]{2,1,0:T(1,128)S(1)} %broadcast_in_dim.16), channel_id=1, replica_groups=mesh['slab'=8,'col'=4] {'slab','col'}, dimensions={0} | all-to-all | bytes 6656 | tf_op jit(solution)/shard_map/all_to_all | solution.py:72
  160.5 3.1 %collective-permute-start.17 = (f32[3,3,8,384]{3,2,1,0:T(8,128)}, f32[3,3,8,384]{3,2,1,0:T(8,128)}, u32[]{:S(2)}, u32[]{:S(2)}) collective-permute-start(f32[3,3,8,384]{3,2,1,0:T(8,128)} %get-tuple-element.243), channel_id=1, source_target_pairs={{0,4},{1,5},{2,6},{3,7},{4,8},{5,9},{6,10},{7,11},{8,12},{9,13},{1... | collective-permute-start | bytes 331784 | tf_op jit(solution)/shard_map/ppermute | solution.py:51
  164.9 4.0 %collective-permute-start.16 = (f32[3,3,3,384]{3,2,1,0:T(4,128)}, f32[3,3,3,384]{3,2,1,0:T(4,128)}, u32[]{:S(2)}, u32[]{:S(2)}) collective-permute-start(f32[3,3,3,384]{3,2,1,0:T(4,128)} %get-tuple-element.239), channel_id=1, source_target_pairs={{0,5},{1,6},{2,7},{4,9},{5,10},{6,11},{8,13},{9,14},{10,15},{12,17... | collective-permute-start | bytes 124424 | tf_op jit(solution)/shard_map/ppermute | solution.py:51
  174.6 5.6 %collective-permute-start.19 = (f32[3,4,3,384]{3,2,1,0:T(4,128)}, f32[3,4,3,384]{3,2,1,0:T(4,128)}, u32[]{:S(2)}, u32[]{:S(2)}) collective-permute-start(f32[3,4,3,384]{3,2,1,0:T(4,128)} %get-tuple-element.245), channel_id=1, source_target_pairs={{0,1},{1,2},{2,3},{4,5},{5,6},{6,7},{8,9},{9,10},{10,11},{12,13},{... | collective-permute-start | bytes 165896 | tf_op jit(solution)/shard_map/ppermute | solution.py:51
  186.0 12.5 %add_bitcast_fusion.2 = (f32[1,4,8,384]{3,2,1,0:T(8,128)S(1)}, f32[4,8,384]{2,1,0:T(8,128)S(1)}, f32[4,8,384]{2,1,0:T(8,128)S(1)}, f32[4,8,384]{2,1,0:T(8,128)S(...) fusion(f32[4,8,384]{2,1,0:T(8,128)} %squeeze.213, ...), kind=kLoop, calls=%fused_computation.2593 | loop fusion | flops 18382848 | bytes 27181056 | tf_op jit(solution)/shard_map/stack | solution.py:200
  199.9 2.6 %pad_maximum_fusion.5 = f32[4]{0:T(128)S(1)} fusion(f32[1]{0:T(128)} %bitcast.93, f32[1]{0:T(128)} %bitcast.92, f32[1]{0:T(128)} %bitcast.91, f32[1]{0:T(128)} %bitcast.83), kind=kLoop, calls=%fused_computation.2720 | loop fusion | flops 12 | bytes 32 | tf_op jit(solution)/shard_map/stack | solution.py:241
  202.6 15.3 %all_to_all.25 = f32[32,1,4]{2,1,0:T(1,128)S(1)} all-to-all(f32[32,1,4]{2,1,0:T(1,128)S(1)} %broadcast_in_dim.17), channel_id=1, replica_groups=mesh['slab'=8,'col'=4] {'slab','col'}, dimensions={0} | all-to-all | bytes 1024 | tf_op jit(solution)/shard_map/all_to_all | solution.py:72
  (225 shorter events, 62.4 us)
Async XLA Ops:
  4.3 45.8 %collective-permute-start.3 = (bf16[62,4,3,384]{3,1,2,0:T(4,128)(2,1)S(1)}, bf16[62,4,3,384]{3,1,2,0:T(4,128)(2,1)}, u32[]{:S(2)}, u32[]{:S(2)}) collective-permute-start(bf16[62,4,3,384]{3,1,2,0:T(4,128)(2,1)S(1)} %copy.91), channel_id=1, source_target_pairs={{0,1},{1,2},{2,3},{4,5},{5,6},{6,7},{8,9},{9,10},{10,11},{12,13},{... | collective-permute-start | bytes 1714184 | tf_op jit(solution)/shard_map/ppermute | solution.py:51
  9.9 41.9 %collective-permute-start.1 = (bf16[62,3,8,384]{3,2,1,0:T(8,128)(2,1)}, bf16[62,3,8,384]{3,2,1,0:T(8,128)(2,1)}, u32[]{:S(2)}, u32[]{:S(2)}) collective-permute-start(bf16[62,3,8,384]{3,2,1,0:T(8,128)(2,1)} %fusion), channel_id=1, source_target_pairs={{0,4},{1,5},{2,6},{3,7},{4,8},{5,9},{6,10},{7,11},{8,12},{9,13},{1... | collective-permute-start | bytes 3428360 | tf_op jit(solution)/shard_map/ppermute | solution.py:51
  15.9 18.4 %collective-permute-start.5 = (bf16[3,3,384]{2,1,0:T(4,128)(2,1)S(1)}, bf16[3,3,384]{2,1,0:T(4,128)(2,1)S(1)}, u32[]{:S(2)}, u32[]{:S(2)}) collective-permute-start(bf16[3,3,384]{2,1,0:T(4,128)(2,1)S(1)} %get-tuple-element.255), channel_id=1, source_target_pairs={{4,1},{5,2},{6,3},{8,5},{9,6},{10,7},{12,9},{13,10},{14,11},{16,13... | collective-permute-start | bytes 20744 | tf_op jit(solution)/shard_map/ppermute | solution.py:51
  16.6 19.0 %collective-permute-start.7 = (bf16[3,3,384]{2,1,0:T(4,128)(2,1)S(1)}, bf16[3,3,384]{2,1,0:T(4,128)(2,1)S(1)}, u32[]{:S(2)}, u32[]{:S(2)}) collective-permute-start(bf16[3,3,384]{2,1,0:T(4,128)(2,1)S(1)} %get-tuple-element.256), channel_id=1, source_target_pairs={{5,0},{6,1},{7,2},{9,4},{10,5},{11,6},{13,8},{14,9},{15,10},{17,12... | collective-permute-start | bytes 20744 | tf_op jit(solution)/shard_map/ppermute | solution.py:51
  17.9 22.9 %collective-permute-start.6 = (bf16[3,8,384]{2,1,0:T(8,128)(2,1)S(1)}, bf16[3,8,384]{2,1,0:T(8,128)(2,1)S(1)}, u32[]{:S(2)}, u32[]{:S(2)}) collective-permute-start(bf16[3,8,384]{2,1,0:T(8,128)(2,1)S(1)} %slice.6185), channel_id=1, source_target_pairs={{4,0},{5,1},{6,2},{7,3},{8,4},{9,5},{10,6},{11,7},{12,8},{13,9},{1... | collective-permute-start | bytes 55304 | tf_op jit(solution)/shard_map/ppermute | solution.py:51
  21.1 21.4 %all-to-all-start = ((f32[32,1,24]{2,1,0:T(1,128)}), f32[32,1,24]{2,1,0:T(1,128)S(1)}, u32[]{:S(2)}, u32[]{:S(2)}) async-start(f32[32,1,24]{2,1,0:T(1,128)} %broadcast_in_dim.15), calls=%async_computation | async-start | bytes 32768 | tf_op jit(solution)/shard_map/all_to_all | solution.py:72
  34.4 17.1 %collective-permute-start.4 = (bf16[62,4,3,384]{3,1,2,0:T(4,128)(2,1)}, bf16[62,4,3,384]{3,1,2,0:T(4,128)(2,1)S(1)}, u32[]{:S(2)}, u32[]{:S(2)}) collective-permute-start(bf16[62,4,3,384]{3,1,2,0:T(4,128)(2,1)} %copy.92), channel_id=1, source_target_pairs={{1,0},{2,1},{3,2},{5,4},{6,5},{7,6},{9,8},{10,9},{11,10},{13,12},{... | collective-permute-start | bytes 1714184 | tf_op jit(solution)/shard_map/ppermute | solution.py:51
  35.7 11.6 %collective-permute-start = (bf16[62,3,3,384]{3,0,2,1:T(8,128)(2,1)}, bf16[62,3,3,384]{3,0,2,1:T(8,128)(2,1)}, u32[]{:S(2)}, u32[]{:S(2)}) collective-permute-start(bf16[62,3,3,384]{3,0,2,1:T(8,128)(2,1)} %copy.87), channel_id=1, source_target_pairs={{0,5},{1,6},{2,7},{4,9},{5,10},{6,11},{8,13},{9,14},{10,15},{12,17... | collective-permute-start | bytes 1285640 | tf_op jit(solution)/shard_map/ppermute | solution.py:51
  40.9 7.8 %collective-permute-start.2 = (bf16[62,3,3,384]{3,0,2,1:T(8,128)(2,1)}, bf16[62,3,3,384]{3,0,2,1:T(8,128)(2,1)}, u32[]{:S(2)}, u32[]{:S(2)}) collective-permute-start(bf16[62,3,3,384]{3,0,2,1:T(8,128)(2,1)} %copy.88), channel_id=1, source_target_pairs={{1,4},{2,5},{3,6},{5,8},{6,9},{7,10},{9,12},{10,13},{11,14},{13,16... | collective-permute-start | bytes 1285640 | tf_op jit(solution)/shard_map/ppermute | solution.py:51
  83.6 39.5 %collective-permute-start.14 = (f32[3,3,8,384]{3,2,1,0:T(8,128)}, f32[3,3,8,384]{3,2,1,0:T(8,128)}, u32[]{:S(2)}, u32[]{:S(2)}) collective-permute-start(f32[3,3,8,384]{3,2,1,0:T(8,128)} %get-tuple-element.252), channel_id=1, source_target_pairs={{4,0},{5,1},{6,2},{7,3},{8,4},{9,5},{10,6},{11,7},{12,8},{13,9},{1... | collective-permute-start | bytes 331784 | tf_op jit(solution)/shard_map/ppermute | solution.py:51
  84.9 38.2 %collective-permute-start.9 = (f32[3,3,8,384]{3,2,1,0:T(8,128)}, f32[3,3,8,384]{3,2,1,0:T(8,128)}, u32[]{:S(2)}, u32[]{:S(2)}) collective-permute-start(f32[3,3,8,384]{3,2,1,0:T(8,128)} %get-tuple-element.251), channel_id=1, source_target_pairs={{0,4},{1,5},{2,6},{3,7},{4,8},{5,9},{6,10},{7,11},{8,12},{9,13},{1... | collective-permute-start | bytes 331784 | tf_op jit(solution)/shard_map/ppermute | solution.py:51
  97.6 6.4 %collective-permute-start.10 = (f32[3,3,3,384]{3,2,1,0:T(4,128)}, f32[3,3,3,384]{3,2,1,0:T(4,128)}, u32[]{:S(2)}, u32[]{:S(2)}) collective-permute-start(f32[3,3,3,384]{3,2,1,0:T(4,128)} %get-tuple-element.250), channel_id=1, source_target_pairs={{1,4},{2,5},{3,6},{5,8},{6,9},{7,10},{9,12},{10,13},{11,14},{13,16... | collective-permute-start | bytes 124424 | tf_op jit(solution)/shard_map/ppermute | solution.py:51
  98.8 17.4 %collective-permute-start.13 = (f32[3,3,3,384]{3,2,1,0:T(4,128)}, f32[3,3,3,384]{3,2,1,0:T(4,128)}, u32[]{:S(2)}, u32[]{:S(2)}) collective-permute-start(f32[3,3,3,384]{3,2,1,0:T(4,128)} %get-tuple-element.249), channel_id=1, source_target_pairs={{4,1},{5,2},{6,3},{8,5},{9,6},{10,7},{12,9},{13,10},{14,11},{16,13... | collective-permute-start | bytes 124424 | tf_op jit(solution)/shard_map/ppermute | solution.py:51
  100.1 19.5 %collective-permute-start.15 = (f32[3,3,3,384]{3,2,1,0:T(4,128)}, f32[3,3,3,384]{3,2,1,0:T(4,128)}, u32[]{:S(2)}, u32[]{:S(2)}) collective-permute-start(f32[3,3,3,384]{3,2,1,0:T(4,128)} %get-tuple-element.248), channel_id=1, source_target_pairs={{5,0},{6,1},{7,2},{9,4},{10,5},{11,6},{13,8},{14,9},{15,10},{17,12... | collective-permute-start | bytes 124424 | tf_op jit(solution)/shard_map/ppermute | solution.py:51
  103.9 17.9 %collective-permute-start.8 = (f32[3,3,3,384]{3,2,1,0:T(4,128)}, f32[3,3,3,384]{3,2,1,0:T(4,128)}, u32[]{:S(2)}, u32[]{:S(2)}) collective-permute-start(f32[3,3,3,384]{3,2,1,0:T(4,128)} %get-tuple-element.247), channel_id=1, source_target_pairs={{0,5},{1,6},{2,7},{4,9},{5,10},{6,11},{8,13},{9,14},{10,15},{12,17... | collective-permute-start | bytes 124424 | tf_op jit(solution)/shard_map/ppermute | solution.py:51
  116.2 5.6 %collective-permute-start.11 = (f32[3,4,3,384]{3,2,1,0:T(4,128)}, f32[3,4,3,384]{3,2,1,0:T(4,128)}, u32[]{:S(2)}, u32[]{:S(2)}) collective-permute-start(f32[3,4,3,384]{3,2,1,0:T(4,128)} %get-tuple-element.253), channel_id=1, source_target_pairs={{0,1},{1,2},{2,3},{4,5},{5,6},{6,7},{8,9},{9,10},{10,11},{12,13},{... | collective-permute-start | bytes 165896 | tf_op jit(solution)/shard_map/ppermute | solution.py:51
  160.5 23.7 %collective-permute-start.17 = (f32[3,3,8,384]{3,2,1,0:T(8,128)}, f32[3,3,8,384]{3,2,1,0:T(8,128)}, u32[]{:S(2)}, u32[]{:S(2)}) collective-permute-start(f32[3,3,8,384]{3,2,1,0:T(8,128)} %get-tuple-element.243), channel_id=1, source_target_pairs={{0,4},{1,5},{2,6},{3,7},{4,8},{5,9},{6,10},{7,11},{8,12},{9,13},{1... | collective-permute-start | bytes 331784 | tf_op jit(solution)/shard_map/ppermute | solution.py:51
  163.6 20.6 %collective-permute-start.22 = (f32[3,3,8,384]{3,2,1,0:T(8,128)}, f32[3,3,8,384]{3,2,1,0:T(8,128)}, u32[]{:S(2)}, u32[]{:S(2)}) collective-permute-start(f32[3,3,8,384]{3,2,1,0:T(8,128)} %get-tuple-element.244), channel_id=1, source_target_pairs={{4,0},{5,1},{6,2},{7,3},{8,4},{9,5},{10,6},{11,7},{12,8},{13,9},{1... | collective-permute-start | bytes 331784 | tf_op jit(solution)/shard_map/ppermute | solution.py:51
  164.9 8.4 %collective-permute-start.16 = (f32[3,3,3,384]{3,2,1,0:T(4,128)}, f32[3,3,3,384]{3,2,1,0:T(4,128)}, u32[]{:S(2)}, u32[]{:S(2)}) collective-permute-start(f32[3,3,3,384]{3,2,1,0:T(4,128)} %get-tuple-element.239), channel_id=1, source_target_pairs={{0,5},{1,6},{2,7},{4,9},{5,10},{6,11},{8,13},{9,14},{10,15},{12,17... | collective-permute-start | bytes 124424 | tf_op jit(solution)/shard_map/ppermute | solution.py:51
  168.9 5.7 %collective-permute-start.18 = (f32[3,3,3,384]{3,2,1,0:T(4,128)}, f32[3,3,3,384]{3,2,1,0:T(4,128)}, u32[]{:S(2)}, u32[]{:S(2)}) collective-permute-start(f32[3,3,3,384]{3,2,1,0:T(4,128)} %get-tuple-element.242), channel_id=1, source_target_pairs={{1,4},{2,5},{3,6},{5,8},{6,9},{7,10},{9,12},{10,13},{11,14},{13,16... | collective-permute-start | bytes 124424 | tf_op jit(solution)/shard_map/ppermute | solution.py:51
  170.2 10.0 %collective-permute-start.21 = (f32[3,3,3,384]{3,2,1,0:T(4,128)}, f32[3,3,3,384]{3,2,1,0:T(4,128)}, u32[]{:S(2)}, u32[]{:S(2)}) collective-permute-start(f32[3,3,3,384]{3,2,1,0:T(4,128)} %get-tuple-element.241), channel_id=1, source_target_pairs={{4,1},{5,2},{6,3},{8,5},{9,6},{10,7},{12,9},{13,10},{14,11},{16,13... | collective-permute-start | bytes 124424 | tf_op jit(solution)/shard_map/ppermute | solution.py:51
  173.3 10.5 %collective-permute-start.23 = (f32[3,3,3,384]{3,2,1,0:T(4,128)}, f32[3,3,3,384]{3,2,1,0:T(4,128)}, u32[]{:S(2)}, u32[]{:S(2)}) collective-permute-start(f32[3,3,3,384]{3,2,1,0:T(4,128)} %get-tuple-element.240), channel_id=1, source_target_pairs={{5,0},{6,1},{7,2},{9,4},{10,5},{11,6},{13,8},{14,9},{15,10},{17,12... | collective-permute-start | bytes 124424 | tf_op jit(solution)/shard_map/ppermute | solution.py:51
  174.6 9.2 %collective-permute-start.19 = (f32[3,4,3,384]{3,2,1,0:T(4,128)}, f32[3,4,3,384]{3,2,1,0:T(4,128)}, u32[]{:S(2)}, u32[]{:S(2)}) collective-permute-start(f32[3,4,3,384]{3,2,1,0:T(4,128)} %get-tuple-element.245), channel_id=1, source_target_pairs={{0,1},{1,2},{2,3},{4,5},{5,6},{6,7},{8,9},{9,10},{10,11},{12,13},{... | collective-permute-start | bytes 165896 | tf_op jit(solution)/shard_map/ppermute | solution.py:51
  180.2 3.9 %collective-permute-start.20 = (f32[3,4,3,384]{3,2,1,0:T(4,128)S(1)}, f32[3,4,3,384]{3,2,1,0:T(4,128)}, u32[]{:S(2)}, u32[]{:S(2)}) collective-permute-start(f32[3,4,3,384]{3,2,1,0:T(4,128)S(1)} %get-tuple-element.246), channel_id=1, source_target_pairs={{1,0},{2,1},{3,2},{5,4},{6,5},{7,6},{9,8},{10,9},{11,10},{13,12},{... | collective-permute-start | bytes 165896 | tf_op jit(solution)/shard_map/ppermute | solution.py:51
  (48 other events, 743.8 us)

commit v4 on v2

--- a/solution.py
+++ b/solution.py
@@ -96,17 +96,27 @@
     def rimmed(vector):
         return pad_depth(with_halo(vector, (("slab", 1), ("col", 2)), 3))
 
-    lower_x = with_halo(integrity, (("slab", 1),), 3, high=False)
+    contact_flags = contact.astype(jnp.bfloat16)
+    stacked = jnp.concatenate([integrity, contact_flags[None]], axis=0)
+    lower_x = with_halo(stacked, (("slab", 1),), 3, high=False)
+    upper_x = with_halo(contact_flags, (("slab", 0),), 3, low=False)[cells_x:]
+    lower_x = jnp.concatenate(
+        [
+            lower_x,
+            jnp.concatenate(
+                [jnp.zeros((bond_count,) + upper_x.shape, upper_x.dtype), upper_x[None]], axis=0
+            ),
+        ],
+        axis=1,
+    )
     spread = pad_depth(with_halo(lower_x, (("col", 2),), 3))
-    contact_pad = pad_depth(
-        with_halo(contact.astype(jnp.bfloat16), (("slab", 0), ("col", 1)), 3)
-    ).astype(jnp.float32)
+    contact_pad = spread[bond_count].astype(jnp.float32)
     near_contact = window(contact_pad, 0, 0, 0, extent)
 
     def bond_pair(bond_index):
         shift_x, shift_y, shift_z = bond_shift(bond_index)
         weight = float(weights[bond_index])
-        level_pad = jnp.pad(spread[bond_index], ((0, 3), (0, 0), (0, 0)))
+        level_pad = spread[bond_index]
         intact = window(level_pad, 0, 0, 0, extent).astype(jnp.float32)
         prior = window(level_pad, -shift_x, -shift_y, -shift_z, extent).astype(jnp.float32)
         forward = weight * intact

time: 197 us -> 236 us (1.20)
  other arithmetic: 63.4 us -> 94.6 us
  waiting for transfers between devices: 16.1 us -> 47.3 us
  starting transfers between devices: 51.8 us -> 31.3 us
  blocking collectives: 34 us -> 28.2 us
  local copies, waits for them, and re-layouts: 21.8 us -> 24.9 us
    concatenate x6 -> x5, other arithmetic: 13.3 us -> 37.5 us  [with_halo(): x = jnp.concatenate(parts, axis=dim)]
    ppermute x8 -> x6, starting transfers between devices: 38.7 us -> 14.9 us  [with_halo(): parts.insert(0, lax.ppermute(last, axis, up))]
    all_to_all x1, waiting for transfers between devices: 0.01 us -> 12.9 us  [device_rows(): return lax.all_to_all(tiled, axes, 0, 0, tiled=True)]
    ppermute x7 -> x6, waiting for transfers between devices: 1.46 us -> 14.1 us  [with_halo(): parts.append(lax.ppermute(first, axis, down))]
    all_to_all x2, blocking collectives: 34 us -> 28.2 us  [device_rows(): return lax.all_to_all(tiled, axes, 0, 0, tiled=True)]
    ppermute x8 -> x6, waiting for transfers between devices: 14.6 us -> 20.3 us  [with_halo(): parts.insert(0, lax.ppermute(last, axis, up))]
    all_to_all x1, starting transfers between devices: 3.86 us -> 8.7 us  [device_rows(): return lax.all_to_all(tiled, axes, 0, 0, tiled=True)]
    concatenate x0 -> x2, other arithmetic: none -> 3.43 us  [the longest x1 2.04 us: on_device(): jnp.concatenate([lower_x, jnp.concatenate([jnp.zeros((bond_count,) + uppe...]
  transfers between devices with their start and end apart: 16 -> 13, of which waited for: 6 -> 8; matrix products, arithmetic and copies ran while one was open for 8% -> 5% of each run, Pallas kernels for 0% -> 0%
where the time goes in v4:
time: 236 us; the launch traced here: 234 us
  other arithmetic  94.6 us (40%)
  waiting for transfers between devices  47.3 us (20%)
  starting transfers between devices  31.3 us (13%)
  blocking collectives  28.2 us (12%)
  local copies, waits for them, and re-layouts  24.9 us (11%)
  between operations  7.6 us (3%)
    concatenate x5, other arithmetic, with_halo(): x = jnp.concatenate(parts, axis=dim)  37.5 us
    all_to_all x2, blocking collectives, device_rows(): return lax.all_to_all(tiled, axes, 0, 0, tiled=True)  28.2 us
    ppermute x6, waiting for transfers between devices, with_halo(): parts.insert(0, lax.ppermute(last, axis, up))  20.3 us
    ppermute x6, starting transfers between devices, with_halo(): parts.insert(0, lax.ppermute(last, axis, up))  14.9 us
    ppermute x6, waiting for transfers between devices, with_halo(): parts.append(lax.ppermute(first, axis, down))  14.1 us
    add x3, other arithmetic, operator(): summed[component] = summed[component] + heading[component] * stretch  13.8 us
    another operation x3, other arithmetic, operator(): return jnp.stack(summed)  13.7 us
    all_to_all x1, waiting for transfers between devices, device_rows(): return lax.all_to_all(tiled, axes, 0, 0, tiled=True)  12.9 us
  transfers between devices with their start and end apart: 13, of which 8 were waited for; matrix products, arithmetic and copies ran while one was open for 5% of the time, Pallas kernels for 0%

profile of v4, /device:TPU:0, one launch (start us, length us, event | category | flops | bytes accessed | tf_op | source)
XLA Modules:
  0.0 234.3 jit_solution(1683198923059137763)
XLA Ops:
  2.8 4.9 %collective-permute-start = (bf16[62,3,8,384]{3,2,1,0:T(8,128)(2,1)S(1)}, bf16[62,3,8,384]{3,2,1,0:T(8,128)(2,1)S(1)}, u32[]{:S(2)}, u32[]{:S(2)}) collective-permute-start(bf16[62,3,8,384]{3,2,1,0:T(8,128)(2,1)S(1)} %pad_maximum_fusion.1), channel_id=1, source_target_pairs={{0,4},{4,8},{8,12},{12,16},{16,20},{20,24},{24,28},{1,5},{5,9},{9,... | collective-permute-start | bytes 3428360 | tf_op jit(solution)/shard_map/ppermute | solution.py:24
  9.9 4.4 %collective-permute-done.1 = bf16[3,8,384]{2,1,0:T(8,128)(2,1)S(1)} collective-permute-done((bf16[3,8,384]{2,1,0:T(8,128)(2,1)S(1)}, bf16[3,8,384]{2,1,0:T(8,128)(2,1)S(1)}, u32[]{:S(2)}, u32[]{:S(2)}) %collective-permute-start.1) | collective-permute-done | bytes 18464 | tf_op jit(solution)/shard_map/ppermute | solution.py:26
  14.3 18.2 %collective-permute-done = bf16[62,3,8,384]{3,2,1,0:T(8,128)(2,1)S(1)} collective-permute-done((bf16[62,3,8,384]{3,2,1,0:T(8,128)(2,1)S(1)}, bf16[62,3,8,384]{3,2,1,0:T(8,128)(2,1)S(1)}, u32[]{:S(2)}, u32[]{:S(2)}) %collective-permute-start) | collective-permute-done | bytes 1142816 | tf_op jit(solution)/shard_map/ppermute | solution.py:24
  33.5 2.0 pad_maximum_fusion
  38.3 2.5 %collective-permute-start.2 = (bf16[62,10,3,384]{3,0,2,1:T(8,128)(2,1)}, bf16[62,10,3,384]{3,0,2,1:T(8,128)(2,1)}, u32[]{:S(2)}, u32[]{:S(2)}) collective-permute-start(bf16[62,10,3,384]{3,0,2,1:T(8,128)(2,1)} %copy.79), channel_id=1, source_target_pairs={{0,1},{1,2},{2,3},{4,5},{5,6},{6,7},{8,9},{9,10},{10,11},{12,13},{... | collective-permute-start | bytes 4285448 | tf_op jit(solution)/shard_map/ppermute | solution.py:24
  44.5 8.7 %all-to-all-start = ((f32[32,1,24]{2,1,0:T(1,128)}), f32[32,1,24]{2,1,0:T(1,128)S(1)}, u32[]{:S(2)}, u32[]{:S(2)}) async-start(f32[32,1,24]{2,1,0:T(1,128)} %broadcast_in_dim.15), calls=%async_computation | async-start | bytes 32768 | tf_op jit(solution)/shard_map/all_to_all | solution.py:36
  53.5 12.9 %all-to-all-done = f32[32,1,24]{2,1,0:T(1,128)S(1)} async-done(((f32[32,1,24]{2,1,0:T(1,128)}), f32[32,1,24]{2,1,0:T(1,128)S(1)}, u32[]{:S(2)}, u32[]{:S(2)}) %all-to-all-start) | async-done | bytes 3104 | tf_op jit(solution)/shard_map/all_to_all | solution.py:36
  68.2 2.7 %copy.81 = bf16[62,10,3,384]{3,2,1,0:T(4,128)(2,1)S(1)} copy(bf16[62,10,3,384]{3,0,2,1:T(8,128)(2,1)} %collective-permute-done.2) | data formatting | bytes 2856960 | tf_op jit(solution)/shard_map/ppermute | solution.py:24
  70.9 2.6 %copy.82 = bf16[62,10,3,384]{3,2,1,0:T(4,128)(2,1)S(1)} copy(bf16[62,10,3,384]{3,0,2,1:T(8,128)(2,1)} %collective-permute-done.3) | data formatting | bytes 2856960 | tf_op jit(solution)/shard_map/ppermute | solution.py:26
  73.6 32.2 %select_maximum_fusion = bf16[62,10,14,390]{3,2,1,0:T(8,128)(2,1)S(1)} fusion(bf16[62,10,3,384]{3,2,1,0:T(4,128)(2,1)S(1)} %copy.82, bf16[62,10,3,384]{3,2,1,0:T(4,128)(2,1)S(1)} %copy.81, bf16[62,3,8,384]{3,2,1,0:T(8,128)(2,1)S(1)} %concatenate.29, bf16[62,3,8,384]{3,2,1,0:T(8,128)(2,1)S(1)} %copy-done.3, bf16[1,4,8,384]{3,2,1,0:T(8,128)(2,1)S(1)} %convert_bitcast_fusion, ...), kind=kLoop, calls=%fused_computation.3 | loop fusion | flops 71089200 | bytes 13436640 | tf_op jit(solution)/shard_map/concatenate | solution.py:27
  109.4 4.8 %add_bitcast_fusion.5 = (f32[1,4,8,384]{3,2,1,0:T(8,128)}, f32[4,8,384]{2,1,0:T(8,128)S(1)}, f32[4,8,384]{2,1,0:T(8,128)S(1)}, f32[4,8,384]{2,1,0:T(8,128)S(1)},...) fusion(bf16[10,14,390]{2,1,0:T(8,128)(2,1)} %get-tuple-element., ...), kind=kLoop, calls=%fused_computation.2524 | loop fusion | flops 6967296 | bytes 7913472 | tf_op jit(solution)/shard_map/stack | solution.py:143
  114.2 4.1 %add_bitcast_fusion.4 = f32[1,4,8,384]{3,2,1,0:T(8,128)} fusion(f32[4,8,384]{2,1,0:T(8,128)S(1)} %get-tuple-element.143, bf16[10,14,390]{2,1,0:T(8,128)(2,1)} %get-tuple-element.220, bf16[10,14,390]{2,1,0:T(8,128)(2,1)} %get-tuple-element.215, bf16[10,14,390]{2,1,0:T(8,128)(2,1)} %get-tuple-element.214, bf16[10,14,390]{2,1,0:T(8,128)(2,1)} %get-tuple-element.213, ...), kind=kLoop, calls=%fused_computation.2523 | loop fusion | flops 5173248 | bytes 5799936 | tf_op jit(solution)/shard_map/stack | solution.py:143
  118.7 3.8 %add_bitcast_fusion.3 = f32[1,4,8,384]{3,2,1,0:T(8,128)S(1)} fusion(f32[4,8,384]{2,1,0:T(8,128)S(1)} %get-tuple-element.161, f32[4,8,384]{2,1,0:T(8,128)S(1)} %get-tuple-element.160, bf16[10,14,390]{2,1,0:T(8,128)(2,1)} %get-tuple-element.221, bf16[10,14,390]{2,1,0:T(8,128)(2,1)} %get-tuple-element.222, bf16[10,14,390]{2,1,0:T(8,128)(2,1)} %get-tuple-element.220, ...), kind=kLoop, calls=%fused_computation.2522 | loop fusion | flops 5406720 | bytes 6045696 | tf_op jit(solution)/shard_map/stack | solution.py:143
  124.2 2.5 %collective-permute-start.4 = (f32[3,3,8,384]{3,2,1,0:T(8,128)}, f32[3,3,8,384]{3,2,1,0:T(8,128)S(1)}, u32[]{:S(2)}, u32[]{:S(2)}) collective-permute-start(f32[3,3,8,384]{3,2,1,0:T(8,128)} %get-tuple-element.244), channel_id=1, source_target_pairs={{0,4},{4,8},{8,12},{12,16},{16,20},{20,24},{24,28},{1,5},{5,9},{9,... | collective-permute-start | bytes 331784 | tf_op jit(solution)/shard_map/ppermute | solution.py:24
  129.4 5.0 %collective-permute-done.5 = f32[3,3,8,384]{3,2,1,0:T(8,128)} collective-permute-done((f32[3,3,8,384]{3,2,1,0:T(8,128)}, f32[3,3,8,384]{3,2,1,0:T(8,128)}, u32[]{:S(2)}, u32[]{:S(2)}) %collective-permute-start.5) | collective-permute-done | bytes 110624 | tf_op jit(solution)/shard_map/ppermute | solution.py:26
  141.6 1.8 select_maximum_fusion.6
  143.5 13.1 %add_add_fusion.2 = (f32[4,8,384]{2,1,0:T(8,128)S(1)}, f32[4,8,384]{2,1,0:T(8,128)S(1)}, f32[4,8,384]{2,1,0:T(8,128)S(1)}, f32[4,8,384]{2,1,0:T(8,128)S(1)}, f32...) fusion(f32[4,8,384]{2,1,0:T(8,128)} %squeeze.207, ...), kind=kLoop, calls=%fused_computation.2521 | loop fusion | flops 18382848 | bytes 27181056 | tf_op jit(solution)/shard_map/add | solution.py:168
  160.0 15.0 %all_to_all.24 = f32[32,1,26]{2,1,0:T(1,128)S(1)} all-to-all(f32[32,1,26]{2,1,0:T(1,128)S(1)} %broadcast_in_dim.16), channel_id=1, replica_groups=mesh['slab'=8,'col'=4] {'slab','col'}, dimensions={0} | all-to-all | bytes 6656 | tf_op jit(solution)/shard_map/all_to_all | solution.py:36
  179.4 2.4 %collective-permute-start.8 = (f32[3,3,8,384]{3,2,1,0:T(8,128)}, f32[3,3,8,384]{3,2,1,0:T(8,128)S(1)}, u32[]{:S(2)}, u32[]{:S(2)}) collective-permute-start(f32[3,3,8,384]{3,2,1,0:T(8,128)} %get-tuple-element.242), channel_id=1, source_target_pairs={{0,4},{4,8},{8,12},{12,16},{16,20},{20,24},{24,28},{1,5},{5,9},{9,... | collective-permute-start | bytes 331784 | tf_op jit(solution)/shard_map/ppermute | solution.py:24
  184.4 4.3 %collective-permute-done.9 = f32[3,3,8,384]{3,2,1,0:T(8,128)} collective-permute-done((f32[3,3,8,384]{3,2,1,0:T(8,128)}, f32[3,3,8,384]{3,2,1,0:T(8,128)}, u32[]{:S(2)}, u32[]{:S(2)}) %collective-permute-start.9) | collective-permute-done | bytes 110624 | tf_op jit(solution)/shard_map/ppermute | solution.py:26
  196.3 1.7 select_maximum_fusion.2
  198.1 13.0 %add_bitcast_fusion.2 = (f32[1,4,8,384]{3,2,1,0:T(8,128)S(1)}, f32[4,8,384]{2,1,0:T(8,128)S(1)}, f32[4,8,384]{2,1,0:T(8,128)S(1)}, f32[4,8,384]{2,1,0:T(8,128)S(...) fusion(f32[4,8,384]{2,1,0:T(8,128)} %squeeze.213, ...), kind=kLoop, calls=%fused_computation.2518 | loop fusion | flops 18382848 | bytes 27181056 | tf_op jit(solution)/shard_map/stack | solution.py:169
  212.6 2.6 %pad_maximum_fusion.8 = f32[4]{0:T(128)S(1)} fusion(f32[1]{0:T(128)} %bitcast.95, f32[1]{0:T(128)} %bitcast.94, f32[1]{0:T(128)} %bitcast.93, f32[1]{0:T(128)} %bitcast.85), kind=kLoop, calls=%fused_computation.2645 | loop fusion | flops 12 | bytes 32 | tf_op jit(solution)/shard_map/stack | solution.py:210
  215.1 13.3 %all_to_all.25 = f32[32,1,4]{2,1,0:T(1,128)S(1)} all-to-all(f32[32,1,4]{2,1,0:T(1,128)S(1)} %broadcast_in_dim.17), channel_id=1, replica_groups=mesh['slab'=8,'col'=4] {'slab','col'}, dimensions={0} | all-to-all | bytes 1024 | tf_op jit(solution)/shard_map/all_to_all | solution.py:36
  (207 shorter events, 48.2 us)
Async XLA Ops:
  2.8 29.7 %collective-permute-start = (bf16[62,3,8,384]{3,2,1,0:T(8,128)(2,1)S(1)}, bf16[62,3,8,384]{3,2,1,0:T(8,128)(2,1)S(1)}, u32[]{:S(2)}, u32[]{:S(2)}) collective-permute-start(bf16[62,3,8,384]{3,2,1,0:T(8,128)(2,1)S(1)} %pad_maximum_fusion.1), channel_id=1, source_target_pairs={{0,4},{4,8},{8,12},{12,16},{16,20},{20,24},{24,28},{1,5},{5,9},{9,... | collective-permute-start | bytes 3428360 | tf_op jit(solution)/shard_map/ppermute | solution.py:24
  8.6 5.7 %collective-permute-start.1 = (bf16[3,8,384]{2,1,0:T(8,128)(2,1)S(1)}, bf16[3,8,384]{2,1,0:T(8,128)(2,1)S(1)}, u32[]{:S(2)}, u32[]{:S(2)}) collective-permute-start(bf16[3,8,384]{2,1,0:T(8,128)(2,1)S(1)} %slice.6097), channel_id=1, source_target_pairs={{4,0},{8,4},{12,8},{16,12},{20,16},{24,20},{28,24},{5,1},{9,5},{13... | collective-permute-start | bytes 55304 | tf_op jit(solution)/shard_map/ppermute | solution.py:26
  36.9 16.6 %copy-start.54 = (f32[24,768]{1,0:T(8,128)S(1)}, f32[24,768]{1,0:T(8,128)}, u32[]{:S(2)}) copy-start(f32[24,768]{1,0:T(8,128)} %param.7) | copy-start | bytes 221188
  38.3 29.9 %collective-permute-start.2 = (bf16[62,10,3,384]{3,0,2,1:T(8,128)(2,1)}, bf16[62,10,3,384]{3,0,2,1:T(8,128)(2,1)}, u32[]{:S(2)}, u32[]{:S(2)}) collective-permute-start(bf16[62,10,3,384]{3,0,2,1:T(8,128)(2,1)} %copy.79), channel_id=1, source_target_pairs={{0,1},{1,2},{2,3},{4,5},{5,6},{6,7},{8,9},{9,10},{10,11},{12,13},{... | collective-permute-start | bytes 4285448 | tf_op jit(solution)/shard_map/ppermute | solution.py:24
  40.8 32.8 %copy-start = (bf16[61,4,8,384]{3,2,1,0:T(8,128)(2,1)S(1)}, bf16[61,4,8,384]{3,2,1,0:T(8,128)(2,1)}, u32[]{:S(2)}) copy-start(bf16[61,4,8,384]{3,2,1,0:T(8,128)(2,1)} %param.5) | copy-start | bytes 4497412
  42.2 28.7 %collective-permute-start.3 = (bf16[62,10,3,384]{3,0,2,1:T(8,128)(2,1)}, bf16[62,10,3,384]{3,0,2,1:T(8,128)(2,1)}, u32[]{:S(2)}, u32[]{:S(2)}) collective-permute-start(bf16[62,10,3,384]{3,0,2,1:T(8,128)(2,1)} %copy.80), channel_id=1, source_target_pairs={{1,0},{2,1},{3,2},{5,4},{6,5},{7,6},{9,8},{10,9},{11,10},{13,12},{... | collective-permute-start | bytes 4285448 | tf_op jit(solution)/shard_map/ppermute | solution.py:26
  44.5 21.9 %all-to-all-start = ((f32[32,1,24]{2,1,0:T(1,128)}), f32[32,1,24]{2,1,0:T(1,128)S(1)}, u32[]{:S(2)}, u32[]{:S(2)}) async-start(f32[32,1,24]{2,1,0:T(1,128)} %broadcast_in_dim.15), calls=%async_computation | async-start | bytes 32768 | tf_op jit(solution)/shard_map/all_to_all | solution.py:36
  106.2 16.3 %copy-start.5 = (bf16[10,14,390]{2,1,0:T(8,128)(2,1)}, bf16[10,14,390]{2,1,0:T(8,128)(2,1)S(1)}, u32[]{:S(2)}) copy-start(bf16[10,14,390]{2,1,0:T(8,128)(2,1)S(1)} %get-tuple-element.168) | copy-start | bytes 327604
  106.2 16.3 %copy-start.6 = (bf16[10,14,390]{2,1,0:T(8,128)(2,1)}, bf16[10,14,390]{2,1,0:T(8,128)(2,1)S(1)}, u32[]{:S(2)}) copy-start(bf16[10,14,390]{2,1,0:T(8,128)(2,1)S(1)} %get-tuple-element.169) | copy-start | bytes 327604
  106.2 16.3 %copy-start.7 = (bf16[10,14,390]{2,1,0:T(8,128)(2,1)}, bf16[10,14,390]{2,1,0:T(8,128)(2,1)S(1)}, u32[]{:S(2)}) copy-start(bf16[10,14,390]{2,1,0:T(8,128)(2,1)S(1)} %get-tuple-element.170) | copy-start | bytes 327604
  106.3 37.2 %copy-start.4 = (bf16[10,14,390]{2,1,0:T(8,128)(2,1)}, bf16[10,14,390]{2,1,0:T(8,128)(2,1)S(1)}, u32[]{:S(2)}) copy-start(bf16[10,14,390]{2,1,0:T(8,128)(2,1)S(1)} %get-tuple-element.167) | copy-start | bytes 327604
  122.6 18.3 %copy-start.43 = (f32[1,4,8,384]{3,2,1,0:T(8,128)}, f32[1,4,8,384]{3,2,1,0:T(8,128)S(1)}, u32[]{:S(2)}) copy-start(f32[1,4,8,384]{3,2,1,0:T(8,128)S(1)} %add_bitcast_fusion.3) | copy-start | bytes 147460
  124.2 5.2 %collective-permute-start.4 = (f32[3,3,8,384]{3,2,1,0:T(8,128)}, f32[3,3,8,384]{3,2,1,0:T(8,128)S(1)}, u32[]{:S(2)}, u32[]{:S(2)}) collective-permute-start(f32[3,3,8,384]{3,2,1,0:T(8,128)} %get-tuple-element.244), channel_id=1, source_target_pairs={{0,4},{4,8},{8,12},{12,16},{16,20},{20,24},{24,28},{1,5},{5,9},{9,... | collective-permute-start | bytes 331784 | tf_op jit(solution)/shard_map/ppermute | solution.py:24
  126.6 7.8 %collective-permute-start.5 = (f32[3,3,8,384]{3,2,1,0:T(8,128)}, f32[3,3,8,384]{3,2,1,0:T(8,128)}, u32[]{:S(2)}, u32[]{:S(2)}) collective-permute-start(f32[3,3,8,384]{3,2,1,0:T(8,128)} %get-tuple-element.245), channel_id=1, source_target_pairs={{4,0},{8,4},{12,8},{16,12},{20,16},{24,20},{28,24},{5,1},{9,5},{13... | collective-permute-start | bytes 331784 | tf_op jit(solution)/shard_map/ppermute | solution.py:26
  136.1 4.8 %collective-permute-start.6 = (f32[3,10,3,384]{3,2,1,0:T(4,128)}, f32[3,10,3,384]{3,2,1,0:T(4,128)S(1)}, u32[]{:S(2)}, u32[]{:S(2)}) collective-permute-start(f32[3,10,3,384]{3,2,1,0:T(4,128)} %get-tuple-element.240), channel_id=1, source_target_pairs={{0,1},{1,2},{2,3},{4,5},{5,6},{6,7},{8,9},{9,10},{10,11},{12,13},{... | collective-permute-start | bytes 414728 | tf_op jit(solution)/shard_map/ppermute | solution.py:24
  137.4 4.2 %collective-permute-start.7 = (f32[3,10,3,384]{3,2,1,0:T(4,128)}, f32[3,10,3,384]{3,2,1,0:T(4,128)}, u32[]{:S(2)}, u32[]{:S(2)}) collective-permute-start(f32[3,10,3,384]{3,2,1,0:T(4,128)} %get-tuple-element.241), channel_id=1, source_target_pairs={{1,0},{2,1},{3,2},{5,4},{6,5},{7,6},{9,8},{10,9},{11,10},{13,12},{... | collective-permute-start | bytes 414728 | tf_op jit(solution)/shard_map/ppermute | solution.py:26
  143.5 13.5 %copy-start.49 = (f32[4,8,384]{2,1,0:T(8,128)S(1)}, f32[4,8,384]{2,1,0:T(8,128)}, u32[]{:S(2)}) copy-start(f32[4,8,384]{2,1,0:T(8,128)} %squeeze.211) | copy-start | bytes 147460
  156.6 20.6 %copy-start.53 = (f32[32,1,24]{2,1,0:T(1,128)S(1)}, f32[32,1,24]{2,1,0:T(1,128)}, u32[]{:S(2)}) copy-start(f32[32,1,24]{2,1,0:T(1,128)} %copy-done.52) | copy-start | bytes 9220
  156.6 21.1 %copy-start.44 = (f32[1,4,8,384]{3,2,1,0:T(8,128)S(1)}, f32[1,4,8,384]{3,2,1,0:T(8,128)}, u32[]{:S(2)}) copy-start(f32[1,4,8,384]{3,2,1,0:T(8,128)} %copy-done.43) | copy-start | bytes 147460
  179.4 5.1 %collective-permute-start.8 = (f32[3,3,8,384]{3,2,1,0:T(8,128)}, f32[3,3,8,384]{3,2,1,0:T(8,128)S(1)}, u32[]{:S(2)}, u32[]{:S(2)}) collective-permute-start(f32[3,3,8,384]{3,2,1,0:T(8,128)} %get-tuple-element.242), channel_id=1, source_target_pairs={{0,4},{4,8},{8,12},{12,16},{16,20},{20,24},{24,28},{1,5},{5,9},{9,... | collective-permute-start | bytes 331784 | tf_op jit(solution)/shard_map/ppermute | solution.py:24
  181.8 7.0 %collective-permute-start.9 = (f32[3,3,8,384]{3,2,1,0:T(8,128)}, f32[3,3,8,384]{3,2,1,0:T(8,128)}, u32[]{:S(2)}, u32[]{:S(2)}) collective-permute-start(f32[3,3,8,384]{3,2,1,0:T(8,128)} %get-tuple-element.243), channel_id=1, source_target_pairs={{4,0},{8,4},{12,8},{16,12},{20,16},{24,20},{28,24},{5,1},{9,5},{13... | collective-permute-start | bytes 331784 | tf_op jit(solution)/shard_map/ppermute | solution.py:26
  190.5 4.8 %collective-permute-start.10 = (f32[3,10,3,384]{3,2,1,0:T(4,128)}, f32[3,10,3,384]{3,2,1,0:T(4,128)S(1)}, u32[]{:S(2)}, u32[]{:S(2)}) collective-permute-start(f32[3,10,3,384]{3,2,1,0:T(4,128)} %get-tuple-element.238), channel_id=1, source_target_pairs={{0,1},{1,2},{2,3},{4,5},{5,6},{6,7},{8,9},{9,10},{10,11},{12,13},{... | collective-permute-start | bytes 414728 | tf_op jit(solution)/shard_map/ppermute | solution.py:24
  191.8 4.5 %collective-permute-start.11 = (f32[3,10,3,384]{3,2,1,0:T(4,128)}, f32[3,10,3,384]{3,2,1,0:T(4,128)}, u32[]{:S(2)}, u32[]{:S(2)}) collective-permute-start(f32[3,10,3,384]{3,2,1,0:T(4,128)} %get-tuple-element.239), channel_id=1, source_target_pairs={{1,0},{2,1},{3,2},{5,4},{6,5},{7,6},{9,8},{10,9},{11,10},{13,12},{... | collective-permute-start | bytes 414728 | tf_op jit(solution)/shard_map/ppermute | solution.py:26
  198.1 13.4 %copy-start.47 = (f32[4,8,384]{2,1,0:T(8,128)S(1)}, f32[4,8,384]{2,1,0:T(8,128)}, u32[]{:S(2)}) copy-start(f32[4,8,384]{2,1,0:T(8,128)} %squeeze.217) | copy-start | bytes 147460
  (44 other events, 459.8 us)

commit v5 on v2

--- a/solution.py
+++ b/solution.py
@@ -28,6 +28,24 @@
     return x
 
 
+def lower_rows(levels, reach, width):
+    count, length = (lax.axis_size("slab"), levels.shape[1])
+    up = [(i, i + 1) for i in range(count - 1)]
+    starts = [int(np.argmax(reach >= depth)) for depth in range(1, width + 1)]
+    sent = jnp.concatenate(
+        [levels[start:, length - depth] for depth, start in zip(range(1, width + 1), starts)], axis=0
+    )
+    got = lax.ppermute(sent, "slab", up)
+    rows, at = ({}, 0)
+    for depth, start in zip(range(1, width + 1), starts):
+        size = levels.shape[0] - start
+        rows[depth] = jnp.concatenate(
+            [jnp.zeros((start,) + levels.shape[2:], levels.dtype), got[at : at + size]], axis=0
+        )
+        at = at + size
+    return jnp.stack([rows[depth] for depth in range(width, 0, -1)], axis=1)
+
+
 def device_rows(vector, axes):
     count = 1
     for axis in axes:
@@ -96,7 +114,7 @@
     def rimmed(vector):
         return pad_depth(with_halo(vector, (("slab", 1), ("col", 2)), 3))
 
-    lower_x = with_halo(integrity, (("slab", 1),), 3, high=False)
+    lower_x = jnp.concatenate([lower_rows(integrity, offsets[:, 0], 3), integrity], axis=1)
     spread = pad_depth(with_halo(lower_x, (("col", 2),), 3))
     contact_pad = pad_depth(
         with_halo(contact.astype(jnp.bfloat16), (("slab", 0), ("col", 1)), 3)

time: 197 us -> 193 us (0.980)
  other arithmetic: 63.4 us -> 72.3 us
  blocking collectives: 34 us -> 28.2 us
  starting transfers between devices: 51.8 us -> 48.1 us
  waiting for transfers between devices: 16.1 us -> 13.1 us
    ppermute x8 -> x7, waiting for transfers between devices: 14.6 us -> 0.02 us  [with_halo(): parts.insert(0, lax.ppermute(last, axis, up))]
    ppermute x7, waiting for transfers between devices: 1.46 us -> 13.1 us  [with_halo(): parts.append(lax.ppermute(first, axis, down))]
    ppermute x8 -> x7, starting transfers between devices: 38.7 us -> 27.3 us  [with_halo(): parts.insert(0, lax.ppermute(last, axis, up))]
    concatenate x6, other arithmetic: 13.3 us -> 19.7 us  [with_halo(): x = jnp.concatenate(parts, axis=dim)]
    all_to_all x2, blocking collectives: 34 us -> 28.2 us  [device_rows(): return lax.all_to_all(tiled, axes, 0, 0, tiled=True)]
    ppermute x0 -> x1, starting transfers between devices: none -> 4.9 us  [lower_rows(): got = lax.ppermute(sent, 'slab', up)]
    all_to_all x1, starting transfers between devices: 3.86 us -> 6.92 us  [device_rows(): return lax.all_to_all(tiled, axes, 0, 0, tiled=True)]
    squeeze x0 -> x3, local copies, waits for them, and re-layouts: none -> 2.61 us  [lower_rows(): levels[start:, length - depth]]
  transfers between devices with their start and end apart: 16 -> 16, of which waited for: 6 -> 4; matrix products, arithmetic and copies ran while one was open for 8% -> 9% of each run, Pallas kernels for 0% -> 0%
where the time goes in v5:
time: 193 us; the launch traced here: 192 us
  other arithmetic  72.3 us (37%)
  starting transfers between devices  48.1 us (25%)
  blocking collectives  28.2 us (15%)
  local copies, waits for them, and re-layouts  21.9 us (11%)
  waiting for transfers between devices  13.1 us (7%)
  between operations  7.79 us (4%)
    all_to_all x2, blocking collectives, device_rows(): return lax.all_to_all(tiled, axes, 0, 0, tiled=True)  28.2 us
    ppermute x7, starting transfers between devices, with_halo(): parts.insert(0, lax.ppermute(last, axis, up))  27.3 us
    concatenate x6, other arithmetic, with_halo(): x = jnp.concatenate(parts, axis=dim)  19.7 us
    ppermute x7, waiting for transfers between devices, with_halo(): parts.append(lax.ppermute(first, axis, down))  13.1 us
    another operation x3, other arithmetic, operator(): return jnp.stack(summed)  12.7 us
    add x3, other arithmetic, operator(): summed[component] = summed[component] + heading[component] * stretch  12.6 us
    another operation x3, other arithmetic, on_device(): diagonal = jnp.stack(diag_list)  10.6 us
    ppermute x7, starting transfers between devices, with_halo(): parts.append(lax.ppermute(first, axis, down))  8.98 us
  transfers between devices with their start and end apart: 16, of which 4 were waited for; matrix products, arithmetic and copies ran while one was open for 9% of the time, Pallas kernels for 0%

profile of v5, /device:TPU:0, one launch (start us, length us, event | category | flops | bytes accessed | tf_op | source)
XLA Modules:
  0.0 191.7 jit_solution(466346881033426238)
XLA Ops:
  3.3 4.9 %collective-permute-start = (bf16[70,8,384]{2,1,0:T(8,128)(2,1)S(1)}, bf16[70,8,384]{2,1,0:T(8,128)(2,1)S(1)}, u32[]{:S(2)}, u32[]{:S(2)}) collective-permute-start(bf16[70,8,384]{2,1,0:T(8,128)(2,1)S(1)} %pad_maximum_fusion.1), channel_id=1, source_target_pairs={{0,4},{4,8},{8,12},{12,16},{16,20},{20,24},{24,28},{1,5},{5,9},{9,... | collective-permute-start | bytes 1290248 | tf_op jit(solution)/shard_map/ppermute | solution.py:38
  9.0 3.4 %collective-permute-start.3 = (bf16[3,8,384]{2,1,0:T(8,128)(2,1)S(1)}, bf16[3,8,384]{2,1,0:T(8,128)(2,1)S(1)}, u32[]{:S(2)}, u32[]{:S(2)}) collective-permute-start(bf16[3,8,384]{2,1,0:T(8,128)(2,1)S(1)} %get-tuple-element.247), channel_id=1, source_target_pairs={{0,4},{4,8},{8,12},{12,16},{16,20},{20,24},{24,28},{1,5},{5,9},{9,... | collective-permute-start | bytes 55304 | tf_op jit(solution)/shard_map/ppermute | solution.py:24
  15.7 6.9 %all-to-all-start = ((f32[32,1,24]{2,1,0:T(1,128)}), f32[32,1,24]{2,1,0:T(1,128)S(1)}, u32[]{:S(2)}, u32[]{:S(2)}) async-start(f32[32,1,24]{2,1,0:T(1,128)} %broadcast_in_dim.9), calls=%async_computation | async-start | bytes 32768 | tf_op jit(solution)/shard_map/all_to_all | solution.py:54
  22.9 1.8 pad_maximum_fusion
  26.8 3.1 %collective-permute-start.1 = (bf16[61,7,3,384]{3,0,2,1:T(8,128)(2,1)}, bf16[61,7,3,384]{3,0,2,1:T(8,128)(2,1)}, u32[]{:S(2)}, u32[]{:S(2)}) collective-permute-start(bf16[61,7,3,384]{3,0,2,1:T(8,128)(2,1)} %copy.95), channel_id=1, source_target_pairs={{0,1},{1,2},{2,3},{4,5},{5,6},{6,7},{8,9},{9,10},{10,11},{12,13},{... | collective-permute-start | bytes 2951432 | tf_op jit(solution)/shard_map/ppermute | solution.py:24
  33.9 3.2 %collective-permute-start.5 = (bf16[10,3,384]{2,1,0:T(4,128)(2,1)S(1)}, bf16[10,3,384]{2,1,0:T(4,128)(2,1)S(1)}, u32[]{:S(2)}, u32[]{:S(2)}) collective-permute-start(bf16[10,3,384]{2,1,0:T(4,128)(2,1)S(1)} %get-tuple-element.245), channel_id=1, source_target_pairs={{0,1},{1,2},{2,3},{4,5},{5,6},{6,7},{8,9},{9,10},{10,11},{12,13},{... | collective-permute-start | bytes 69128 | tf_op jit(solution)/shard_map/ppermute | solution.py:24
  38.9 2.6 %collective-permute-done.6 = bf16[10,3,384]{2,1,0:T(4,128)(2,1)S(1)} collective-permute-done((bf16[10,3,384]{2,1,0:T(4,128)(2,1)S(1)}, bf16[10,3,384]{2,1,0:T(4,128)(2,1)S(1)}, u32[]{:S(2)}, u32[]{:S(2)}) %collective-permute-start.6) | collective-permute-done | bytes 23072 | tf_op jit(solution)/shard_map/ppermute | solution.py:26
  41.6 2.1 %copy.97 = bf16[61,7,3,384]{3,2,1,0:T(4,128)(2,1)S(1)} copy(bf16[61,7,3,384]{3,0,2,1:T(8,128)(2,1)} %collective-permute-done.1) | data formatting | bytes 1967616 | tf_op jit(solution)/shard_map/ppermute | solution.py:24
  43.7 2.1 %copy.98 = bf16[61,7,3,384]{3,2,1,0:T(4,128)(2,1)S(1)} copy(bf16[61,7,3,384]{3,0,2,1:T(8,128)(2,1)} %collective-permute-done.2) | data formatting | bytes 1967616 | tf_op jit(solution)/shard_map/ppermute | solution.py:26
  45.8 14.2 %select_maximum_fusion = bf16[61,7,14,390]{3,2,1,0:T(8,128)(2,1)S(1)} fusion(bf16[61,7,3,384]{3,2,1,0:T(4,128)(2,1)S(1)} %copy.98, bf16[61,7,3,384]{3,2,1,0:T(4,128)(2,1)S(1)} %copy.97, bf16[61,4,8,384]{3,2,1,0:T(8,128)(2,1)S(1)} %copy-done, bf16[61,1,8,384]{3,2,1,0:T(8,128)(2,1)S(1)} %get-tuple-element.249, ...), kind=kLoop, calls=%fused_computation.3 | loop fusion | flops 48959820 | bytes 9253944 | tf_op jit(solution)/shard_map/concatenate | solution.py:27
  62.0 4.4 %add_bitcast_fusion.5 = (f32[1,4,8,384]{3,2,1,0:T(8,128)}, f32[4,8,384]{2,1,0:T(8,128)S(1)}, f32[4,8,384]{2,1,0:T(8,128)S(1)}, f32[4,8,384]{2,1,0:T(8,128)S(1)},...) fusion(bf16[7,14,390]{2,1,0:T(8,128)(2,1)S(1)} %get-tuple-eleme, ...), kind=kLoop, calls=%fused_computation.2539 | loop fusion | flops 6967296 | bytes 7913472 | tf_op jit(solution)/shard_map/stack | solution.py:151
  66.4 2.9 %add_bitcast_fusion.4 = f32[1,4,8,384]{3,2,1,0:T(8,128)} fusion(f32[4,8,384]{2,1,0:T(8,128)S(1)} %get-tuple-element.143, bf16[7,14,390]{2,1,0:T(8,128)(2,1)S(1)} %get-tuple-element.220, bf16[7,14,390]{2,1,0:T(8,128)(2,1)S(1)} %get-tuple-element.215, bf16[7,14,390]{2,1,0:T(8,128)(2,1)S(1)} %get-tuple-element.214, ...), kind=kLoop, calls=%fused_computation.2538 | loop fusion | flops 5173248 | bytes 5799936 | tf_op jit(solution)/shard_map/stack | solution.py:151
  69.6 3.4 %add_bitcast_fusion.3 = f32[1,4,8,384]{3,2,1,0:T(8,128)S(1)} fusion(f32[4,8,384]{2,1,0:T(8,128)} %get-tuple-element.161, f32[4,8,384]{2,1,0:T(8,128)S(1)} %get-tuple-element.160, bf16[7,14,390]{2,1,0:T(8,128)(2,1)} %get-tuple-element.221, bf16[7,14,390]{2,1,0:T(8,128)(2,1)S(1)} %get-tuple-element.219, bf16[7,14,390]{2,1,0:T(8,128)(2,1)S(1)} %get-tuple-element.220, ...), kind=kLoop, calls=%fused_computation.2537 | loop fusion | flops 5406720 | bytes 6045696 | tf_op jit(solution)/shard_map/stack | solution.py:151
  75.3 4.0 %collective-permute-start.7 = (f32[3,3,8,384]{3,2,1,0:T(8,128)}, f32[3,3,8,384]{3,2,1,0:T(8,128)}, u32[]{:S(2)}, u32[]{:S(2)}) collective-permute-start(f32[3,3,8,384]{3,2,1,0:T(8,128)} %get-tuple-element.243), channel_id=1, source_target_pairs={{0,4},{4,8},{8,12},{12,16},{16,20},{20,24},{24,28},{1,5},{5,9},{9,... | collective-permute-start | bytes 331784 | tf_op jit(solution)/shard_map/ppermute | solution.py:24
  81.8 4.4 %collective-permute-done.8 = f32[3,3,8,384]{3,2,1,0:T(8,128)} collective-permute-done((f32[3,3,8,384]{3,2,1,0:T(8,128)}, f32[3,3,8,384]{3,2,1,0:T(8,128)}, u32[]{:S(2)}, u32[]{:S(2)}) %collective-permute-start.8) | collective-permute-done | bytes 110624 | tf_op jit(solution)/shard_map/ppermute | solution.py:26
  89.3 8.5 %collective-permute-start.9 = (f32[3,10,3,384]{3,2,1,0:T(4,128)}, f32[3,10,3,384]{3,2,1,0:T(4,128)}, u32[]{:S(2)}, u32[]{:S(2)}) collective-permute-start(f32[3,10,3,384]{3,2,1,0:T(4,128)} %get-tuple-element.239), channel_id=1, source_target_pairs={{0,1},{1,2},{2,3},{4,5},{5,6},{6,7},{8,9},{9,10},{10,11},{12,13},{... | collective-permute-start | bytes 414728 | tf_op jit(solution)/shard_map/ppermute | solution.py:24
  100.6 11.9 %add_add_fusion.2 = (f32[4,8,384]{2,1,0:T(8,128)S(1)}, f32[4,8,384]{2,1,0:T(8,128)S(1)}, f32[4,8,384]{2,1,0:T(8,128)S(1)}, f32[4,8,384]{2,1,0:T(8,128)S(1)}, f32...) fusion(f32[4,8,384]{2,1,0:T(8,128)} %squeeze.216, ...), kind=kLoop, calls=%fused_computation.2536 | loop fusion | flops 18382848 | bytes 27181056 | tf_op jit(solution)/shard_map/add | solution.py:176
  116.0 15.6 %all_to_all.24 = f32[32,1,26]{2,1,0:T(1,128)S(1)} all-to-all(f32[32,1,26]{2,1,0:T(1,128)S(1)} %broadcast_in_dim.10), channel_id=1, replica_groups=mesh['slab'=8,'col'=4] {'slab','col'}, dimensions={0} | all-to-all | bytes 6656 | tf_op jit(solution)/shard_map/all_to_all | solution.py:54
  136.6 3.1 %collective-permute-start.11 = (f32[3,3,8,384]{3,2,1,0:T(8,128)}, f32[3,3,8,384]{3,2,1,0:T(8,128)}, u32[]{:S(2)}, u32[]{:S(2)}) collective-permute-start(f32[3,3,8,384]{3,2,1,0:T(8,128)} %get-tuple-element.241), channel_id=1, source_target_pairs={{0,4},{4,8},{8,12},{12,16},{16,20},{20,24},{24,28},{1,5},{5,9},{9,... | collective-permute-start | bytes 331784 | tf_op jit(solution)/shard_map/ppermute | solution.py:24
  142.2 4.5 %collective-permute-done.12 = f32[3,3,8,384]{3,2,1,0:T(8,128)} collective-permute-done((f32[3,3,8,384]{3,2,1,0:T(8,128)}, f32[3,3,8,384]{3,2,1,0:T(8,128)}, u32[]{:S(2)}, u32[]{:S(2)}) %collective-permute-start.12) | collective-permute-done | bytes 110624 | tf_op jit(solution)/shard_map/ppermute | solution.py:26
  148.4 2.0 %collective-permute-start.13 = (f32[3,10,3,384]{3,2,1,0:T(4,128)}, f32[3,10,3,384]{3,2,1,0:T(4,128)}, u32[]{:S(2)}, u32[]{:S(2)}) collective-permute-start(f32[3,10,3,384]{3,2,1,0:T(4,128)} %get-tuple-element.237), channel_id=1, source_target_pairs={{0,1},{1,2},{2,3},{4,5},{5,6},{6,7},{8,9},{9,10},{10,11},{12,13},{... | collective-permute-start | bytes 414728 | tf_op jit(solution)/shard_map/ppermute | solution.py:24
  156.1 12.1 %add_bitcast_fusion.2 = (f32[1,4,8,384]{3,2,1,0:T(8,128)S(1)}, f32[4,8,384]{2,1,0:T(8,128)S(1)}, f32[4,8,384]{2,1,0:T(8,128)S(1)}, f32[4,8,384]{2,1,0:T(8,128)S(...) fusion(f32[4,8,384]{2,1,0:T(8,128)} %squeeze.222, ...), kind=kLoop, calls=%fused_computation.2533 | loop fusion | flops 18382848 | bytes 27181056 | tf_op jit(solution)/shard_map/stack | solution.py:177
  169.6 2.7 %pad_maximum_fusion.9 = f32[4]{0:T(128)S(1)} fusion(f32[1]{0:T(128)} %bitcast.99, f32[1]{0:T(128)} %bitcast.98, f32[1]{0:T(128)} %bitcast.97, f32[1]{0:T(128)} %bitcast.89), kind=kLoop, calls=%fused_computation.2661 | loop fusion | flops 12 | bytes 32 | tf_op jit(solution)/shard_map/stack | solution.py:218
  172.3 12.6 %all_to_all.25 = f32[32,1,4]{2,1,0:T(1,128)S(1)} all-to-all(f32[32,1,4]{2,1,0:T(1,128)S(1)} %broadcast_in_dim.11), channel_id=1, replica_groups=mesh['slab'=8,'col'=4] {'slab','col'}, dimensions={0} | all-to-all | bytes 1024 | tf_op jit(solution)/shard_map/all_to_all | solution.py:54
  (203 shorter events, 47.6 us)
Async XLA Ops:
  3.3 19.4 %collective-permute-start = (bf16[70,8,384]{2,1,0:T(8,128)(2,1)S(1)}, bf16[70,8,384]{2,1,0:T(8,128)(2,1)S(1)}, u32[]{:S(2)}, u32[]{:S(2)}) collective-permute-start(bf16[70,8,384]{2,1,0:T(8,128)(2,1)S(1)} %pad_maximum_fusion.1), channel_id=1, source_target_pairs={{0,4},{4,8},{8,12},{12,16},{16,20},{20,24},{24,28},{1,5},{5,9},{9,... | collective-permute-start | bytes 1290248 | tf_op jit(solution)/shard_map/ppermute | solution.py:38
  9.0 24.8 %collective-permute-start.3 = (bf16[3,8,384]{2,1,0:T(8,128)(2,1)S(1)}, bf16[3,8,384]{2,1,0:T(8,128)(2,1)S(1)}, u32[]{:S(2)}, u32[]{:S(2)}) collective-permute-start(bf16[3,8,384]{2,1,0:T(8,128)(2,1)S(1)} %get-tuple-element.247), channel_id=1, source_target_pairs={{0,4},{4,8},{8,12},{12,16},{16,20},{20,24},{24,28},{1,5},{5,9},{9,... | collective-permute-start | bytes 55304 | tf_op jit(solution)/shard_map/ppermute | solution.py:24
  12.5 21.4 %collective-permute-start.4 = (bf16[3,8,384]{2,1,0:T(8,128)(2,1)S(1)}, bf16[3,8,384]{2,1,0:T(8,128)(2,1)S(1)}, u32[]{:S(2)}, u32[]{:S(2)}) collective-permute-start(bf16[3,8,384]{2,1,0:T(8,128)(2,1)S(1)} %get-tuple-element.248), channel_id=1, source_target_pairs={{4,0},{8,4},{12,8},{16,12},{20,16},{24,20},{28,24},{5,1},{9,5},{13... | collective-permute-start | bytes 55304 | tf_op jit(solution)/shard_map/ppermute | solution.py:26
  15.7 16.9 %all-to-all-start = ((f32[32,1,24]{2,1,0:T(1,128)}), f32[32,1,24]{2,1,0:T(1,128)S(1)}, u32[]{:S(2)}, u32[]{:S(2)}) async-start(f32[32,1,24]{2,1,0:T(1,128)} %broadcast_in_dim.9), calls=%async_computation | async-start | bytes 32768 | tf_op jit(solution)/shard_map/all_to_all | solution.py:54
  24.7 21.1 %copy-start = (bf16[61,4,8,384]{3,2,1,0:T(8,128)(2,1)S(1)}, bf16[61,4,8,384]{3,2,1,0:T(8,128)(2,1)}, u32[]{:S(2)}) copy-start(bf16[61,4,8,384]{3,2,1,0:T(8,128)(2,1)} %param.5) | copy-start | bytes 4497412
  26.8 14.9 %collective-permute-start.1 = (bf16[61,7,3,384]{3,0,2,1:T(8,128)(2,1)}, bf16[61,7,3,384]{3,0,2,1:T(8,128)(2,1)}, u32[]{:S(2)}, u32[]{:S(2)}) collective-permute-start(bf16[61,7,3,384]{3,0,2,1:T(8,128)(2,1)} %copy.95), channel_id=1, source_target_pairs={{0,1},{1,2},{2,3},{4,5},{5,6},{6,7},{8,9},{9,10},{10,11},{12,13},{... | collective-permute-start | bytes 2951432 | tf_op jit(solution)/shard_map/ppermute | solution.py:24
  31.1 12.7 %collective-permute-start.2 = (bf16[61,7,3,384]{3,0,2,1:T(8,128)(2,1)}, bf16[61,7,3,384]{3,0,2,1:T(8,128)(2,1)}, u32[]{:S(2)}, u32[]{:S(2)}) collective-permute-start(bf16[61,7,3,384]{3,0,2,1:T(8,128)(2,1)} %copy.96), channel_id=1, source_target_pairs={{1,0},{2,1},{3,2},{5,4},{6,5},{7,6},{9,8},{10,9},{11,10},{13,12},{... | collective-permute-start | bytes 2951432 | tf_op jit(solution)/shard_map/ppermute | solution.py:26
  32.5 13.3 %copy-start.41 = (f32[8,3,768]{2,1,0:T(4,128)}, f32[8,3,768]{2,1,0:T(4,128)S(1)}, u32[]{:S(2)}) copy-start(f32[8,3,768]{2,1,0:T(4,128)S(1)} %dot_general.8) | copy-start | bytes 221188
  33.9 5.0 %collective-permute-start.5 = (bf16[10,3,384]{2,1,0:T(4,128)(2,1)S(1)}, bf16[10,3,384]{2,1,0:T(4,128)(2,1)S(1)}, u32[]{:S(2)}, u32[]{:S(2)}) collective-permute-start(bf16[10,3,384]{2,1,0:T(4,128)(2,1)S(1)} %get-tuple-element.245), channel_id=1, source_target_pairs={{0,1},{1,2},{2,3},{4,5},{5,6},{6,7},{8,9},{9,10},{10,11},{12,13},{... | collective-permute-start | bytes 69128 | tf_op jit(solution)/shard_map/ppermute | solution.py:24
  37.1 4.3 %collective-permute-start.6 = (bf16[10,3,384]{2,1,0:T(4,128)(2,1)S(1)}, bf16[10,3,384]{2,1,0:T(4,128)(2,1)S(1)}, u32[]{:S(2)}, u32[]{:S(2)}) collective-permute-start(bf16[10,3,384]{2,1,0:T(4,128)(2,1)S(1)} %get-tuple-element.246), channel_id=1, source_target_pairs={{1,0},{2,1},{3,2},{5,4},{6,5},{7,6},{9,8},{10,9},{11,10},{13,12},{... | collective-permute-start | bytes 69128 | tf_op jit(solution)/shard_map/ppermute | solution.py:26
  60.3 12.7 %copy-start.4 = (bf16[7,14,390]{2,1,0:T(8,128)(2,1)}, bf16[7,14,390]{2,1,0:T(8,128)(2,1)S(1)}, u32[]{:S(2)}) copy-start(bf16[7,14,390]{2,1,0:T(8,128)(2,1)S(1)} %get-tuple-element.175) | copy-start | bytes 229324
  60.3 20.3 %copy-start.5 = (bf16[7,14,390]{2,1,0:T(8,128)(2,1)}, bf16[7,14,390]{2,1,0:T(8,128)(2,1)S(1)}, u32[]{:S(2)}) copy-start(bf16[7,14,390]{2,1,0:T(8,128)(2,1)S(1)} %get-tuple-element.176) | copy-start | bytes 229324
  60.3 52.3 %copy-start.2 = (bf16[7,14,390]{2,1,0:T(8,128)(2,1)}, bf16[7,14,390]{2,1,0:T(8,128)(2,1)S(1)}, u32[]{:S(2)}) copy-start(bf16[7,14,390]{2,1,0:T(8,128)(2,1)S(1)} %get-tuple-element.173) | copy-start | bytes 229324
  60.3 52.3 %copy-start.3 = (bf16[7,14,390]{2,1,0:T(8,128)(2,1)}, bf16[7,14,390]{2,1,0:T(8,128)(2,1)S(1)}, u32[]{:S(2)}) copy-start(bf16[7,14,390]{2,1,0:T(8,128)(2,1)S(1)} %get-tuple-element.174) | copy-start | bytes 229324
  62.0 11.0 %copy-start.40 = (bf16[7,14,390]{2,1,0:T(8,128)(2,1)}, bf16[7,14,390]{2,1,0:T(8,128)(2,1)S(1)}, u32[]{:S(2)}) copy-start(bf16[7,14,390]{2,1,0:T(8,128)(2,1)S(1)} %get-tuple-element.219) | copy-start | bytes 229324
  75.3 6.5 %collective-permute-start.7 = (f32[3,3,8,384]{3,2,1,0:T(8,128)}, f32[3,3,8,384]{3,2,1,0:T(8,128)}, u32[]{:S(2)}, u32[]{:S(2)}) collective-permute-start(f32[3,3,8,384]{3,2,1,0:T(8,128)} %get-tuple-element.243), channel_id=1, source_target_pairs={{0,4},{4,8},{8,12},{12,16},{16,20},{20,24},{24,28},{1,5},{5,9},{9,... | collective-permute-start | bytes 331784 | tf_op jit(solution)/shard_map/ppermute | solution.py:24
  79.3 6.9 %collective-permute-start.8 = (f32[3,3,8,384]{3,2,1,0:T(8,128)}, f32[3,3,8,384]{3,2,1,0:T(8,128)}, u32[]{:S(2)}, u32[]{:S(2)}) collective-permute-start(f32[3,3,8,384]{3,2,1,0:T(8,128)} %get-tuple-element.244), channel_id=1, source_target_pairs={{4,0},{8,4},{12,8},{16,12},{20,16},{24,20},{28,24},{5,1},{9,5},{13... | collective-permute-start | bytes 331784 | tf_op jit(solution)/shard_map/ppermute | solution.py:26
  88.0 10.8 %collective-permute-start.10 = (f32[3,10,3,384]{3,2,1,0:T(4,128)}, f32[3,10,3,384]{3,2,1,0:T(4,128)}, u32[]{:S(2)}, u32[]{:S(2)}) collective-permute-start(f32[3,10,3,384]{3,2,1,0:T(4,128)} %get-tuple-element.240), channel_id=1, source_target_pairs={{1,0},{2,1},{3,2},{5,4},{6,5},{7,6},{9,8},{10,9},{11,10},{13,12},{... | collective-permute-start | bytes 414728 | tf_op jit(solution)/shard_map/ppermute | solution.py:26
  89.3 9.5 %collective-permute-start.9 = (f32[3,10,3,384]{3,2,1,0:T(4,128)}, f32[3,10,3,384]{3,2,1,0:T(4,128)}, u32[]{:S(2)}, u32[]{:S(2)}) collective-permute-start(f32[3,10,3,384]{3,2,1,0:T(4,128)} %get-tuple-element.239), channel_id=1, source_target_pairs={{0,1},{1,2},{2,3},{4,5},{5,6},{6,7},{8,9},{9,10},{10,11},{12,13},{... | collective-permute-start | bytes 414728 | tf_op jit(solution)/shard_map/ppermute | solution.py:24
  112.6 21.3 %copy-start.42 = (f32[8,3,768]{2,1,0:T(4,128)S(1)}, f32[8,3,768]{2,1,0:T(4,128)}, u32[]{:S(2)}) copy-start(f32[8,3,768]{2,1,0:T(4,128)} %copy-done.41) | copy-start | bytes 221188
  136.6 5.6 %collective-permute-start.11 = (f32[3,3,8,384]{3,2,1,0:T(8,128)}, f32[3,3,8,384]{3,2,1,0:T(8,128)}, u32[]{:S(2)}, u32[]{:S(2)}) collective-permute-start(f32[3,3,8,384]{3,2,1,0:T(8,128)} %get-tuple-element.241), channel_id=1, source_target_pairs={{0,4},{4,8},{8,12},{12,16},{16,20},{20,24},{24,28},{1,5},{5,9},{9,... | collective-permute-start | bytes 331784 | tf_op jit(solution)/shard_map/ppermute | solution.py:24
  139.7 6.9 %collective-permute-start.12 = (f32[3,3,8,384]{3,2,1,0:T(8,128)}, f32[3,3,8,384]{3,2,1,0:T(8,128)}, u32[]{:S(2)}, u32[]{:S(2)}) collective-permute-start(f32[3,3,8,384]{3,2,1,0:T(8,128)} %get-tuple-element.242), channel_id=1, source_target_pairs={{4,0},{8,4},{12,8},{16,12},{20,16},{24,20},{28,24},{5,1},{9,5},{13... | collective-permute-start | bytes 331784 | tf_op jit(solution)/shard_map/ppermute | solution.py:26
  148.4 4.2 %collective-permute-start.13 = (f32[3,10,3,384]{3,2,1,0:T(4,128)}, f32[3,10,3,384]{3,2,1,0:T(4,128)}, u32[]{:S(2)}, u32[]{:S(2)}) collective-permute-start(f32[3,10,3,384]{3,2,1,0:T(4,128)} %get-tuple-element.237), channel_id=1, source_target_pairs={{0,1},{1,2},{2,3},{4,5},{5,6},{6,7},{8,9},{9,10},{10,11},{12,13},{... | collective-permute-start | bytes 414728 | tf_op jit(solution)/shard_map/ppermute | solution.py:24
  150.4 3.8 %collective-permute-start.14 = (f32[3,10,3,384]{3,2,1,0:T(4,128)}, f32[3,10,3,384]{3,2,1,0:T(4,128)}, u32[]{:S(2)}, u32[]{:S(2)}) collective-permute-start(f32[3,10,3,384]{3,2,1,0:T(4,128)} %get-tuple-element.238), channel_id=1, source_target_pairs={{1,0},{2,1},{3,2},{5,4},{6,5},{7,6},{9,8},{10,9},{11,10},{13,12},{... | collective-permute-start | bytes 414728 | tf_op jit(solution)/shard_map/ppermute | solution.py:26
  (37 other events, 320.8 us)

commit v6 on v5

--- a/solution.py
+++ b/solution.py
@@ -139,9 +139,12 @@
         forward = window(inside_pad, shift_x, shift_y, shift_z, extent) * forward
         return (forward, backward)
 
+    coefficients = lax.optimization_barrier(
+        jnp.stack([jnp.stack(bond_pair(bond_index)) for bond_index in range(bond_count)])
+    )
     diag_list = [jnp.full(extent, FOUNDATION, jnp.float32) for component in range(3)]
     for bond_index in range(bond_count):
-        forward, backward = bond_pair(bond_index)
+        forward, backward = (coefficients[bond_index, 0], coefficients[bond_index, 1])
         heading = heading_of(bond_index)
         both_ends = forward + backward
         for component in range(3):
@@ -155,7 +158,7 @@
         summed = [FOUNDATION * vector[component] for component in range(3)]
         for bond_index in range(bond_count):
             shift_x, shift_y, shift_z = bond_shift(bond_index)
-            forward, backward = bond_pair(bond_index)
+            forward, backward = (coefficients[bond_index, 0], coefficients[bond_index, 1])
             heading = heading_of(bond_index)
             ahead_part = heading[0] * (
                 vector[0] - window(padded[0], shift_x, shift_y, shift_z, extent)

time: 193 us -> 196 us (1.016)
  waiting for transfers between devices: 13.1 us -> 28.7 us
  other arithmetic: 72.3 us -> 66.7 us
  local copies, waits for them, and re-layouts: 21.9 us -> 17 us
  starting transfers between devices: 48.1 us -> 44.5 us
    ppermute x1, waiting for transfers between devices: 0.01 us -> 8.76 us  [lower_rows(): got = lax.ppermute(sent, 'slab', up)]
    ppermute x7, waiting for transfers between devices: 13.1 us -> 18.5 us  [with_halo(): parts.append(lax.ppermute(first, axis, down))]
    another operation x3 -> x53, other arithmetic: 10.6 us -> 6.03 us  [the longest x52 6.02 us: on_device(): jnp.stack(bond_pair(bond_index))]
    concatenate x6, other arithmetic: 19.7 us -> 15.3 us  [with_halo(): x = jnp.concatenate(parts, axis=dim)]
    ppermute x7, starting transfers between devices: 27.3 us -> 23.2 us  [with_halo(): parts.insert(0, lax.ppermute(last, axis, up))]
    add x4, other arithmetic: 3.26 us -> 0.27 us  [precondition(): (vector / diagonal).reshape(3, cells_x * cells_y, aggregates, agg_depth)]
    slice x8, local copies, waits for them, and re-layouts: 5.08 us -> 2.19 us  [with_halo(): last = lax.slice_in_dim(x, length - width, length, axis=dim)]
    add x3, other arithmetic: 12.6 us -> 14.9 us  [operator(): summed[component] = summed[component] + heading[component] * stretch]
  transfers between devices with their start and end apart: 16 -> 16, of which waited for: 4 -> 8; matrix products, arithmetic and copies ran while one was open for 9% -> 8% of each run, Pallas kernels for 0% -> 0%
where the time goes in v6:
time: 196 us; the launch traced here: 194 us
  other arithmetic  66.7 us (34%)
  starting transfers between devices  44.5 us (23%)
  blocking collectives  29 us (15%)
  waiting for transfers between devices  28.7 us (15%)
  local copies, waits for them, and re-layouts  17 us (9%)
  between operations  7.75 us (4%)
    all_to_all x2, blocking collectives, device_rows(): return lax.all_to_all(tiled, axes, 0, 0, tiled=True)  29 us
    ppermute x7, starting transfers between devices, with_halo(): parts.insert(0, lax.ppermute(last, axis, up))  23.2 us
    ppermute x7, waiting for transfers between devices, with_halo(): parts.append(lax.ppermute(first, axis, down))  18.5 us
    concatenate x6, other arithmetic, with_halo(): x = jnp.concatenate(parts, axis=dim)  15.3 us
    another operation x3, other arithmetic, operator(): return jnp.stack(summed)  15 us
    add x3, other arithmetic, operator(): summed[component] = summed[component] + heading[component] * stretch  14.9 us
    ppermute x7, starting transfers between devices, with_halo(): parts.append(lax.ppermute(first, axis, down))  9.43 us
    ppermute x1, waiting for transfers between devices, lower_rows(): got = lax.ppermute(sent, 'slab', up)  8.76 us
  transfers between devices with their start and end apart: 16, of which 8 were waited for; matrix products, arithmetic and copies ran while one was open for 8% of the time, Pallas kernels for 0%

profile of v6, /device:TPU:0, one launch (start us, length us, event | category | flops | bytes accessed | tf_op | source)
XLA Modules:
  0.0 194.0 jit_solution(3214018255962701589)
XLA Ops:
  2.5 7.3 %all-to-all-start = ((f32[32,1,24]{2,1,0:T(1,128)}), f32[32,1,24]{2,1,0:T(1,128)S(1)}, u32[]{:S(2)}, u32[]{:S(2)}) async-start(f32[32,1,24]{2,1,0:T(1,128)} %broadcast_in_dim.9), calls=%async_computation | async-start | bytes 32768 | tf_op jit(solution)/shard_map/all_to_all | solution.py:54
  10.7 3.7 %collective-permute-start.3 = (bf16[3,8,384]{2,1,0:T(8,128)(2,1)S(1)}, bf16[3,8,384]{2,1,0:T(8,128)(2,1)S(1)}, u32[]{:S(2)}, u32[]{:S(2)}) collective-permute-start(bf16[3,8,384]{2,1,0:T(8,128)(2,1)S(1)} %get-tuple-element.309), channel_id=1, source_target_pairs={{0,4},{4,8},{8,12},{12,16},{16,20},{20,24},{24,28},{1,5},{5,9},{9,... | collective-permute-start | bytes 55304 | tf_op jit(solution)/shard_map/ppermute | solution.py:24
  18.3 4.6 %collective-permute-start = (bf16[70,8,384]{2,1,0:T(8,128)(2,1)S(1)}, bf16[70,8,384]{2,1,0:T(8,128)(2,1)S(1)}, u32[]{:S(2)}, u32[]{:S(2)}) collective-permute-start(bf16[70,8,384]{2,1,0:T(8,128)(2,1)S(1)} %pad_maximum_fusion.1), channel_id=1, source_target_pairs={{0,4},{4,8},{8,12},{12,16},{16,20},{20,24},{24,28},{1,5},{5,9},{9,... | collective-permute-start | bytes 1290248 | tf_op jit(solution)/shard_map/ppermute | solution.py:38
  23.0 8.8 %collective-permute-done = bf16[70,8,384]{2,1,0:T(8,128)(2,1)S(1)} collective-permute-done((bf16[70,8,384]{2,1,0:T(8,128)(2,1)S(1)}, bf16[70,8,384]{2,1,0:T(8,128)(2,1)S(1)}, u32[]{:S(2)}, u32[]{:S(2)}) %collective-permute-start) | collective-permute-done | bytes 430112 | tf_op jit(solution)/shard_map/ppermute | solution.py:38
  32.0 1.8 pad_maximum_fusion
  38.3 4.1 %collective-permute-start.1 = (bf16[61,7,3,384]{3,0,2,1:T(8,128)(2,1)}, bf16[61,7,3,384]{3,0,2,1:T(8,128)(2,1)}, u32[]{:S(2)}, u32[]{:S(2)}) collective-permute-start(bf16[61,7,3,384]{3,0,2,1:T(8,128)(2,1)} %copy.95), channel_id=1, source_target_pairs={{0,1},{1,2},{2,3},{4,5},{5,6},{6,7},{8,9},{9,10},{10,11},{12,13},{... | collective-permute-start | bytes 2951432 | tf_op jit(solution)/shard_map/ppermute | solution.py:24
  43.9 2.0 %collective-permute-start.5 = (bf16[10,3,384]{2,1,0:T(4,128)(2,1)S(1)}, bf16[10,3,384]{2,1,0:T(4,128)(2,1)S(1)}, u32[]{:S(2)}, u32[]{:S(2)}) collective-permute-start(bf16[10,3,384]{2,1,0:T(4,128)(2,1)S(1)} %get-tuple-element.307), channel_id=1, source_target_pairs={{0,1},{1,2},{2,3},{4,5},{5,6},{6,7},{8,9},{9,10},{10,11},{12,13},{... | collective-permute-start | bytes 69128 | tf_op jit(solution)/shard_map/ppermute | solution.py:24
  47.8 2.1 %collective-permute-done.6 = bf16[10,3,384]{2,1,0:T(4,128)(2,1)S(1)} collective-permute-done((bf16[10,3,384]{2,1,0:T(4,128)(2,1)S(1)}, bf16[10,3,384]{2,1,0:T(4,128)(2,1)S(1)}, u32[]{:S(2)}, u32[]{:S(2)}) %collective-permute-start.6) | collective-permute-done | bytes 23072 | tf_op jit(solution)/shard_map/ppermute | solution.py:26
  50.1 2.1 %copy.98 = bf16[61,7,3,384]{3,2,1,0:T(4,128)(2,1)S(1)} copy(bf16[61,7,3,384]{3,0,2,1:T(8,128)(2,1)} %collective-permute-done.2) | data formatting | bytes 1967616 | tf_op jit(solution)/shard_map/ppermute | solution.py:26
  52.2 2.1 %copy.97 = bf16[61,7,3,384]{3,2,1,0:T(4,128)(2,1)S(1)} copy(bf16[61,7,3,384]{3,0,2,1:T(8,128)(2,1)} %collective-permute-done.1) | data formatting | bytes 1967616 | tf_op jit(solution)/shard_map/ppermute | solution.py:24
  54.3 14.0 %select_maximum_fusion = bf16[61,7,14,390]{3,2,1,0:T(8,128)(2,1)S(1)} fusion(bf16[61,7,3,384]{3,2,1,0:T(4,128)(2,1)S(1)} %copy.98, bf16[61,7,3,384]{3,2,1,0:T(4,128)(2,1)S(1)} %copy.97, bf16[61,4,8,384]{3,2,1,0:T(8,128)(2,1)S(1)} %copy-done.1, bf16[61,1,8,384]{3,2,1,0:T(8,128)(2,1)S(1)} %get-tuple-element.311, ...), kind=kLoop, calls=%fused_computation.3 | loop fusion | flops 48959820 | bytes 9253944 | tf_op jit(solution)/shard_map/concatenate | solution.py:27
  79.2 4.4 %collective-permute-start.7 = (f32[3,3,8,384]{3,2,1,0:T(8,128)S(1)}, f32[3,3,8,384]{3,2,1,0:T(8,128)S(1)}, u32[]{:S(2)}, u32[]{:S(2)}) collective-permute-start(f32[3,3,8,384]{3,2,1,0:T(8,128)S(1)} %get-tuple-element.295), channel_id=1, source_target_pairs={{0,4},{4,8},{8,12},{12,16},{16,20},{20,24},{24,28},{1,5},{5,9},{9,... | collective-permute-start | bytes 331784 | tf_op jit(solution)/shard_map/ppermute | solution.py:24
  85.9 5.6 %collective-permute-done.8 = f32[3,3,8,384]{3,2,1,0:T(8,128)S(1)} collective-permute-done((f32[3,3,8,384]{3,2,1,0:T(8,128)S(1)}, f32[3,3,8,384]{3,2,1,0:T(8,128)S(1)}, u32[]{:S(2)}, u32[]{:S(2)}) %collective-permute-start.8) | collective-permute-done | bytes 110624 | tf_op jit(solution)/shard_map/ppermute | solution.py:26
  91.5 5.3 %collective-permute-start.9 = (f32[3,10,3,384]{3,2,1,0:T(4,128)S(1)}, f32[3,10,3,384]{3,2,1,0:T(4,128)S(1)}, u32[]{:S(2)}, u32[]{:S(2)}) collective-permute-start(f32[3,10,3,384]{3,2,1,0:T(4,128)S(1)} %get-tuple-element.233), channel_id=1, source_target_pairs={{0,1},{1,2},{2,3},{4,5},{5,6},{6,7},{8,9},{9,10},{10,11},{12,13},{... | collective-permute-start | bytes 414728 | tf_op jit(solution)/shard_map/ppermute | solution.py:24
  98.8 4.6 %collective-permute-done.10 = f32[3,10,3,384]{3,2,1,0:T(4,128)S(1)} collective-permute-done((f32[3,10,3,384]{3,2,1,0:T(4,128)S(1)}, f32[3,10,3,384]{3,2,1,0:T(4,128)S(1)}, u32[]{:S(2)}, u32[]{:S(2)}) %collective-permute-start.10) | collective-permute-done | bytes 138272 | tf_op jit(solution)/shard_map/ppermute | solution.py:26
  104.0 11.7 %add_add_fusion.2 = (f32[4,8,384]{2,1,0:T(8,128)S(1)}, f32[4,8,384]{2,1,0:T(8,128)S(1)}, f32[4,8,384]{2,1,0:T(8,128)S(1)}, f32[4,8,384]{2,1,0:T(8,128)S(1)}, f32...) fusion(f32[4,8,384]{2,1,0:T(8,128)S(1)} %squeeze.460, ...), kind=kLoop, calls=%fused_computation.2879 | loop fusion | flops 15187968 | bytes 27181056 | tf_op jit(solution)/shard_map/add | solution.py:179
  117.3 1.6 add_add_fusion
  121.7 15.7 %all_to_all.24 = f32[32,1,26]{2,1,0:T(1,128)S(1)} all-to-all(f32[32,1,26]{2,1,0:T(1,128)S(1)} %broadcast_in_dim.10), channel_id=1, replica_groups=mesh['slab'=8,'col'=4] {'slab','col'}, dimensions={0} | all-to-all | bytes 6656 | tf_op jit(solution)/shard_map/all_to_all | solution.py:54
  140.2 2.5 %collective-permute-start.11 = (f32[3,3,8,384]{3,2,1,0:T(8,128)S(1)}, f32[3,3,8,384]{3,2,1,0:T(8,128)S(1)}, u32[]{:S(2)}, u32[]{:S(2)}) collective-permute-start(f32[3,3,8,384]{3,2,1,0:T(8,128)S(1)} %get-tuple-element.293), channel_id=1, source_target_pairs={{0,4},{4,8},{8,12},{12,16},{16,20},{20,24},{24,28},{1,5},{5,9},{9,... | collective-permute-start | bytes 331784 | tf_op jit(solution)/shard_map/ppermute | solution.py:24
  145.0 4.3 %collective-permute-done.12 = f32[3,3,8,384]{3,2,1,0:T(8,128)S(1)} collective-permute-done((f32[3,3,8,384]{3,2,1,0:T(8,128)S(1)}, f32[3,3,8,384]{3,2,1,0:T(8,128)S(1)}, u32[]{:S(2)}, u32[]{:S(2)}) %collective-permute-start.12) | collective-permute-done | bytes 110624 | tf_op jit(solution)/shard_map/ppermute | solution.py:26
  153.0 1.9 collective-permute-done.14
  155.6 11.7 %add_bitcast_fusion.2 = (f32[1,4,8,384]{3,2,1,0:T(8,128)S(1)}, f32[4,8,384]{2,1,0:T(8,128)S(1)}, f32[4,8,384]{2,1,0:T(8,128)S(1)}, f32[4,8,384]{2,1,0:T(8,128)S(...) fusion(f32[4,8,384]{2,1,0:T(8,128)} %squeeze.588, ...), kind=kLoop, calls=%fused_computation.2876 | loop fusion | flops 15187968 | bytes 27181056 | tf_op jit(solution)/shard_map/stack | solution.py:180
  171.4 2.6 %pad_maximum_fusion.9 = f32[4]{0:T(128)S(1)} fusion(f32[1]{0:T(128)} %bitcast.502, f32[1]{0:T(128)} %bitcast.501, f32[1]{0:T(128)} %bitcast.500, f32[1]{0:T(128)} %bitcast.492), kind=kLoop, calls=%fused_computation.3010 | loop fusion | flops 12 | bytes 32 | tf_op jit(solution)/shard_map/stack | solution.py:221
  174.0 13.3 %all_to_all.25 = f32[32,1,4]{2,1,0:T(1,128)S(1)} all-to-all(f32[32,1,4]{2,1,0:T(1,128)S(1)} %broadcast_in_dim.11), channel_id=1, replica_groups=mesh['slab'=8,'col'=4] {'slab','col'}, dimensions={0} | all-to-all | bytes 1024 | tf_op jit(solution)/shard_map/all_to_all | solution.py:54
  (234 shorter events, 48.6 us)
Async XLA Ops:
  2.5 39.9 %all-to-all-start = ((f32[32,1,24]{2,1,0:T(1,128)}), f32[32,1,24]{2,1,0:T(1,128)S(1)}, u32[]{:S(2)}, u32[]{:S(2)}) async-start(f32[32,1,24]{2,1,0:T(1,128)} %broadcast_in_dim.9), calls=%async_computation | async-start | bytes 32768 | tf_op jit(solution)/shard_map/all_to_all | solution.py:54
  10.7 33.1 %collective-permute-start.3 = (bf16[3,8,384]{2,1,0:T(8,128)(2,1)S(1)}, bf16[3,8,384]{2,1,0:T(8,128)(2,1)S(1)}, u32[]{:S(2)}, u32[]{:S(2)}) collective-permute-start(bf16[3,8,384]{2,1,0:T(8,128)(2,1)S(1)} %get-tuple-element.309), channel_id=1, source_target_pairs={{0,4},{4,8},{8,12},{12,16},{16,20},{20,24},{24,28},{1,5},{5,9},{9,... | collective-permute-start | bytes 55304 | tf_op jit(solution)/shard_map/ppermute | solution.py:24
  14.3 29.5 %collective-permute-start.4 = (bf16[3,8,384]{2,1,0:T(8,128)(2,1)S(1)}, bf16[3,8,384]{2,1,0:T(8,128)(2,1)S(1)}, u32[]{:S(2)}, u32[]{:S(2)}) collective-permute-start(bf16[3,8,384]{2,1,0:T(8,128)(2,1)S(1)} %get-tuple-element.310), channel_id=1, source_target_pairs={{4,0},{8,4},{12,8},{16,12},{20,16},{24,20},{28,24},{5,1},{9,5},{13... | collective-permute-start | bytes 55304 | tf_op jit(solution)/shard_map/ppermute | solution.py:26
  18.3 13.5 %collective-permute-start = (bf16[70,8,384]{2,1,0:T(8,128)(2,1)S(1)}, bf16[70,8,384]{2,1,0:T(8,128)(2,1)S(1)}, u32[]{:S(2)}, u32[]{:S(2)}) collective-permute-start(bf16[70,8,384]{2,1,0:T(8,128)(2,1)S(1)} %pad_maximum_fusion.1), channel_id=1, source_target_pairs={{0,4},{4,8},{8,12},{12,16},{16,20},{20,24},{24,28},{1,5},{5,9},{9,... | collective-permute-start | bytes 1290248 | tf_op jit(solution)/shard_map/ppermute | solution.py:38
  33.8 8.7 %copy-start.3 = (f32[24,768]{1,0:T(8,128)S(1)}, f32[24,768]{1,0:T(8,128)}, u32[]{:S(2)}) copy-start(f32[24,768]{1,0:T(8,128)} %param.7) | copy-start | bytes 221188
  34.6 19.7 %copy-start.1 = (bf16[61,4,8,384]{3,2,1,0:T(8,128)(2,1)S(1)}, bf16[61,4,8,384]{3,2,1,0:T(8,128)(2,1)}, u32[]{:S(2)}) copy-start(bf16[61,4,8,384]{3,2,1,0:T(8,128)(2,1)} %param.5) | copy-start | bytes 4497412
  37.0 13.1 %collective-permute-start.2 = (bf16[61,7,3,384]{3,0,2,1:T(8,128)(2,1)}, bf16[61,7,3,384]{3,0,2,1:T(8,128)(2,1)}, u32[]{:S(2)}, u32[]{:S(2)}) collective-permute-start(bf16[61,7,3,384]{3,0,2,1:T(8,128)(2,1)} %copy.96), channel_id=1, source_target_pairs={{1,0},{2,1},{3,2},{5,4},{6,5},{7,6},{9,8},{10,9},{11,10},{13,12},{... | collective-permute-start | bytes 2951432 | tf_op jit(solution)/shard_map/ppermute | solution.py:26
  38.3 13.9 %collective-permute-start.1 = (bf16[61,7,3,384]{3,0,2,1:T(8,128)(2,1)}, bf16[61,7,3,384]{3,0,2,1:T(8,128)(2,1)}, u32[]{:S(2)}, u32[]{:S(2)}) collective-permute-start(bf16[61,7,3,384]{3,0,2,1:T(8,128)(2,1)} %copy.95), channel_id=1, source_target_pairs={{0,1},{1,2},{2,3},{4,5},{5,6},{6,7},{8,9},{9,10},{10,11},{12,13},{... | collective-permute-start | bytes 2951432 | tf_op jit(solution)/shard_map/ppermute | solution.py:24
  43.9 3.9 %collective-permute-start.5 = (bf16[10,3,384]{2,1,0:T(4,128)(2,1)S(1)}, bf16[10,3,384]{2,1,0:T(4,128)(2,1)S(1)}, u32[]{:S(2)}, u32[]{:S(2)}) collective-permute-start(bf16[10,3,384]{2,1,0:T(4,128)(2,1)S(1)} %get-tuple-element.307), channel_id=1, source_target_pairs={{0,1},{1,2},{2,3},{4,5},{5,6},{6,7},{8,9},{9,10},{10,11},{12,13},{... | collective-permute-start | bytes 69128 | tf_op jit(solution)/shard_map/ppermute | solution.py:24
  45.9 4.1 %collective-permute-start.6 = (bf16[10,3,384]{2,1,0:T(4,128)(2,1)S(1)}, bf16[10,3,384]{2,1,0:T(4,128)(2,1)S(1)}, u32[]{:S(2)}, u32[]{:S(2)}) collective-permute-start(bf16[10,3,384]{2,1,0:T(4,128)(2,1)S(1)} %get-tuple-element.308), channel_id=1, source_target_pairs={{1,0},{2,1},{3,2},{5,4},{6,5},{7,6},{9,8},{10,9},{11,10},{13,12},{... | collective-permute-start | bytes 69128 | tf_op jit(solution)/shard_map/ppermute | solution.py:26
  76.1 2.6 %copy-start = (f32[61,2,4,8,384]{4,3,2,1,0:T(8,128)}, f32[61,2,4,8,384]{4,3,2,1,0:T(8,128)S(1)}, u32[]{:S(2)}) copy-start(f32[61,2,4,8,384]{4,3,2,1,0:T(8,128)S(1)} %constant_dynamic-update-slice_fusion) | copy-start | bytes 17989636
  76.5 2.5 %copy-start.2 = (f32[3,4,8,384]{3,2,1,0:T(8,128)S(1)}, f32[3,4,8,384]{3,2,1,0:T(8,128)}, u32[]{:S(2)}) copy-start(f32[3,4,8,384]{3,2,1,0:T(8,128)} %param.4) | copy-start | bytes 442372
  79.2 6.7 %collective-permute-start.7 = (f32[3,3,8,384]{3,2,1,0:T(8,128)S(1)}, f32[3,3,8,384]{3,2,1,0:T(8,128)S(1)}, u32[]{:S(2)}, u32[]{:S(2)}) collective-permute-start(f32[3,3,8,384]{3,2,1,0:T(8,128)S(1)} %get-tuple-element.295), channel_id=1, source_target_pairs={{0,4},{4,8},{8,12},{12,16},{16,20},{20,24},{24,28},{1,5},{5,9},{9,... | collective-permute-start | bytes 331784 | tf_op jit(solution)/shard_map/ppermute | solution.py:24
  83.6 7.9 %collective-permute-start.8 = (f32[3,3,8,384]{3,2,1,0:T(8,128)S(1)}, f32[3,3,8,384]{3,2,1,0:T(8,128)S(1)}, u32[]{:S(2)}, u32[]{:S(2)}) collective-permute-start(f32[3,3,8,384]{3,2,1,0:T(8,128)S(1)} %get-tuple-element.296), channel_id=1, source_target_pairs={{4,0},{8,4},{12,8},{16,12},{20,16},{24,20},{28,24},{5,1},{9,5},{13... | collective-permute-start | bytes 331784 | tf_op jit(solution)/shard_map/ppermute | solution.py:26
  91.5 7.2 %collective-permute-start.9 = (f32[3,10,3,384]{3,2,1,0:T(4,128)S(1)}, f32[3,10,3,384]{3,2,1,0:T(4,128)S(1)}, u32[]{:S(2)}, u32[]{:S(2)}) collective-permute-start(f32[3,10,3,384]{3,2,1,0:T(4,128)S(1)} %get-tuple-element.233), channel_id=1, source_target_pairs={{0,1},{1,2},{2,3},{4,5},{5,6},{6,7},{8,9},{9,10},{10,11},{12,13},{... | collective-permute-start | bytes 414728 | tf_op jit(solution)/shard_map/ppermute | solution.py:24
  96.9 6.4 %collective-permute-start.10 = (f32[3,10,3,384]{3,2,1,0:T(4,128)S(1)}, f32[3,10,3,384]{3,2,1,0:T(4,128)S(1)}, u32[]{:S(2)}, u32[]{:S(2)}) collective-permute-start(f32[3,10,3,384]{3,2,1,0:T(4,128)S(1)} %get-tuple-element.234), channel_id=1, source_target_pairs={{1,0},{2,1},{3,2},{5,4},{6,5},{7,6},{9,8},{10,9},{11,10},{13,12},{... | collective-permute-start | bytes 414728 | tf_op jit(solution)/shard_map/ppermute | solution.py:26
  140.2 4.8 %collective-permute-start.11 = (f32[3,3,8,384]{3,2,1,0:T(8,128)S(1)}, f32[3,3,8,384]{3,2,1,0:T(8,128)S(1)}, u32[]{:S(2)}, u32[]{:S(2)}) collective-permute-start(f32[3,3,8,384]{3,2,1,0:T(8,128)S(1)} %get-tuple-element.293), channel_id=1, source_target_pairs={{0,4},{4,8},{8,12},{12,16},{16,20},{20,24},{24,28},{1,5},{5,9},{9,... | collective-permute-start | bytes 331784 | tf_op jit(solution)/shard_map/ppermute | solution.py:24
  142.7 6.6 %collective-permute-start.12 = (f32[3,3,8,384]{3,2,1,0:T(8,128)S(1)}, f32[3,3,8,384]{3,2,1,0:T(8,128)S(1)}, u32[]{:S(2)}, u32[]{:S(2)}) collective-permute-start(f32[3,3,8,384]{3,2,1,0:T(8,128)S(1)} %get-tuple-element.294), channel_id=1, source_target_pairs={{4,0},{8,4},{12,8},{16,12},{20,16},{24,20},{28,24},{5,1},{9,5},{13... | collective-permute-start | bytes 331784 | tf_op jit(solution)/shard_map/ppermute | solution.py:26
  149.4 3.6 %collective-permute-start.13 = (f32[3,10,3,384]{3,2,1,0:T(4,128)S(1)}, f32[3,10,3,384]{3,2,1,0:T(4,128)S(1)}, u32[]{:S(2)}, u32[]{:S(2)}) collective-permute-start(f32[3,10,3,384]{3,2,1,0:T(4,128)S(1)} %get-tuple-element.231), channel_id=1, source_target_pairs={{0,1},{1,2},{2,3},{4,5},{5,6},{6,7},{8,9},{9,10},{10,11},{12,13},{... | collective-permute-start | bytes 414728 | tf_op jit(solution)/shard_map/ppermute | solution.py:24
  150.7 4.2 %collective-permute-start.14 = (f32[3,10,3,384]{3,2,1,0:T(4,128)S(1)}, f32[3,10,3,384]{3,2,1,0:T(4,128)S(1)}, u32[]{:S(2)}, u32[]{:S(2)}) collective-permute-start(f32[3,10,3,384]{3,2,1,0:T(4,128)S(1)} %get-tuple-element.232), channel_id=1, source_target_pairs={{1,0},{2,1},{3,2},{5,4},{6,5},{7,6},{9,8},{10,9},{11,10},{13,12},{... | collective-permute-start | bytes 414728 | tf_op jit(solution)/shard_map/ppermute | solution.py:26

commit v7 on v5

--- a/solution.py
+++ b/solution.py
@@ -112,7 +112,7 @@
         return [float(unit_dirs[bond_index, component]) for component in range(3)]
 
     def rimmed(vector):
-        return pad_depth(with_halo(vector, (("slab", 1), ("col", 2)), 3))
+        return pad_depth(with_halo(vector, (("col", 2), ("slab", 1)), 3))
 
     lower_x = jnp.concatenate([lower_rows(integrity, offsets[:, 0], 3), integrity], axis=1)
     spread = pad_depth(with_halo(lower_x, (("col", 2),), 3))

time: 193 us -> 196 us (1.016)
  waiting for transfers between devices: 13.1 us -> 18.8 us
  blocking collectives: 28.2 us -> 23.5 us
  starting transfers between devices: 48.1 us -> 50.5 us
    ppermute x7, waiting for transfers between devices: 0.02 us -> 6.79 us  [with_halo(): parts.insert(0, lax.ppermute(last, axis, up))]
    all_to_all x2, blocking collectives: 28.2 us -> 23.5 us  [device_rows(): return lax.all_to_all(tiled, axes, 0, 0, tiled=True)]
    ppermute x7, starting transfers between devices: 27.3 us -> 29.7 us  [with_halo(): parts.insert(0, lax.ppermute(last, axis, up))]
  transfers between devices with their start and end apart: 16 -> 16, of which waited for: 4 -> 7; matrix products, arithmetic and copies ran while one was open for 9% -> 8% of each run, Pallas kernels for 0% -> 0%
where the time goes in v7:
time: 196 us; the launch traced here: 195 us
  other arithmetic  72.5 us (37%)
  starting transfers between devices  50.5 us (26%)
  blocking collectives  23.5 us (12%)
  local copies, waits for them, and re-layouts  21.9 us (11%)
  waiting for transfers between devices  18.8 us (10%)
  between operations  7.4 us (4%)
    ppermute x7, starting transfers between devices, with_halo(): parts.insert(0, lax.ppermute(last, axis, up))  29.7 us
    all_to_all x2, blocking collectives, device_rows(): return lax.all_to_all(tiled, axes, 0, 0, tiled=True)  23.5 us
    concatenate x6, other arithmetic, with_halo(): x = jnp.concatenate(parts, axis=dim)  19.3 us
    add x3, other arithmetic, operator(): summed[component] = summed[component] + heading[component] * stretch  13.5 us
    another operation x3, other arithmetic, operator(): return jnp.stack(summed)  12.7 us
    ppermute x7, waiting for transfers between devices, with_halo(): parts.append(lax.ppermute(first, axis, down))  12 us
    another operation x3, other arithmetic, on_device(): diagonal = jnp.stack(diag_list)  10.6 us
    ppermute x7, starting transfers between devices, with_halo(): parts.append(lax.ppermute(first, axis, down))  8.98 us
  transfers between devices with their start and end apart: 16, of which 7 were waited for; matrix products, arithmetic and copies ran while one was open for 8% of the time, Pallas kernels for 0%

profile of v7, /device:TPU:0, one launch (start us, length us, event | category | flops | bytes accessed | tf_op | source)
XLA Modules:
  0.0 194.9 jit_solution(9592476399624579230)
XLA Ops:
  3.3 4.9 %collective-permute-start = (bf16[70,8,384]{2,1,0:T(8,128)(2,1)S(1)}, bf16[70,8,384]{2,1,0:T(8,128)(2,1)S(1)}, u32[]{:S(2)}, u32[]{:S(2)}) collective-permute-start(bf16[70,8,384]{2,1,0:T(8,128)(2,1)S(1)} %pad_maximum_fusion.1), channel_id=1, source_target_pairs={{0,4},{4,8},{8,12},{12,16},{16,20},{20,24},{24,28},{1,5},{5,9},{9,... | collective-permute-start | bytes 1290248 | tf_op jit(solution)/shard_map/ppermute | solution.py:38
  9.0 3.4 %collective-permute-start.3 = (bf16[3,8,384]{2,1,0:T(8,128)(2,1)S(1)}, bf16[3,8,384]{2,1,0:T(8,128)(2,1)S(1)}, u32[]{:S(2)}, u32[]{:S(2)}) collective-permute-start(bf16[3,8,384]{2,1,0:T(8,128)(2,1)S(1)} %get-tuple-element.247), channel_id=1, source_target_pairs={{0,4},{4,8},{8,12},{12,16},{16,20},{20,24},{24,28},{1,5},{5,9},{9,... | collective-permute-start | bytes 55304 | tf_op jit(solution)/shard_map/ppermute | solution.py:24
  15.7 6.9 %all-to-all-start = ((f32[32,1,24]{2,1,0:T(1,128)}), f32[32,1,24]{2,1,0:T(1,128)S(1)}, u32[]{:S(2)}, u32[]{:S(2)}) async-start(f32[32,1,24]{2,1,0:T(1,128)} %broadcast_in_dim.9), calls=%async_computation | async-start | bytes 32768 | tf_op jit(solution)/shard_map/all_to_all | solution.py:54
  26.8 3.1 %collective-permute-start.1 = (bf16[61,7,3,384]{3,0,2,1:T(8,128)(2,1)}, bf16[61,7,3,384]{3,0,2,1:T(8,128)(2,1)}, u32[]{:S(2)}, u32[]{:S(2)}) collective-permute-start(bf16[61,7,3,384]{3,0,2,1:T(8,128)(2,1)} %copy.95), channel_id=1, source_target_pairs={{0,1},{1,2},{2,3},{4,5},{5,6},{6,7},{8,9},{9,10},{10,11},{12,13},{... | collective-permute-start | bytes 2951432 | tf_op jit(solution)/shard_map/ppermute | solution.py:24
  33.9 3.2 %collective-permute-start.5 = (bf16[10,3,384]{2,1,0:T(4,128)(2,1)S(1)}, bf16[10,3,384]{2,1,0:T(4,128)(2,1)S(1)}, u32[]{:S(2)}, u32[]{:S(2)}) collective-permute-start(bf16[10,3,384]{2,1,0:T(4,128)(2,1)S(1)} %get-tuple-element.245), channel_id=1, source_target_pairs={{0,1},{1,2},{2,3},{4,5},{5,6},{6,7},{8,9},{9,10},{10,11},{12,13},{... | collective-permute-start | bytes 69128 | tf_op jit(solution)/shard_map/ppermute | solution.py:24
  38.9 2.6 %collective-permute-done.6 = bf16[10,3,384]{2,1,0:T(4,128)(2,1)S(1)} collective-permute-done((bf16[10,3,384]{2,1,0:T(4,128)(2,1)S(1)}, bf16[10,3,384]{2,1,0:T(4,128)(2,1)S(1)}, u32[]{:S(2)}, u32[]{:S(2)}) %collective-permute-start.6) | collective-permute-done | bytes 23072 | tf_op jit(solution)/shard_map/ppermute | solution.py:26
  41.6 2.1 %copy.97 = bf16[61,7,3,384]{3,2,1,0:T(4,128)(2,1)S(1)} copy(bf16[61,7,3,384]{3,0,2,1:T(8,128)(2,1)} %collective-permute-done.1) | data formatting | bytes 1967616 | tf_op jit(solution)/shard_map/ppermute | solution.py:24
  43.7 2.1 %copy.98 = bf16[61,7,3,384]{3,2,1,0:T(4,128)(2,1)S(1)} copy(bf16[61,7,3,384]{3,0,2,1:T(8,128)(2,1)} %collective-permute-done.2) | data formatting | bytes 1967616 | tf_op jit(solution)/shard_map/ppermute | solution.py:26
  45.8 14.2 %select_maximum_fusion = bf16[61,7,14,390]{3,2,1,0:T(8,128)(2,1)S(1)} fusion(bf16[61,7,3,384]{3,2,1,0:T(4,128)(2,1)S(1)} %copy.98, bf16[61,7,3,384]{3,2,1,0:T(4,128)(2,1)S(1)} %copy.97, bf16[61,4,8,384]{3,2,1,0:T(8,128)(2,1)S(1)} %copy-done, bf16[61,1,8,384]{3,2,1,0:T(8,128)(2,1)S(1)} %get-tuple-element.249, ...), kind=kLoop, calls=%fused_computation.3 | loop fusion | flops 48959820 | bytes 9253944 | tf_op jit(solution)/shard_map/concatenate | solution.py:27
  62.0 4.4 %add_bitcast_fusion.5 = (f32[1,4,8,384]{3,2,1,0:T(8,128)}, f32[4,8,384]{2,1,0:T(8,128)S(1)}, f32[4,8,384]{2,1,0:T(8,128)S(1)}, f32[4,8,384]{2,1,0:T(8,128)S(1)},...) fusion(bf16[7,14,390]{2,1,0:T(8,128)(2,1)S(1)} %get-tuple-eleme, ...), kind=kLoop, calls=%fused_computation.2539 | loop fusion | flops 6967296 | bytes 7913472 | tf_op jit(solution)/shard_map/stack | solution.py:151
  66.4 2.9 %add_bitcast_fusion.4 = f32[1,4,8,384]{3,2,1,0:T(8,128)} fusion(f32[4,8,384]{2,1,0:T(8,128)S(1)} %get-tuple-element.143, bf16[7,14,390]{2,1,0:T(8,128)(2,1)S(1)} %get-tuple-element.220, bf16[7,14,390]{2,1,0:T(8,128)(2,1)S(1)} %get-tuple-element.215, bf16[7,14,390]{2,1,0:T(8,128)(2,1)S(1)} %get-tuple-element.214, ...), kind=kLoop, calls=%fused_computation.2538 | loop fusion | flops 5173248 | bytes 5799936 | tf_op jit(solution)/shard_map/stack | solution.py:151
  69.6 3.4 %add_bitcast_fusion.3 = f32[1,4,8,384]{3,2,1,0:T(8,128)S(1)} fusion(f32[4,8,384]{2,1,0:T(8,128)} %get-tuple-element.161, f32[4,8,384]{2,1,0:T(8,128)S(1)} %get-tuple-element.160, bf16[7,14,390]{2,1,0:T(8,128)(2,1)} %get-tuple-element.221, bf16[7,14,390]{2,1,0:T(8,128)(2,1)S(1)} %get-tuple-element.219, bf16[7,14,390]{2,1,0:T(8,128)(2,1)S(1)} %get-tuple-element.220, ...), kind=kLoop, calls=%fused_computation.2537 | loop fusion | flops 5406720 | bytes 6045696 | tf_op jit(solution)/shard_map/stack | solution.py:151
  75.2 9.3 %collective-permute-start.7 = (f32[3,4,3,384]{3,2,1,0:T(4,128)}, f32[3,4,3,384]{3,2,1,0:T(4,128)}, u32[]{:S(2)}, u32[]{:S(2)}) collective-permute-start(f32[3,4,3,384]{3,2,1,0:T(4,128)} %get-tuple-element.243), channel_id=1, source_target_pairs={{0,1},{1,2},{2,3},{4,5},{5,6},{6,7},{8,9},{9,10},{10,11},{12,13},{... | collective-permute-start | bytes 165896 | tf_op jit(solution)/shard_map/ppermute | solution.py:24
  91.1 5.2 %collective-permute-start.9 = (f32[3,3,14,384]{3,2,1,0:T(8,128)}, f32[3,3,14,384]{3,2,1,0:T(8,128)}, u32[]{:S(2)}, u32[]{:S(2)}) collective-permute-start(f32[3,3,14,384]{3,2,1,0:T(8,128)} %get-tuple-element.239), channel_id=1, source_target_pairs={{0,4},{4,8},{8,12},{12,16},{16,20},{20,24},{24,28},{1,5},{5,9},{9,... | collective-permute-start | bytes 580616 | tf_op jit(solution)/shard_map/ppermute | solution.py:24
  97.3 2.1 %collective-permute-done.10 = f32[3,3,14,384]{3,2,1,0:T(8,128)} collective-permute-done((f32[3,3,14,384]{3,2,1,0:T(8,128)}, f32[3,3,14,384]{3,2,1,0:T(8,128)}, u32[]{:S(2)}, u32[]{:S(2)}) %collective-permute-start.10) | collective-permute-done | bytes 193568 | tf_op jit(solution)/shard_map/ppermute | solution.py:26
  99.4 5.5 %collective-permute-done.9 = f32[3,3,14,384]{3,2,1,0:T(8,128)} collective-permute-done((f32[3,3,14,384]{3,2,1,0:T(8,128)}, f32[3,3,14,384]{3,2,1,0:T(8,128)}, u32[]{:S(2)}, u32[]{:S(2)}) %collective-permute-start.9) | collective-permute-done | bytes 193568 | tf_op jit(solution)/shard_map/ppermute | solution.py:24
  106.5 11.9 %add_add_fusion.2 = (f32[4,8,384]{2,1,0:T(8,128)S(1)}, f32[4,8,384]{2,1,0:T(8,128)S(1)}, f32[4,8,384]{2,1,0:T(8,128)S(1)}, f32[4,8,384]{2,1,0:T(8,128)S(1)}, f32...) fusion(f32[4,8,384]{2,1,0:T(8,128)} %squeeze.216, ...), kind=kLoop, calls=%fused_computation.2536 | loop fusion | flops 18382848 | bytes 27181056 | tf_op jit(solution)/shard_map/add | solution.py:176
  122.7 11.6 %all_to_all.24 = f32[32,1,26]{2,1,0:T(1,128)S(1)} all-to-all(f32[32,1,26]{2,1,0:T(1,128)S(1)} %broadcast_in_dim.10), channel_id=1, replica_groups=mesh['slab'=8,'col'=4] {'slab','col'}, dimensions={0} | all-to-all | bytes 6656 | tf_op jit(solution)/shard_map/all_to_all | solution.py:54
  139.1 2.4 %collective-permute-start.11 = (f32[3,4,3,384]{3,2,1,0:T(4,128)}, f32[3,4,3,384]{3,2,1,0:T(4,128)}, u32[]{:S(2)}, u32[]{:S(2)}) collective-permute-start(f32[3,4,3,384]{3,2,1,0:T(4,128)} %get-tuple-element.241), channel_id=1, source_target_pairs={{0,1},{1,2},{2,3},{4,5},{5,6},{6,7},{8,9},{9,10},{10,11},{12,13},{... | collective-permute-start | bytes 165896 | tf_op jit(solution)/shard_map/ppermute | solution.py:24
  146.8 3.1 %collective-permute-start.13 = (f32[3,3,14,384]{3,2,1,0:T(8,128)}, f32[3,3,14,384]{3,2,1,0:T(8,128)}, u32[]{:S(2)}, u32[]{:S(2)}) collective-permute-start(f32[3,3,14,384]{3,2,1,0:T(8,128)} %get-tuple-element.237), channel_id=1, source_target_pairs={{0,4},{4,8},{8,12},{12,16},{16,20},{20,24},{24,28},{1,5},{5,9},{9,... | collective-permute-start | bytes 580616 | tf_op jit(solution)/shard_map/ppermute | solution.py:24
  153.5 5.3 %collective-permute-done.14 = f32[3,3,14,384]{3,2,1,0:T(8,128)} collective-permute-done((f32[3,3,14,384]{3,2,1,0:T(8,128)}, f32[3,3,14,384]{3,2,1,0:T(8,128)}, u32[]{:S(2)}, u32[]{:S(2)}) %collective-permute-start.14) | collective-permute-done | bytes 193568 | tf_op jit(solution)/shard_map/ppermute | solution.py:26
  160.5 12.1 %add_bitcast_fusion.2 = (f32[1,4,8,384]{3,2,1,0:T(8,128)S(1)}, f32[4,8,384]{2,1,0:T(8,128)S(1)}, f32[4,8,384]{2,1,0:T(8,128)S(1)}, f32[4,8,384]{2,1,0:T(8,128)S(...) fusion(f32[4,8,384]{2,1,0:T(8,128)} %squeeze.222, ...), kind=kLoop, calls=%fused_computation.2533 | loop fusion | flops 18382848 | bytes 27181056 | tf_op jit(solution)/shard_map/stack | solution.py:177
  174.0 2.6 %pad_maximum_fusion.9 = f32[4]{0:T(128)S(1)} fusion(f32[1]{0:T(128)} %bitcast.99, f32[1]{0:T(128)} %bitcast.98, f32[1]{0:T(128)} %bitcast.97, f32[1]{0:T(128)} %bitcast.89), kind=kLoop, calls=%fused_computation.2661 | loop fusion | flops 12 | bytes 32 | tf_op jit(solution)/shard_map/stack | solution.py:218
  176.6 11.9 %all_to_all.25 = f32[32,1,4]{2,1,0:T(1,128)S(1)} all-to-all(f32[32,1,4]{2,1,0:T(1,128)S(1)} %broadcast_in_dim.11), channel_id=1, replica_groups=mesh['slab'=8,'col'=4] {'slab','col'}, dimensions={0} | all-to-all | bytes 1024 | tf_op jit(solution)/shard_map/all_to_all | solution.py:54
  (205 shorter events, 51.5 us)
Async XLA Ops:
  3.3 19.4 %collective-permute-start = (bf16[70,8,384]{2,1,0:T(8,128)(2,1)S(1)}, bf16[70,8,384]{2,1,0:T(8,128)(2,1)S(1)}, u32[]{:S(2)}, u32[]{:S(2)}) collective-permute-start(bf16[70,8,384]{2,1,0:T(8,128)(2,1)S(1)} %pad_maximum_fusion.1), channel_id=1, source_target_pairs={{0,4},{4,8},{8,12},{12,16},{16,20},{20,24},{24,28},{1,5},{5,9},{9,... | collective-permute-start | bytes 1290248 | tf_op jit(solution)/shard_map/ppermute | solution.py:38
  9.0 24.8 %collective-permute-start.3 = (bf16[3,8,384]{2,1,0:T(8,128)(2,1)S(1)}, bf16[3,8,384]{2,1,0:T(8,128)(2,1)S(1)}, u32[]{:S(2)}, u32[]{:S(2)}) collective-permute-start(bf16[3,8,384]{2,1,0:T(8,128)(2,1)S(1)} %get-tuple-element.247), channel_id=1, source_target_pairs={{0,4},{4,8},{8,12},{12,16},{16,20},{20,24},{24,28},{1,5},{5,9},{9,... | collective-permute-start | bytes 55304 | tf_op jit(solution)/shard_map/ppermute | solution.py:24
  12.5 21.4 %collective-permute-start.4 = (bf16[3,8,384]{2,1,0:T(8,128)(2,1)S(1)}, bf16[3,8,384]{2,1,0:T(8,128)(2,1)S(1)}, u32[]{:S(2)}, u32[]{:S(2)}) collective-permute-start(bf16[3,8,384]{2,1,0:T(8,128)(2,1)S(1)} %get-tuple-element.248), channel_id=1, source_target_pairs={{4,0},{8,4},{12,8},{16,12},{20,16},{24,20},{28,24},{5,1},{9,5},{13... | collective-permute-start | bytes 55304 | tf_op jit(solution)/shard_map/ppermute | solution.py:26
  15.7 16.9 %all-to-all-start = ((f32[32,1,24]{2,1,0:T(1,128)}), f32[32,1,24]{2,1,0:T(1,128)S(1)}, u32[]{:S(2)}, u32[]{:S(2)}) async-start(f32[32,1,24]{2,1,0:T(1,128)} %broadcast_in_dim.9), calls=%async_computation | async-start | bytes 32768 | tf_op jit(solution)/shard_map/all_to_all | solution.py:54
  24.7 21.1 %copy-start = (bf16[61,4,8,384]{3,2,1,0:T(8,128)(2,1)S(1)}, bf16[61,4,8,384]{3,2,1,0:T(8,128)(2,1)}, u32[]{:S(2)}) copy-start(bf16[61,4,8,384]{3,2,1,0:T(8,128)(2,1)} %param.5) | copy-start | bytes 4497412
  26.8 14.9 %collective-permute-start.1 = (bf16[61,7,3,384]{3,0,2,1:T(8,128)(2,1)}, bf16[61,7,3,384]{3,0,2,1:T(8,128)(2,1)}, u32[]{:S(2)}, u32[]{:S(2)}) collective-permute-start(bf16[61,7,3,384]{3,0,2,1:T(8,128)(2,1)} %copy.95), channel_id=1, source_target_pairs={{0,1},{1,2},{2,3},{4,5},{5,6},{6,7},{8,9},{9,10},{10,11},{12,13},{... | collective-permute-start | bytes 2951432 | tf_op jit(solution)/shard_map/ppermute | solution.py:24
  31.1 12.7 %collective-permute-start.2 = (bf16[61,7,3,384]{3,0,2,1:T(8,128)(2,1)}, bf16[61,7,3,384]{3,0,2,1:T(8,128)(2,1)}, u32[]{:S(2)}, u32[]{:S(2)}) collective-permute-start(bf16[61,7,3,384]{3,0,2,1:T(8,128)(2,1)} %copy.96), channel_id=1, source_target_pairs={{1,0},{2,1},{3,2},{5,4},{6,5},{7,6},{9,8},{10,9},{11,10},{13,12},{... | collective-permute-start | bytes 2951432 | tf_op jit(solution)/shard_map/ppermute | solution.py:26
  32.5 13.3 %copy-start.41 = (f32[8,3,768]{2,1,0:T(4,128)}, f32[8,3,768]{2,1,0:T(4,128)S(1)}, u32[]{:S(2)}) copy-start(f32[8,3,768]{2,1,0:T(4,128)S(1)} %dot_general.8) | copy-start | bytes 221188
  33.9 5.0 %collective-permute-start.5 = (bf16[10,3,384]{2,1,0:T(4,128)(2,1)S(1)}, bf16[10,3,384]{2,1,0:T(4,128)(2,1)S(1)}, u32[]{:S(2)}, u32[]{:S(2)}) collective-permute-start(bf16[10,3,384]{2,1,0:T(4,128)(2,1)S(1)} %get-tuple-element.245), channel_id=1, source_target_pairs={{0,1},{1,2},{2,3},{4,5},{5,6},{6,7},{8,9},{9,10},{10,11},{12,13},{... | collective-permute-start | bytes 69128 | tf_op jit(solution)/shard_map/ppermute | solution.py:24
  37.1 4.3 %collective-permute-start.6 = (bf16[10,3,384]{2,1,0:T(4,128)(2,1)S(1)}, bf16[10,3,384]{2,1,0:T(4,128)(2,1)S(1)}, u32[]{:S(2)}, u32[]{:S(2)}) collective-permute-start(bf16[10,3,384]{2,1,0:T(4,128)(2,1)S(1)} %get-tuple-element.246), channel_id=1, source_target_pairs={{1,0},{2,1},{3,2},{5,4},{6,5},{7,6},{9,8},{10,9},{11,10},{13,12},{... | collective-permute-start | bytes 69128 | tf_op jit(solution)/shard_map/ppermute | solution.py:26
  60.3 12.7 %copy-start.4 = (bf16[7,14,390]{2,1,0:T(8,128)(2,1)}, bf16[7,14,390]{2,1,0:T(8,128)(2,1)S(1)}, u32[]{:S(2)}) copy-start(bf16[7,14,390]{2,1,0:T(8,128)(2,1)S(1)} %get-tuple-element.175) | copy-start | bytes 229324
  60.3 25.5 %copy-start.5 = (bf16[7,14,390]{2,1,0:T(8,128)(2,1)}, bf16[7,14,390]{2,1,0:T(8,128)(2,1)S(1)}, u32[]{:S(2)}) copy-start(bf16[7,14,390]{2,1,0:T(8,128)(2,1)S(1)} %get-tuple-element.176) | copy-start | bytes 229324
  60.3 58.1 %copy-start.2 = (bf16[7,14,390]{2,1,0:T(8,128)(2,1)}, bf16[7,14,390]{2,1,0:T(8,128)(2,1)S(1)}, u32[]{:S(2)}) copy-start(bf16[7,14,390]{2,1,0:T(8,128)(2,1)S(1)} %get-tuple-element.173) | copy-start | bytes 229324
  60.3 58.1 %copy-start.3 = (bf16[7,14,390]{2,1,0:T(8,128)(2,1)}, bf16[7,14,390]{2,1,0:T(8,128)(2,1)S(1)}, u32[]{:S(2)}) copy-start(bf16[7,14,390]{2,1,0:T(8,128)(2,1)S(1)} %get-tuple-element.174) | copy-start | bytes 229324
  73.0 12.8 %copy-start.43 = (f32[1,4,8,384]{3,2,1,0:T(8,128)}, f32[1,4,8,384]{3,2,1,0:T(8,128)S(1)}, u32[]{:S(2)}) copy-start(f32[1,4,8,384]{3,2,1,0:T(8,128)S(1)} %add_bitcast_fusion.3) | copy-start | bytes 147460
  75.2 11.8 %collective-permute-start.7 = (f32[3,4,3,384]{3,2,1,0:T(4,128)}, f32[3,4,3,384]{3,2,1,0:T(4,128)}, u32[]{:S(2)}, u32[]{:S(2)}) collective-permute-start(f32[3,4,3,384]{3,2,1,0:T(4,128)} %get-tuple-element.243), channel_id=1, source_target_pairs={{0,1},{1,2},{2,3},{4,5},{5,6},{6,7},{8,9},{9,10},{10,11},{12,13},{... | collective-permute-start | bytes 165896 | tf_op jit(solution)/shard_map/ppermute | solution.py:24
  84.5 3.5 %collective-permute-start.8 = (f32[3,4,3,384]{3,2,1,0:T(4,128)}, f32[3,4,3,384]{3,2,1,0:T(4,128)}, u32[]{:S(2)}, u32[]{:S(2)}) collective-permute-start(f32[3,4,3,384]{3,2,1,0:T(4,128)} %get-tuple-element.244), channel_id=1, source_target_pairs={{1,0},{2,1},{3,2},{5,4},{6,5},{7,6},{9,8},{10,9},{11,10},{13,12},{... | collective-permute-start | bytes 165896 | tf_op jit(solution)/shard_map/ppermute | solution.py:26
  89.8 9.6 %collective-permute-start.10 = (f32[3,3,14,384]{3,2,1,0:T(8,128)}, f32[3,3,14,384]{3,2,1,0:T(8,128)}, u32[]{:S(2)}, u32[]{:S(2)}) collective-permute-start(f32[3,3,14,384]{3,2,1,0:T(8,128)} %get-tuple-element.240), channel_id=1, source_target_pairs={{4,0},{8,4},{12,8},{16,12},{20,16},{24,20},{28,24},{5,1},{9,5},{13... | collective-permute-start | bytes 580616 | tf_op jit(solution)/shard_map/ppermute | solution.py:26
  91.1 13.8 %collective-permute-start.9 = (f32[3,3,14,384]{3,2,1,0:T(8,128)}, f32[3,3,14,384]{3,2,1,0:T(8,128)}, u32[]{:S(2)}, u32[]{:S(2)}) collective-permute-start(f32[3,3,14,384]{3,2,1,0:T(8,128)} %get-tuple-element.239), channel_id=1, source_target_pairs={{0,4},{4,8},{8,12},{12,16},{16,20},{20,24},{24,28},{1,5},{5,9},{9,... | collective-permute-start | bytes 580616 | tf_op jit(solution)/shard_map/ppermute | solution.py:24
  118.5 18.0 %copy-start.42 = (f32[8,3,768]{2,1,0:T(4,128)S(1)}, f32[8,3,768]{2,1,0:T(4,128)}, u32[]{:S(2)}) copy-start(f32[8,3,768]{2,1,0:T(4,128)} %copy-done.41) | copy-start | bytes 221188
  139.1 4.9 %collective-permute-start.11 = (f32[3,4,3,384]{3,2,1,0:T(4,128)}, f32[3,4,3,384]{3,2,1,0:T(4,128)}, u32[]{:S(2)}, u32[]{:S(2)}) collective-permute-start(f32[3,4,3,384]{3,2,1,0:T(4,128)} %get-tuple-element.241), channel_id=1, source_target_pairs={{0,1},{1,2},{2,3},{4,5},{5,6},{6,7},{8,9},{9,10},{10,11},{12,13},{... | collective-permute-start | bytes 165896 | tf_op jit(solution)/shard_map/ppermute | solution.py:24
  141.5 3.5 %collective-permute-start.12 = (f32[3,4,3,384]{3,2,1,0:T(4,128)}, f32[3,4,3,384]{3,2,1,0:T(4,128)}, u32[]{:S(2)}, u32[]{:S(2)}) collective-permute-start(f32[3,4,3,384]{3,2,1,0:T(4,128)} %get-tuple-element.242), channel_id=1, source_target_pairs={{1,0},{2,1},{3,2},{5,4},{6,5},{7,6},{9,8},{10,9},{11,10},{13,12},{... | collective-permute-start | bytes 165896 | tf_op jit(solution)/shard_map/ppermute | solution.py:26
  146.8 6.6 %collective-permute-start.13 = (f32[3,3,14,384]{3,2,1,0:T(8,128)}, f32[3,3,14,384]{3,2,1,0:T(8,128)}, u32[]{:S(2)}, u32[]{:S(2)}) collective-permute-start(f32[3,3,14,384]{3,2,1,0:T(8,128)} %get-tuple-element.237), channel_id=1, source_target_pairs={{0,4},{4,8},{8,12},{12,16},{16,20},{20,24},{24,28},{1,5},{5,9},{9,... | collective-permute-start | bytes 580616 | tf_op jit(solution)/shard_map/ppermute | solution.py:24
  149.9 8.9 %collective-permute-start.14 = (f32[3,3,14,384]{3,2,1,0:T(8,128)}, f32[3,3,14,384]{3,2,1,0:T(8,128)}, u32[]{:S(2)}, u32[]{:S(2)}) collective-permute-start(f32[3,3,14,384]{3,2,1,0:T(8,128)} %get-tuple-element.238), channel_id=1, source_target_pairs={{4,0},{8,4},{12,8},{16,12},{20,16},{24,20},{28,24},{5,1},{9,5},{13... | collective-permute-start | bytes 580616 | tf_op jit(solution)/shard_map/ppermute | solution.py:26
  (38 other events, 332.6 us)

commit v8 on v5

--- a/solution.py
+++ b/solution.py
@@ -28,22 +28,34 @@
     return x
 
 
-def lower_rows(levels, reach, width):
+def lower_rows(levels, reach, width, flags):
     count, length = (lax.axis_size("slab"), levels.shape[1])
     up = [(i, i + 1) for i in range(count - 1)]
+    down = [(j, i) for i, j in up]
     starts = [int(np.argmax(reach >= depth)) for depth in range(1, width + 1)]
     sent = jnp.concatenate(
-        [levels[start:, length - depth] for depth, start in zip(range(1, width + 1), starts)], axis=0
+        [levels[start:, length - depth] for depth, start in zip(range(1, width + 1), starts)]
+        + [flags[length - 1 :]],
+        axis=0,
     )
     got = lax.ppermute(sent, "slab", up)
+    above = lax.ppermute(flags[:1], "slab", down)
+    plane = levels.shape[2:]
     rows, at = ({}, 0)
     for depth, start in zip(range(1, width + 1), starts):
         size = levels.shape[0] - start
         rows[depth] = jnp.concatenate(
-            [jnp.zeros((start,) + levels.shape[2:], levels.dtype), got[at : at + size]], axis=0
+            [jnp.zeros((start,) + plane, levels.dtype), got[at : at + size]], axis=0
         )
         at = at + size
-    return jnp.stack([rows[depth] for depth in range(width, 0, -1)], axis=1)
+    below = jnp.stack([rows[depth] for depth in range(width, 0, -1)], axis=1)
+    bonds = jnp.concatenate(
+        [below, levels, jnp.zeros((levels.shape[0], 1) + plane, levels.dtype)], axis=1
+    )
+    contact_rows = jnp.concatenate(
+        [jnp.zeros((width - 1,) + plane, flags.dtype), got[at:], flags, above], axis=0
+    )
+    return jnp.concatenate([bonds, contact_rows[None]], axis=0)
 
 
 def device_rows(vector, axes):
@@ -114,17 +126,17 @@
     def rimmed(vector):
         return pad_depth(with_halo(vector, (("slab", 1), ("col", 2)), 3))
 
-    lower_x = jnp.concatenate([lower_rows(integrity, offsets[:, 0], 3), integrity], axis=1)
-    spread = pad_depth(with_halo(lower_x, (("col", 2),), 3))
-    contact_pad = pad_depth(
-        with_halo(contact.astype(jnp.bfloat16), (("slab", 0), ("col", 1)), 3)
-    ).astype(jnp.float32)
+    lower_x = lower_rows(integrity, offsets[:, 0], 3, contact.astype(jnp.bfloat16))
+    spread = jnp.pad(
+        pad_depth(with_halo(lower_x, (("col", 2),), 3)), ((0, 0), (0, 2), (0, 0), (0, 0))
+    )
+    contact_pad = spread[bond_count].astype(jnp.float32)
     near_contact = window(contact_pad, 0, 0, 0, extent)
 
     def bond_pair(bond_index):
         shift_x, shift_y, shift_z = bond_shift(bond_index)
         weight = float(weights[bond_index])
-        level_pad = jnp.pad(spread[bond_index], ((0, 3), (0, 0), (0, 0)))
+        level_pad = spread[bond_index]
         intact = window(level_pad, 0, 0, 0, extent).astype(jnp.float32)
         prior = window(level_pad, -shift_x, -shift_y, -shift_z, extent).astype(jnp.float32)
         forward = weight * intact

time: 193 us -> 198 us (1.026)
  starting transfers between devices: 48.1 us -> 33.1 us
  waiting for transfers between devices: 13.1 us -> 28 us
  local copies, waits for them, and re-layouts: 21.9 us -> 26.5 us
    ppermute x7 -> x5, starting transfers between devices: 27.3 us -> 11.8 us  [with_halo(): parts.insert(0, lax.ppermute(last, axis, up))]
    all_to_all x1, waiting for transfers between devices: 0.01 us -> 8.85 us  [device_rows(): return lax.all_to_all(tiled, axes, 0, 0, tiled=True)]
    ppermute x1, waiting for transfers between devices: 0.01 us -> 6.96 us  [lower_rows(): got = lax.ppermute(sent, 'slab', up)]
    unnamed x90 -> x100, local copies, waits for them, and re-layouts: 0.19 us -> 3.38 us
    ppermute x7 -> x5, starting transfers between devices: 8.98 us -> 6.41 us  [with_halo(): parts.append(lax.ppermute(first, axis, down))]
    concatenate x6 -> x5, other arithmetic: 19.7 us -> 17.5 us  [with_halo(): x = jnp.concatenate(parts, axis=dim)]
    ppermute x7 -> x5, waiting for transfers between devices: 13.1 us -> 12.1 us  [with_halo(): parts.append(lax.ppermute(first, axis, down))]
    slice x8 -> x5, local copies, waits for them, and re-layouts: 5.08 us -> 4.24 us  [with_halo(): last = lax.slice_in_dim(x, length - width, length, axis=dim)]
  transfers between devices with their start and end apart: 16 -> 13, of which waited for: 4 -> 6; matrix products, arithmetic and copies ran while one was open for 9% -> 8% of each run, Pallas kernels for 0% -> 0%
where the time goes in v8:
time: 198 us; the launch traced here: 197 us
  other arithmetic  73.3 us (37%)
  starting transfers between devices  33.1 us (17%)
  waiting for transfers between devices  28 us (14%)
  blocking collectives  28 us (14%)
  local copies, waits for them, and re-layouts  26.5 us (13%)
  between operations  7.56 us (4%)
    all_to_all x2, blocking collectives, device_rows(): return lax.all_to_all(tiled, axes, 0, 0, tiled=True)  28 us
    concatenate x5, other arithmetic, with_halo(): x = jnp.concatenate(parts, axis=dim)  17.5 us
    add x3, other arithmetic, operator(): summed[component] = summed[component] + heading[component] * stretch  13.3 us
    another operation x3, other arithmetic, operator(): return jnp.stack(summed)  13 us
    ppermute x5, waiting for transfers between devices, with_halo(): parts.append(lax.ppermute(first, axis, down))  12.1 us
    another operation x3, other arithmetic, on_device(): diagonal = jnp.stack(diag_list)  12.1 us
    ppermute x5, starting transfers between devices, with_halo(): parts.insert(0, lax.ppermute(last, axis, up))  11.8 us
    all_to_all x1, waiting for transfers between devices, device_rows(): return lax.all_to_all(tiled, axes, 0, 0, tiled=True)  8.85 us
  transfers between devices with their start and end apart: 13, of which 6 were waited for; matrix products, arithmetic and copies ran while one was open for 8% of the time, Pallas kernels for 0%

profile of v8, /device:TPU:0, one launch (start us, length us, event | category | flops | bytes accessed | tf_op | source)
XLA Modules:
  0.0 196.8 jit_solution(15399889009948225105)
XLA Ops:
  4.2 4.9 %collective-permute-start = (bf16[71,8,384]{2,1,0:T(8,128)(2,1)S(1)}, bf16[71,8,384]{2,1,0:T(8,128)(2,1)S(1)}, u32[]{:S(2)}, u32[]{:S(2)}) collective-permute-start(bf16[71,8,384]{2,1,0:T(8,128)(2,1)S(1)} %pad_maximum_fusion.1), channel_id=1, source_target_pairs={{0,4},{4,8},{8,12},{12,16},{16,20},{20,24},{24,28},{1,5},{5,9},{9,... | collective-permute-start | bytes 1308680 | tf_op jit(solution)/shard_map/ppermute | solution.py:41
  11.5 7.0 %collective-permute-done = bf16[71,8,384]{2,1,0:T(8,128)(2,1)S(1)} collective-permute-done((bf16[71,8,384]{2,1,0:T(8,128)(2,1)S(1)}, bf16[71,8,384]{2,1,0:T(8,128)(2,1)S(1)}, u32[]{:S(2)}, u32[]{:S(2)}) %collective-permute-start) | collective-permute-done | bytes 436256 | tf_op jit(solution)/shard_map/ppermute | solution.py:41
  21.4 1.7 constant_dynamic-update-slice_fusion
  25.7 2.3 %collective-permute-start.2 = (bf16[62,8,3,384]{3,1,2,0:T(8,128)(2,1)}, bf16[62,8,3,384]{3,1,2,0:T(8,128)(2,1)}, u32[]{:S(2)}, u32[]{:S(2)}) collective-permute-start(bf16[62,8,3,384]{3,1,2,0:T(8,128)(2,1)} %copy.48), channel_id=1, source_target_pairs={{0,1},{1,2},{2,3},{4,5},{5,6},{6,7},{8,9},{9,10},{10,11},{12,13},{... | collective-permute-start | bytes 3428360 | tf_op jit(solution)/shard_map/ppermute | solution.py:24
  31.3 8.7 %all-to-all-start = ((f32[32,1,24]{2,1,0:T(1,128)}), f32[32,1,24]{2,1,0:T(1,128)S(1)}, u32[]{:S(2)}, u32[]{:S(2)}) async-start(f32[32,1,24]{2,1,0:T(1,128)} %broadcast_in_dim.18), calls=%async_computation | async-start | bytes 32768 | tf_op jit(solution)/shard_map/all_to_all | solution.py:66
  41.1 8.8 %all-to-all-done = f32[32,1,24]{2,1,0:T(1,128)S(1)} async-done(((f32[32,1,24]{2,1,0:T(1,128)}), f32[32,1,24]{2,1,0:T(1,128)S(1)}, u32[]{:S(2)}, u32[]{:S(2)}) %all-to-all-start) | async-done | bytes 3104 | tf_op jit(solution)/shard_map/all_to_all | solution.py:66
  52.3 1.9 copy.50
  54.2 1.9 copy.51
  56.1 12.1 %select_maximum_fusion = bf16[62,8,14,390]{3,2,1,0:T(8,128)(2,1)S(1)} fusion(bf16[62,8,3,384]{3,2,1,0:T(4,128)(2,1)S(1)} %copy.51, bf16[62,8,3,384]{3,2,1,0:T(4,128)(2,1)S(1)} %copy.50, bf16[1,8,8,384]{3,2,1,0:T(8,128)(2,1)S(1)} %maximum_bitcast_fusion, bf16[61,8,8,384]{3,2,1,0:T(8,128)(2,1)S(1)} %broadcast_dynamic-update-slice_fusion), kind=kLoop, calls=%fused_computation.3 | loop fusion | flops 40622400 | bytes 10749312 | tf_op jit(solution)/shard_map/concatenate | solution.py:27
  72.1 4.4 %add_bitcast_fusion.5 = (f32[1,4,8,384]{3,2,1,0:T(8,128)S(1)}, f32[4,8,384]{2,1,0:T(8,128)S(1)}, f32[4,8,384]{2,1,0:T(8,128)S(1)}, f32[4,8,384]{2,1,0:T(8,128)S(...) fusion(bf16[10,14,390]{2,1,0:T(8,128)(2,1)S(1)} %get-tuple-elem, ...), kind=kLoop, calls=%fused_computation.2529 | loop fusion | flops 6967296 | bytes 7913472 | tf_op jit(solution)/shard_map/stack | solution.py:163
  76.5 4.1 %add_bitcast_fusion.4 = f32[1,4,8,384]{3,2,1,0:T(8,128)} fusion(f32[4,8,384]{2,1,0:T(8,128)S(1)} %get-tuple-element.145, bf16[10,14,390]{2,1,0:T(8,128)(2,1)S(1)} %get-tuple-element.168, bf16[10,14,390]{2,1,0:T(8,128)(2,1)S(1)} %get-tuple-element.172, bf16[10,14,390]{2,1,0:T(8,128)(2,1)S(1)} %get-tuple-element.174, ...), kind=kLoop, calls=%fused_computation.2528 | loop fusion | flops 5173248 | bytes 5799936 | tf_op jit(solution)/shard_map/stack | solution.py:163
  80.9 3.7 %add_bitcast_fusion.3 = f32[1,4,8,384]{3,2,1,0:T(8,128)S(1)} fusion(f32[4,8,384]{2,1,0:T(8,128)S(1)} %get-tuple-element.163, f32[4,8,384]{2,1,0:T(8,128)S(1)} %get-tuple-element.162, bf16[10,14,390]{2,1,0:T(8,128)(2,1)} %get-tuple-element.167, bf16[10,14,390]{2,1,0:T(8,128)(2,1)} %get-tuple-element.166, bf16[10,14,390]{2,1,0:T(8,128)(2,1)S(1)} %get-tuple-element.168, ...), kind=kLoop, calls=%fused_computation.2527 | loop fusion | flops 5406720 | bytes 6045696 | tf_op jit(solution)/shard_map/stack | solution.py:163
  86.1 3.1 %collective-permute-start.4 = (f32[3,3,8,384]{3,2,1,0:T(8,128)}, f32[3,3,8,384]{3,2,1,0:T(8,128)}, u32[]{:S(2)}, u32[]{:S(2)}) collective-permute-start(f32[3,3,8,384]{3,2,1,0:T(8,128)} %get-tuple-element.248), channel_id=1, source_target_pairs={{0,4},{4,8},{8,12},{12,16},{16,20},{20,24},{24,28},{1,5},{5,9},{9,... | collective-permute-start | bytes 331784 | tf_op jit(solution)/shard_map/ppermute | solution.py:24
  91.5 4.8 %collective-permute-done.5 = f32[3,3,8,384]{3,2,1,0:T(8,128)} collective-permute-done((f32[3,3,8,384]{3,2,1,0:T(8,128)}, f32[3,3,8,384]{3,2,1,0:T(8,128)}, u32[]{:S(2)}, u32[]{:S(2)}) %collective-permute-start.5) | collective-permute-done | bytes 110624 | tf_op jit(solution)/shard_map/ppermute | solution.py:26
  104.8 12.6 %add_add_fusion.2 = (f32[4,8,384]{2,1,0:T(8,128)S(1)}, f32[4,8,384]{2,1,0:T(8,128)S(1)}, f32[4,8,384]{2,1,0:T(8,128)S(1)}, f32[4,8,384]{2,1,0:T(8,128)S(1)}, f32...) fusion(f32[4,8,384]{2,1,0:T(8,128)} %squeeze.216, ...), kind=kLoop, calls=%fused_computation.2526 | loop fusion | flops 18382848 | bytes 27181056 | tf_op jit(solution)/shard_map/add | solution.py:188
  120.8 15.4 %all_to_all.24 = f32[32,1,26]{2,1,0:T(1,128)S(1)} all-to-all(f32[32,1,26]{2,1,0:T(1,128)S(1)} %broadcast_in_dim.19), channel_id=1, replica_groups=mesh['slab'=8,'col'=4] {'slab','col'}, dimensions={0} | all-to-all | bytes 6656 | tf_op jit(solution)/shard_map/all_to_all | solution.py:66
  142.4 3.1 %collective-permute-start.8 = (f32[3,3,8,384]{3,2,1,0:T(8,128)}, f32[3,3,8,384]{3,2,1,0:T(8,128)}, u32[]{:S(2)}, u32[]{:S(2)}) collective-permute-start(f32[3,3,8,384]{3,2,1,0:T(8,128)} %get-tuple-element.246), channel_id=1, source_target_pairs={{0,4},{4,8},{8,12},{12,16},{16,20},{20,24},{24,28},{1,5},{5,9},{9,... | collective-permute-start | bytes 331784 | tf_op jit(solution)/shard_map/ppermute | solution.py:24
  148.6 3.8 %collective-permute-done.9 = f32[3,3,8,384]{3,2,1,0:T(8,128)} collective-permute-done((f32[3,3,8,384]{3,2,1,0:T(8,128)}, f32[3,3,8,384]{3,2,1,0:T(8,128)}, u32[]{:S(2)}, u32[]{:S(2)}) %collective-permute-start.9) | collective-permute-done | bytes 110624 | tf_op jit(solution)/shard_map/ppermute | solution.py:26
  154.2 2.0 %collective-permute-start.10 = (f32[3,10,3,384]{3,2,1,0:T(4,128)}, f32[3,10,3,384]{3,2,1,0:T(4,128)}, u32[]{:S(2)}, u32[]{:S(2)}) collective-permute-start(f32[3,10,3,384]{3,2,1,0:T(4,128)} %get-tuple-element.242), channel_id=1, source_target_pairs={{0,1},{1,2},{2,3},{4,5},{5,6},{6,7},{8,9},{9,10},{10,11},{12,13},{... | collective-permute-start | bytes 414728 | tf_op jit(solution)/shard_map/ppermute | solution.py:24
  157.8 2.2 %collective-permute-done.11 = f32[3,10,3,384]{3,2,1,0:T(4,128)} collective-permute-done((f32[3,10,3,384]{3,2,1,0:T(4,128)}, f32[3,10,3,384]{3,2,1,0:T(4,128)}, u32[]{:S(2)}, u32[]{:S(2)}) %collective-permute-start.11) | collective-permute-done | bytes 138272 | tf_op jit(solution)/shard_map/ppermute | solution.py:26
  160.0 1.7 select_maximum_fusion.2
  161.9 12.3 %add_bitcast_fusion.2 = (f32[1,4,8,384]{3,2,1,0:T(8,128)S(1)}, f32[4,8,384]{2,1,0:T(8,128)S(1)}, f32[4,8,384]{2,1,0:T(8,128)S(1)}, f32[4,8,384]{2,1,0:T(8,128)S(...) fusion(f32[4,8,384]{2,1,0:T(8,128)S(1)} %squeeze.222, ...), kind=kLoop, calls=%fused_computation.2523 | loop fusion | flops 18382848 | bytes 27181056 | tf_op jit(solution)/shard_map/stack | solution.py:189
  175.6 2.6 %pad_maximum_fusion.8 = f32[4]{0:T(128)S(1)} fusion(f32[1]{0:T(128)} %bitcast.103, f32[1]{0:T(128)} %bitcast.102, f32[1]{0:T(128)} %bitcast.101, f32[1]{0:T(128)} %bitcast.93), kind=kLoop, calls=%fused_computation.2652 | loop fusion | flops 12 | bytes 32 | tf_op jit(solution)/shard_map/stack | solution.py:230
  178.2 12.6 %all_to_all.25 = f32[32,1,4]{2,1,0:T(1,128)S(1)} all-to-all(f32[32,1,4]{2,1,0:T(1,128)S(1)} %broadcast_in_dim.20), channel_id=1, replica_groups=mesh['slab'=8,'col'=4] {'slab','col'}, dimensions={0} | all-to-all | bytes 1024 | tf_op jit(solution)/shard_map/all_to_all | solution.py:66
  (207 shorter events, 51.7 us)
Async XLA Ops:
  4.2 14.3 %collective-permute-start = (bf16[71,8,384]{2,1,0:T(8,128)(2,1)S(1)}, bf16[71,8,384]{2,1,0:T(8,128)(2,1)S(1)}, u32[]{:S(2)}, u32[]{:S(2)}) collective-permute-start(bf16[71,8,384]{2,1,0:T(8,128)(2,1)S(1)} %pad_maximum_fusion.1), channel_id=1, source_target_pairs={{0,4},{4,8},{8,12},{12,16},{16,20},{20,24},{24,28},{1,5},{5,9},{9,... | collective-permute-start | bytes 1308680 | tf_op jit(solution)/shard_map/ppermute | solution.py:41
  9.1 14.1 %collective-permute-start.1 = (bf16[1,8,384]{2,1,0:T(8,128)(2,1)S(1)}, bf16[1,8,384]{2,1,0:T(8,128)(2,1)S(1)}, u32[]{:S(2)}, u32[]{:S(2)}) collective-permute-start(bf16[1,8,384]{2,1,0:T(8,128)(2,1)S(1)} %get-tuple-element.251), channel_id=1, source_target_pairs={{4,0},{8,4},{12,8},{16,12},{20,16},{24,20},{28,24},{5,1},{9,5},{13... | collective-permute-start | bytes 18440 | tf_op jit(solution)/shard_map/ppermute | solution.py:42
  25.7 26.6 %collective-permute-start.2 = (bf16[62,8,3,384]{3,1,2,0:T(8,128)(2,1)}, bf16[62,8,3,384]{3,1,2,0:T(8,128)(2,1)}, u32[]{:S(2)}, u32[]{:S(2)}) collective-permute-start(bf16[62,8,3,384]{3,1,2,0:T(8,128)(2,1)} %copy.48), channel_id=1, source_target_pairs={{0,1},{1,2},{2,3},{4,5},{5,6},{6,7},{8,9},{9,10},{10,11},{12,13},{... | collective-permute-start | bytes 3428360 | tf_op jit(solution)/shard_map/ppermute | solution.py:24
  29.2 25.0 %collective-permute-start.3 = (bf16[62,8,3,384]{3,1,2,0:T(8,128)(2,1)}, bf16[62,8,3,384]{3,1,2,0:T(8,128)(2,1)}, u32[]{:S(2)}, u32[]{:S(2)}) collective-permute-start(bf16[62,8,3,384]{3,1,2,0:T(8,128)(2,1)} %copy.49), channel_id=1, source_target_pairs={{1,0},{2,1},{3,2},{5,4},{6,5},{7,6},{9,8},{10,9},{11,10},{13,12},{... | collective-permute-start | bytes 3428360 | tf_op jit(solution)/shard_map/ppermute | solution.py:26
  31.3 18.7 %all-to-all-start = ((f32[32,1,24]{2,1,0:T(1,128)}), f32[32,1,24]{2,1,0:T(1,128)S(1)}, u32[]{:S(2)}, u32[]{:S(2)}) async-start(f32[32,1,24]{2,1,0:T(1,128)} %broadcast_in_dim.18), calls=%async_computation | async-start | bytes 32768 | tf_op jit(solution)/shard_map/all_to_all | solution.py:66
  41.1 27.1 %copy-start.40 = (f32[8,3,768]{2,1,0:T(4,128)}, f32[8,3,768]{2,1,0:T(4,128)S(1)}, u32[]{:S(2)}) copy-start(f32[8,3,768]{2,1,0:T(4,128)S(1)} %dot_general.8) | copy-start | bytes 221188
  50.0 18.2 %copy-start.44 = (f32[32,1,24]{2,1,0:T(1,128)}, f32[32,1,24]{2,1,0:T(1,128)S(1)}, u32[]{:S(2)}) copy-start(f32[32,1,24]{2,1,0:T(1,128)S(1)} %all-to-all-done) | copy-start | bytes 9220
  51.5 16.7 %copy-start.46 = (f32[1,8,3]{1,2,0:T(4,128)}, f32[1,8,3]{1,2,0:T(4,128)S(1)}, u32[]{:S(2)}) copy-start(f32[1,8,3]{1,2,0:T(4,128)S(1)} %copy.56) | copy-start | bytes 292
  72.0 12.5 %copy-start.36 = (bf16[10,14,390]{2,1,0:T(8,128)(2,1)}, bf16[10,14,390]{2,1,0:T(8,128)(2,1)S(1)}, u32[]{:S(2)}) copy-start(bf16[10,14,390]{2,1,0:T(8,128)(2,1)S(1)} %get-tuple-element.219) | copy-start | bytes 327604
  72.0 12.5 %copy-start.37 = (bf16[10,14,390]{2,1,0:T(8,128)(2,1)}, bf16[10,14,390]{2,1,0:T(8,128)(2,1)S(1)}, u32[]{:S(2)}) copy-start(bf16[10,14,390]{2,1,0:T(8,128)(2,1)S(1)} %get-tuple-element.220) | copy-start | bytes 327604
  72.0 12.5 %copy-start.38 = (bf16[10,14,390]{2,1,0:T(8,128)(2,1)}, bf16[10,14,390]{2,1,0:T(8,128)(2,1)S(1)}, u32[]{:S(2)}) copy-start(bf16[10,14,390]{2,1,0:T(8,128)(2,1)S(1)} %get-tuple-element.221) | copy-start | bytes 327604
  72.0 12.5 %copy-start.39 = (bf16[10,14,390]{2,1,0:T(8,128)(2,1)}, bf16[10,14,390]{2,1,0:T(8,128)(2,1)S(1)}, u32[]{:S(2)}) copy-start(bf16[10,14,390]{2,1,0:T(8,128)(2,1)S(1)} %get-tuple-element.222) | copy-start | bytes 327604
  72.1 12.5 %copy-start = (f32[3,4,8,384]{3,2,1,0:T(8,128)S(1)}, f32[3,4,8,384]{3,2,1,0:T(8,128)}, u32[]{:S(2)}) copy-start(f32[3,4,8,384]{3,2,1,0:T(8,128)} %param.4) | copy-start | bytes 442372
  72.1 12.5 %copy-start.45 = (f32[3,384]{1,0:T(4,128)S(1)}, f32[3,384]{1,0:T(4,128)}, u32[]{:S(2)}) copy-start(f32[3,384]{1,0:T(4,128)} %add.4100) | copy-start | bytes 13828
  84.6 32.9 %copy-start.42 = (f32[1,4,8,384]{3,2,1,0:T(8,128)}, f32[1,4,8,384]{3,2,1,0:T(8,128)S(1)}, u32[]{:S(2)}) copy-start(f32[1,4,8,384]{3,2,1,0:T(8,128)S(1)} %add_bitcast_fusion.3) | copy-start | bytes 147460
  86.1 5.4 %collective-permute-start.4 = (f32[3,3,8,384]{3,2,1,0:T(8,128)}, f32[3,3,8,384]{3,2,1,0:T(8,128)}, u32[]{:S(2)}, u32[]{:S(2)}) collective-permute-start(f32[3,3,8,384]{3,2,1,0:T(8,128)} %get-tuple-element.248), channel_id=1, source_target_pairs={{0,4},{4,8},{8,12},{12,16},{16,20},{20,24},{24,28},{1,5},{5,9},{9,... | collective-permute-start | bytes 331784 | tf_op jit(solution)/shard_map/ppermute | solution.py:24
  89.3 7.0 %collective-permute-start.5 = (f32[3,3,8,384]{3,2,1,0:T(8,128)}, f32[3,3,8,384]{3,2,1,0:T(8,128)}, u32[]{:S(2)}, u32[]{:S(2)}) collective-permute-start(f32[3,3,8,384]{3,2,1,0:T(8,128)} %get-tuple-element.249), channel_id=1, source_target_pairs={{4,0},{8,4},{12,8},{16,12},{20,16},{24,20},{28,24},{5,1},{9,5},{13... | collective-permute-start | bytes 331784 | tf_op jit(solution)/shard_map/ppermute | solution.py:26
  98.1 3.6 %collective-permute-start.6 = (f32[3,10,3,384]{3,2,1,0:T(4,128)}, f32[3,10,3,384]{3,2,1,0:T(4,128)S(1)}, u32[]{:S(2)}, u32[]{:S(2)}) collective-permute-start(f32[3,10,3,384]{3,2,1,0:T(4,128)} %get-tuple-element.244), channel_id=1, source_target_pairs={{0,1},{1,2},{2,3},{4,5},{5,6},{6,7},{8,9},{9,10},{10,11},{12,13},{... | collective-permute-start | bytes 414728 | tf_op jit(solution)/shard_map/ppermute | solution.py:24
  99.4 3.7 %collective-permute-start.7 = (f32[3,10,3,384]{3,2,1,0:T(4,128)}, f32[3,10,3,384]{3,2,1,0:T(4,128)}, u32[]{:S(2)}, u32[]{:S(2)}) collective-permute-start(f32[3,10,3,384]{3,2,1,0:T(4,128)} %get-tuple-element.245), channel_id=1, source_target_pairs={{1,0},{2,1},{3,2},{5,4},{6,5},{7,6},{9,8},{10,9},{11,10},{13,12},{... | collective-permute-start | bytes 414728 | tf_op jit(solution)/shard_map/ppermute | solution.py:26
  104.8 34.4 %copy-start.41 = (f32[8,3,768]{2,1,0:T(4,128)S(1)}, f32[8,3,768]{2,1,0:T(4,128)}, u32[]{:S(2)}) copy-start(f32[8,3,768]{2,1,0:T(4,128)} %copy-done.40) | copy-start | bytes 221188
  142.4 6.2 %collective-permute-start.8 = (f32[3,3,8,384]{3,2,1,0:T(8,128)}, f32[3,3,8,384]{3,2,1,0:T(8,128)}, u32[]{:S(2)}, u32[]{:S(2)}) collective-permute-start(f32[3,3,8,384]{3,2,1,0:T(8,128)} %get-tuple-element.246), channel_id=1, source_target_pairs={{0,4},{4,8},{8,12},{12,16},{16,20},{20,24},{24,28},{1,5},{5,9},{9,... | collective-permute-start | bytes 331784 | tf_op jit(solution)/shard_map/ppermute | solution.py:24
  145.5 6.9 %collective-permute-start.9 = (f32[3,3,8,384]{3,2,1,0:T(8,128)}, f32[3,3,8,384]{3,2,1,0:T(8,128)}, u32[]{:S(2)}, u32[]{:S(2)}) collective-permute-start(f32[3,3,8,384]{3,2,1,0:T(8,128)} %get-tuple-element.247), channel_id=1, source_target_pairs={{4,0},{8,4},{12,8},{16,12},{20,16},{24,20},{28,24},{5,1},{9,5},{13... | collective-permute-start | bytes 331784 | tf_op jit(solution)/shard_map/ppermute | solution.py:26
  154.2 3.6 %collective-permute-start.10 = (f32[3,10,3,384]{3,2,1,0:T(4,128)}, f32[3,10,3,384]{3,2,1,0:T(4,128)}, u32[]{:S(2)}, u32[]{:S(2)}) collective-permute-start(f32[3,10,3,384]{3,2,1,0:T(4,128)} %get-tuple-element.242), channel_id=1, source_target_pairs={{0,1},{1,2},{2,3},{4,5},{5,6},{6,7},{8,9},{9,10},{10,11},{12,13},{... | collective-permute-start | bytes 414728 | tf_op jit(solution)/shard_map/ppermute | solution.py:24
  156.2 3.8 %collective-permute-start.11 = (f32[3,10,3,384]{3,2,1,0:T(4,128)}, f32[3,10,3,384]{3,2,1,0:T(4,128)}, u32[]{:S(2)}, u32[]{:S(2)}) collective-permute-start(f32[3,10,3,384]{3,2,1,0:T(4,128)} %get-tuple-element.243), channel_id=1, source_target_pairs={{1,0},{2,1},{3,2},{5,4},{6,5},{7,6},{9,8},{10,9},{11,10},{13,12},{... | collective-permute-start | bytes 414728 | tf_op jit(solution)/shard_map/ppermute | solution.py:26
  (37 other events, 371.2 us)

commit v9 on v8

--- a/solution.py
+++ b/solution.py
@@ -127,6 +127,10 @@
         return pad_depth(with_halo(vector, (("slab", 1), ("col", 2)), 3))
 
     lower_x = lower_rows(integrity, offsets[:, 0], 3, contact.astype(jnp.bfloat16))
+    load_blocks = rhs_force.reshape(3, cells_x * cells_y, aggregates, agg_depth)
+    load_means = (jnp.sum(load_blocks, axis=(1, 3)) / agg_cells).T.reshape(3 * aggregates)
+    first_coarse = device_rows(load_means, ("slab", "col")).reshape(-1)
+    first_coarse, lower_x = lax.optimization_barrier((first_coarse, lower_x))
     spread = jnp.pad(
         pad_depth(with_halo(lower_x, (("col", 2),), 3)), ((0, 0), (0, 2), (0, 0), (0, 0))
     )
@@ -203,7 +207,7 @@
     every = ("slab", "col")
 
     residual = rhs_force
-    coarse_now = device_rows(local_means(residual), every).reshape(-1)
+    coarse_now = first_coarse
     direction = precondition(residual, coarse_now)
     image_vec = operator(direction)
     sums = device_rows(

time: 198 us -> 190 us (0.960)
  starting transfers between devices: 33.1 us -> 41.1 us
  waiting for transfers between devices: 28 us -> 20.4 us
  other arithmetic: 73.3 us -> 69.1 us
  local copies, waits for them, and re-layouts: 26.5 us -> 23.5 us
    ppermute x5, starting transfers between devices: 11.8 us -> 23.6 us  [with_halo(): parts.insert(0, lax.ppermute(last, axis, up))]
    ppermute x1, waiting for transfers between devices: 6.96 us -> 0.01 us  [lower_rows(): got = lax.ppermute(sent, 'slab', up)]
    all_to_all x1, starting transfers between devices: 8.7 us -> 4.87 us  [device_rows(): return lax.all_to_all(tiled, axes, 0, 0, tiled=True)]
    all_to_all x1, waiting for transfers between devices: 8.85 us -> 5.75 us  [device_rows(): return lax.all_to_all(tiled, axes, 0, 0, tiled=True)]
    ppermute x5, waiting for transfers between devices: 12.1 us -> 14.3 us  [with_halo(): parts.append(lax.ppermute(first, axis, down))]
    slice x5 -> x6, local copies, waits for them, and re-layouts: 4.24 us -> 5.16 us  [with_halo(): last = lax.slice_in_dim(x, length - width, length, axis=dim)]
  transfers between devices with their start and end apart: 13 -> 13, of which waited for: 6 -> 7; matrix products, arithmetic and copies ran while one was open for 8% -> 7% of each run, Pallas kernels for 0% -> 0%
where the time goes in v9:
time: 190 us; the launch traced here: 189 us
  other arithmetic  69.1 us (36%)
  starting transfers between devices  41.1 us (22%)
  blocking collectives  26.8 us (14%)
  local copies, waits for them, and re-layouts  23.5 us (12%)
  waiting for transfers between devices  20.4 us (11%)
  between operations  7.43 us (4%)
    all_to_all x2, blocking collectives, device_rows(): return lax.all_to_all(tiled, axes, 0, 0, tiled=True)  26.8 us
    ppermute x5, starting transfers between devices, with_halo(): parts.insert(0, lax.ppermute(last, axis, up))  23.6 us
    concatenate x5, other arithmetic, with_halo(): x = jnp.concatenate(parts, axis=dim)  15.7 us
    ppermute x5, waiting for transfers between devices, with_halo(): parts.append(lax.ppermute(first, axis, down))  14.3 us
    add x3, other arithmetic, operator(): summed[component] = summed[component] + heading[component] * stretch  13.3 us
    another operation x3, other arithmetic, operator(): return jnp.stack(summed)  13.1 us
    another operation x3, other arithmetic, on_device(): diagonal = jnp.stack(diag_list)  12.5 us
    ppermute x5, starting transfers between devices, with_halo(): parts.append(lax.ppermute(first, axis, down))  6.41 us
  transfers between devices with their start and end apart: 13, of which 7 were waited for; matrix products, arithmetic and copies ran while one was open for 7% of the time, Pallas kernels for 0%

profile of v9, /device:TPU:0, one launch (start us, length us, event | category | flops | bytes accessed | tf_op | source)
XLA Modules:
  0.0 188.6 jit_solution(15466206321177714008)
XLA Ops:
  4.2 4.9 %collective-permute-start = (bf16[71,8,384]{2,1,0:T(8,128)(2,1)S(1)}, bf16[71,8,384]{2,1,0:T(8,128)(2,1)S(1)}, u32[]{:S(2)}, u32[]{:S(2)}) collective-permute-start(bf16[71,8,384]{2,1,0:T(8,128)(2,1)S(1)} %pad_maximum_fusion.1), channel_id=1, source_target_pairs={{0,4},{4,8},{8,12},{12,16},{16,20},{20,24},{24,28},{1,5},{5,9},{9,... | collective-permute-start | bytes 1308680 | tf_op jit(solution)/shard_map/ppermute | solution.py:41
  11.0 4.9 %all-to-all-start = ((f32[32,1,24]{2,1,0:T(1,128)}), f32[32,1,24]{2,1,0:T(1,128)S(1)}, u32[]{:S(2)}, u32[]{:S(2)}) async-start(f32[32,1,24]{2,1,0:T(1,128)} %broadcast_in_dim.15), calls=%async_computation | async-start | bytes 32768 | tf_op jit(solution)/shard_map/all_to_all | solution.py:66
  17.2 5.8 %all-to-all-done = f32[32,1,24]{2,1,0:T(1,128)S(1)} async-done(((f32[32,1,24]{2,1,0:T(1,128)}), f32[32,1,24]{2,1,0:T(1,128)S(1)}, u32[]{:S(2)}, u32[]{:S(2)}) %all-to-all-start) | async-done | bytes 3104 | tf_op jit(solution)/shard_map/all_to_all | solution.py:66
  24.6 1.7 constant_dynamic-update-slice_fusion
  29.0 2.8 %collective-permute-start.2 = (bf16[62,8,3,384]{3,1,2,0:T(8,128)(2,1)}, bf16[62,8,3,384]{3,1,2,0:T(8,128)(2,1)}, u32[]{:S(2)}, u32[]{:S(2)}) collective-permute-start(bf16[62,8,3,384]{3,1,2,0:T(8,128)(2,1)} %copy.65), channel_id=1, source_target_pairs={{0,1},{1,2},{2,3},{4,5},{5,6},{6,7},{8,9},{9,10},{10,11},{12,13},{... | collective-permute-start | bytes 3428360 | tf_op jit(solution)/shard_map/ppermute | solution.py:24
  35.0 1.9 copy.67
  38.0 1.9 copy.68
  39.9 10.3 %fusion.5 = bf16[62,8,14,390]{3,2,1,0:T(8,128)(2,1)S(1)} fusion(bf16[62,8,3,384]{3,2,1,0:T(4,128)(2,1)S(1)} %copy.68, bf16[62,8,8,384]{3,2,1,0:T(8,128)(2,1)S(1)} %pad_maximum_fusion, bf16[62,8,3,384]{3,2,1,0:T(4,128)(2,1)S(1)} %copy.67), kind=kLoop, calls=%fused_computation.7 | loop fusion | flops 32497920 | bytes 10749312 | tf_op jit(solution)/shard_map/concatenate | solution.py:27
  54.0 4.9 %add_bitcast_fusion.5 = (f32[1,4,8,384]{3,2,1,0:T(8,128)S(1)}, f32[4,8,384]{2,1,0:T(8,128)S(1)}, f32[4,8,384]{2,1,0:T(8,128)S(1)}, f32[4,8,384]{2,1,0:T(8,128)S(...) fusion(bf16[10,14,390]{2,1,0:T(8,128)(2,1)S(1)} %get-tuple-elem, ...), kind=kLoop, calls=%fused_computation.2524 | loop fusion | flops 6967296 | bytes 7913472 | tf_op jit(solution)/shard_map/stack | solution.py:167
  59.0 3.9 %add_bitcast_fusion.4 = f32[1,4,8,384]{3,2,1,0:T(8,128)} fusion(f32[4,8,384]{2,1,0:T(8,128)S(1)} %get-tuple-element.149, bf16[10,14,390]{2,1,0:T(8,128)(2,1)S(1)} %get-tuple-element.172, bf16[10,14,390]{2,1,0:T(8,128)(2,1)S(1)} %get-tuple-element.176, bf16[10,14,390]{2,1,0:T(8,128)(2,1)S(1)} %get-tuple-element.178, ...), kind=kLoop, calls=%fused_computation.2523 | loop fusion | flops 5173248 | bytes 5799936 | tf_op jit(solution)/shard_map/stack | solution.py:167
  63.2 3.7 %add_bitcast_fusion.3 = f32[1,4,8,384]{3,2,1,0:T(8,128)S(1)} fusion(f32[4,8,384]{2,1,0:T(8,128)} %get-tuple-element.167, f32[4,8,384]{2,1,0:T(8,128)S(1)} %get-tuple-element.166, bf16[10,14,390]{2,1,0:T(8,128)(2,1)} %get-tuple-element.171, bf16[10,14,390]{2,1,0:T(8,128)(2,1)} %get-tuple-element.170, bf16[10,14,390]{2,1,0:T(8,128)(2,1)S(1)} %get-tuple-element.172, ...), kind=kLoop, calls=%fused_computation.2522 | loop fusion | flops 5406720 | bytes 6045696 | tf_op jit(solution)/shard_map/stack | solution.py:167
  68.5 3.0 %collective-permute-start.4 = (f32[3,3,8,384]{3,2,1,0:T(8,128)}, f32[3,3,8,384]{3,2,1,0:T(8,128)}, u32[]{:S(2)}, u32[]{:S(2)}) collective-permute-start(f32[3,3,8,384]{3,2,1,0:T(8,128)} %get-tuple-element.252), channel_id=1, source_target_pairs={{0,4},{4,8},{8,12},{12,16},{16,20},{20,24},{24,28},{1,5},{5,9},{9,... | collective-permute-start | bytes 331784 | tf_op jit(solution)/shard_map/ppermute | solution.py:24
  73.5 5.0 %collective-permute-done.5 = f32[3,3,8,384]{3,2,1,0:T(8,128)} collective-permute-done((f32[3,3,8,384]{3,2,1,0:T(8,128)}, f32[3,3,8,384]{3,2,1,0:T(8,128)}, u32[]{:S(2)}, u32[]{:S(2)}) %collective-permute-start.5) | collective-permute-done | bytes 110624 | tf_op jit(solution)/shard_map/ppermute | solution.py:26
  80.2 12.8 %collective-permute-start.6 = (f32[3,10,3,384]{3,2,1,0:T(4,128)}, f32[3,10,3,384]{3,2,1,0:T(4,128)S(1)}, u32[]{:S(2)}, u32[]{:S(2)}) collective-permute-start(f32[3,10,3,384]{3,2,1,0:T(4,128)} %get-tuple-element.248), channel_id=1, source_target_pairs={{0,1},{1,2},{2,3},{4,5},{5,6},{6,7},{8,9},{9,10},{10,11},{12,13},{... | collective-permute-start | bytes 414728 | tf_op jit(solution)/shard_map/ppermute | solution.py:24
  95.3 2.2 %collective-permute-done.7 = f32[3,10,3,384]{3,2,1,0:T(4,128)} collective-permute-done((f32[3,10,3,384]{3,2,1,0:T(4,128)}, f32[3,10,3,384]{3,2,1,0:T(4,128)}, u32[]{:S(2)}, u32[]{:S(2)}) %collective-permute-start.7) | collective-permute-done | bytes 138272 | tf_op jit(solution)/shard_map/ppermute | solution.py:26
  99.2 12.6 %add_add_fusion.2 = (f32[4,8,384]{2,1,0:T(8,128)S(1)}, f32[4,8,384]{2,1,0:T(8,128)S(1)}, f32[4,8,384]{2,1,0:T(8,128)S(1)}, f32[4,8,384]{2,1,0:T(8,128)S(1)}, f32...) fusion(f32[4,8,384]{2,1,0:T(8,128)} %squeeze.216, ...), kind=kLoop, calls=%fused_computation.2521 | loop fusion | flops 18382848 | bytes 27181056 | tf_op jit(solution)/shard_map/add | solution.py:192
  115.2 14.1 %all_to_all.24 = f32[32,1,26]{2,1,0:T(1,128)S(1)} all-to-all(f32[32,1,26]{2,1,0:T(1,128)S(1)} %broadcast_in_dim.19), channel_id=1, replica_groups=mesh['slab'=8,'col'=4] {'slab','col'}, dimensions={0} | all-to-all | bytes 6656 | tf_op jit(solution)/shard_map/all_to_all | solution.py:66
  134.2 3.1 %collective-permute-start.8 = (f32[3,3,8,384]{3,2,1,0:T(8,128)}, f32[3,3,8,384]{3,2,1,0:T(8,128)}, u32[]{:S(2)}, u32[]{:S(2)}) collective-permute-start(f32[3,3,8,384]{3,2,1,0:T(8,128)} %get-tuple-element.250), channel_id=1, source_target_pairs={{0,4},{4,8},{8,12},{12,16},{16,20},{20,24},{24,28},{1,5},{5,9},{9,... | collective-permute-start | bytes 331784 | tf_op jit(solution)/shard_map/ppermute | solution.py:24
  139.8 4.5 %collective-permute-done.9 = f32[3,3,8,384]{3,2,1,0:T(8,128)} collective-permute-done((f32[3,3,8,384]{3,2,1,0:T(8,128)}, f32[3,3,8,384]{3,2,1,0:T(8,128)}, u32[]{:S(2)}, u32[]{:S(2)}) %collective-permute-start.9) | collective-permute-done | bytes 110624 | tf_op jit(solution)/shard_map/ppermute | solution.py:26
  146.0 2.0 %collective-permute-start.10 = (f32[3,10,3,384]{3,2,1,0:T(4,128)}, f32[3,10,3,384]{3,2,1,0:T(4,128)}, u32[]{:S(2)}, u32[]{:S(2)}) collective-permute-start(f32[3,10,3,384]{3,2,1,0:T(4,128)} %get-tuple-element.246), channel_id=1, source_target_pairs={{0,1},{1,2},{2,3},{4,5},{5,6},{6,7},{8,9},{9,10},{10,11},{12,13},{... | collective-permute-start | bytes 414728 | tf_op jit(solution)/shard_map/ppermute | solution.py:24
  151.8 1.8 select_maximum_fusion
  153.7 12.4 %add_bitcast_fusion.2 = (f32[1,4,8,384]{3,2,1,0:T(8,128)S(1)}, f32[4,8,384]{2,1,0:T(8,128)S(1)}, f32[4,8,384]{2,1,0:T(8,128)S(1)}, f32[4,8,384]{2,1,0:T(8,128)S(...) fusion(f32[4,8,384]{2,1,0:T(8,128)} %squeeze.222, ...), kind=kLoop, calls=%fused_computation.2518 | loop fusion | flops 18382848 | bytes 27181056 | tf_op jit(solution)/shard_map/stack | solution.py:193
  167.5 2.6 %pad_maximum_fusion.8 = f32[4]{0:T(128)S(1)} fusion(f32[1]{0:T(128)} %bitcast.100, f32[1]{0:T(128)} %bitcast.99, f32[1]{0:T(128)} %bitcast.98, f32[1]{0:T(128)} %bitcast.91), kind=kLoop, calls=%fused_computation.2646 | loop fusion | flops 12 | bytes 32 | tf_op jit(solution)/shard_map/stack | solution.py:234
  170.1 12.6 %all_to_all.25 = f32[32,1,4]{2,1,0:T(1,128)S(1)} all-to-all(f32[32,1,4]{2,1,0:T(1,128)S(1)} %broadcast_in_dim.20), channel_id=1, replica_groups=mesh['slab'=8,'col'=4] {'slab','col'}, dimensions={0} | all-to-all | bytes 1024 | tf_op jit(solution)/shard_map/all_to_all | solution.py:66
  (201 shorter events, 46.0 us)
Async XLA Ops:
  0.6 33.9 %copy-start = (f32[24,768]{1,0:T(8,128)S(1)}, f32[24,768]{1,0:T(8,128)}, u32[]{:S(2)}) copy-start(f32[24,768]{1,0:T(8,128)} %param.7) | copy-start | bytes 221188
  4.2 20.1 %collective-permute-start = (bf16[71,8,384]{2,1,0:T(8,128)(2,1)S(1)}, bf16[71,8,384]{2,1,0:T(8,128)(2,1)S(1)}, u32[]{:S(2)}, u32[]{:S(2)}) collective-permute-start(bf16[71,8,384]{2,1,0:T(8,128)(2,1)S(1)} %pad_maximum_fusion.1), channel_id=1, source_target_pairs={{0,4},{4,8},{8,12},{12,16},{16,20},{20,24},{24,28},{1,5},{5,9},{9,... | collective-permute-start | bytes 1308680 | tf_op jit(solution)/shard_map/ppermute | solution.py:41
  11.0 12.0 %all-to-all-start = ((f32[32,1,24]{2,1,0:T(1,128)}), f32[32,1,24]{2,1,0:T(1,128)S(1)}, u32[]{:S(2)}, u32[]{:S(2)}) async-start(f32[32,1,24]{2,1,0:T(1,128)} %broadcast_in_dim.15), calls=%async_computation | async-start | bytes 32768 | tf_op jit(solution)/shard_map/all_to_all | solution.py:66
  15.9 10.5 %collective-permute-start.1 = (bf16[1,8,384]{2,1,0:T(8,128)(2,1)S(1)}, bf16[1,8,384]{2,1,0:T(8,128)(2,1)S(1)}, u32[]{:S(2)}, u32[]{:S(2)}) collective-permute-start(bf16[1,8,384]{2,1,0:T(8,128)(2,1)S(1)} %get-tuple-element.255), channel_id=1, source_target_pairs={{4,0},{8,4},{12,8},{16,12},{20,16},{24,20},{28,24},{5,1},{9,5},{13... | collective-permute-start | bytes 18440 | tf_op jit(solution)/shard_map/ppermute | solution.py:42
  29.0 6.0 %collective-permute-start.2 = (bf16[62,8,3,384]{3,1,2,0:T(8,128)(2,1)}, bf16[62,8,3,384]{3,1,2,0:T(8,128)(2,1)}, u32[]{:S(2)}, u32[]{:S(2)}) collective-permute-start(bf16[62,8,3,384]{3,1,2,0:T(8,128)(2,1)} %copy.65), channel_id=1, source_target_pairs={{0,1},{1,2},{2,3},{4,5},{5,6},{6,7},{8,9},{9,10},{10,11},{12,13},{... | collective-permute-start | bytes 3428360 | tf_op jit(solution)/shard_map/ppermute | solution.py:24
  33.0 5.0 %collective-permute-start.3 = (bf16[62,8,3,384]{3,1,2,0:T(8,128)(2,1)}, bf16[62,8,3,384]{3,1,2,0:T(8,128)(2,1)}, u32[]{:S(2)}, u32[]{:S(2)}) collective-permute-start(bf16[62,8,3,384]{3,1,2,0:T(8,128)(2,1)} %copy.66), channel_id=1, source_target_pairs={{1,0},{2,1},{3,2},{5,4},{6,5},{7,6},{9,8},{10,9},{11,10},{13,12},{... | collective-permute-start | bytes 3428360 | tf_op jit(solution)/shard_map/ppermute | solution.py:26
  51.4 11.4 %copy-start.2 = (bf16[10,14,390]{2,1,0:T(8,128)(2,1)}, bf16[10,14,390]{2,1,0:T(8,128)(2,1)S(1)}, u32[]{:S(2)}) copy-start(bf16[10,14,390]{2,1,0:T(8,128)(2,1)S(1)} %get-tuple-element.184) | copy-start | bytes 327604
  51.4 11.4 %copy-start.3 = (bf16[10,14,390]{2,1,0:T(8,128)(2,1)}, bf16[10,14,390]{2,1,0:T(8,128)(2,1)S(1)}, u32[]{:S(2)}) copy-start(bf16[10,14,390]{2,1,0:T(8,128)(2,1)S(1)} %get-tuple-element.185) | copy-start | bytes 327604
  51.7 11.2 %copy-start.4 = (bf16[10,14,390]{2,1,0:T(8,128)(2,1)}, bf16[10,14,390]{2,1,0:T(8,128)(2,1)S(1)}, u32[]{:S(2)}) copy-start(bf16[10,14,390]{2,1,0:T(8,128)(2,1)S(1)} %get-tuple-element.187) | copy-start | bytes 327604
  54.0 12.8 %copy-start.36 = (bf16[10,14,390]{2,1,0:T(8,128)(2,1)}, bf16[10,14,390]{2,1,0:T(8,128)(2,1)S(1)}, u32[]{:S(2)}) copy-start(bf16[10,14,390]{2,1,0:T(8,128)(2,1)S(1)} %get-tuple-element.222) | copy-start | bytes 327604
  54.0 12.9 %copy-start.37 = (bf16[10,14,390]{2,1,0:T(8,128)(2,1)}, bf16[10,14,390]{2,1,0:T(8,128)(2,1)S(1)}, u32[]{:S(2)}) copy-start(bf16[10,14,390]{2,1,0:T(8,128)(2,1)S(1)} %get-tuple-element.223) | copy-start | bytes 327604
  54.0 12.9 %copy-start.38 = (bf16[10,14,390]{2,1,0:T(8,128)(2,1)}, bf16[10,14,390]{2,1,0:T(8,128)(2,1)S(1)}, u32[]{:S(2)}) copy-start(bf16[10,14,390]{2,1,0:T(8,128)(2,1)S(1)} %get-tuple-element.224) | copy-start | bytes 327604
  54.0 12.9 %copy-start.39 = (bf16[10,14,390]{2,1,0:T(8,128)(2,1)}, bf16[10,14,390]{2,1,0:T(8,128)(2,1)S(1)}, u32[]{:S(2)}) copy-start(bf16[10,14,390]{2,1,0:T(8,128)(2,1)S(1)} %get-tuple-element.225) | copy-start | bytes 327604
  54.0 12.9 %copy-start.40 = (bf16[10,14,390]{2,1,0:T(8,128)(2,1)}, bf16[10,14,390]{2,1,0:T(8,128)(2,1)S(1)}, u32[]{:S(2)}) copy-start(bf16[10,14,390]{2,1,0:T(8,128)(2,1)S(1)} %get-tuple-element.226) | copy-start | bytes 327604
  54.0 12.9 %copy-start.1 = (f32[3,4,8,384]{3,2,1,0:T(8,128)S(1)}, f32[3,4,8,384]{3,2,1,0:T(8,128)}, u32[]{:S(2)}) copy-start(f32[3,4,8,384]{3,2,1,0:T(8,128)} %param.4) | copy-start | bytes 442372
  68.5 5.0 %collective-permute-start.4 = (f32[3,3,8,384]{3,2,1,0:T(8,128)}, f32[3,3,8,384]{3,2,1,0:T(8,128)}, u32[]{:S(2)}, u32[]{:S(2)}) collective-permute-start(f32[3,3,8,384]{3,2,1,0:T(8,128)} %get-tuple-element.252), channel_id=1, source_target_pairs={{0,4},{4,8},{8,12},{12,16},{16,20},{20,24},{24,28},{1,5},{5,9},{9,... | collective-permute-start | bytes 331784 | tf_op jit(solution)/shard_map/ppermute | solution.py:24
  71.5 6.9 %collective-permute-start.5 = (f32[3,3,8,384]{3,2,1,0:T(8,128)}, f32[3,3,8,384]{3,2,1,0:T(8,128)}, u32[]{:S(2)}, u32[]{:S(2)}) collective-permute-start(f32[3,3,8,384]{3,2,1,0:T(8,128)} %get-tuple-element.253), channel_id=1, source_target_pairs={{4,0},{8,4},{12,8},{16,12},{20,16},{24,20},{28,24},{5,1},{9,5},{13... | collective-permute-start | bytes 331784 | tf_op jit(solution)/shard_map/ppermute | solution.py:26
  80.2 15.1 %collective-permute-start.6 = (f32[3,10,3,384]{3,2,1,0:T(4,128)}, f32[3,10,3,384]{3,2,1,0:T(4,128)S(1)}, u32[]{:S(2)}, u32[]{:S(2)}) collective-permute-start(f32[3,10,3,384]{3,2,1,0:T(4,128)} %get-tuple-element.248), channel_id=1, source_target_pairs={{0,1},{1,2},{2,3},{4,5},{5,6},{6,7},{8,9},{9,10},{10,11},{12,13},{... | collective-permute-start | bytes 414728 | tf_op jit(solution)/shard_map/ppermute | solution.py:24
  93.0 4.4 %collective-permute-start.7 = (f32[3,10,3,384]{3,2,1,0:T(4,128)}, f32[3,10,3,384]{3,2,1,0:T(4,128)}, u32[]{:S(2)}, u32[]{:S(2)}) collective-permute-start(f32[3,10,3,384]{3,2,1,0:T(4,128)} %get-tuple-element.249), channel_id=1, source_target_pairs={{1,0},{2,1},{3,2},{5,4},{6,5},{7,6},{9,8},{10,9},{11,10},{13,12},{... | collective-permute-start | bytes 414728 | tf_op jit(solution)/shard_map/ppermute | solution.py:26
  99.2 32.7 %copy-start.42 = (f32[1,4,8,384]{3,2,1,0:T(8,128)S(1)}, f32[1,4,8,384]{3,2,1,0:T(8,128)}, u32[]{:S(2)}) copy-start(f32[1,4,8,384]{3,2,1,0:T(8,128)} %copy-done.41) | copy-start | bytes 147460
  134.2 5.6 %collective-permute-start.8 = (f32[3,3,8,384]{3,2,1,0:T(8,128)}, f32[3,3,8,384]{3,2,1,0:T(8,128)}, u32[]{:S(2)}, u32[]{:S(2)}) collective-permute-start(f32[3,3,8,384]{3,2,1,0:T(8,128)} %get-tuple-element.250), channel_id=1, source_target_pairs={{0,4},{4,8},{8,12},{12,16},{16,20},{20,24},{24,28},{1,5},{5,9},{9,... | collective-permute-start | bytes 331784 | tf_op jit(solution)/shard_map/ppermute | solution.py:24
  137.3 6.9 %collective-permute-start.9 = (f32[3,3,8,384]{3,2,1,0:T(8,128)}, f32[3,3,8,384]{3,2,1,0:T(8,128)}, u32[]{:S(2)}, u32[]{:S(2)}) collective-permute-start(f32[3,3,8,384]{3,2,1,0:T(8,128)} %get-tuple-element.251), channel_id=1, source_target_pairs={{4,0},{8,4},{12,8},{16,12},{20,16},{24,20},{28,24},{5,1},{9,5},{13... | collective-permute-start | bytes 331784 | tf_op jit(solution)/shard_map/ppermute | solution.py:26
  146.0 4.2 %collective-permute-start.10 = (f32[3,10,3,384]{3,2,1,0:T(4,128)}, f32[3,10,3,384]{3,2,1,0:T(4,128)}, u32[]{:S(2)}, u32[]{:S(2)}) collective-permute-start(f32[3,10,3,384]{3,2,1,0:T(4,128)} %get-tuple-element.246), channel_id=1, source_target_pairs={{0,1},{1,2},{2,3},{4,5},{5,6},{6,7},{8,9},{9,10},{10,11},{12,13},{... | collective-permute-start | bytes 414728 | tf_op jit(solution)/shard_map/ppermute | solution.py:24
  147.9 3.9 %collective-permute-start.11 = (f32[3,10,3,384]{3,2,1,0:T(4,128)}, f32[3,10,3,384]{3,2,1,0:T(4,128)}, u32[]{:S(2)}, u32[]{:S(2)}) collective-permute-start(f32[3,10,3,384]{3,2,1,0:T(4,128)} %get-tuple-element.247), channel_id=1, source_target_pairs={{1,0},{2,1},{3,2},{5,4},{6,5},{7,6},{9,8},{10,9},{11,10},{13,12},{... | collective-permute-start | bytes 414728 | tf_op jit(solution)/shard_map/ppermute | solution.py:26
  (32 other events, 339.2 us)

commit v10 on v9

--- a/solution.py
+++ b/solution.py
@@ -155,16 +155,11 @@
         forward = window(inside_pad, shift_x, shift_y, shift_z, extent) * forward
         return (forward, backward)
 
-    diag_list = [jnp.full(extent, FOUNDATION, jnp.float32) for component in range(3)]
+    diagonal = jnp.full((3,) + extent, FOUNDATION, jnp.float32)
     for bond_index in range(bond_count):
         forward, backward = bond_pair(bond_index)
-        heading = heading_of(bond_index)
-        both_ends = forward + backward
-        for component in range(3):
-            diag_list[component] = (
-                diag_list[component] + heading[component] * heading[component] * both_ends
-            )
-    diagonal = jnp.stack(diag_list)
+        squares = np.array([entry * entry for entry in heading_of(bond_index)], np.float32)
+        diagonal = diagonal + jnp.asarray(squares).reshape(3, 1, 1, 1) * (forward + backward)[None]
 
     def operator(vector):
         padded = rimmed(vector)

time: 190 us -> 184 us (0.968)
  other arithmetic: 69.1 us -> 61.7 us
    another operation x3 -> x0, other arithmetic: 12.5 us -> none  [on_device(): diagonal = jnp.stack(diag_list)]
    add x0 -> x12, other arithmetic: none -> 5.26 us  [on_device(): forward + backward]
  transfers between devices with their start and end apart: 13 -> 13, of which waited for: 7 -> 6; matrix products, arithmetic and copies ran while one was open for 7% -> 7% of each run, Pallas kernels for 0% -> 0%
where the time goes in v10:
time: 184 us; the launch traced here: 183 us
  other arithmetic  61.7 us (34%)
  starting transfers between devices  41.6 us (23%)
  blocking collectives  26.7 us (15%)
  local copies, waits for them, and re-layouts  23.4 us (13%)
  waiting for transfers between devices  21.1 us (11%)
  between operations  8.06 us (4%)
    all_to_all x2, blocking collectives, device_rows(): return lax.all_to_all(tiled, axes, 0, 0, tiled=True)  26.7 us
    ppermute x5, starting transfers between devices, with_halo(): parts.insert(0, lax.ppermute(last, axis, up))  23.9 us
    concatenate x5, other arithmetic, with_halo(): x = jnp.concatenate(parts, axis=dim)  15.6 us
    ppermute x5, waiting for transfers between devices, with_halo(): parts.append(lax.ppermute(first, axis, down))  15 us
    another operation x3, other arithmetic, operator(): return jnp.stack(summed)  13.5 us
    add x3, other arithmetic, operator(): summed[component] = summed[component] + heading[component] * stretch  13.4 us
    ppermute x5, starting transfers between devices, with_halo(): parts.append(lax.ppermute(first, axis, down))  6.62 us
    all_to_all x1, waiting for transfers between devices, device_rows(): return lax.all_to_all(tiled, axes, 0, 0, tiled=True)  5.75 us
  transfers between devices with their start and end apart: 13, of which 6 were waited for; matrix products, arithmetic and copies ran while one was open for 7% of the time, Pallas kernels for 0%

profile of v10, /device:TPU:0, one launch (start us, length us, event | category | flops | bytes accessed | tf_op | source)
XLA Modules:
  0.0 182.8 jit_solution(13484399410256001220)
XLA Ops:
  4.2 4.9 %collective-permute-start = (bf16[71,8,384]{2,1,0:T(8,128)(2,1)S(1)}, bf16[71,8,384]{2,1,0:T(8,128)(2,1)S(1)}, u32[]{:S(2)}, u32[]{:S(2)}) collective-permute-start(bf16[71,8,384]{2,1,0:T(8,128)(2,1)S(1)} %pad_maximum_fusion.1), channel_id=1, source_target_pairs={{0,4},{4,8},{8,12},{12,16},{16,20},{20,24},{24,28},{1,5},{5,9},{9,... | collective-permute-start | bytes 1308680 | tf_op jit(solution)/shard_map/ppermute | solution.py:41
  11.0 4.9 %all-to-all-start = ((f32[32,1,24]{2,1,0:T(1,128)}), f32[32,1,24]{2,1,0:T(1,128)S(1)}, u32[]{:S(2)}, u32[]{:S(2)}) async-start(f32[32,1,24]{2,1,0:T(1,128)} %broadcast_in_dim.17), calls=%async_computation | async-start | bytes 32768 | tf_op jit(solution)/shard_map/all_to_all | solution.py:66
  17.2 5.8 %all-to-all-done = f32[32,1,24]{2,1,0:T(1,128)S(1)} async-done(((f32[32,1,24]{2,1,0:T(1,128)}), f32[32,1,24]{2,1,0:T(1,128)S(1)}, u32[]{:S(2)}, u32[]{:S(2)}) %all-to-all-start) | async-done | bytes 3104 | tf_op jit(solution)/shard_map/all_to_all | solution.py:66
  24.6 1.7 constant_dynamic-update-slice_fusion
  31.6 4.1 %collective-permute-start.2 = (bf16[62,8,3,384]{3,1,2,0:T(8,128)(2,1)}, bf16[62,8,3,384]{3,1,2,0:T(8,128)(2,1)}, u32[]{:S(2)}, u32[]{:S(2)}) collective-permute-start(bf16[62,8,3,384]{3,1,2,0:T(8,128)(2,1)} %copy.126), channel_id=1, source_target_pairs={{0,1},{1,2},{2,3},{4,5},{5,6},{6,7},{8,9},{9,10},{10,11},{12,13},{... | collective-permute-start | bytes 3428360 | tf_op jit(solution)/shard_map/ppermute | solution.py:24
  36.4 1.9 %copy.129 = bf16[62,8,3,384]{3,2,1,0:T(4,128)(2,1)S(1)} copy(bf16[62,8,3,384]{3,1,2,0:T(8,128)(2,1)} %collective-permute-done.3) | data formatting | bytes 2285568 | tf_op jit(solution)/shard_map/ppermute | solution.py:26
  38.3 1.9 %copy.128 = bf16[62,8,3,384]{3,2,1,0:T(4,128)(2,1)S(1)} copy(bf16[62,8,3,384]{3,1,2,0:T(8,128)(2,1)} %collective-permute-done.2) | data formatting | bytes 2285568 | tf_op jit(solution)/shard_map/ppermute | solution.py:24
  40.1 10.2 %fusion.5 = bf16[62,8,14,390]{3,2,1,0:T(8,128)(2,1)S(1)} fusion(bf16[62,8,3,384]{3,2,1,0:T(4,128)(2,1)S(1)} %copy.129, bf16[62,8,8,384]{3,2,1,0:T(8,128)(2,1)S(1)} %pad_maximum_fusion, bf16[62,8,3,384]{3,2,1,0:T(4,128)(2,1)S(1)} %copy.128), kind=kLoop, calls=%fused_computation.7 | loop fusion | flops 32497920 | bytes 10749312 | tf_op jit(solution)/shard_map/concatenate | solution.py:27
  60.0 3.1 %collective-permute-start.4 = (f32[3,3,8,384]{3,2,1,0:T(8,128)}, f32[3,3,8,384]{3,2,1,0:T(8,128)}, u32[]{:S(2)}, u32[]{:S(2)}) collective-permute-start(f32[3,3,8,384]{3,2,1,0:T(8,128)} %get-tuple-element.330), channel_id=1, source_target_pairs={{0,4},{4,8},{8,12},{12,16},{16,20},{20,24},{24,28},{1,5},{5,9},{9,... | collective-permute-start | bytes 331784 | tf_op jit(solution)/shard_map/ppermute | solution.py:24
  65.1 5.0 %collective-permute-done.5 = f32[3,3,8,384]{3,2,1,0:T(8,128)} collective-permute-done((f32[3,3,8,384]{3,2,1,0:T(8,128)}, f32[3,3,8,384]{3,2,1,0:T(8,128)}, u32[]{:S(2)}, u32[]{:S(2)}) %collective-permute-start.5) | collective-permute-done | bytes 110624 | tf_op jit(solution)/shard_map/ppermute | solution.py:26
  71.9 11.6 %collective-permute-start.6 = (f32[3,10,3,384]{3,2,1,0:T(4,128)}, f32[3,10,3,384]{3,2,1,0:T(4,128)}, u32[]{:S(2)}, u32[]{:S(2)}) collective-permute-start(f32[3,10,3,384]{3,2,1,0:T(4,128)} %get-tuple-element.274), channel_id=1, source_target_pairs={{0,1},{1,2},{2,3},{4,5},{5,6},{6,7},{8,9},{9,10},{10,11},{12,13},{... | collective-permute-start | bytes 414728 | tf_op jit(solution)/shard_map/ppermute | solution.py:24
  83.5 1.5 collective-permute-start.7
  85.3 4.5 %collective-permute-done.7 = f32[3,10,3,384]{3,2,1,0:T(4,128)} collective-permute-done((f32[3,10,3,384]{3,2,1,0:T(4,128)}, f32[3,10,3,384]{3,2,1,0:T(4,128)}, u32[]{:S(2)}, u32[]{:S(2)}) %collective-permute-start.7) | collective-permute-done | bytes 138272 | tf_op jit(solution)/shard_map/ppermute | solution.py:26
  89.9 1.8 select_maximum_fusion.4
  91.7 12.8 %add_add_fusion.2 = (f32[4,8,384]{2,1,0:T(8,128)S(1)}, f32[4,8,384]{2,1,0:T(8,128)S(1)}, f32[4,8,384]{2,1,0:T(8,128)S(1)}, f32[4,8,384]{2,1,0:T(8,128)S(1)}, f32...) fusion(f32[4,8,384]{2,1,0:T(8,128)S(1)} %squeeze.216, ...), kind=kLoop, calls=%fused_computation.2519 | loop fusion | flops 18382848 | bytes 27181056 | tf_op jit(solution)/shard_map/add | solution.py:187
  108.0 1.4 pad_maximum_fusion.6
  109.4 14.1 %all_to_all.24 = f32[32,1,26]{2,1,0:T(1,128)S(1)} all-to-all(f32[32,1,26]{2,1,0:T(1,128)S(1)} %broadcast_in_dim.22), channel_id=1, replica_groups=mesh['slab'=8,'col'=4] {'slab','col'}, dimensions={0} | all-to-all | bytes 6656 | tf_op jit(solution)/shard_map/all_to_all | solution.py:66
  127.7 3.1 %collective-permute-start.8 = (f32[3,3,8,384]{3,2,1,0:T(8,128)}, f32[3,3,8,384]{3,2,1,0:T(8,128)}, u32[]{:S(2)}, u32[]{:S(2)}) collective-permute-start(f32[3,3,8,384]{3,2,1,0:T(8,128)} %get-tuple-element.328), channel_id=1, source_target_pairs={{0,4},{4,8},{8,12},{12,16},{16,20},{20,24},{24,28},{1,5},{5,9},{9,... | collective-permute-start | bytes 331784 | tf_op jit(solution)/shard_map/ppermute | solution.py:24
  133.3 4.5 %collective-permute-done.9 = f32[3,3,8,384]{3,2,1,0:T(8,128)} collective-permute-done((f32[3,3,8,384]{3,2,1,0:T(8,128)}, f32[3,3,8,384]{3,2,1,0:T(8,128)}, u32[]{:S(2)}, u32[]{:S(2)}) %collective-permute-start.9) | collective-permute-done | bytes 110624 | tf_op jit(solution)/shard_map/ppermute | solution.py:26
  139.5 2.0 %collective-permute-start.10 = (f32[3,10,3,384]{3,2,1,0:T(4,128)}, f32[3,10,3,384]{3,2,1,0:T(4,128)}, u32[]{:S(2)}, u32[]{:S(2)}) collective-permute-start(f32[3,10,3,384]{3,2,1,0:T(4,128)} %get-tuple-element.272), channel_id=1, source_target_pairs={{0,1},{1,2},{2,3},{4,5},{5,6},{6,7},{8,9},{9,10},{10,11},{12,13},{... | collective-permute-start | bytes 414728 | tf_op jit(solution)/shard_map/ppermute | solution.py:24
  145.3 1.8 select_maximum_fusion
  147.2 12.8 %add_bitcast_fusion.2 = (f32[1,4,8,384]{3,2,1,0:T(8,128)S(1)}, f32[4,8,384]{2,1,0:T(8,128)S(1)}, f32[4,8,384]{2,1,0:T(8,128)S(1)}, f32[4,8,384]{2,1,0:T(8,128)S(...) fusion(f32[4,8,384]{2,1,0:T(8,128)} %squeeze.222, ...), kind=kLoop, calls=%fused_computation.2516 | loop fusion | flops 18382848 | bytes 27181056 | tf_op jit(solution)/shard_map/stack | solution.py:188
  161.5 2.6 %pad_maximum_fusion.7 = f32[4]{0:T(128)S(1)} fusion(f32[1]{0:T(128)} %bitcast.97, f32[1]{0:T(128)} %bitcast.96, f32[1]{0:T(128)} %bitcast.95, f32[1]{0:T(128)} %bitcast.88), kind=kLoop, calls=%fused_computation.2641 | loop fusion | flops 12 | bytes 32 | tf_op jit(solution)/shard_map/stack | solution.py:229
  164.1 12.6 %all_to_all.25 = f32[32,1,4]{2,1,0:T(1,128)S(1)} all-to-all(f32[32,1,4]{2,1,0:T(1,128)S(1)} %broadcast_in_dim.23), channel_id=1, replica_groups=mesh['slab'=8,'col'=4] {'slab','col'}, dimensions={0} | all-to-all | bytes 1024 | tf_op jit(solution)/shard_map/all_to_all | solution.py:66
  (244 shorter events, 44.5 us)
Async XLA Ops:
  0.6 35.2 %copy-start = (f32[24,768]{1,0:T(8,128)S(1)}, f32[24,768]{1,0:T(8,128)}, u32[]{:S(2)}) copy-start(f32[24,768]{1,0:T(8,128)} %param.68) | copy-start | bytes 221188
  4.2 20.1 %collective-permute-start = (bf16[71,8,384]{2,1,0:T(8,128)(2,1)S(1)}, bf16[71,8,384]{2,1,0:T(8,128)(2,1)S(1)}, u32[]{:S(2)}, u32[]{:S(2)}) collective-permute-start(bf16[71,8,384]{2,1,0:T(8,128)(2,1)S(1)} %pad_maximum_fusion.1), channel_id=1, source_target_pairs={{0,4},{4,8},{8,12},{12,16},{16,20},{20,24},{24,28},{1,5},{5,9},{9,... | collective-permute-start | bytes 1308680 | tf_op jit(solution)/shard_map/ppermute | solution.py:41
  11.0 12.0 %all-to-all-start = ((f32[32,1,24]{2,1,0:T(1,128)}), f32[32,1,24]{2,1,0:T(1,128)S(1)}, u32[]{:S(2)}, u32[]{:S(2)}) async-start(f32[32,1,24]{2,1,0:T(1,128)} %broadcast_in_dim.17), calls=%async_computation | async-start | bytes 32768 | tf_op jit(solution)/shard_map/all_to_all | solution.py:66
  15.9 10.5 %collective-permute-start.1 = (bf16[1,8,384]{2,1,0:T(8,128)(2,1)S(1)}, bf16[1,8,384]{2,1,0:T(8,128)(2,1)S(1)}, u32[]{:S(2)}, u32[]{:S(2)}) collective-permute-start(bf16[1,8,384]{2,1,0:T(8,128)(2,1)S(1)} %get-tuple-element.333), channel_id=1, source_target_pairs={{4,0},{8,4},{12,8},{16,12},{20,16},{24,20},{28,24},{5,1},{9,5},{13... | collective-permute-start | bytes 18440 | tf_op jit(solution)/shard_map/ppermute | solution.py:42
  29.1 7.3 %collective-permute-start.3 = (bf16[62,8,3,384]{3,1,2,0:T(8,128)(2,1)}, bf16[62,8,3,384]{3,1,2,0:T(8,128)(2,1)}, u32[]{:S(2)}, u32[]{:S(2)}) collective-permute-start(bf16[62,8,3,384]{3,1,2,0:T(8,128)(2,1)} %copy.127), channel_id=1, source_target_pairs={{1,0},{2,1},{3,2},{5,4},{6,5},{7,6},{9,8},{10,9},{11,10},{13,12},{... | collective-permute-start | bytes 3428360 | tf_op jit(solution)/shard_map/ppermute | solution.py:26
  31.6 6.7 %collective-permute-start.2 = (bf16[62,8,3,384]{3,1,2,0:T(8,128)(2,1)}, bf16[62,8,3,384]{3,1,2,0:T(8,128)(2,1)}, u32[]{:S(2)}, u32[]{:S(2)}) collective-permute-start(bf16[62,8,3,384]{3,1,2,0:T(8,128)(2,1)} %copy.126), channel_id=1, source_target_pairs={{0,1},{1,2},{2,3},{4,5},{5,6},{6,7},{8,9},{9,10},{10,11},{12,13},{... | collective-permute-start | bytes 3428360 | tf_op jit(solution)/shard_map/ppermute | solution.py:24
  50.8 6.9 %copy-start.4 = (bf16[10,14,390]{2,1,0:T(8,128)(2,1)}, bf16[10,14,390]{2,1,0:T(8,128)(2,1)S(1)}, u32[]{:S(2)}) copy-start(bf16[10,14,390]{2,1,0:T(8,128)(2,1)S(1)} %get-tuple-element.228) | copy-start | bytes 327604
  50.8 6.9 %copy-start.5 = (bf16[10,14,390]{2,1,0:T(8,128)(2,1)}, bf16[10,14,390]{2,1,0:T(8,128)(2,1)S(1)}, u32[]{:S(2)}) copy-start(bf16[10,14,390]{2,1,0:T(8,128)(2,1)S(1)} %get-tuple-element.229) | copy-start | bytes 327604
  50.8 7.2 %copy-start.2 = (bf16[10,14,390]{2,1,0:T(8,128)(2,1)}, bf16[10,14,390]{2,1,0:T(8,128)(2,1)S(1)}, u32[]{:S(2)}) copy-start(bf16[10,14,390]{2,1,0:T(8,128)(2,1)S(1)} %get-tuple-element.226) | copy-start | bytes 327604
  50.8 7.2 %copy-start.3 = (bf16[10,14,390]{2,1,0:T(8,128)(2,1)}, bf16[10,14,390]{2,1,0:T(8,128)(2,1)S(1)}, u32[]{:S(2)}) copy-start(bf16[10,14,390]{2,1,0:T(8,128)(2,1)S(1)} %get-tuple-element.227) | copy-start | bytes 327604
  52.1 6.1 %copy-start.1 = (f32[3,4,8,384]{3,2,1,0:T(8,128)S(1)}, f32[3,4,8,384]{3,2,1,0:T(8,128)}, u32[]{:S(2)}) copy-start(f32[3,4,8,384]{3,2,1,0:T(8,128)} %param.65) | copy-start | bytes 442372
  52.6 11.8 %copy-start.37 = (bf16[10,14,390]{2,1,0:T(8,128)(2,1)}, bf16[10,14,390]{2,1,0:T(8,128)(2,1)S(1)}, u32[]{:S(2)}) copy-start(bf16[10,14,390]{2,1,0:T(8,128)(2,1)S(1)} %get-tuple-element.178) | copy-start | bytes 327604
  52.6 11.8 %copy-start.38 = (bf16[10,14,390]{2,1,0:T(8,128)(2,1)}, bf16[10,14,390]{2,1,0:T(8,128)(2,1)S(1)}, u32[]{:S(2)}) copy-start(bf16[10,14,390]{2,1,0:T(8,128)(2,1)S(1)} %get-tuple-element.179) | copy-start | bytes 327604
  52.6 11.8 %copy-start.39 = (bf16[10,14,390]{2,1,0:T(8,128)(2,1)}, bf16[10,14,390]{2,1,0:T(8,128)(2,1)S(1)}, u32[]{:S(2)}) copy-start(bf16[10,14,390]{2,1,0:T(8,128)(2,1)S(1)} %get-tuple-element.180) | copy-start | bytes 327604
  52.6 11.8 %copy-start.40 = (bf16[10,14,390]{2,1,0:T(8,128)(2,1)}, bf16[10,14,390]{2,1,0:T(8,128)(2,1)S(1)}, u32[]{:S(2)}) copy-start(bf16[10,14,390]{2,1,0:T(8,128)(2,1)S(1)} %get-tuple-element.184) | copy-start | bytes 327604
  60.0 5.1 %collective-permute-start.4 = (f32[3,3,8,384]{3,2,1,0:T(8,128)}, f32[3,3,8,384]{3,2,1,0:T(8,128)}, u32[]{:S(2)}, u32[]{:S(2)}) collective-permute-start(f32[3,3,8,384]{3,2,1,0:T(8,128)} %get-tuple-element.330), channel_id=1, source_target_pairs={{0,4},{4,8},{8,12},{12,16},{16,20},{20,24},{24,28},{1,5},{5,9},{9,... | collective-permute-start | bytes 331784 | tf_op jit(solution)/shard_map/ppermute | solution.py:24
  63.1 6.9 %collective-permute-start.5 = (f32[3,3,8,384]{3,2,1,0:T(8,128)}, f32[3,3,8,384]{3,2,1,0:T(8,128)}, u32[]{:S(2)}, u32[]{:S(2)}) collective-permute-start(f32[3,3,8,384]{3,2,1,0:T(8,128)} %get-tuple-element.331), channel_id=1, source_target_pairs={{4,0},{8,4},{12,8},{16,12},{20,16},{24,20},{28,24},{5,1},{9,5},{13... | collective-permute-start | bytes 331784 | tf_op jit(solution)/shard_map/ppermute | solution.py:26
  71.9 13.5 %collective-permute-start.6 = (f32[3,10,3,384]{3,2,1,0:T(4,128)}, f32[3,10,3,384]{3,2,1,0:T(4,128)}, u32[]{:S(2)}, u32[]{:S(2)}) collective-permute-start(f32[3,10,3,384]{3,2,1,0:T(4,128)} %get-tuple-element.274), channel_id=1, source_target_pairs={{0,1},{1,2},{2,3},{4,5},{5,6},{6,7},{8,9},{9,10},{10,11},{12,13},{... | collective-permute-start | bytes 414728 | tf_op jit(solution)/shard_map/ppermute | solution.py:24
  83.5 6.4 %collective-permute-start.7 = (f32[3,10,3,384]{3,2,1,0:T(4,128)}, f32[3,10,3,384]{3,2,1,0:T(4,128)}, u32[]{:S(2)}, u32[]{:S(2)}) collective-permute-start(f32[3,10,3,384]{3,2,1,0:T(4,128)} %get-tuple-element.275), channel_id=1, source_target_pairs={{1,0},{2,1},{3,2},{5,4},{6,5},{7,6},{9,8},{10,9},{11,10},{13,12},{... | collective-permute-start | bytes 414728 | tf_op jit(solution)/shard_map/ppermute | solution.py:26
  127.7 5.6 %collective-permute-start.8 = (f32[3,3,8,384]{3,2,1,0:T(8,128)}, f32[3,3,8,384]{3,2,1,0:T(8,128)}, u32[]{:S(2)}, u32[]{:S(2)}) collective-permute-start(f32[3,3,8,384]{3,2,1,0:T(8,128)} %get-tuple-element.328), channel_id=1, source_target_pairs={{0,4},{4,8},{8,12},{12,16},{16,20},{20,24},{24,28},{1,5},{5,9},{9,... | collective-permute-start | bytes 331784 | tf_op jit(solution)/shard_map/ppermute | solution.py:24
  130.8 6.9 %collective-permute-start.9 = (f32[3,3,8,384]{3,2,1,0:T(8,128)}, f32[3,3,8,384]{3,2,1,0:T(8,128)}, u32[]{:S(2)}, u32[]{:S(2)}) collective-permute-start(f32[3,3,8,384]{3,2,1,0:T(8,128)} %get-tuple-element.329), channel_id=1, source_target_pairs={{4,0},{8,4},{12,8},{16,12},{20,16},{24,20},{28,24},{5,1},{9,5},{13... | collective-permute-start | bytes 331784 | tf_op jit(solution)/shard_map/ppermute | solution.py:26
  139.5 4.8 %collective-permute-start.10 = (f32[3,10,3,384]{3,2,1,0:T(4,128)}, f32[3,10,3,384]{3,2,1,0:T(4,128)}, u32[]{:S(2)}, u32[]{:S(2)}) collective-permute-start(f32[3,10,3,384]{3,2,1,0:T(4,128)} %get-tuple-element.272), channel_id=1, source_target_pairs={{0,1},{1,2},{2,3},{4,5},{5,6},{6,7},{8,9},{9,10},{10,11},{12,13},{... | collective-permute-start | bytes 414728 | tf_op jit(solution)/shard_map/ppermute | solution.py:24
  141.5 3.8 %collective-permute-start.11 = (f32[3,10,3,384]{3,2,1,0:T(4,128)}, f32[3,10,3,384]{3,2,1,0:T(4,128)}, u32[]{:S(2)}, u32[]{:S(2)}) collective-permute-start(f32[3,10,3,384]{3,2,1,0:T(4,128)} %get-tuple-element.273), channel_id=1, source_target_pairs={{1,0},{2,1},{3,2},{5,4},{6,5},{7,6},{9,8},{10,9},{11,10},{13,12},{... | collective-permute-start | bytes 414728 | tf_op jit(solution)/shard_map/ppermute | solution.py:26
  147.2 12.9 %copy-start.41 = (f32[4,8,384]{2,1,0:T(8,128)S(1)}, f32[4,8,384]{2,1,0:T(8,128)}, u32[]{:S(2)}) copy-start(f32[4,8,384]{2,1,0:T(8,128)} %squeeze.224) | copy-start | bytes 147460
  (49 other events, 253.9 us)

commit v11 on v10

--- a/solution.py
+++ b/solution.py
@@ -12,18 +12,24 @@
 FOUNDATION = 1.0
 
 
-def with_halo(x, sides, width, low=True, high=True):
+def with_halo(x, sides, width, low=True, high=True, whole=False):
     for axis, dim in sides:
         count, length = (lax.axis_size(axis), x.shape[dim])
         up = [(i, (i + 1) % count) for i in range(count - 1)]
         down = [(j, i) for i, j in up]
-        last = lax.slice_in_dim(x, length - width, length, axis=dim)
-        first = lax.slice_in_dim(x, 0, width, axis=dim)
+        last = x if whole else lax.slice_in_dim(x, length - width, length, axis=dim)
+        first = x if whole else lax.slice_in_dim(x, 0, width, axis=dim)
         parts = [x]
         if low:
-            parts.insert(0, lax.ppermute(last, axis, up))
+            below = lax.ppermute(last, axis, up)
+            if whole:
+                below = lax.slice_in_dim(below, length - width, length, axis=dim)
+            parts.insert(0, below)
         if high:
-            parts.append(lax.ppermute(first, axis, down))
+            above = lax.ppermute(first, axis, down)
+            if whole:
+                above = lax.slice_in_dim(above, 0, width, axis=dim)
+            parts.append(above)
         x = jnp.concatenate(parts, axis=dim)
     return x
 
@@ -132,7 +138,7 @@
     first_coarse = device_rows(load_means, ("slab", "col")).reshape(-1)
     first_coarse, lower_x = lax.optimization_barrier((first_coarse, lower_x))
     spread = jnp.pad(
-        pad_depth(with_halo(lower_x, (("col", 2),), 3)), ((0, 0), (0, 2), (0, 0), (0, 0))
+        pad_depth(with_halo(lower_x, (("col", 2),), 3, whole=True)), ((0, 0), (0, 2), (0, 0), (0, 0))
     )
     contact_pad = spread[bond_count].astype(jnp.float32)
     near_contact = window(contact_pad, 0, 0, 0, extent)

time: 184 us -> 201 us (1.092)
  starting transfers between devices: 41.6 us -> 61.6 us
  local copies, waits for them, and re-layouts: 23.4 us -> 21.2 us
    ppermute x10, starting transfers between devices: 30.5 us -> 50.5 us  [the longest x5 43.9 us: with_halo(): below = lax.ppermute(last, axis, up)]
    ppermute x2 -> x0, local copies, waits for them, and re-layouts: 3.73 us -> none  [the longest x1 1.86 us: with_halo(): parts.append(lax.ppermute(first, axis, down))]
    slice x7 -> x6, local copies, waits for them, and re-layouts: 6.49 us -> 8.05 us  [the longest x4 3.05 us: with_halo(): last = x if whole else lax.slice_in_dim(x, length - width, length, axis=dim)]
  transfers between devices with their start and end apart: 13 -> 13, of which waited for: 6 -> 7; matrix products, arithmetic and copies ran while one was open for 7% -> 6% of each run, Pallas kernels for 0% -> 0%
where the time goes in v11:
time: 201 us; the launch traced here: 200 us
  other arithmetic  61.6 us (31%)
  starting transfers between devices  61.6 us (31%)
  blocking collectives  26.7 us (13%)
  local copies, waits for them, and re-layouts  21.2 us (11%)
  waiting for transfers between devices  20.8 us (10%)
  between operations  8 us (4%)
    ppermute x5, starting transfers between devices, with_halo(): below = lax.ppermute(last, axis, up)  43.9 us
    all_to_all x2, blocking collectives, device_rows(): return lax.all_to_all(tiled, axes, 0, 0, tiled=True)  26.7 us
    concatenate x5, other arithmetic, with_halo(): x = jnp.concatenate(parts, axis=dim)  15.6 us
    ppermute x5, waiting for transfers between devices, with_halo(): above = lax.ppermute(first, axis, down)  14.7 us
    another operation x3, other arithmetic, operator(): return jnp.stack(summed)  13.5 us
    add x3, other arithmetic, operator(): summed[component] = summed[component] + heading[component] * stretch  13.4 us
    ppermute x5, starting transfers between devices, with_halo(): above = lax.ppermute(first, axis, down)  6.59 us
    all_to_all x1, waiting for transfers between devices, device_rows(): return lax.all_to_all(tiled, axes, 0, 0, tiled=True)  5.75 us
  transfers between devices with their start and end apart: 13, of which 7 were waited for; matrix products, arithmetic and copies ran while one was open for 6% of the time, Pallas kernels for 0%

profile of v11, /device:TPU:0, one launch (start us, length us, event | category | flops | bytes accessed | tf_op | source)
XLA Modules:
  0.0 200.2 jit_solution(6828916764572599109)
XLA Ops:
  4.2 4.9 %collective-permute-start = (bf16[71,8,384]{2,1,0:T(8,128)(2,1)S(1)}, bf16[71,8,384]{2,1,0:T(8,128)(2,1)S(1)}, u32[]{:S(2)}, u32[]{:S(2)}) collective-permute-start(bf16[71,8,384]{2,1,0:T(8,128)(2,1)S(1)} %pad_maximum_fusion.1), channel_id=1, source_target_pairs={{0,4},{4,8},{8,12},{12,16},{16,20},{20,24},{24,28},{1,5},{5,9},{9,... | collective-permute-start | bytes 1308680 | tf_op jit(solution)/shard_map/ppermute | solution.py:47
  11.0 4.9 %all-to-all-start = ((f32[32,1,24]{2,1,0:T(1,128)}), f32[32,1,24]{2,1,0:T(1,128)S(1)}, u32[]{:S(2)}, u32[]{:S(2)}) async-start(f32[32,1,24]{2,1,0:T(1,128)} %broadcast_in_dim.17), calls=%async_computation | async-start | bytes 32768 | tf_op jit(solution)/shard_map/all_to_all | solution.py:72
  17.2 5.8 %all-to-all-done = f32[32,1,24]{2,1,0:T(1,128)S(1)} async-done(((f32[32,1,24]{2,1,0:T(1,128)}), f32[32,1,24]{2,1,0:T(1,128)S(1)}, u32[]{:S(2)}, u32[]{:S(2)}) %all-to-all-start) | async-done | bytes 3104 | tf_op jit(solution)/shard_map/all_to_all | solution.py:72
  24.6 1.7 constant_dynamic-update-slice_fusion
  28.1 4.7 %collective-permute-start.2 = (bf16[62,8,8,384]{3,2,1,0:T(8,128)(2,1)S(1)}, bf16[62,8,8,384]{3,2,1,0:T(8,128)(2,1)}, u32[]{:S(2)}, u32[]{:S(2)}) collective-permute-start(bf16[62,8,8,384]{3,2,1,0:T(8,128)(2,1)S(1)} %pad_maximum_fusion), channel_id=1, source_target_pairs={{0,1},{1,2},{2,3},{4,5},{5,6},{6,7},{8,9},{9,10},{10,11},{12,13},{... | collective-permute-start | bytes 9142280 | tf_op jit(solution)/shard_map/ppermute | solution.py:24
  34.4 2.4 %slice.6132 = bf16[62,8,3,384]{3,2,1,0:T(4,128)(2,1)S(1)} slice(bf16[62,8,8,384]{3,2,1,0:T(8,128)(2,1)} %collective-permute-done.3), slice={[0:62], [0:8], [0:3], [0:384]} | slice | bytes 2285568 | tf_op jit(solution)/shard_map/slice | solution.py:31
  36.7 2.6 %slice.6131 = bf16[62,8,3,384]{3,2,1,0:T(4,128)(2,1)S(1)} slice(bf16[62,8,8,384]{3,2,1,0:T(8,128)(2,1)} %collective-permute-done.2), slice={[0:62], [0:8], [5:8], [0:384]} | slice | bytes 2285568 | tf_op jit(solution)/shard_map/slice | solution.py:26
  39.4 10.2 %fusion.5 = bf16[62,8,14,390]{3,2,1,0:T(8,128)(2,1)S(1)} fusion(bf16[62,8,3,384]{3,2,1,0:T(4,128)(2,1)S(1)} %slice.6132, bf16[62,8,8,384]{3,2,1,0:T(8,128)(2,1)S(1)} %pad_maximum_fusion, bf16[62,8,3,384]{3,2,1,0:T(4,128)(2,1)S(1)} %slice.6131), kind=kLoop, calls=%fused_computation.7 | loop fusion | flops 32497920 | bytes 10749312 | tf_op jit(solution)/shard_map/concatenate | solution.py:33
  59.3 3.1 %collective-permute-start.4 = (f32[3,3,8,384]{3,2,1,0:T(8,128)}, f32[3,3,8,384]{3,2,1,0:T(8,128)}, u32[]{:S(2)}, u32[]{:S(2)}) collective-permute-start(f32[3,3,8,384]{3,2,1,0:T(8,128)} %get-tuple-element.326), channel_id=1, source_target_pairs={{0,4},{4,8},{8,12},{12,16},{16,20},{20,24},{24,28},{1,5},{5,9},{9,... | collective-permute-start | bytes 331784 | tf_op jit(solution)/shard_map/ppermute | solution.py:24
  64.3 5.0 %collective-permute-done.5 = f32[3,3,8,384]{3,2,1,0:T(8,128)} collective-permute-done((f32[3,3,8,384]{3,2,1,0:T(8,128)}, f32[3,3,8,384]{3,2,1,0:T(8,128)}, u32[]{:S(2)}, u32[]{:S(2)}) %collective-permute-start.5) | collective-permute-done | bytes 110624 | tf_op jit(solution)/shard_map/ppermute | solution.py:29
  71.1 31.1 %collective-permute-start.6 = (f32[3,10,3,384]{3,2,1,0:T(4,128)}, f32[3,10,3,384]{3,2,1,0:T(4,128)}, u32[]{:S(2)}, u32[]{:S(2)}) collective-permute-start(f32[3,10,3,384]{3,2,1,0:T(4,128)} %get-tuple-element.270), channel_id=1, source_target_pairs={{0,1},{1,2},{2,3},{4,5},{5,6},{6,7},{8,9},{9,10},{10,11},{12,13},{... | collective-permute-start | bytes 414728 | tf_op jit(solution)/shard_map/ppermute | solution.py:24
  102.2 1.5 collective-permute-start.7
  104.0 3.4 %collective-permute-done.7 = f32[3,10,3,384]{3,2,1,0:T(4,128)} collective-permute-done((f32[3,10,3,384]{3,2,1,0:T(4,128)}, f32[3,10,3,384]{3,2,1,0:T(4,128)}, u32[]{:S(2)}, u32[]{:S(2)}) %collective-permute-start.7) | collective-permute-done | bytes 138272 | tf_op jit(solution)/shard_map/ppermute | solution.py:29
  107.4 1.8 select_maximum_fusion.4
  109.3 12.8 %add_add_fusion.2 = (f32[4,8,384]{2,1,0:T(8,128)S(1)}, f32[4,8,384]{2,1,0:T(8,128)S(1)}, f32[4,8,384]{2,1,0:T(8,128)S(1)}, f32[4,8,384]{2,1,0:T(8,128)S(1)}, f32...) fusion(f32[4,8,384]{2,1,0:T(8,128)S(1)} %squeeze.216, ...), kind=kLoop, calls=%fused_computation.2519 | loop fusion | flops 18382848 | bytes 27181056 | tf_op jit(solution)/shard_map/add | solution.py:193
  125.5 1.4 pad_maximum_fusion.6
  126.9 14.1 %all_to_all.24 = f32[32,1,26]{2,1,0:T(1,128)S(1)} all-to-all(f32[32,1,26]{2,1,0:T(1,128)S(1)} %broadcast_in_dim.22), channel_id=1, replica_groups=mesh['slab'=8,'col'=4] {'slab','col'}, dimensions={0} | all-to-all | bytes 6656 | tf_op jit(solution)/shard_map/all_to_all | solution.py:72
  145.2 3.1 %collective-permute-start.8 = (f32[3,3,8,384]{3,2,1,0:T(8,128)}, f32[3,3,8,384]{3,2,1,0:T(8,128)}, u32[]{:S(2)}, u32[]{:S(2)}) collective-permute-start(f32[3,3,8,384]{3,2,1,0:T(8,128)} %get-tuple-element.324), channel_id=1, source_target_pairs={{0,4},{4,8},{8,12},{12,16},{16,20},{20,24},{24,28},{1,5},{5,9},{9,... | collective-permute-start | bytes 331784 | tf_op jit(solution)/shard_map/ppermute | solution.py:24
  150.8 4.5 %collective-permute-done.9 = f32[3,3,8,384]{3,2,1,0:T(8,128)} collective-permute-done((f32[3,3,8,384]{3,2,1,0:T(8,128)}, f32[3,3,8,384]{3,2,1,0:T(8,128)}, u32[]{:S(2)}, u32[]{:S(2)}) %collective-permute-start.9) | collective-permute-done | bytes 110624 | tf_op jit(solution)/shard_map/ppermute | solution.py:29
  157.1 2.0 collective-permute-start.10
  162.9 1.8 select_maximum_fusion
  164.8 12.8 %add_bitcast_fusion.2 = (f32[1,4,8,384]{3,2,1,0:T(8,128)S(1)}, f32[4,8,384]{2,1,0:T(8,128)S(1)}, f32[4,8,384]{2,1,0:T(8,128)S(1)}, f32[4,8,384]{2,1,0:T(8,128)S(...) fusion(f32[4,8,384]{2,1,0:T(8,128)} %squeeze.222, ...), kind=kLoop, calls=%fused_computation.2516 | loop fusion | flops 18382848 | bytes 27181056 | tf_op jit(solution)/shard_map/stack | solution.py:194
  179.0 2.6 %pad_maximum_fusion.7 = f32[4]{0:T(128)S(1)} fusion(f32[1]{0:T(128)} %bitcast.97, f32[1]{0:T(128)} %bitcast.96, f32[1]{0:T(128)} %bitcast.95, f32[1]{0:T(128)} %bitcast.88), kind=kLoop, calls=%fused_computation.2641 | loop fusion | flops 12 | bytes 32 | tf_op jit(solution)/shard_map/stack | solution.py:235
  181.6 12.6 %all_to_all.25 = f32[32,1,4]{2,1,0:T(1,128)S(1)} all-to-all(f32[32,1,4]{2,1,0:T(1,128)S(1)} %broadcast_in_dim.23), channel_id=1, replica_groups=mesh['slab'=8,'col'=4] {'slab','col'}, dimensions={0} | all-to-all | bytes 1024 | tf_op jit(solution)/shard_map/all_to_all | solution.py:72
  (241 shorter events, 41.8 us)
Async XLA Ops:
  0.6 32.4 %copy-start = (f32[24,768]{1,0:T(8,128)S(1)}, f32[24,768]{1,0:T(8,128)}, u32[]{:S(2)}) copy-start(f32[24,768]{1,0:T(8,128)} %param.68) | copy-start | bytes 221188
  4.2 20.1 %collective-permute-start = (bf16[71,8,384]{2,1,0:T(8,128)(2,1)S(1)}, bf16[71,8,384]{2,1,0:T(8,128)(2,1)S(1)}, u32[]{:S(2)}, u32[]{:S(2)}) collective-permute-start(bf16[71,8,384]{2,1,0:T(8,128)(2,1)S(1)} %pad_maximum_fusion.1), channel_id=1, source_target_pairs={{0,4},{4,8},{8,12},{12,16},{16,20},{20,24},{24,28},{1,5},{5,9},{9,... | collective-permute-start | bytes 1308680 | tf_op jit(solution)/shard_map/ppermute | solution.py:47
  11.0 12.0 %all-to-all-start = ((f32[32,1,24]{2,1,0:T(1,128)}), f32[32,1,24]{2,1,0:T(1,128)S(1)}, u32[]{:S(2)}, u32[]{:S(2)}) async-start(f32[32,1,24]{2,1,0:T(1,128)} %broadcast_in_dim.17), calls=%async_computation | async-start | bytes 32768 | tf_op jit(solution)/shard_map/all_to_all | solution.py:72
  15.9 10.5 %collective-permute-start.1 = (bf16[1,8,384]{2,1,0:T(8,128)(2,1)S(1)}, bf16[1,8,384]{2,1,0:T(8,128)(2,1)S(1)}, u32[]{:S(2)}, u32[]{:S(2)}) collective-permute-start(bf16[1,8,384]{2,1,0:T(8,128)(2,1)S(1)} %get-tuple-element.329), channel_id=1, source_target_pairs={{4,0},{8,4},{12,8},{16,12},{20,16},{24,20},{28,24},{5,1},{9,5},{13... | collective-permute-start | bytes 18440 | tf_op jit(solution)/shard_map/ppermute | solution.py:48
  26.8 7.5 %collective-permute-start.3 = (bf16[62,8,8,384]{3,2,1,0:T(8,128)(2,1)S(1)}, bf16[62,8,8,384]{3,2,1,0:T(8,128)(2,1)}, u32[]{:S(2)}, u32[]{:S(2)}) collective-permute-start(bf16[62,8,8,384]{3,2,1,0:T(8,128)(2,1)S(1)} %pad_maximum_fusion), channel_id=1, source_target_pairs={{1,0},{2,1},{3,2},{5,4},{6,5},{7,6},{9,8},{10,9},{11,10},{13,12},{... | collective-permute-start | bytes 9142280 | tf_op jit(solution)/shard_map/ppermute | solution.py:29
  28.1 8.6 %collective-permute-start.2 = (bf16[62,8,8,384]{3,2,1,0:T(8,128)(2,1)S(1)}, bf16[62,8,8,384]{3,2,1,0:T(8,128)(2,1)}, u32[]{:S(2)}, u32[]{:S(2)}) collective-permute-start(bf16[62,8,8,384]{3,2,1,0:T(8,128)(2,1)S(1)} %pad_maximum_fusion), channel_id=1, source_target_pairs={{0,1},{1,2},{2,3},{4,5},{5,6},{6,7},{8,9},{9,10},{10,11},{12,13},{... | collective-permute-start | bytes 9142280 | tf_op jit(solution)/shard_map/ppermute | solution.py:24
  50.1 6.9 %copy-start.4 = (bf16[10,14,390]{2,1,0:T(8,128)(2,1)}, bf16[10,14,390]{2,1,0:T(8,128)(2,1)S(1)}, u32[]{:S(2)}) copy-start(bf16[10,14,390]{2,1,0:T(8,128)(2,1)S(1)} %get-tuple-element.226) | copy-start | bytes 327604
  50.1 6.9 %copy-start.5 = (bf16[10,14,390]{2,1,0:T(8,128)(2,1)}, bf16[10,14,390]{2,1,0:T(8,128)(2,1)S(1)}, u32[]{:S(2)}) copy-start(bf16[10,14,390]{2,1,0:T(8,128)(2,1)S(1)} %get-tuple-element.227) | copy-start | bytes 327604
  50.1 7.2 %copy-start.2 = (bf16[10,14,390]{2,1,0:T(8,128)(2,1)}, bf16[10,14,390]{2,1,0:T(8,128)(2,1)S(1)}, u32[]{:S(2)}) copy-start(bf16[10,14,390]{2,1,0:T(8,128)(2,1)S(1)} %get-tuple-element.224) | copy-start | bytes 327604
  50.1 7.2 %copy-start.3 = (bf16[10,14,390]{2,1,0:T(8,128)(2,1)}, bf16[10,14,390]{2,1,0:T(8,128)(2,1)S(1)}, u32[]{:S(2)}) copy-start(bf16[10,14,390]{2,1,0:T(8,128)(2,1)S(1)} %get-tuple-element.225) | copy-start | bytes 327604
  51.4 6.1 %copy-start.1 = (f32[3,4,8,384]{3,2,1,0:T(8,128)S(1)}, f32[3,4,8,384]{3,2,1,0:T(8,128)}, u32[]{:S(2)}) copy-start(f32[3,4,8,384]{3,2,1,0:T(8,128)} %param.65) | copy-start | bytes 442372
  51.9 11.8 %copy-start.37 = (bf16[10,14,390]{2,1,0:T(8,128)(2,1)}, bf16[10,14,390]{2,1,0:T(8,128)(2,1)S(1)}, u32[]{:S(2)}) copy-start(bf16[10,14,390]{2,1,0:T(8,128)(2,1)S(1)} %get-tuple-element.176) | copy-start | bytes 327604
  51.9 11.8 %copy-start.38 = (bf16[10,14,390]{2,1,0:T(8,128)(2,1)}, bf16[10,14,390]{2,1,0:T(8,128)(2,1)S(1)}, u32[]{:S(2)}) copy-start(bf16[10,14,390]{2,1,0:T(8,128)(2,1)S(1)} %get-tuple-element.177) | copy-start | bytes 327604
  51.9 11.8 %copy-start.39 = (bf16[10,14,390]{2,1,0:T(8,128)(2,1)}, bf16[10,14,390]{2,1,0:T(8,128)(2,1)S(1)}, u32[]{:S(2)}) copy-start(bf16[10,14,390]{2,1,0:T(8,128)(2,1)S(1)} %get-tuple-element.178) | copy-start | bytes 327604
  51.9 11.8 %copy-start.40 = (bf16[10,14,390]{2,1,0:T(8,128)(2,1)}, bf16[10,14,390]{2,1,0:T(8,128)(2,1)S(1)}, u32[]{:S(2)}) copy-start(bf16[10,14,390]{2,1,0:T(8,128)(2,1)S(1)} %get-tuple-element.182) | copy-start | bytes 327604
  59.3 5.1 %collective-permute-start.4 = (f32[3,3,8,384]{3,2,1,0:T(8,128)}, f32[3,3,8,384]{3,2,1,0:T(8,128)}, u32[]{:S(2)}, u32[]{:S(2)}) collective-permute-start(f32[3,3,8,384]{3,2,1,0:T(8,128)} %get-tuple-element.326), channel_id=1, source_target_pairs={{0,4},{4,8},{8,12},{12,16},{16,20},{20,24},{24,28},{1,5},{5,9},{9,... | collective-permute-start | bytes 331784 | tf_op jit(solution)/shard_map/ppermute | solution.py:24
  62.4 6.9 %collective-permute-start.5 = (f32[3,3,8,384]{3,2,1,0:T(8,128)}, f32[3,3,8,384]{3,2,1,0:T(8,128)}, u32[]{:S(2)}, u32[]{:S(2)}) collective-permute-start(f32[3,3,8,384]{3,2,1,0:T(8,128)} %get-tuple-element.327), channel_id=1, source_target_pairs={{4,0},{8,4},{12,8},{16,12},{20,16},{24,20},{28,24},{5,1},{9,5},{13... | collective-permute-start | bytes 331784 | tf_op jit(solution)/shard_map/ppermute | solution.py:29
  71.1 32.9 %collective-permute-start.6 = (f32[3,10,3,384]{3,2,1,0:T(4,128)}, f32[3,10,3,384]{3,2,1,0:T(4,128)}, u32[]{:S(2)}, u32[]{:S(2)}) collective-permute-start(f32[3,10,3,384]{3,2,1,0:T(4,128)} %get-tuple-element.270), channel_id=1, source_target_pairs={{0,1},{1,2},{2,3},{4,5},{5,6},{6,7},{8,9},{9,10},{10,11},{12,13},{... | collective-permute-start | bytes 414728 | tf_op jit(solution)/shard_map/ppermute | solution.py:24
  102.2 5.2 %collective-permute-start.7 = (f32[3,10,3,384]{3,2,1,0:T(4,128)}, f32[3,10,3,384]{3,2,1,0:T(4,128)}, u32[]{:S(2)}, u32[]{:S(2)}) collective-permute-start(f32[3,10,3,384]{3,2,1,0:T(4,128)} %get-tuple-element.271), channel_id=1, source_target_pairs={{1,0},{2,1},{3,2},{5,4},{6,5},{7,6},{9,8},{10,9},{11,10},{13,12},{... | collective-permute-start | bytes 414728 | tf_op jit(solution)/shard_map/ppermute | solution.py:29
  145.2 5.6 %collective-permute-start.8 = (f32[3,3,8,384]{3,2,1,0:T(8,128)}, f32[3,3,8,384]{3,2,1,0:T(8,128)}, u32[]{:S(2)}, u32[]{:S(2)}) collective-permute-start(f32[3,3,8,384]{3,2,1,0:T(8,128)} %get-tuple-element.324), channel_id=1, source_target_pairs={{0,4},{4,8},{8,12},{12,16},{16,20},{20,24},{24,28},{1,5},{5,9},{9,... | collective-permute-start | bytes 331784 | tf_op jit(solution)/shard_map/ppermute | solution.py:24
  148.3 6.9 %collective-permute-start.9 = (f32[3,3,8,384]{3,2,1,0:T(8,128)}, f32[3,3,8,384]{3,2,1,0:T(8,128)}, u32[]{:S(2)}, u32[]{:S(2)}) collective-permute-start(f32[3,3,8,384]{3,2,1,0:T(8,128)} %get-tuple-element.325), channel_id=1, source_target_pairs={{4,0},{8,4},{12,8},{16,12},{20,16},{24,20},{28,24},{5,1},{9,5},{13... | collective-permute-start | bytes 331784 | tf_op jit(solution)/shard_map/ppermute | solution.py:29
  157.1 4.8 %collective-permute-start.10 = (f32[3,10,3,384]{3,2,1,0:T(4,128)}, f32[3,10,3,384]{3,2,1,0:T(4,128)}, u32[]{:S(2)}, u32[]{:S(2)}) collective-permute-start(f32[3,10,3,384]{3,2,1,0:T(4,128)} %get-tuple-element.268), channel_id=1, source_target_pairs={{0,1},{1,2},{2,3},{4,5},{5,6},{6,7},{8,9},{9,10},{10,11},{12,13},{... | collective-permute-start | bytes 414728 | tf_op jit(solution)/shard_map/ppermute | solution.py:24
  159.0 3.9 %collective-permute-start.11 = (f32[3,10,3,384]{3,2,1,0:T(4,128)}, f32[3,10,3,384]{3,2,1,0:T(4,128)}, u32[]{:S(2)}, u32[]{:S(2)}) collective-permute-start(f32[3,10,3,384]{3,2,1,0:T(4,128)} %get-tuple-element.269), channel_id=1, source_target_pairs={{1,0},{2,1},{3,2},{5,4},{6,5},{7,6},{9,8},{10,9},{11,10},{13,12},{... | collective-permute-start | bytes 414728 | tf_op jit(solution)/shard_map/ppermute | solution.py:29
  164.8 12.9 %copy-start.41 = (f32[4,8,384]{2,1,0:T(8,128)S(1)}, f32[4,8,384]{2,1,0:T(8,128)}, u32[]{:S(2)}) copy-start(f32[4,8,384]{2,1,0:T(8,128)} %squeeze.224) | copy-start | bytes 147460
  (49 other events, 253.7 us)

commit v12 on v10

--- a/solution.py
+++ b/solution.py
@@ -161,8 +161,9 @@
         squares = np.array([entry * entry for entry in heading_of(bond_index)], np.float32)
         diagonal = diagonal + jnp.asarray(squares).reshape(3, 1, 1, 1) * (forward + backward)[None]
 
-    def operator(vector):
-        padded = rimmed(vector)
+    def operator(vector, padded=None):
+        if padded is None:
+            padded = rimmed(vector)
         summed = [FOUNDATION * vector[component] for component in range(3)]
         for bond_index in range(bond_count):
             shift_x, shift_y, shift_z = bond_shift(bond_index)
@@ -204,12 +205,18 @@
     residual = rhs_force
     coarse_now = first_coarse
     direction = precondition(residual, coarse_now)
-    image_vec = operator(direction)
+    first_pad = rimmed(direction)
+    image_vec = operator(direction, first_pad)
+    image_means_local = local_means(image_vec)
+    scaled_pad = rimmed(image_vec / diagonal)
+    reach = jnp.dot(coarse_inverse.T, image_means_local, precision=lax.Precision.HIGHEST)
+    head = 2 + image_means_local.shape[0]
     sums = device_rows(
         jnp.concatenate(
             [
                 jnp.stack([jnp.sum(residual * direction), jnp.sum(direction * image_vec)]),
-                local_means(image_vec),
+                image_means_local,
+                reach,
             ]
         ),
         every,
@@ -217,14 +224,30 @@
     rz_now = jnp.sum(sums[:, 0])
     curvature = jnp.sum(sums[:, 1])
     step_size = rz_now / curvature
-    image_means = sums[:, 2:].reshape(-1)
+    image_means = sums[:, 2:head].reshape(-1)
+    solved_image = jnp.sum(sums[:, head:], axis=0).reshape(
+        lax.axis_size("slab"), lax.axis_size("col"), aggregates, 3
+    )
+    around = lax.dynamic_slice(
+        jnp.pad(solved_image, ((1, 1), (1, 1), (0, 0), (0, 0))),
+        (lax.axis_index("slab"), lax.axis_index("col"), 0, 0),
+        (3, 3, aggregates, 3),
+    )
+    around = jnp.repeat(around, np.array([3, cells_x, 3]), axis=0, total_repeat_length=cells_x + 6)
+    around = jnp.repeat(around, np.array([3, cells_y, 3]), axis=1, total_repeat_length=cells_y + 6)
+    around = pad_depth(jnp.repeat(around, agg_depth, axis=2).transpose(3, 0, 1, 2))
+    next_pad = first_pad - step_size * (scaled_pad + around)
     displacement = step_size * direction
     residual = residual - step_size * image_vec
     for iteration in range(1, ITERS):
         more = iteration + 1 < ITERS
         coarse_now = coarse_now - step_size * image_means
-        precond_r = precondition(residual, coarse_now)
-        image_z = operator(precond_r)
+        if iteration == 1:
+            precond_r = window(next_pad, 0, 0, 0, extent)
+            image_z = operator(precond_r, next_pad)
+        else:
+            precond_r = precondition(residual, coarse_now)
+            image_z = operator(precond_r)
         parts = [
             jnp.stack(
                 [

time: 184 us -> 184 us (level)
  blocking collectives: 26.7 us -> 11.2 us
  starting transfers between devices: 41.6 us -> 50.5 us
  other arithmetic: 61.7 us -> 68.7 us
  waiting for transfers between devices: 21.1 us -> 15.8 us
  local copies, waits for them, and re-layouts: 23.4 us -> 27.7 us
    all_to_all x2 -> x1, blocking collectives: 26.7 us -> 11.2 us  [device_rows(): return lax.all_to_all(tiled, axes, 0, 0, tiled=True)]
    ppermute x5, waiting for transfers between devices: 15 us -> 5.98 us  [with_halo(): parts.append(lax.ppermute(first, axis, down))]
    all_to_all x1 -> x2, starting transfers between devices: 4.87 us -> 13 us  [device_rows(): return lax.all_to_all(tiled, axes, 0, 0, tiled=True)]
    add x12, other arithmetic: 5.26 us -> 11.1 us  [on_device(): forward + backward]
    concatenate x5 -> x4, other arithmetic: 15.6 us -> 10.8 us  [with_halo(): x = jnp.concatenate(parts, axis=dim)]
    all_to_all x1 -> x2, waiting for transfers between devices: 5.75 us -> 8.79 us  [device_rows(): return lax.all_to_all(tiled, axes, 0, 0, tiled=True)]
    sub x1, other arithmetic: 0.01 us -> 2.85 us  [on_device(): next_pad = first_pad - step_size * (scaled_pad + around)]
  transfers between devices with their start and end apart: 13 -> 14, of which waited for: 6 -> 5; matrix products, arithmetic and copies ran while one was open for 7% -> 11% of each run, Pallas kernels for 0% -> 0%
where the time goes in v12:
time: 184 us; the launch traced here: 182 us
  other arithmetic  68.7 us (37%)
  starting transfers between devices  50.5 us (27%)
  local copies, waits for them, and re-layouts  27.7 us (15%)
  waiting for transfers between devices  15.8 us (9%)
  blocking collectives  11.2 us (6%)
  between operations  8.15 us (4%)
    ppermute x5, starting transfers between devices, with_halo(): parts.insert(0, lax.ppermute(last, axis, up))  24.6 us
    another operation x3, other arithmetic, operator(): return jnp.stack(summed)  14.9 us
    add x3, other arithmetic, operator(): summed[component] = summed[component] + heading[component] * stretch  13.7 us
    all_to_all x2, starting transfers between devices, device_rows(): return lax.all_to_all(tiled, axes, 0, 0, tiled=True)  13 us
    all_to_all x1, blocking collectives, device_rows(): return lax.all_to_all(tiled, axes, 0, 0, tiled=True)  11.2 us
    add x12, other arithmetic, on_device(): forward + backward  11.1 us
    concatenate x4, other arithmetic, with_halo(): x = jnp.concatenate(parts, axis=dim)  10.8 us
    all_to_all x2, waiting for transfers between devices, device_rows(): return lax.all_to_all(tiled, axes, 0, 0, tiled=True)  8.79 us
  transfers between devices with their start and end apart: 14, of which 5 were waited for; matrix products, arithmetic and copies ran while one was open for 11% of the time, Pallas kernels for 0%

profile of v12, /device:TPU:0, one launch (start us, length us, event | category | flops | bytes accessed | tf_op | source)
XLA Modules:
  0.0 182.4 jit_solution(2755961632228142175)
XLA Ops:
  4.2 4.9 %collective-permute-start = (bf16[71,8,384]{2,1,0:T(8,128)(2,1)S(1)}, bf16[71,8,384]{2,1,0:T(8,128)(2,1)S(1)}, u32[]{:S(2)}, u32[]{:S(2)}) collective-permute-start(bf16[71,8,384]{2,1,0:T(8,128)(2,1)S(1)} %pad_maximum_fusion.1), channel_id=1, source_target_pairs={{0,4},{4,8},{8,12},{12,16},{16,20},{20,24},{24,28},{1,5},{5,9},{9,... | collective-permute-start | bytes 1308680 | tf_op jit(solution)/shard_map/ppermute | solution.py:41
  11.0 4.9 %all-to-all-start = ((f32[32,1,24]{2,1,0:T(1,128)}), f32[32,1,24]{2,1,0:T(1,128)S(1)}, u32[]{:S(2)}, u32[]{:S(2)}) async-start(f32[32,1,24]{2,1,0:T(1,128)} %broadcast_in_dim.33), calls=%async_computation | async-start | bytes 32768 | tf_op jit(solution)/shard_map/all_to_all | solution.py:66
  17.2 5.8 %all-to-all-done = f32[32,1,24]{2,1,0:T(1,128)S(1)} async-done(((f32[32,1,24]{2,1,0:T(1,128)}), f32[32,1,24]{2,1,0:T(1,128)S(1)}, u32[]{:S(2)}, u32[]{:S(2)}) %all-to-all-start) | async-done | bytes 3104 | tf_op jit(solution)/shard_map/all_to_all | solution.py:66
  24.6 1.7 constant_dynamic-update-slice_fusion
  31.6 4.1 %collective-permute-start.2 = (bf16[62,8,3,384]{3,1,2,0:T(8,128)(2,1)}, bf16[62,8,3,384]{3,1,2,0:T(8,128)(2,1)}, u32[]{:S(2)}, u32[]{:S(2)}) collective-permute-start(bf16[62,8,3,384]{3,1,2,0:T(8,128)(2,1)} %copy.158), channel_id=1, source_target_pairs={{0,1},{1,2},{2,3},{4,5},{5,6},{6,7},{8,9},{9,10},{10,11},{12,13},{... | collective-permute-start | bytes 3428360 | tf_op jit(solution)/shard_map/ppermute | solution.py:24
  36.4 1.9 %copy.161 = bf16[62,8,3,384]{3,2,1,0:T(4,128)(2,1)S(1)} copy(bf16[62,8,3,384]{3,1,2,0:T(8,128)(2,1)} %collective-permute-done.3) | data formatting | bytes 2285568 | tf_op jit(solution)/shard_map/ppermute | solution.py:26
  38.3 1.9 %copy.160 = bf16[62,8,3,384]{3,2,1,0:T(4,128)(2,1)S(1)} copy(bf16[62,8,3,384]{3,1,2,0:T(8,128)(2,1)} %collective-permute-done.2) | data formatting | bytes 2285568 | tf_op jit(solution)/shard_map/ppermute | solution.py:24
  40.1 10.2 %fusion.5 = bf16[62,8,14,390]{3,2,1,0:T(8,128)(2,1)S(1)} fusion(bf16[62,8,3,384]{3,2,1,0:T(4,128)(2,1)S(1)} %copy.161, bf16[62,8,8,384]{3,2,1,0:T(8,128)(2,1)S(1)} %pad_maximum_fusion, bf16[62,8,3,384]{3,2,1,0:T(4,128)(2,1)S(1)} %copy.160), kind=kLoop, calls=%fused_computation.9 | loop fusion | flops 32497920 | bytes 10749312 | tf_op jit(solution)/shard_map/concatenate | solution.py:27
  51.9 1.7 slice_bitcast_fusion.32
  66.5 1.6 broadcast_add_fusion.1
  68.7 2.4 %collective-permute-start.4 = (f32[3,3,8,384]{3,2,1,0:T(8,128)}, f32[3,3,8,384]{3,2,1,0:T(8,128)S(1)}, u32[]{:S(2)}, u32[]{:S(2)}) collective-permute-start(f32[3,3,8,384]{3,2,1,0:T(8,128)} %get-tuple-element.350), channel_id=1, source_target_pairs={{0,4},{4,8},{8,12},{12,16},{16,20},{20,24},{24,28},{1,5},{5,9},{9,... | collective-permute-start | bytes 331784 | tf_op jit(solution)/shard_map/ppermute | solution.py:24
  73.8 4.0 %collective-permute-done.5 = f32[3,3,8,384]{3,2,1,0:T(8,128)S(1)} collective-permute-done((f32[3,3,8,384]{3,2,1,0:T(8,128)S(1)}, f32[3,3,8,384]{3,2,1,0:T(8,128)S(1)}, u32[]{:S(2)}, u32[]{:S(2)}) %collective-permute-start.5) | collective-permute-done | bytes 110624 | tf_op jit(solution)/shard_map/ppermute | solution.py:26
  78.7 10.9 %collective-permute-start.6 = (f32[3,10,3,384]{3,2,1,0:T(4,128)}, f32[3,10,3,384]{3,2,1,0:T(4,128)S(1)}, u32[]{:S(2)}, u32[]{:S(2)}) collective-permute-start(f32[3,10,3,384]{3,2,1,0:T(4,128)} %get-tuple-element.293), channel_id=1, source_target_pairs={{0,1},{1,2},{2,3},{4,5},{5,6},{6,7},{8,9},{9,10},{10,11},{12,13},{... | collective-permute-start | bytes 414728 | tf_op jit(solution)/shard_map/ppermute | solution.py:24
  94.5 2.0 %collective-permute-done.7 = f32[3,10,3,384]{3,2,1,0:T(4,128)S(1)} collective-permute-done((f32[3,10,3,384]{3,2,1,0:T(4,128)}, f32[3,10,3,384]{3,2,1,0:T(4,128)S(1)}, u32[]{:S(2)}, u32[]{:S(2)}) %collective-permute-start.7) | collective-permute-done | bytes 138272 | tf_op jit(solution)/shard_map/ppermute | solution.py:26
  97.3 13.1 %add_add_fusion.2 = (f32[4,8,384]{2,1,0:T(8,128)S(1)}, f32[4,8,384]{2,1,0:T(8,128)S(1)}, f32[4,8,384]{2,1,0:T(8,128)S(1)}, f32[4,8,384]{2,1,0:T(8,128)S(1)}, f32...) fusion(f32[4,8,384]{2,1,0:T(8,128)} %squeeze.216, ...), kind=kLoop, calls=%fused_computation.2530 | loop fusion | flops 18382848 | bytes 27181056 | tf_op jit(solution)/shard_map/add | solution.py:188
  112.7 4.3 %collective-permute-start.8 = (f32[3,3,8,384]{3,2,1,0:T(8,128)S(1)}, f32[3,3,8,384]{3,2,1,0:T(8,128)S(1)}, u32[]{:S(2)}, u32[]{:S(2)}) collective-permute-start(f32[3,3,8,384]{3,2,1,0:T(8,128)S(1)} %get-tuple-element.348), channel_id=1, source_target_pairs={{0,4},{4,8},{8,12},{12,16},{16,20},{20,24},{24,28},{1,5},{5,9},{9,... | collective-permute-start | bytes 331784 | tf_op jit(solution)/shard_map/ppermute | solution.py:24
  120.4 8.2 %all-to-all-start.1 = ((f32[32,1,794]{2,1,0:T(1,128)}), f32[32,1,794]{2,1,0:T(1,128)S(1)}, u32[]{:S(2)}, u32[]{:S(2)}) async-start(f32[32,1,794]{2,1,0:T(1,128)} %broadcast_in_dim.38), calls=%async_computation.1 | async-start | bytes 229376 | tf_op jit(solution)/shard_map/all_to_all | solution.py:66
  129.4 2.8 %collective-permute-start.10 = (f32[3,10,3,384]{3,2,1,0:T(4,128)}, f32[3,10,3,384]{3,2,1,0:T(4,128)}, u32[]{:S(2)}, u32[]{:S(2)}) collective-permute-start(f32[3,10,3,384]{3,2,1,0:T(4,128)} %get-tuple-element.291), channel_id=1, source_target_pairs={{0,1},{1,2},{2,3},{4,5},{5,6},{6,7},{8,9},{9,10},{10,11},{12,13},{... | collective-permute-start | bytes 414728 | tf_op jit(solution)/shard_map/ppermute | solution.py:24
  133.5 3.0 %all-to-all-done.1 = f32[32,1,794]{2,1,0:T(1,128)S(1)} async-done(((f32[32,1,794]{2,1,0:T(1,128)}), f32[32,1,794]{2,1,0:T(1,128)S(1)}, u32[]{:S(2)}, u32[]{:S(2)}) %all-to-all-start.1) | async-done | bytes 101664 | tf_op jit(solution)/shard_map/all_to_all | solution.py:66
  140.2 1.6 slice_reduce_fusion.1
  143.2 2.9 %fusion.8 = f32[3,10,14,390]{3,2,1,0:T(8,128)S(1)} fusion(f32[3,10,3,384]{3,2,1,0:T(4,128)} %collective-permute-done.11, f32[3,10,3,384]{3,2,1,0:T(4,128)} %collective-permute-done.10, f32[3,3,8,384]{3,2,1,0:T(8,128)} %copy-done.48, f32[3,4,8,384]{3,2,1,0:T(8,128)S(1)} %get-tuple-element.347, f32[3,3,8,384]{3,2,1,0:T(8,128)} %copy-done.47, ...), kind=kLoop, calls=%fused_computation.18 | loop fusion | flops 3931200 | bytes 2590564 | tf_op jit(solution)/shard_map/sub | solution.py:239
  146.1 14.1 %add_bitcast_fusion.2 = (f32[1,4,8,384]{3,2,1,0:T(8,128)S(1)}, f32[4,8,384]{2,1,0:T(8,128)S(1)}, f32[4,8,384]{2,1,0:T(8,128)S(1)}, f32[4,8,384]{2,1,0:T(8,128)S(...) fusion(f32[3,10,14,390]{3,2,1,0:T(8,128)S(1)} %fusion.8, ...), kind=kLoop, calls=%fused_computation.2527 | loop fusion | flops 18382848 | bytes 27181056 | tf_op jit(solution)/shard_map/stack | solution.py:189
  161.8 2.6 %pad_maximum_fusion.7 = f32[4]{0:T(128)S(1)} fusion(f32[1]{0:T(128)} %bitcast.100, f32[1]{0:T(128)} %bitcast.99, f32[1]{0:T(128)} %bitcast.98, f32[1]{0:T(128)} %bitcast.88), kind=kLoop, calls=%fused_computation.2652 | loop fusion | flops 12 | bytes 32 | tf_op jit(solution)/shard_map/stack | solution.py:252
  164.4 11.2 %all_to_all.24 = f32[32,1,4]{2,1,0:T(1,128)S(1)} all-to-all(f32[32,1,4]{2,1,0:T(1,128)S(1)} %broadcast_in_dim.44), channel_id=1, replica_groups=mesh['slab'=8,'col'=4] {'slab','col'}, dimensions={0} | all-to-all | bytes 1024 | tf_op jit(solution)/shard_map/all_to_all | solution.py:66
  (267 shorter events, 52.7 us)
Async XLA Ops:
  4.2 20.1 %collective-permute-start = (bf16[71,8,384]{2,1,0:T(8,128)(2,1)S(1)}, bf16[71,8,384]{2,1,0:T(8,128)(2,1)S(1)}, u32[]{:S(2)}, u32[]{:S(2)}) collective-permute-start(bf16[71,8,384]{2,1,0:T(8,128)(2,1)S(1)} %pad_maximum_fusion.1), channel_id=1, source_target_pairs={{0,4},{4,8},{8,12},{12,16},{16,20},{20,24},{24,28},{1,5},{5,9},{9,... | collective-permute-start | bytes 1308680 | tf_op jit(solution)/shard_map/ppermute | solution.py:41
  11.0 12.0 %all-to-all-start = ((f32[32,1,24]{2,1,0:T(1,128)}), f32[32,1,24]{2,1,0:T(1,128)S(1)}, u32[]{:S(2)}, u32[]{:S(2)}) async-start(f32[32,1,24]{2,1,0:T(1,128)} %broadcast_in_dim.33), calls=%async_computation | async-start | bytes 32768 | tf_op jit(solution)/shard_map/all_to_all | solution.py:66
  15.9 10.5 %collective-permute-start.1 = (bf16[1,8,384]{2,1,0:T(8,128)(2,1)S(1)}, bf16[1,8,384]{2,1,0:T(8,128)(2,1)S(1)}, u32[]{:S(2)}, u32[]{:S(2)}) collective-permute-start(bf16[1,8,384]{2,1,0:T(8,128)(2,1)S(1)} %get-tuple-element.353), channel_id=1, source_target_pairs={{4,0},{8,4},{12,8},{16,12},{20,16},{24,20},{28,24},{5,1},{9,5},{13... | collective-permute-start | bytes 18440 | tf_op jit(solution)/shard_map/ppermute | solution.py:42
  29.1 7.3 %collective-permute-start.3 = (bf16[62,8,3,384]{3,1,2,0:T(8,128)(2,1)}, bf16[62,8,3,384]{3,1,2,0:T(8,128)(2,1)}, u32[]{:S(2)}, u32[]{:S(2)}) collective-permute-start(bf16[62,8,3,384]{3,1,2,0:T(8,128)(2,1)} %copy.159), channel_id=1, source_target_pairs={{1,0},{2,1},{3,2},{5,4},{6,5},{7,6},{9,8},{10,9},{11,10},{13,12},{... | collective-permute-start | bytes 3428360 | tf_op jit(solution)/shard_map/ppermute | solution.py:26
  31.6 6.7 %collective-permute-start.2 = (bf16[62,8,3,384]{3,1,2,0:T(8,128)(2,1)}, bf16[62,8,3,384]{3,1,2,0:T(8,128)(2,1)}, u32[]{:S(2)}, u32[]{:S(2)}) collective-permute-start(bf16[62,8,3,384]{3,1,2,0:T(8,128)(2,1)} %copy.158), channel_id=1, source_target_pairs={{0,1},{1,2},{2,3},{4,5},{5,6},{6,7},{8,9},{9,10},{10,11},{12,13},{... | collective-permute-start | bytes 3428360 | tf_op jit(solution)/shard_map/ppermute | solution.py:24
  50.5 46.7 %copy-start.6 = (bf16[10,14,390]{2,1,0:T(8,128)(2,1)}, bf16[10,14,390]{2,1,0:T(8,128)(2,1)S(1)}, u32[]{:S(2)}) copy-start(bf16[10,14,390]{2,1,0:T(8,128)(2,1)S(1)} %get-tuple-element.252) | copy-start | bytes 327604
  50.5 46.7 %copy-start.7 = (bf16[10,14,390]{2,1,0:T(8,128)(2,1)}, bf16[10,14,390]{2,1,0:T(8,128)(2,1)S(1)}, u32[]{:S(2)}) copy-start(bf16[10,14,390]{2,1,0:T(8,128)(2,1)S(1)} %get-tuple-element.253) | copy-start | bytes 327604
  50.5 46.7 %copy-start.8 = (bf16[10,14,390]{2,1,0:T(8,128)(2,1)}, bf16[10,14,390]{2,1,0:T(8,128)(2,1)S(1)}, u32[]{:S(2)}) copy-start(bf16[10,14,390]{2,1,0:T(8,128)(2,1)S(1)} %get-tuple-element.254) | copy-start | bytes 327604
  50.5 46.7 %copy-start.9 = (bf16[10,14,390]{2,1,0:T(8,128)(2,1)}, bf16[10,14,390]{2,1,0:T(8,128)(2,1)S(1)}, u32[]{:S(2)}) copy-start(bf16[10,14,390]{2,1,0:T(8,128)(2,1)S(1)} %get-tuple-element.255) | copy-start | bytes 327604
  50.5 46.7 %copy-start.10 = (bf16[10,14,390]{2,1,0:T(8,128)(2,1)}, bf16[10,14,390]{2,1,0:T(8,128)(2,1)S(1)}, u32[]{:S(2)}) copy-start(bf16[10,14,390]{2,1,0:T(8,128)(2,1)S(1)} %get-tuple-element.256) | copy-start | bytes 327604
  50.6 46.7 %copy-start.11 = (bf16[10,14,390]{2,1,0:T(8,128)(2,1)}, bf16[10,14,390]{2,1,0:T(8,128)(2,1)S(1)}, u32[]{:S(2)}) copy-start(bf16[10,14,390]{2,1,0:T(8,128)(2,1)S(1)} %get-tuple-element.257) | copy-start | bytes 327604
  50.6 46.7 %copy-start.12 = (bf16[10,14,390]{2,1,0:T(8,128)(2,1)}, bf16[10,14,390]{2,1,0:T(8,128)(2,1)S(1)}, u32[]{:S(2)}) copy-start(bf16[10,14,390]{2,1,0:T(8,128)(2,1)S(1)} %get-tuple-element.258) | copy-start | bytes 327604
  50.6 46.7 %copy-start.13 = (bf16[10,14,390]{2,1,0:T(8,128)(2,1)}, bf16[10,14,390]{2,1,0:T(8,128)(2,1)S(1)}, u32[]{:S(2)}) copy-start(bf16[10,14,390]{2,1,0:T(8,128)(2,1)S(1)} %get-tuple-element.259) | copy-start | bytes 327604
  68.7 5.1 %collective-permute-start.4 = (f32[3,3,8,384]{3,2,1,0:T(8,128)}, f32[3,3,8,384]{3,2,1,0:T(8,128)S(1)}, u32[]{:S(2)}, u32[]{:S(2)}) collective-permute-start(f32[3,3,8,384]{3,2,1,0:T(8,128)} %get-tuple-element.350), channel_id=1, source_target_pairs={{0,4},{4,8},{8,12},{12,16},{16,20},{20,24},{24,28},{1,5},{5,9},{9,... | collective-permute-start | bytes 331784 | tf_op jit(solution)/shard_map/ppermute | solution.py:24
  71.2 6.6 %collective-permute-start.5 = (f32[3,3,8,384]{3,2,1,0:T(8,128)S(1)}, f32[3,3,8,384]{3,2,1,0:T(8,128)S(1)}, u32[]{:S(2)}, u32[]{:S(2)}) collective-permute-start(f32[3,3,8,384]{3,2,1,0:T(8,128)S(1)} %get-tuple-element.351), channel_id=1, source_target_pairs={{4,0},{8,4},{12,8},{16,12},{20,16},{24,20},{28,24},{5,1},{9,5},{13... | collective-permute-start | bytes 331784 | tf_op jit(solution)/shard_map/ppermute | solution.py:26
  73.8 64.8 %copy-start.2 = (f32[3,3,8,384]{3,2,1,0:T(8,128)}, f32[3,3,8,384]{3,2,1,0:T(8,128)S(1)}, u32[]{:S(2)}) copy-start(f32[3,3,8,384]{3,2,1,0:T(8,128)S(1)} %collective-permute-done.4) | copy-start | bytes 331780
  77.8 60.7 %copy-start.3 = (f32[3,3,8,384]{3,2,1,0:T(8,128)}, f32[3,3,8,384]{3,2,1,0:T(8,128)S(1)}, u32[]{:S(2)}) copy-start(f32[3,3,8,384]{3,2,1,0:T(8,128)S(1)} %collective-permute-done.5) | copy-start | bytes 331780
  78.7 15.9 %collective-permute-start.6 = (f32[3,10,3,384]{3,2,1,0:T(4,128)}, f32[3,10,3,384]{3,2,1,0:T(4,128)S(1)}, u32[]{:S(2)}, u32[]{:S(2)}) collective-permute-start(f32[3,10,3,384]{3,2,1,0:T(4,128)} %get-tuple-element.293), channel_id=1, source_target_pairs={{0,1},{1,2},{2,3},{4,5},{5,6},{6,7},{8,9},{9,10},{10,11},{12,13},{... | collective-permute-start | bytes 414728 | tf_op jit(solution)/shard_map/ppermute | solution.py:24
  89.6 6.9 %collective-permute-start.7 = (f32[3,10,3,384]{3,2,1,0:T(4,128)}, f32[3,10,3,384]{3,2,1,0:T(4,128)S(1)}, u32[]{:S(2)}, u32[]{:S(2)}) collective-permute-start(f32[3,10,3,384]{3,2,1,0:T(4,128)} %get-tuple-element.294), channel_id=1, source_target_pairs={{1,0},{2,1},{3,2},{5,4},{6,5},{7,6},{9,8},{10,9},{11,10},{13,12},{... | collective-permute-start | bytes 414728 | tf_op jit(solution)/shard_map/ppermute | solution.py:26
  112.7 15.9 %collective-permute-start.8 = (f32[3,3,8,384]{3,2,1,0:T(8,128)S(1)}, f32[3,3,8,384]{3,2,1,0:T(8,128)S(1)}, u32[]{:S(2)}, u32[]{:S(2)}) collective-permute-start(f32[3,3,8,384]{3,2,1,0:T(8,128)S(1)} %get-tuple-element.348), channel_id=1, source_target_pairs={{0,4},{4,8},{8,12},{12,16},{16,20},{20,24},{24,28},{1,5},{5,9},{9,... | collective-permute-start | bytes 331784 | tf_op jit(solution)/shard_map/ppermute | solution.py:24
  117.0 11.6 %collective-permute-start.9 = (f32[3,3,8,384]{3,2,1,0:T(8,128)S(1)}, f32[3,3,8,384]{3,2,1,0:T(8,128)S(1)}, u32[]{:S(2)}, u32[]{:S(2)}) collective-permute-start(f32[3,3,8,384]{3,2,1,0:T(8,128)S(1)} %get-tuple-element.349), channel_id=1, source_target_pairs={{4,0},{8,4},{12,8},{16,12},{20,16},{24,20},{28,24},{5,1},{9,5},{13... | collective-permute-start | bytes 331784 | tf_op jit(solution)/shard_map/ppermute | solution.py:26
  120.4 16.2 %all-to-all-start.1 = ((f32[32,1,794]{2,1,0:T(1,128)}), f32[32,1,794]{2,1,0:T(1,128)S(1)}, u32[]{:S(2)}, u32[]{:S(2)}) async-start(f32[32,1,794]{2,1,0:T(1,128)} %broadcast_in_dim.38), calls=%async_computation.1 | async-start | bytes 229376 | tf_op jit(solution)/shard_map/all_to_all | solution.py:66
  129.4 13.7 %collective-permute-start.10 = (f32[3,10,3,384]{3,2,1,0:T(4,128)}, f32[3,10,3,384]{3,2,1,0:T(4,128)}, u32[]{:S(2)}, u32[]{:S(2)}) collective-permute-start(f32[3,10,3,384]{3,2,1,0:T(4,128)} %get-tuple-element.291), channel_id=1, source_target_pairs={{0,1},{1,2},{2,3},{4,5},{5,6},{6,7},{8,9},{9,10},{10,11},{12,13},{... | collective-permute-start | bytes 414728 | tf_op jit(solution)/shard_map/ppermute | solution.py:24
  132.3 10.9 %collective-permute-start.11 = (f32[3,10,3,384]{3,2,1,0:T(4,128)}, f32[3,10,3,384]{3,2,1,0:T(4,128)}, u32[]{:S(2)}, u32[]{:S(2)}) collective-permute-start(f32[3,10,3,384]{3,2,1,0:T(4,128)} %get-tuple-element.292), channel_id=1, source_target_pairs={{1,0},{2,1},{3,2},{5,4},{6,5},{7,6},{9,8},{10,9},{11,10},{13,12},{... | collective-permute-start | bytes 414728 | tf_op jit(solution)/shard_map/ppermute | solution.py:26
  (61 other events, 819.3 us)

commit v13 on v12

--- a/solution.py
+++ b/solution.py
@@ -209,7 +209,9 @@
     image_vec = operator(direction, first_pad)
     image_means_local = local_means(image_vec)
     scaled_pad = rimmed(image_vec / diagonal)
-    reach = jnp.dot(coarse_inverse.T, image_means_local, precision=lax.Precision.HIGHEST)
+    reach = lax.dot_general(
+        image_means_local, coarse_inverse, (((0,), (0,)), ((), ())), precision=lax.Precision.HIGHEST
+    )
     head = 2 + image_means_local.shape[0]
     sums = device_rows(
         jnp.concatenate(

time: 184 us -> 184 us (level)
  no operation moved by 1% of the time
where the time goes in v13:
time: 184 us; the launch traced here: 182 us
  other arithmetic  68.7 us (37%)
  starting transfers between devices  50.5 us (27%)
  local copies, waits for them, and re-layouts  27.7 us (15%)
  waiting for transfers between devices  15.8 us (9%)
  blocking collectives  11.2 us (6%)
  between operations  8.15 us (4%)
    ppermute x5, starting transfers between devices, with_halo(): parts.insert(0, lax.ppermute(last, axis, up))  24.6 us
    another operation x3, other arithmetic, operator(): return jnp.stack(summed)  14.9 us
    add x3, other arithmetic, operator(): summed[component] = summed[component] + heading[component] * stretch  13.7 us
    all_to_all x2, starting transfers between devices, device_rows(): return lax.all_to_all(tiled, axes, 0, 0, tiled=True)  13 us
    all_to_all x1, blocking collectives, device_rows(): return lax.all_to_all(tiled, axes, 0, 0, tiled=True)  11.2 us
    add x12, other arithmetic, on_device(): forward + backward  11.1 us
    concatenate x4, other arithmetic, with_halo(): x = jnp.concatenate(parts, axis=dim)  10.8 us
    all_to_all x2, waiting for transfers between devices, device_rows(): return lax.all_to_all(tiled, axes, 0, 0, tiled=True)  8.79 us
  transfers between devices with their start and end apart: 14, of which 5 were waited for; matrix products, arithmetic and copies ran while one was open for 11% of the time, Pallas kernels for 0%

profile of v13, /device:TPU:0, one launch (start us, length us, event | category | flops | bytes accessed | tf_op | source)
XLA Modules:
  0.0 182.4 jit_solution(2755961632228142175)
XLA Ops:
  4.2 4.9 %collective-permute-start = (bf16[71,8,384]{2,1,0:T(8,128)(2,1)S(1)}, bf16[71,8,384]{2,1,0:T(8,128)(2,1)S(1)}, u32[]{:S(2)}, u32[]{:S(2)}) collective-permute-start(bf16[71,8,384]{2,1,0:T(8,128)(2,1)S(1)} %pad_maximum_fusion.1), channel_id=1, source_target_pairs={{0,4},{4,8},{8,12},{12,16},{16,20},{20,24},{24,28},{1,5},{5,9},{9,... | collective-permute-start | bytes 1308680 | tf_op jit(solution)/shard_map/ppermute | solution.py:41
  11.0 4.9 %all-to-all-start = ((f32[32,1,24]{2,1,0:T(1,128)}), f32[32,1,24]{2,1,0:T(1,128)S(1)}, u32[]{:S(2)}, u32[]{:S(2)}) async-start(f32[32,1,24]{2,1,0:T(1,128)} %broadcast_in_dim.33), calls=%async_computation | async-start | bytes 32768 | tf_op jit(solution)/shard_map/all_to_all | solution.py:66
  17.2 5.8 %all-to-all-done = f32[32,1,24]{2,1,0:T(1,128)S(1)} async-done(((f32[32,1,24]{2,1,0:T(1,128)}), f32[32,1,24]{2,1,0:T(1,128)S(1)}, u32[]{:S(2)}, u32[]{:S(2)}) %all-to-all-start) | async-done | bytes 3104 | tf_op jit(solution)/shard_map/all_to_all | solution.py:66
  24.6 1.7 constant_dynamic-update-slice_fusion
  31.6 4.1 %collective-permute-start.2 = (bf16[62,8,3,384]{3,1,2,0:T(8,128)(2,1)}, bf16[62,8,3,384]{3,1,2,0:T(8,128)(2,1)}, u32[]{:S(2)}, u32[]{:S(2)}) collective-permute-start(bf16[62,8,3,384]{3,1,2,0:T(8,128)(2,1)} %copy.158), channel_id=1, source_target_pairs={{0,1},{1,2},{2,3},{4,5},{5,6},{6,7},{8,9},{9,10},{10,11},{12,13},{... | collective-permute-start | bytes 3428360 | tf_op jit(solution)/shard_map/ppermute | solution.py:24
  36.4 1.9 %copy.161 = bf16[62,8,3,384]{3,2,1,0:T(4,128)(2,1)S(1)} copy(bf16[62,8,3,384]{3,1,2,0:T(8,128)(2,1)} %collective-permute-done.3) | data formatting | bytes 2285568 | tf_op jit(solution)/shard_map/ppermute | solution.py:26
  38.3 1.9 %copy.160 = bf16[62,8,3,384]{3,2,1,0:T(4,128)(2,1)S(1)} copy(bf16[62,8,3,384]{3,1,2,0:T(8,128)(2,1)} %collective-permute-done.2) | data formatting | bytes 2285568 | tf_op jit(solution)/shard_map/ppermute | solution.py:24
  40.1 10.2 %fusion.5 = bf16[62,8,14,390]{3,2,1,0:T(8,128)(2,1)S(1)} fusion(bf16[62,8,3,384]{3,2,1,0:T(4,128)(2,1)S(1)} %copy.161, bf16[62,8,8,384]{3,2,1,0:T(8,128)(2,1)S(1)} %pad_maximum_fusion, bf16[62,8,3,384]{3,2,1,0:T(4,128)(2,1)S(1)} %copy.160), kind=kLoop, calls=%fused_computation.9 | loop fusion | flops 32497920 | bytes 10749312 | tf_op jit(solution)/shard_map/concatenate | solution.py:27
  51.9 1.7 slice_bitcast_fusion.32
  66.5 1.6 broadcast_add_fusion.1
  68.7 2.4 %collective-permute-start.4 = (f32[3,3,8,384]{3,2,1,0:T(8,128)}, f32[3,3,8,384]{3,2,1,0:T(8,128)S(1)}, u32[]{:S(2)}, u32[]{:S(2)}) collective-permute-start(f32[3,3,8,384]{3,2,1,0:T(8,128)} %get-tuple-element.350), channel_id=1, source_target_pairs={{0,4},{4,8},{8,12},{12,16},{16,20},{20,24},{24,28},{1,5},{5,9},{9,... | collective-permute-start | bytes 331784 | tf_op jit(solution)/shard_map/ppermute | solution.py:24
  73.8 4.0 %collective-permute-done.5 = f32[3,3,8,384]{3,2,1,0:T(8,128)S(1)} collective-permute-done((f32[3,3,8,384]{3,2,1,0:T(8,128)S(1)}, f32[3,3,8,384]{3,2,1,0:T(8,128)S(1)}, u32[]{:S(2)}, u32[]{:S(2)}) %collective-permute-start.5) | collective-permute-done | bytes 110624 | tf_op jit(solution)/shard_map/ppermute | solution.py:26
  78.7 10.9 %collective-permute-start.6 = (f32[3,10,3,384]{3,2,1,0:T(4,128)}, f32[3,10,3,384]{3,2,1,0:T(4,128)S(1)}, u32[]{:S(2)}, u32[]{:S(2)}) collective-permute-start(f32[3,10,3,384]{3,2,1,0:T(4,128)} %get-tuple-element.293), channel_id=1, source_target_pairs={{0,1},{1,2},{2,3},{4,5},{5,6},{6,7},{8,9},{9,10},{10,11},{12,13},{... | collective-permute-start | bytes 414728 | tf_op jit(solution)/shard_map/ppermute | solution.py:24
  94.5 2.0 %collective-permute-done.7 = f32[3,10,3,384]{3,2,1,0:T(4,128)S(1)} collective-permute-done((f32[3,10,3,384]{3,2,1,0:T(4,128)}, f32[3,10,3,384]{3,2,1,0:T(4,128)S(1)}, u32[]{:S(2)}, u32[]{:S(2)}) %collective-permute-start.7) | collective-permute-done | bytes 138272 | tf_op jit(solution)/shard_map/ppermute | solution.py:26
  97.3 13.1 %add_add_fusion.2 = (f32[4,8,384]{2,1,0:T(8,128)S(1)}, f32[4,8,384]{2,1,0:T(8,128)S(1)}, f32[4,8,384]{2,1,0:T(8,128)S(1)}, f32[4,8,384]{2,1,0:T(8,128)S(1)}, f32...) fusion(f32[4,8,384]{2,1,0:T(8,128)} %squeeze.216, ...), kind=kLoop, calls=%fused_computation.2529 | loop fusion | flops 18382848 | bytes 27181056 | tf_op jit(solution)/shard_map/add | solution.py:188
  112.7 4.3 %collective-permute-start.8 = (f32[3,3,8,384]{3,2,1,0:T(8,128)S(1)}, f32[3,3,8,384]{3,2,1,0:T(8,128)S(1)}, u32[]{:S(2)}, u32[]{:S(2)}) collective-permute-start(f32[3,3,8,384]{3,2,1,0:T(8,128)S(1)} %get-tuple-element.348), channel_id=1, source_target_pairs={{0,4},{4,8},{8,12},{12,16},{16,20},{20,24},{24,28},{1,5},{5,9},{9,... | collective-permute-start | bytes 331784 | tf_op jit(solution)/shard_map/ppermute | solution.py:24
  120.4 8.2 %all-to-all-start.1 = ((f32[32,1,794]{2,1,0:T(1,128)}), f32[32,1,794]{2,1,0:T(1,128)S(1)}, u32[]{:S(2)}, u32[]{:S(2)}) async-start(f32[32,1,794]{2,1,0:T(1,128)} %broadcast_in_dim.38), calls=%async_computation.1 | async-start | bytes 229376 | tf_op jit(solution)/shard_map/all_to_all | solution.py:66
  129.4 2.8 %collective-permute-start.10 = (f32[3,10,3,384]{3,2,1,0:T(4,128)}, f32[3,10,3,384]{3,2,1,0:T(4,128)}, u32[]{:S(2)}, u32[]{:S(2)}) collective-permute-start(f32[3,10,3,384]{3,2,1,0:T(4,128)} %get-tuple-element.291), channel_id=1, source_target_pairs={{0,1},{1,2},{2,3},{4,5},{5,6},{6,7},{8,9},{9,10},{10,11},{12,13},{... | collective-permute-start | bytes 414728 | tf_op jit(solution)/shard_map/ppermute | solution.py:24
  133.5 3.0 %all-to-all-done.1 = f32[32,1,794]{2,1,0:T(1,128)S(1)} async-done(((f32[32,1,794]{2,1,0:T(1,128)}), f32[32,1,794]{2,1,0:T(1,128)S(1)}, u32[]{:S(2)}, u32[]{:S(2)}) %all-to-all-start.1) | async-done | bytes 101664 | tf_op jit(solution)/shard_map/all_to_all | solution.py:66
  140.2 1.6 slice_reduce_fusion.1
  143.2 2.9 %fusion.8 = f32[3,10,14,390]{3,2,1,0:T(8,128)S(1)} fusion(f32[3,10,3,384]{3,2,1,0:T(4,128)} %collective-permute-done.11, f32[3,10,3,384]{3,2,1,0:T(4,128)} %collective-permute-done.10, f32[3,3,8,384]{3,2,1,0:T(8,128)} %copy-done.48, f32[3,4,8,384]{3,2,1,0:T(8,128)S(1)} %get-tuple-element.347, f32[3,3,8,384]{3,2,1,0:T(8,128)} %copy-done.47, ...), kind=kLoop, calls=%fused_computation.18 | loop fusion | flops 3931200 | bytes 2590564 | tf_op jit(solution)/shard_map/sub | solution.py:241
  146.1 14.1 %add_bitcast_fusion.2 = (f32[1,4,8,384]{3,2,1,0:T(8,128)S(1)}, f32[4,8,384]{2,1,0:T(8,128)S(1)}, f32[4,8,384]{2,1,0:T(8,128)S(1)}, f32[4,8,384]{2,1,0:T(8,128)S(...) fusion(f32[3,10,14,390]{3,2,1,0:T(8,128)S(1)} %fusion.8, ...), kind=kLoop, calls=%fused_computation.2526 | loop fusion | flops 18382848 | bytes 27181056 | tf_op jit(solution)/shard_map/stack | solution.py:189
  161.8 2.6 %pad_maximum_fusion.7 = f32[4]{0:T(128)S(1)} fusion(f32[1]{0:T(128)} %bitcast.99, f32[1]{0:T(128)} %bitcast.98, f32[1]{0:T(128)} %bitcast.97, f32[1]{0:T(128)} %bitcast.87), kind=kLoop, calls=%fused_computation.2651 | loop fusion | flops 12 | bytes 32 | tf_op jit(solution)/shard_map/stack | solution.py:254
  164.4 11.2 %all_to_all.24 = f32[32,1,4]{2,1,0:T(1,128)S(1)} all-to-all(f32[32,1,4]{2,1,0:T(1,128)S(1)} %broadcast_in_dim.44), channel_id=1, replica_groups=mesh['slab'=8,'col'=4] {'slab','col'}, dimensions={0} | all-to-all | bytes 1024 | tf_op jit(solution)/shard_map/all_to_all | solution.py:66
  (267 shorter events, 52.7 us)
Async XLA Ops:
  4.2 20.1 %collective-permute-start = (bf16[71,8,384]{2,1,0:T(8,128)(2,1)S(1)}, bf16[71,8,384]{2,1,0:T(8,128)(2,1)S(1)}, u32[]{:S(2)}, u32[]{:S(2)}) collective-permute-start(bf16[71,8,384]{2,1,0:T(8,128)(2,1)S(1)} %pad_maximum_fusion.1), channel_id=1, source_target_pairs={{0,4},{4,8},{8,12},{12,16},{16,20},{20,24},{24,28},{1,5},{5,9},{9,... | collective-permute-start | bytes 1308680 | tf_op jit(solution)/shard_map/ppermute | solution.py:41
  11.0 12.0 %all-to-all-start = ((f32[32,1,24]{2,1,0:T(1,128)}), f32[32,1,24]{2,1,0:T(1,128)S(1)}, u32[]{:S(2)}, u32[]{:S(2)}) async-start(f32[32,1,24]{2,1,0:T(1,128)} %broadcast_in_dim.33), calls=%async_computation | async-start | bytes 32768 | tf_op jit(solution)/shard_map/all_to_all | solution.py:66
  15.9 10.5 %collective-permute-start.1 = (bf16[1,8,384]{2,1,0:T(8,128)(2,1)S(1)}, bf16[1,8,384]{2,1,0:T(8,128)(2,1)S(1)}, u32[]{:S(2)}, u32[]{:S(2)}) collective-permute-start(bf16[1,8,384]{2,1,0:T(8,128)(2,1)S(1)} %get-tuple-element.353), channel_id=1, source_target_pairs={{4,0},{8,4},{12,8},{16,12},{20,16},{24,20},{28,24},{5,1},{9,5},{13... | collective-permute-start | bytes 18440 | tf_op jit(solution)/shard_map/ppermute | solution.py:42
  29.1 7.3 %collective-permute-start.3 = (bf16[62,8,3,384]{3,1,2,0:T(8,128)(2,1)}, bf16[62,8,3,384]{3,1,2,0:T(8,128)(2,1)}, u32[]{:S(2)}, u32[]{:S(2)}) collective-permute-start(bf16[62,8,3,384]{3,1,2,0:T(8,128)(2,1)} %copy.159), channel_id=1, source_target_pairs={{1,0},{2,1},{3,2},{5,4},{6,5},{7,6},{9,8},{10,9},{11,10},{13,12},{... | collective-permute-start | bytes 3428360 | tf_op jit(solution)/shard_map/ppermute | solution.py:26
  31.6 6.7 %collective-permute-start.2 = (bf16[62,8,3,384]{3,1,2,0:T(8,128)(2,1)}, bf16[62,8,3,384]{3,1,2,0:T(8,128)(2,1)}, u32[]{:S(2)}, u32[]{:S(2)}) collective-permute-start(bf16[62,8,3,384]{3,1,2,0:T(8,128)(2,1)} %copy.158), channel_id=1, source_target_pairs={{0,1},{1,2},{2,3},{4,5},{5,6},{6,7},{8,9},{9,10},{10,11},{12,13},{... | collective-permute-start | bytes 3428360 | tf_op jit(solution)/shard_map/ppermute | solution.py:24
  50.5 46.7 %copy-start.6 = (bf16[10,14,390]{2,1,0:T(8,128)(2,1)}, bf16[10,14,390]{2,1,0:T(8,128)(2,1)S(1)}, u32[]{:S(2)}) copy-start(bf16[10,14,390]{2,1,0:T(8,128)(2,1)S(1)} %get-tuple-element.252) | copy-start | bytes 327604
  50.5 46.7 %copy-start.7 = (bf16[10,14,390]{2,1,0:T(8,128)(2,1)}, bf16[10,14,390]{2,1,0:T(8,128)(2,1)S(1)}, u32[]{:S(2)}) copy-start(bf16[10,14,390]{2,1,0:T(8,128)(2,1)S(1)} %get-tuple-element.253) | copy-start | bytes 327604
  50.5 46.7 %copy-start.8 = (bf16[10,14,390]{2,1,0:T(8,128)(2,1)}, bf16[10,14,390]{2,1,0:T(8,128)(2,1)S(1)}, u32[]{:S(2)}) copy-start(bf16[10,14,390]{2,1,0:T(8,128)(2,1)S(1)} %get-tuple-element.254) | copy-start | bytes 327604
  50.5 46.7 %copy-start.9 = (bf16[10,14,390]{2,1,0:T(8,128)(2,1)}, bf16[10,14,390]{2,1,0:T(8,128)(2,1)S(1)}, u32[]{:S(2)}) copy-start(bf16[10,14,390]{2,1,0:T(8,128)(2,1)S(1)} %get-tuple-element.255) | copy-start | bytes 327604
  50.5 46.7 %copy-start.10 = (bf16[10,14,390]{2,1,0:T(8,128)(2,1)}, bf16[10,14,390]{2,1,0:T(8,128)(2,1)S(1)}, u32[]{:S(2)}) copy-start(bf16[10,14,390]{2,1,0:T(8,128)(2,1)S(1)} %get-tuple-element.256) | copy-start | bytes 327604
  50.6 46.7 %copy-start.11 = (bf16[10,14,390]{2,1,0:T(8,128)(2,1)}, bf16[10,14,390]{2,1,0:T(8,128)(2,1)S(1)}, u32[]{:S(2)}) copy-start(bf16[10,14,390]{2,1,0:T(8,128)(2,1)S(1)} %get-tuple-element.257) | copy-start | bytes 327604
  50.6 46.7 %copy-start.12 = (bf16[10,14,390]{2,1,0:T(8,128)(2,1)}, bf16[10,14,390]{2,1,0:T(8,128)(2,1)S(1)}, u32[]{:S(2)}) copy-start(bf16[10,14,390]{2,1,0:T(8,128)(2,1)S(1)} %get-tuple-element.258) | copy-start | bytes 327604
  50.6 46.7 %copy-start.13 = (bf16[10,14,390]{2,1,0:T(8,128)(2,1)}, bf16[10,14,390]{2,1,0:T(8,128)(2,1)S(1)}, u32[]{:S(2)}) copy-start(bf16[10,14,390]{2,1,0:T(8,128)(2,1)S(1)} %get-tuple-element.259) | copy-start | bytes 327604
  68.7 5.1 %collective-permute-start.4 = (f32[3,3,8,384]{3,2,1,0:T(8,128)}, f32[3,3,8,384]{3,2,1,0:T(8,128)S(1)}, u32[]{:S(2)}, u32[]{:S(2)}) collective-permute-start(f32[3,3,8,384]{3,2,1,0:T(8,128)} %get-tuple-element.350), channel_id=1, source_target_pairs={{0,4},{4,8},{8,12},{12,16},{16,20},{20,24},{24,28},{1,5},{5,9},{9,... | collective-permute-start | bytes 331784 | tf_op jit(solution)/shard_map/ppermute | solution.py:24
  71.2 6.6 %collective-permute-start.5 = (f32[3,3,8,384]{3,2,1,0:T(8,128)S(1)}, f32[3,3,8,384]{3,2,1,0:T(8,128)S(1)}, u32[]{:S(2)}, u32[]{:S(2)}) collective-permute-start(f32[3,3,8,384]{3,2,1,0:T(8,128)S(1)} %get-tuple-element.351), channel_id=1, source_target_pairs={{4,0},{8,4},{12,8},{16,12},{20,16},{24,20},{28,24},{5,1},{9,5},{13... | collective-permute-start | bytes 331784 | tf_op jit(solution)/shard_map/ppermute | solution.py:26
  73.8 64.8 %copy-start.2 = (f32[3,3,8,384]{3,2,1,0:T(8,128)}, f32[3,3,8,384]{3,2,1,0:T(8,128)S(1)}, u32[]{:S(2)}) copy-start(f32[3,3,8,384]{3,2,1,0:T(8,128)S(1)} %collective-permute-done.4) | copy-start | bytes 331780
  77.8 60.7 %copy-start.3 = (f32[3,3,8,384]{3,2,1,0:T(8,128)}, f32[3,3,8,384]{3,2,1,0:T(8,128)S(1)}, u32[]{:S(2)}) copy-start(f32[3,3,8,384]{3,2,1,0:T(8,128)S(1)} %collective-permute-done.5) | copy-start | bytes 331780
  78.7 15.9 %collective-permute-start.6 = (f32[3,10,3,384]{3,2,1,0:T(4,128)}, f32[3,10,3,384]{3,2,1,0:T(4,128)S(1)}, u32[]{:S(2)}, u32[]{:S(2)}) collective-permute-start(f32[3,10,3,384]{3,2,1,0:T(4,128)} %get-tuple-element.293), channel_id=1, source_target_pairs={{0,1},{1,2},{2,3},{4,5},{5,6},{6,7},{8,9},{9,10},{10,11},{12,13},{... | collective-permute-start | bytes 414728 | tf_op jit(solution)/shard_map/ppermute | solution.py:24
  89.6 6.9 %collective-permute-start.7 = (f32[3,10,3,384]{3,2,1,0:T(4,128)}, f32[3,10,3,384]{3,2,1,0:T(4,128)S(1)}, u32[]{:S(2)}, u32[]{:S(2)}) collective-permute-start(f32[3,10,3,384]{3,2,1,0:T(4,128)} %get-tuple-element.294), channel_id=1, source_target_pairs={{1,0},{2,1},{3,2},{5,4},{6,5},{7,6},{9,8},{10,9},{11,10},{13,12},{... | collective-permute-start | bytes 414728 | tf_op jit(solution)/shard_map/ppermute | solution.py:26
  112.7 15.9 %collective-permute-start.8 = (f32[3,3,8,384]{3,2,1,0:T(8,128)S(1)}, f32[3,3,8,384]{3,2,1,0:T(8,128)S(1)}, u32[]{:S(2)}, u32[]{:S(2)}) collective-permute-start(f32[3,3,8,384]{3,2,1,0:T(8,128)S(1)} %get-tuple-element.348), channel_id=1, source_target_pairs={{0,4},{4,8},{8,12},{12,16},{16,20},{20,24},{24,28},{1,5},{5,9},{9,... | collective-permute-start | bytes 331784 | tf_op jit(solution)/shard_map/ppermute | solution.py:24
  117.0 11.6 %collective-permute-start.9 = (f32[3,3,8,384]{3,2,1,0:T(8,128)S(1)}, f32[3,3,8,384]{3,2,1,0:T(8,128)S(1)}, u32[]{:S(2)}, u32[]{:S(2)}) collective-permute-start(f32[3,3,8,384]{3,2,1,0:T(8,128)S(1)} %get-tuple-element.349), channel_id=1, source_target_pairs={{4,0},{8,4},{12,8},{16,12},{20,16},{24,20},{28,24},{5,1},{9,5},{13... | collective-permute-start | bytes 331784 | tf_op jit(solution)/shard_map/ppermute | solution.py:26
  120.4 16.2 %all-to-all-start.1 = ((f32[32,1,794]{2,1,0:T(1,128)}), f32[32,1,794]{2,1,0:T(1,128)S(1)}, u32[]{:S(2)}, u32[]{:S(2)}) async-start(f32[32,1,794]{2,1,0:T(1,128)} %broadcast_in_dim.38), calls=%async_computation.1 | async-start | bytes 229376 | tf_op jit(solution)/shard_map/all_to_all | solution.py:66
  129.4 13.7 %collective-permute-start.10 = (f32[3,10,3,384]{3,2,1,0:T(4,128)}, f32[3,10,3,384]{3,2,1,0:T(4,128)}, u32[]{:S(2)}, u32[]{:S(2)}) collective-permute-start(f32[3,10,3,384]{3,2,1,0:T(4,128)} %get-tuple-element.291), channel_id=1, source_target_pairs={{0,1},{1,2},{2,3},{4,5},{5,6},{6,7},{8,9},{9,10},{10,11},{12,13},{... | collective-permute-start | bytes 414728 | tf_op jit(solution)/shard_map/ppermute | solution.py:24
  132.3 10.9 %collective-permute-start.11 = (f32[3,10,3,384]{3,2,1,0:T(4,128)}, f32[3,10,3,384]{3,2,1,0:T(4,128)}, u32[]{:S(2)}, u32[]{:S(2)}) collective-permute-start(f32[3,10,3,384]{3,2,1,0:T(4,128)} %get-tuple-element.292), channel_id=1, source_target_pairs={{1,0},{2,1},{3,2},{5,4},{6,5},{7,6},{9,8},{10,9},{11,10},{13,12},{... | collective-permute-start | bytes 414728 | tf_op jit(solution)/shard_map/ppermute | solution.py:26
  (61 other events, 819.3 us)

commit v14 on v10

--- a/solution.py
+++ b/solution.py
@@ -135,13 +135,13 @@
         pad_depth(with_halo(lower_x, (("col", 2),), 3)), ((0, 0), (0, 2), (0, 0), (0, 0))
     )
     contact_pad = spread[bond_count].astype(jnp.float32)
-    near_contact = window(contact_pad, 0, 0, 0, extent)
+    near_contact = contact.astype(jnp.float32)
 
     def bond_pair(bond_index):
         shift_x, shift_y, shift_z = bond_shift(bond_index)
         weight = float(weights[bond_index])
         level_pad = spread[bond_index]
-        intact = window(level_pad, 0, 0, 0, extent).astype(jnp.float32)
+        intact = integrity[bond_index].astype(jnp.float32)
         prior = window(level_pad, -shift_x, -shift_y, -shift_z, extent).astype(jnp.float32)
         forward = weight * intact
         backward = weight * prior

time: 184 us -> 182 us (0.989)
  other arithmetic: 61.7 us -> 59.2 us
  starting transfers between devices: 41.6 us -> 39.7 us
  waiting for transfers between devices: 21.1 us -> 23 us
    add x12, other arithmetic: 5.26 us -> 8.32 us  [on_device(): forward + backward]
    concatenate x5, other arithmetic: 15.6 us -> 13.5 us  [with_halo(): x = jnp.concatenate(parts, axis=dim)]
    ppermute x5, starting transfers between devices: 23.9 us -> 22 us  [with_halo(): parts.insert(0, lax.ppermute(last, axis, up))]
  transfers between devices with their start and end apart: 13 -> 13, of which waited for: 6 -> 7; matrix products, arithmetic and copies ran while one was open for 7% -> 6% of each run, Pallas kernels for 0% -> 0%
where the time goes in v14:
time: 182 us; the launch traced here: 181 us
  other arithmetic  59.2 us (33%)
  starting transfers between devices  39.7 us (22%)
  blocking collectives  28 us (15%)
  waiting for transfers between devices  23 us (13%)
  local copies, waits for them, and re-layouts  22.7 us (12%)
  between operations  8.02 us (4%)
    all_to_all x2, blocking collectives, device_rows(): return lax.all_to_all(tiled, axes, 0, 0, tiled=True)  28 us
    ppermute x5, starting transfers between devices, with_halo(): parts.insert(0, lax.ppermute(last, axis, up))  22 us
    ppermute x5, waiting for transfers between devices, with_halo(): parts.append(lax.ppermute(first, axis, down))  15.2 us
    concatenate x5, other arithmetic, with_halo(): x = jnp.concatenate(parts, axis=dim)  13.5 us
    another operation x3, other arithmetic, operator(): return jnp.stack(summed)  12.2 us
    add x3, other arithmetic, operator(): summed[component] = summed[component] + heading[component] * stretch  12 us
    add x12, other arithmetic, on_device(): forward + backward  8.32 us
    ppermute x5, starting transfers between devices, with_halo(): parts.append(lax.ppermute(first, axis, down))  6.64 us
  transfers between devices with their start and end apart: 13, of which 7 were waited for; matrix products, arithmetic and copies ran while one was open for 6% of the time, Pallas kernels for 0%

profile of v14, /device:TPU:0, one launch (start us, length us, event | category | flops | bytes accessed | tf_op | source)
XLA Modules:
  0.0 180.9 jit_solution(3767846355677847460)
XLA Ops:
  4.2 4.9 %collective-permute-start = (bf16[71,8,384]{2,1,0:T(8,128)(2,1)S(1)}, bf16[71,8,384]{2,1,0:T(8,128)(2,1)S(1)}, u32[]{:S(2)}, u32[]{:S(2)}) collective-permute-start(bf16[71,8,384]{2,1,0:T(8,128)(2,1)S(1)} %pad_maximum_fusion.1), channel_id=1, source_target_pairs={{0,4},{4,8},{8,12},{12,16},{16,20},{20,24},{24,28},{1,5},{5,9},{9,... | collective-permute-start | bytes 1308680 | tf_op jit(solution)/shard_map/ppermute | solution.py:41
  11.0 4.9 %all-to-all-start = ((f32[32,1,24]{2,1,0:T(1,128)}), f32[32,1,24]{2,1,0:T(1,128)S(1)}, u32[]{:S(2)}, u32[]{:S(2)}) async-start(f32[32,1,24]{2,1,0:T(1,128)} %broadcast_in_dim.17), calls=%async_computation | async-start | bytes 32768 | tf_op jit(solution)/shard_map/all_to_all | solution.py:66
  17.2 5.8 %all-to-all-done = f32[32,1,24]{2,1,0:T(1,128)S(1)} async-done(((f32[32,1,24]{2,1,0:T(1,128)}), f32[32,1,24]{2,1,0:T(1,128)S(1)}, u32[]{:S(2)}, u32[]{:S(2)}) %all-to-all-start) | async-done | bytes 3104 | tf_op jit(solution)/shard_map/all_to_all | solution.py:66
  24.6 1.7 constant_dynamic-update-slice_fusion
  31.5 4.1 %collective-permute-start.2 = (bf16[62,8,3,384]{3,1,2,0:T(8,128)(2,1)}, bf16[62,8,3,384]{3,1,2,0:T(8,128)(2,1)}, u32[]{:S(2)}, u32[]{:S(2)}) collective-permute-start(bf16[62,8,3,384]{3,1,2,0:T(8,128)(2,1)} %copy.188), channel_id=1, source_target_pairs={{0,1},{1,2},{2,3},{4,5},{5,6},{6,7},{8,9},{9,10},{10,11},{12,13},{... | collective-permute-start | bytes 3428360 | tf_op jit(solution)/shard_map/ppermute | solution.py:24
  36.9 1.9 %copy.191 = bf16[62,8,3,384]{3,2,1,0:T(4,128)(2,1)S(1)} copy(bf16[62,8,3,384]{3,1,2,0:T(8,128)(2,1)} %collective-permute-done.3) | data formatting | bytes 2285568 | tf_op jit(solution)/shard_map/ppermute | solution.py:26
  38.8 1.9 %copy.190 = bf16[62,8,3,384]{3,2,1,0:T(4,128)(2,1)S(1)} copy(bf16[62,8,3,384]{3,1,2,0:T(8,128)(2,1)} %collective-permute-done.2) | data formatting | bytes 2285568 | tf_op jit(solution)/shard_map/ppermute | solution.py:24
  40.7 10.2 %fusion.5 = bf16[62,8,14,390]{3,2,1,0:T(8,128)(2,1)S(1)} fusion(bf16[62,8,3,384]{3,2,1,0:T(4,128)(2,1)S(1)} %copy.191, bf16[62,8,8,384]{3,2,1,0:T(8,128)(2,1)S(1)} %pad_maximum_fusion, bf16[62,8,3,384]{3,2,1,0:T(4,128)(2,1)S(1)} %copy.190), kind=kLoop, calls=%fused_computation.7 | loop fusion | flops 32497920 | bytes 10749312 | tf_op jit(solution)/shard_map/concatenate | solution.py:27
  55.9 1.7 fusion.1768
  57.6 1.8 %fusion.1759 = (f32[4,8,384]{2,1,0:T(8,128)S(1)}, f32[4,8,384]{2,1,0:T(8,128)}, f32[4,8,384]{2,1,0:T(8,128)}, f32[4,8,384]{2,1,0:T(8,128)S(1)}, f32[4,8,384]{2,1...) fusion(s32[4,8,384]{2,1,0:T(8,128)S(1)} %copy-done.3, ...), kind=kLoop, calls=%fused_computation.2665 | loop fusion | flops 651264 | bytes 1228800 | tf_op jit(solution)/shard_map/add | solution.py:162
  66.0 2.4 %collective-permute-start.4 = (f32[3,3,8,384]{3,2,1,0:T(8,128)}, f32[3,3,8,384]{3,2,1,0:T(8,128)S(1)}, u32[]{:S(2)}, u32[]{:S(2)}) collective-permute-start(f32[3,3,8,384]{3,2,1,0:T(8,128)} %get-tuple-element.329), channel_id=1, source_target_pairs={{0,4},{4,8},{8,12},{12,16},{16,20},{20,24},{24,28},{1,5},{5,9},{9,... | collective-permute-start | bytes 331784 | tf_op jit(solution)/shard_map/ppermute | solution.py:24
  71.0 4.2 %collective-permute-done.5 = f32[3,3,8,384]{3,2,1,0:T(8,128)S(1)} collective-permute-done((f32[3,3,8,384]{3,2,1,0:T(8,128)}, f32[3,3,8,384]{3,2,1,0:T(8,128)S(1)}, u32[]{:S(2)}, u32[]{:S(2)}) %collective-permute-start.5) | collective-permute-done | bytes 110624 | tf_op jit(solution)/shard_map/ppermute | solution.py:26
  76.1 11.0 %collective-permute-start.6 = (f32[3,10,3,384]{3,2,1,0:T(4,128)}, f32[3,10,3,384]{3,2,1,0:T(4,128)}, u32[]{:S(2)}, u32[]{:S(2)}) collective-permute-start(f32[3,10,3,384]{3,2,1,0:T(4,128)} %get-tuple-element.325), channel_id=1, source_target_pairs={{0,1},{1,2},{2,3},{4,5},{5,6},{6,7},{8,9},{9,10},{10,11},{12,13},{... | collective-permute-start | bytes 414728 | tf_op jit(solution)/shard_map/ppermute | solution.py:24
  89.0 4.5 %collective-permute-done.7 = f32[3,10,3,384]{3,2,1,0:T(4,128)} collective-permute-done((f32[3,10,3,384]{3,2,1,0:T(4,128)}, f32[3,10,3,384]{3,2,1,0:T(4,128)}, u32[]{:S(2)}, u32[]{:S(2)}) %collective-permute-start.7) | collective-permute-done | bytes 138272 | tf_op jit(solution)/shard_map/ppermute | solution.py:26
  95.3 11.4 %add_add_fusion.2 = (f32[4,8,384]{2,1,0:T(8,128)S(1)}, f32[4,8,384]{2,1,0:T(8,128)S(1)}, f32[4,8,384]{2,1,0:T(8,128)S(1)}, f32[4,8,384]{2,1,0:T(8,128)S(1)}, f32...) fusion(f32[4,8,384]{2,1,0:T(8,128)S(1)} %squeeze.216, ...), kind=kLoop, calls=%fused_computation.2537 | loop fusion | flops 18382848 | bytes 27181056 | tf_op jit(solution)/shard_map/add | solution.py:187
  110.0 14.8 %all_to_all.24 = f32[32,1,26]{2,1,0:T(1,128)S(1)} all-to-all(f32[32,1,26]{2,1,0:T(1,128)S(1)} %broadcast_in_dim.22), channel_id=1, replica_groups=mesh['slab'=8,'col'=4] {'slab','col'}, dimensions={0} | all-to-all | bytes 6656 | tf_op jit(solution)/shard_map/all_to_all | solution.py:66
  128.3 2.4 %collective-permute-start.8 = (f32[3,3,8,384]{3,2,1,0:T(8,128)}, f32[3,3,8,384]{3,2,1,0:T(8,128)S(1)}, u32[]{:S(2)}, u32[]{:S(2)}) collective-permute-start(f32[3,3,8,384]{3,2,1,0:T(8,128)} %get-tuple-element.327), channel_id=1, source_target_pairs={{0,4},{4,8},{8,12},{12,16},{16,20},{20,24},{24,28},{1,5},{5,9},{9,... | collective-permute-start | bytes 331784 | tf_op jit(solution)/shard_map/ppermute | solution.py:24
  133.4 4.2 %collective-permute-done.9 = f32[3,3,8,384]{3,2,1,0:T(8,128)S(1)} collective-permute-done((f32[3,3,8,384]{3,2,1,0:T(8,128)}, f32[3,3,8,384]{3,2,1,0:T(8,128)S(1)}, u32[]{:S(2)}, u32[]{:S(2)}) %collective-permute-start.9) | collective-permute-done | bytes 110624 | tf_op jit(solution)/shard_map/ppermute | solution.py:26
  138.4 2.0 %collective-permute-start.10 = (f32[3,10,3,384]{3,2,1,0:T(4,128)}, f32[3,10,3,384]{3,2,1,0:T(4,128)}, u32[]{:S(2)}, u32[]{:S(2)}) collective-permute-start(f32[3,10,3,384]{3,2,1,0:T(4,128)} %get-tuple-element.323), channel_id=1, source_target_pairs={{0,1},{1,2},{2,3},{4,5},{5,6},{6,7},{8,9},{9,10},{10,11},{12,13},{... | collective-permute-start | bytes 414728 | tf_op jit(solution)/shard_map/ppermute | solution.py:24
  142.0 2.2 %collective-permute-done.11 = f32[3,10,3,384]{3,2,1,0:T(4,128)} collective-permute-done((f32[3,10,3,384]{3,2,1,0:T(4,128)}, f32[3,10,3,384]{3,2,1,0:T(4,128)}, u32[]{:S(2)}, u32[]{:S(2)}) %collective-permute-start.11) | collective-permute-done | bytes 138272 | tf_op jit(solution)/shard_map/ppermute | solution.py:26
  144.2 1.6 select_maximum_fusion
  146.0 11.5 %add_bitcast_fusion.2 = (f32[1,4,8,384]{3,2,1,0:T(8,128)S(1)}, f32[4,8,384]{2,1,0:T(8,128)S(1)}, f32[4,8,384]{2,1,0:T(8,128)S(1)}, f32[4,8,384]{2,1,0:T(8,128)S(...) fusion(f32[4,8,384]{2,1,0:T(8,128)S(1)} %squeeze.222, ...), kind=kLoop, calls=%fused_computation.2534 | loop fusion | flops 18382848 | bytes 27181056 | tf_op jit(solution)/shard_map/stack | solution.py:188
  158.9 2.7 %pad_maximum_fusion.7 = f32[4]{0:T(128)S(1)} fusion(f32[1]{0:T(128)} %bitcast.167, f32[1]{0:T(128)} %bitcast.166, f32[1]{0:T(128)} %bitcast.165, f32[1]{0:T(128)} %bitcast.158), kind=kLoop, calls=%fused_computation.2660 | loop fusion | flops 12 | bytes 32 | tf_op jit(solution)/shard_map/stack | solution.py:229
  161.6 13.3 %all_to_all.25 = f32[32,1,4]{2,1,0:T(1,128)S(1)} all-to-all(f32[32,1,4]{2,1,0:T(1,128)S(1)} %broadcast_in_dim.23), channel_id=1, replica_groups=mesh['slab'=8,'col'=4] {'slab','col'}, dimensions={0} | all-to-all | bytes 1024 | tf_op jit(solution)/shard_map/all_to_all | solution.py:66
  (252 shorter events, 45.9 us)
Async XLA Ops:
  0.6 35.2 %copy-start = (f32[24,768]{1,0:T(8,128)S(1)}, f32[24,768]{1,0:T(8,128)}, u32[]{:S(2)}) copy-start(f32[24,768]{1,0:T(8,128)} %param.68) | copy-start | bytes 221188
  4.2 20.1 %collective-permute-start = (bf16[71,8,384]{2,1,0:T(8,128)(2,1)S(1)}, bf16[71,8,384]{2,1,0:T(8,128)(2,1)S(1)}, u32[]{:S(2)}, u32[]{:S(2)}) collective-permute-start(bf16[71,8,384]{2,1,0:T(8,128)(2,1)S(1)} %pad_maximum_fusion.1), channel_id=1, source_target_pairs={{0,4},{4,8},{8,12},{12,16},{16,20},{20,24},{24,28},{1,5},{5,9},{9,... | collective-permute-start | bytes 1308680 | tf_op jit(solution)/shard_map/ppermute | solution.py:41
  11.0 12.0 %all-to-all-start = ((f32[32,1,24]{2,1,0:T(1,128)}), f32[32,1,24]{2,1,0:T(1,128)S(1)}, u32[]{:S(2)}, u32[]{:S(2)}) async-start(f32[32,1,24]{2,1,0:T(1,128)} %broadcast_in_dim.17), calls=%async_computation | async-start | bytes 32768 | tf_op jit(solution)/shard_map/all_to_all | solution.py:66
  15.9 10.5 %collective-permute-start.1 = (bf16[1,8,384]{2,1,0:T(8,128)(2,1)S(1)}, bf16[1,8,384]{2,1,0:T(8,128)(2,1)S(1)}, u32[]{:S(2)}, u32[]{:S(2)}) collective-permute-start(bf16[1,8,384]{2,1,0:T(8,128)(2,1)S(1)} %get-tuple-element.332), channel_id=1, source_target_pairs={{4,0},{8,4},{12,8},{16,12},{20,16},{24,20},{28,24},{5,1},{9,5},{13... | collective-permute-start | bytes 18440 | tf_op jit(solution)/shard_map/ppermute | solution.py:42
  29.1 7.9 %collective-permute-start.3 = (bf16[62,8,3,384]{3,1,2,0:T(8,128)(2,1)}, bf16[62,8,3,384]{3,1,2,0:T(8,128)(2,1)}, u32[]{:S(2)}, u32[]{:S(2)}) collective-permute-start(bf16[62,8,3,384]{3,1,2,0:T(8,128)(2,1)} %copy.189), channel_id=1, source_target_pairs={{1,0},{2,1},{3,2},{5,4},{6,5},{7,6},{9,8},{10,9},{11,10},{13,12},{... | collective-permute-start | bytes 3428360 | tf_op jit(solution)/shard_map/ppermute | solution.py:26
  31.5 7.3 %collective-permute-start.2 = (bf16[62,8,3,384]{3,1,2,0:T(8,128)(2,1)}, bf16[62,8,3,384]{3,1,2,0:T(8,128)(2,1)}, u32[]{:S(2)}, u32[]{:S(2)}) collective-permute-start(bf16[62,8,3,384]{3,1,2,0:T(8,128)(2,1)} %copy.188), channel_id=1, source_target_pairs={{0,1},{1,2},{2,3},{4,5},{5,6},{6,7},{8,9},{9,10},{10,11},{12,13},{... | collective-permute-start | bytes 3428360 | tf_op jit(solution)/shard_map/ppermute | solution.py:24
  52.1 11.0 %copy-start.13 = (bf16[10,14,390]{2,1,0:T(8,128)(2,1)}, bf16[10,14,390]{2,1,0:T(8,128)(2,1)S(1)}, u32[]{:S(2)}) copy-start(bf16[10,14,390]{2,1,0:T(8,128)(2,1)S(1)} %get-tuple-element.221) | copy-start | bytes 327604
  52.1 11.0 %copy-start.14 = (bf16[10,14,390]{2,1,0:T(8,128)(2,1)}, bf16[10,14,390]{2,1,0:T(8,128)(2,1)S(1)}, u32[]{:S(2)}) copy-start(bf16[10,14,390]{2,1,0:T(8,128)(2,1)S(1)} %get-tuple-element.222) | copy-start | bytes 327604
  52.1 11.0 %copy-start.15 = (bf16[10,14,390]{2,1,0:T(8,128)(2,1)}, bf16[10,14,390]{2,1,0:T(8,128)(2,1)S(1)}, u32[]{:S(2)}) copy-start(bf16[10,14,390]{2,1,0:T(8,128)(2,1)S(1)} %get-tuple-element.223) | copy-start | bytes 327604
  52.7 10.4 %copy-start.30 = (bf16[10,14,390]{2,1,0:T(8,128)(2,1)}, bf16[10,14,390]{2,1,0:T(8,128)(2,1)S(1)}, u32[]{:S(2)}) copy-start(bf16[10,14,390]{2,1,0:T(8,128)(2,1)S(1)} %get-tuple-element.179) | copy-start | bytes 327604
  54.1 10.2 %copy-start.45 = (f32[3,384]{1,0:T(4,128)S(1)}, f32[3,384]{1,0:T(4,128)}, u32[]{:S(2)}) copy-start(f32[3,384]{1,0:T(4,128)} %add.3626) | copy-start | bytes 13828
  54.1 10.2 %copy-start.46 = (f32[3]{0:T(128)S(1)}, f32[3]{0:T(128)}, u32[]{:S(2)}) copy-start(f32[3]{0:T(128)} %constant.154.clone) | copy-start | bytes 40
  54.1 10.2 %copy-start.47 = (f32[3]{0:T(128)S(1)}, f32[3]{0:T(128)}, u32[]{:S(2)}) copy-start(f32[3]{0:T(128)} %constant.153.clone) | copy-start | bytes 40
  57.6 49.4 %copy-start.4 = (f32[4,8,384]{2,1,0:T(8,128)}, f32[4,8,384]{2,1,0:T(8,128)S(1)}, u32[]{:S(2)}) copy-start(f32[4,8,384]{2,1,0:T(8,128)S(1)} %get-tuple-element.159) | copy-start | bytes 147460
  57.6 49.4 %copy-start.5 = (f32[4,8,384]{2,1,0:T(8,128)}, f32[4,8,384]{2,1,0:T(8,128)S(1)}, u32[]{:S(2)}) copy-start(f32[4,8,384]{2,1,0:T(8,128)S(1)} %get-tuple-element.160) | copy-start | bytes 147460
  57.6 49.4 %copy-start.6 = (f32[4,8,384]{2,1,0:T(8,128)}, f32[4,8,384]{2,1,0:T(8,128)S(1)}, u32[]{:S(2)}) copy-start(f32[4,8,384]{2,1,0:T(8,128)S(1)} %get-tuple-element.247) | copy-start | bytes 147460
  66.0 5.1 %collective-permute-start.4 = (f32[3,3,8,384]{3,2,1,0:T(8,128)}, f32[3,3,8,384]{3,2,1,0:T(8,128)S(1)}, u32[]{:S(2)}, u32[]{:S(2)}) collective-permute-start(f32[3,3,8,384]{3,2,1,0:T(8,128)} %get-tuple-element.329), channel_id=1, source_target_pairs={{0,4},{4,8},{8,12},{12,16},{16,20},{20,24},{24,28},{1,5},{5,9},{9,... | collective-permute-start | bytes 331784 | tf_op jit(solution)/shard_map/ppermute | solution.py:24
  68.4 6.9 %collective-permute-start.5 = (f32[3,3,8,384]{3,2,1,0:T(8,128)}, f32[3,3,8,384]{3,2,1,0:T(8,128)S(1)}, u32[]{:S(2)}, u32[]{:S(2)}) collective-permute-start(f32[3,3,8,384]{3,2,1,0:T(8,128)} %get-tuple-element.330), channel_id=1, source_target_pairs={{4,0},{8,4},{12,8},{16,12},{20,16},{24,20},{28,24},{5,1},{9,5},{13... | collective-permute-start | bytes 331784 | tf_op jit(solution)/shard_map/ppermute | solution.py:26
  76.1 12.9 %collective-permute-start.6 = (f32[3,10,3,384]{3,2,1,0:T(4,128)}, f32[3,10,3,384]{3,2,1,0:T(4,128)}, u32[]{:S(2)}, u32[]{:S(2)}) collective-permute-start(f32[3,10,3,384]{3,2,1,0:T(4,128)} %get-tuple-element.325), channel_id=1, source_target_pairs={{0,1},{1,2},{2,3},{4,5},{5,6},{6,7},{8,9},{9,10},{10,11},{12,13},{... | collective-permute-start | bytes 414728 | tf_op jit(solution)/shard_map/ppermute | solution.py:24
  87.1 6.4 %collective-permute-start.7 = (f32[3,10,3,384]{3,2,1,0:T(4,128)}, f32[3,10,3,384]{3,2,1,0:T(4,128)}, u32[]{:S(2)}, u32[]{:S(2)}) collective-permute-start(f32[3,10,3,384]{3,2,1,0:T(4,128)} %get-tuple-element.326), channel_id=1, source_target_pairs={{1,0},{2,1},{3,2},{5,4},{6,5},{7,6},{9,8},{10,9},{11,10},{13,12},{... | collective-permute-start | bytes 414728 | tf_op jit(solution)/shard_map/ppermute | solution.py:26
  128.3 5.1 %collective-permute-start.8 = (f32[3,3,8,384]{3,2,1,0:T(8,128)}, f32[3,3,8,384]{3,2,1,0:T(8,128)S(1)}, u32[]{:S(2)}, u32[]{:S(2)}) collective-permute-start(f32[3,3,8,384]{3,2,1,0:T(8,128)} %get-tuple-element.327), channel_id=1, source_target_pairs={{0,4},{4,8},{8,12},{12,16},{16,20},{20,24},{24,28},{1,5},{5,9},{9,... | collective-permute-start | bytes 331784 | tf_op jit(solution)/shard_map/ppermute | solution.py:24
  130.7 6.9 %collective-permute-start.9 = (f32[3,3,8,384]{3,2,1,0:T(8,128)}, f32[3,3,8,384]{3,2,1,0:T(8,128)S(1)}, u32[]{:S(2)}, u32[]{:S(2)}) collective-permute-start(f32[3,3,8,384]{3,2,1,0:T(8,128)} %get-tuple-element.328), channel_id=1, source_target_pairs={{4,0},{8,4},{12,8},{16,12},{20,16},{24,20},{28,24},{5,1},{9,5},{13... | collective-permute-start | bytes 331784 | tf_op jit(solution)/shard_map/ppermute | solution.py:26
  138.4 3.6 %collective-permute-start.10 = (f32[3,10,3,384]{3,2,1,0:T(4,128)}, f32[3,10,3,384]{3,2,1,0:T(4,128)}, u32[]{:S(2)}, u32[]{:S(2)}) collective-permute-start(f32[3,10,3,384]{3,2,1,0:T(4,128)} %get-tuple-element.323), channel_id=1, source_target_pairs={{0,1},{1,2},{2,3},{4,5},{5,6},{6,7},{8,9},{9,10},{10,11},{12,13},{... | collective-permute-start | bytes 414728 | tf_op jit(solution)/shard_map/ppermute | solution.py:24
  140.4 3.8 %collective-permute-start.11 = (f32[3,10,3,384]{3,2,1,0:T(4,128)}, f32[3,10,3,384]{3,2,1,0:T(4,128)}, u32[]{:S(2)}, u32[]{:S(2)}) collective-permute-start(f32[3,10,3,384]{3,2,1,0:T(4,128)} %get-tuple-element.324), channel_id=1, source_target_pairs={{1,0},{2,1},{3,2},{5,4},{6,5},{7,6},{9,8},{10,9},{11,10},{13,12},{... | collective-permute-start | bytes 414728 | tf_op jit(solution)/shard_map/ppermute | solution.py:26
  (53 other events, 425.6 us)

commit v15 on v14

--- a/solution.py
+++ b/solution.py
@@ -152,7 +152,11 @@
             backward = backward + PENALTY * window(
                 contact_pad, -shift_x, -shift_y, -shift_z, extent
             ) * near_contact * (1.0 - prior)
-        forward = window(inside_pad, shift_x, shift_y, shift_z, extent) * forward
+        forward = (
+            slab_mask[3 + shift_x : 3 + shift_x + extent[0], None, None]
+            * col_mask[None, 3 + shift_y : 3 + shift_y + extent[1], None]
+            * depth_mask[None, None, 3 + shift_z : 3 + shift_z + extent[2]]
+        ) * forward
         return (forward, backward)
 
     diagonal = jnp.full((3,) + extent, FOUNDATION, jnp.float32)

time: 182 us -> 200 us (1.099)
  other arithmetic: 59.2 us -> 75.6 us
  local copies, waits for them, and re-layouts: 22.7 us -> 24.8 us
    another operation x3, other arithmetic: 12.2 us -> 17.8 us  [operator(): return jnp.stack(summed)]
    add x3, other arithmetic: 12 us -> 17.6 us  [operator(): summed[component] = summed[component] + heading[component] * stretch]
    add x12, other arithmetic: 8.32 us -> 13.4 us  [on_device(): forward + backward]
where the time goes in v15:
time: 200 us; the launch traced here: 197 us
  other arithmetic  75.6 us (38%)
  starting transfers between devices  38.3 us (19%)
  blocking collectives  28 us (14%)
  local copies, waits for them, and re-layouts  24.8 us (12%)
  waiting for transfers between devices  22.6 us (11%)
  between operations  7.75 us (4%)
    all_to_all x2, blocking collectives, device_rows(): return lax.all_to_all(tiled, axes, 0, 0, tiled=True)  28 us
    ppermute x5, starting transfers between devices, with_halo(): parts.insert(0, lax.ppermute(last, axis, up))  20.6 us
    another operation x3, other arithmetic, operator(): return jnp.stack(summed)  17.8 us
    add x3, other arithmetic, operator(): summed[component] = summed[component] + heading[component] * stretch  17.6 us
    ppermute x5, waiting for transfers between devices, with_halo(): parts.append(lax.ppermute(first, axis, down))  15.1 us
    add x12, other arithmetic, on_device(): forward + backward  13.4 us
    concatenate x5, other arithmetic, with_halo(): x = jnp.concatenate(parts, axis=dim)  13.3 us
    ppermute x5, starting transfers between devices, with_halo(): parts.append(lax.ppermute(first, axis, down))  6.67 us
  transfers between devices with their start and end apart: 13, of which 7 were waited for; matrix products, arithmetic and copies ran while one was open for 6% of the time, Pallas kernels for 0%

profile of v15, /device:TPU:0, one launch (start us, length us, event | category | flops | bytes accessed | tf_op | source)
XLA Modules:
  0.0 197.4 jit_solution(7157974011105143691)
XLA Ops:
  4.2 4.9 %collective-permute-start = (bf16[71,8,384]{2,1,0:T(8,128)(2,1)S(1)}, bf16[71,8,384]{2,1,0:T(8,128)(2,1)S(1)}, u32[]{:S(2)}, u32[]{:S(2)}) collective-permute-start(bf16[71,8,384]{2,1,0:T(8,128)(2,1)S(1)} %pad_maximum_fusion.1), channel_id=1, source_target_pairs={{0,4},{4,8},{8,12},{12,16},{16,20},{20,24},{24,28},{1,5},{5,9},{9,... | collective-permute-start | bytes 1308680 | tf_op jit(solution)/shard_map/ppermute | solution.py:41
  11.0 4.9 %all-to-all-start = ((f32[32,1,24]{2,1,0:T(1,128)}), f32[32,1,24]{2,1,0:T(1,128)S(1)}, u32[]{:S(2)}, u32[]{:S(2)}) async-start(f32[32,1,24]{2,1,0:T(1,128)} %broadcast_in_dim.17), calls=%async_computation | async-start | bytes 32768 | tf_op jit(solution)/shard_map/all_to_all | solution.py:66
  17.3 5.7 %all-to-all-done = f32[32,1,24]{2,1,0:T(1,128)S(1)} async-done(((f32[32,1,24]{2,1,0:T(1,128)}), f32[32,1,24]{2,1,0:T(1,128)S(1)}, u32[]{:S(2)}, u32[]{:S(2)}) %all-to-all-start) | async-done | bytes 3104 | tf_op jit(solution)/shard_map/all_to_all | solution.py:66
  24.6 1.7 constant_dynamic-update-slice_fusion
  31.5 4.0 %collective-permute-start.2 = (bf16[62,8,3,384]{3,1,2,0:T(8,128)(2,1)}, bf16[62,8,3,384]{3,1,2,0:T(8,128)(2,1)}, u32[]{:S(2)}, u32[]{:S(2)}) collective-permute-start(bf16[62,8,3,384]{3,1,2,0:T(8,128)(2,1)} %copy.188), channel_id=1, source_target_pairs={{0,1},{1,2},{2,3},{4,5},{5,6},{6,7},{8,9},{9,10},{10,11},{12,13},{... | collective-permute-start | bytes 3428360 | tf_op jit(solution)/shard_map/ppermute | solution.py:24
  37.6 1.9 copy.191
  39.5 1.9 copy.190
  41.4 10.2 %fusion.5 = bf16[62,8,14,390]{3,2,1,0:T(8,128)(2,1)S(1)} fusion(bf16[62,8,3,384]{3,2,1,0:T(4,128)(2,1)S(1)} %copy.191, bf16[62,8,8,384]{3,2,1,0:T(8,128)(2,1)S(1)} %pad_maximum_fusion, bf16[62,8,3,384]{3,2,1,0:T(4,128)(2,1)S(1)} %copy.190), kind=kLoop, calls=%fused_computation.7 | loop fusion | flops 32497920 | bytes 10749312 | tf_op jit(solution)/shard_map/concatenate | solution.py:27
  72.6 2.5 %collective-permute-start.4 = (f32[3,3,8,384]{3,2,1,0:T(8,128)S(1)}, f32[3,3,8,384]{3,2,1,0:T(8,128)S(1)}, u32[]{:S(2)}, u32[]{:S(2)}) collective-permute-start(f32[3,3,8,384]{3,2,1,0:T(8,128)S(1)} %get-tuple-element.330), channel_id=1, source_target_pairs={{0,4},{4,8},{8,12},{12,16},{16,20},{20,24},{24,28},{1,5},{5,9},{9,... | collective-permute-start | bytes 331784 | tf_op jit(solution)/shard_map/ppermute | solution.py:24
  77.4 4.3 %collective-permute-done.5 = f32[3,3,8,384]{3,2,1,0:T(8,128)S(1)} collective-permute-done((f32[3,3,8,384]{3,2,1,0:T(8,128)S(1)}, f32[3,3,8,384]{3,2,1,0:T(8,128)S(1)}, u32[]{:S(2)}, u32[]{:S(2)}) %collective-permute-start.5) | collective-permute-done | bytes 110624 | tf_op jit(solution)/shard_map/ppermute | solution.py:26
  82.5 10.3 %collective-permute-start.6 = (f32[3,10,3,384]{3,2,1,0:T(4,128)}, f32[3,10,3,384]{3,2,1,0:T(4,128)S(1)}, u32[]{:S(2)}, u32[]{:S(2)}) collective-permute-start(f32[3,10,3,384]{3,2,1,0:T(4,128)} %get-tuple-element.326), channel_id=1, source_target_pairs={{0,1},{1,2},{2,3},{4,5},{5,6},{6,7},{8,9},{9,10},{10,11},{12,13},{... | collective-permute-start | bytes 414728 | tf_op jit(solution)/shard_map/ppermute | solution.py:24
  94.7 4.5 %collective-permute-done.7 = f32[3,10,3,384]{3,2,1,0:T(4,128)} collective-permute-done((f32[3,10,3,384]{3,2,1,0:T(4,128)}, f32[3,10,3,384]{3,2,1,0:T(4,128)}, u32[]{:S(2)}, u32[]{:S(2)}) %collective-permute-start.7) | collective-permute-done | bytes 138272 | tf_op jit(solution)/shard_map/ppermute | solution.py:26
  100.9 13.5 %add_add_fusion.2 = (f32[4,8,384]{2,1,0:T(8,128)S(1)}, f32[4,8,384]{2,1,0:T(8,128)S(1)}, f32[4,8,384]{2,1,0:T(8,128)S(1)}, f32[4,8,384]{2,1,0:T(8,128)S(1)}, f32...) fusion(f32[4,8,384]{2,1,0:T(8,128)S(1)} %squeeze.216, ...), kind=kLoop, calls=%fused_computation.2536 | loop fusion | flops 19021824 | bytes 24636288 | tf_op jit(solution)/shard_map/add | solution.py:191
  115.0 2.0 add_add_fusion.1
  117.0 2.1 %add_add_fusion = f32[4,8,384]{2,1,0:T(8,128)S(1)} fusion(f32[4,8,384]{2,1,0:T(8,128)} %get-tuple-element.145, f32[4,8,384]{2,1,0:T(8,128)} %get-tuple-element.144, f32[4,8,384]{2,1,0:T(8,128)} %get-tuple-element.143, f32[4,8,384]{2,1,0:T(8,128)} %get-tuple-element.142, f32[4,8,384]{2,1,0:T(8,128)} %get-tuple-element.141, ...), kind=kLoop, calls=%fused_computation.2534 | loop fusion | flops 1449984 | bytes 3096576 | tf_op jit(solution)/shard_map/add | solution.py:191
  121.7 14.8 %all_to_all.24 = f32[32,1,26]{2,1,0:T(1,128)S(1)} all-to-all(f32[32,1,26]{2,1,0:T(1,128)S(1)} %broadcast_in_dim.22), channel_id=1, replica_groups=mesh['slab'=8,'col'=4] {'slab','col'}, dimensions={0} | all-to-all | bytes 6656 | tf_op jit(solution)/shard_map/all_to_all | solution.py:66
  139.8 2.4 %collective-permute-start.8 = (f32[3,3,8,384]{3,2,1,0:T(8,128)}, f32[3,3,8,384]{3,2,1,0:T(8,128)S(1)}, u32[]{:S(2)}, u32[]{:S(2)}) collective-permute-start(f32[3,3,8,384]{3,2,1,0:T(8,128)} %get-tuple-element.328), channel_id=1, source_target_pairs={{0,4},{4,8},{8,12},{12,16},{16,20},{20,24},{24,28},{1,5},{5,9},{9,... | collective-permute-start | bytes 331784 | tf_op jit(solution)/shard_map/ppermute | solution.py:24
  144.9 4.0 %collective-permute-done.9 = f32[3,3,8,384]{3,2,1,0:T(8,128)S(1)} collective-permute-done((f32[3,3,8,384]{3,2,1,0:T(8,128)S(1)}, f32[3,3,8,384]{3,2,1,0:T(8,128)S(1)}, u32[]{:S(2)}, u32[]{:S(2)}) %collective-permute-start.9) | collective-permute-done | bytes 110624 | tf_op jit(solution)/shard_map/ppermute | solution.py:26
  153.3 2.2 %collective-permute-done.11 = f32[3,10,3,384]{3,2,1,0:T(4,128)} collective-permute-done((f32[3,10,3,384]{3,2,1,0:T(4,128)}, f32[3,10,3,384]{3,2,1,0:T(4,128)}, u32[]{:S(2)}, u32[]{:S(2)}) %collective-permute-start.11) | collective-permute-done | bytes 138272 | tf_op jit(solution)/shard_map/ppermute | solution.py:26
  157.1 13.5 %add_bitcast_fusion.2 = (f32[1,4,8,384]{3,2,1,0:T(8,128)S(1)}, f32[4,8,384]{2,1,0:T(8,128)S(1)}, f32[4,8,384]{2,1,0:T(8,128)S(1)}, f32[4,8,384]{2,1,0:T(8,128)S(...) fusion(f32[4,8,384]{2,1,0:T(8,128)} %squeeze.222, ...), kind=kLoop, calls=%fused_computation.2533 | loop fusion | flops 19021824 | bytes 24636288 | tf_op jit(solution)/shard_map/stack | solution.py:192
  170.6 2.2 %add_bitcast_fusion.1 = f32[1,4,8,384]{3,2,1,0:T(8,128)S(1)} fusion(f32[4,8,384]{2,1,0:T(8,128)} %get-tuple-element.30, f32[4,8,384]{2,1,0:T(8,128)} %get-tuple-element.78, f32[4,8,384]{2,1,0:T(8,128)} %get-tuple-element.77, f32[4,8,384]{2,1,0:T(8,128)} %get-tuple-element.76, f32[4,8,384]{2,1,0:T(8,128)} %get-tuple-element.29, ...), kind=kLoop, calls=%fused_computation.2532 | loop fusion | flops 1449984 | bytes 3096576 | tf_op jit(solution)/shard_map/stack | solution.py:192
  172.8 2.2 %add_bitcast_fusion = f32[1,4,8,384]{3,2,1,0:T(8,128)S(1)} fusion(f32[4,8,384]{2,1,0:T(8,128)} %get-tuple-element.81, f32[4,8,384]{2,1,0:T(8,128)} %get-tuple-element.80, f32[4,8,384]{2,1,0:T(8,128)} %get-tuple-element.79, f32[4,8,384]{2,1,0:T(8,128)} %get-tuple-element.78, f32[4,8,384]{2,1,0:T(8,128)} %get-tuple-element.77, ...), kind=kLoop, calls=%fused_computation.2531 | loop fusion | flops 1449984 | bytes 3096576 | tf_op jit(solution)/shard_map/stack | solution.py:192
  175.6 2.6 %pad_maximum_fusion.7 = f32[4]{0:T(128)S(1)} fusion(f32[1]{0:T(128)} %bitcast.167, f32[1]{0:T(128)} %bitcast.166, f32[1]{0:T(128)} %bitcast.165, f32[1]{0:T(128)} %bitcast.158), kind=kLoop, calls=%fused_computation.2673 | loop fusion | flops 12 | bytes 32 | tf_op jit(solution)/shard_map/stack | solution.py:233
  178.3 13.3 %all_to_all.25 = f32[32,1,4]{2,1,0:T(1,128)S(1)} all-to-all(f32[32,1,4]{2,1,0:T(1,128)S(1)} %broadcast_in_dim.23), channel_id=1, replica_groups=mesh['slab'=8,'col'=4] {'slab','col'}, dimensions={0} | all-to-all | bytes 1024 | tf_op jit(solution)/shard_map/all_to_all | solution.py:66
  (254 shorter events, 58.2 us)
Async XLA Ops:
  0.6 36.5 %copy-start = (f32[24,768]{1,0:T(8,128)S(1)}, f32[24,768]{1,0:T(8,128)}, u32[]{:S(2)}) copy-start(f32[24,768]{1,0:T(8,128)} %param.68) | copy-start | bytes 221188
  4.2 20.1 %collective-permute-start = (bf16[71,8,384]{2,1,0:T(8,128)(2,1)S(1)}, bf16[71,8,384]{2,1,0:T(8,128)(2,1)S(1)}, u32[]{:S(2)}, u32[]{:S(2)}) collective-permute-start(bf16[71,8,384]{2,1,0:T(8,128)(2,1)S(1)} %pad_maximum_fusion.1), channel_id=1, source_target_pairs={{0,4},{4,8},{8,12},{12,16},{16,20},{20,24},{24,28},{1,5},{5,9},{9,... | collective-permute-start | bytes 1308680 | tf_op jit(solution)/shard_map/ppermute | solution.py:41
  11.0 12.0 %all-to-all-start = ((f32[32,1,24]{2,1,0:T(1,128)}), f32[32,1,24]{2,1,0:T(1,128)S(1)}, u32[]{:S(2)}, u32[]{:S(2)}) async-start(f32[32,1,24]{2,1,0:T(1,128)} %broadcast_in_dim.17), calls=%async_computation | async-start | bytes 32768 | tf_op jit(solution)/shard_map/all_to_all | solution.py:66
  15.9 10.5 %collective-permute-start.1 = (bf16[1,8,384]{2,1,0:T(8,128)(2,1)S(1)}, bf16[1,8,384]{2,1,0:T(8,128)(2,1)S(1)}, u32[]{:S(2)}, u32[]{:S(2)}) collective-permute-start(bf16[1,8,384]{2,1,0:T(8,128)(2,1)S(1)} %get-tuple-element.333), channel_id=1, source_target_pairs={{4,0},{8,4},{12,8},{16,12},{20,16},{24,20},{28,24},{5,1},{9,5},{13... | collective-permute-start | bytes 18440 | tf_op jit(solution)/shard_map/ppermute | solution.py:42
  30.2 7.4 %collective-permute-start.3 = (bf16[62,8,3,384]{3,1,2,0:T(8,128)(2,1)}, bf16[62,8,3,384]{3,1,2,0:T(8,128)(2,1)}, u32[]{:S(2)}, u32[]{:S(2)}) collective-permute-start(bf16[62,8,3,384]{3,1,2,0:T(8,128)(2,1)} %copy.189), channel_id=1, source_target_pairs={{1,0},{2,1},{3,2},{5,4},{6,5},{7,6},{9,8},{10,9},{11,10},{13,12},{... | collective-permute-start | bytes 3428360 | tf_op jit(solution)/shard_map/ppermute | solution.py:26
  31.5 8.0 %collective-permute-start.2 = (bf16[62,8,3,384]{3,1,2,0:T(8,128)(2,1)}, bf16[62,8,3,384]{3,1,2,0:T(8,128)(2,1)}, u32[]{:S(2)}, u32[]{:S(2)}) collective-permute-start(bf16[62,8,3,384]{3,1,2,0:T(8,128)(2,1)} %copy.188), channel_id=1, source_target_pairs={{0,1},{1,2},{2,3},{4,5},{5,6},{6,7},{8,9},{9,10},{10,11},{12,13},{... | collective-permute-start | bytes 3428360 | tf_op jit(solution)/shard_map/ppermute | solution.py:24
  52.5 18.0 %copy-start.9 = (bf16[10,14,390]{2,1,0:T(8,128)(2,1)}, bf16[10,14,390]{2,1,0:T(8,128)(2,1)S(1)}, u32[]{:S(2)}) copy-start(bf16[10,14,390]{2,1,0:T(8,128)(2,1)S(1)} %get-tuple-element.234) | copy-start | bytes 327604
  52.5 18.0 %copy-start.10 = (bf16[10,14,390]{2,1,0:T(8,128)(2,1)}, bf16[10,14,390]{2,1,0:T(8,128)(2,1)S(1)}, u32[]{:S(2)}) copy-start(bf16[10,14,390]{2,1,0:T(8,128)(2,1)S(1)} %get-tuple-element.235) | copy-start | bytes 327604
  52.8 16.6 %copy-start.11 = (bf16[10,14,390]{2,1,0:T(8,128)(2,1)}, bf16[10,14,390]{2,1,0:T(8,128)(2,1)S(1)}, u32[]{:S(2)}) copy-start(bf16[10,14,390]{2,1,0:T(8,128)(2,1)S(1)} %get-tuple-element.221) | copy-start | bytes 327604
  52.8 16.6 %copy-start.12 = (bf16[10,14,390]{2,1,0:T(8,128)(2,1)}, bf16[10,14,390]{2,1,0:T(8,128)(2,1)S(1)}, u32[]{:S(2)}) copy-start(bf16[10,14,390]{2,1,0:T(8,128)(2,1)S(1)} %get-tuple-element.222) | copy-start | bytes 327604
  52.8 16.6 %copy-start.13 = (bf16[10,14,390]{2,1,0:T(8,128)(2,1)}, bf16[10,14,390]{2,1,0:T(8,128)(2,1)S(1)}, u32[]{:S(2)}) copy-start(bf16[10,14,390]{2,1,0:T(8,128)(2,1)S(1)} %get-tuple-element.223) | copy-start | bytes 327604
  52.8 17.7 %copy-start.14 = (bf16[10,14,390]{2,1,0:T(8,128)(2,1)}, bf16[10,14,390]{2,1,0:T(8,128)(2,1)S(1)}, u32[]{:S(2)}) copy-start(bf16[10,14,390]{2,1,0:T(8,128)(2,1)S(1)} %get-tuple-element.224) | copy-start | bytes 327604
  52.9 17.7 %copy-start.15 = (bf16[10,14,390]{2,1,0:T(8,128)(2,1)}, bf16[10,14,390]{2,1,0:T(8,128)(2,1)S(1)}, u32[]{:S(2)}) copy-start(bf16[10,14,390]{2,1,0:T(8,128)(2,1)S(1)} %get-tuple-element.225) | copy-start | bytes 327604
  56.4 15.2 %copy-start.2 = (f32[3,4,8,384]{3,2,1,0:T(8,128)S(1)}, f32[3,4,8,384]{3,2,1,0:T(8,128)}, u32[]{:S(2)}) copy-start(f32[3,4,8,384]{3,2,1,0:T(8,128)} %param.65) | copy-start | bytes 442372
  56.4 15.2 %copy-start.46 = (f32[3]{0:T(128)S(1)}, f32[3]{0:T(128)}, u32[]{:S(2)}) copy-start(f32[3]{0:T(128)} %constant.154.clone) | copy-start | bytes 40
  72.6 4.8 %collective-permute-start.4 = (f32[3,3,8,384]{3,2,1,0:T(8,128)S(1)}, f32[3,3,8,384]{3,2,1,0:T(8,128)S(1)}, u32[]{:S(2)}, u32[]{:S(2)}) collective-permute-start(f32[3,3,8,384]{3,2,1,0:T(8,128)S(1)} %get-tuple-element.330), channel_id=1, source_target_pairs={{0,4},{4,8},{8,12},{12,16},{16,20},{20,24},{24,28},{1,5},{5,9},{9,... | collective-permute-start | bytes 331784 | tf_op jit(solution)/shard_map/ppermute | solution.py:24
  75.1 6.6 %collective-permute-start.5 = (f32[3,3,8,384]{3,2,1,0:T(8,128)S(1)}, f32[3,3,8,384]{3,2,1,0:T(8,128)S(1)}, u32[]{:S(2)}, u32[]{:S(2)}) collective-permute-start(f32[3,3,8,384]{3,2,1,0:T(8,128)S(1)} %get-tuple-element.331), channel_id=1, source_target_pairs={{4,0},{8,4},{12,8},{16,12},{20,16},{24,20},{28,24},{5,1},{9,5},{13... | collective-permute-start | bytes 331784 | tf_op jit(solution)/shard_map/ppermute | solution.py:26
  82.5 12.2 %collective-permute-start.6 = (f32[3,10,3,384]{3,2,1,0:T(4,128)}, f32[3,10,3,384]{3,2,1,0:T(4,128)S(1)}, u32[]{:S(2)}, u32[]{:S(2)}) collective-permute-start(f32[3,10,3,384]{3,2,1,0:T(4,128)} %get-tuple-element.326), channel_id=1, source_target_pairs={{0,1},{1,2},{2,3},{4,5},{5,6},{6,7},{8,9},{9,10},{10,11},{12,13},{... | collective-permute-start | bytes 414728 | tf_op jit(solution)/shard_map/ppermute | solution.py:24
  92.9 6.4 %collective-permute-start.7 = (f32[3,10,3,384]{3,2,1,0:T(4,128)}, f32[3,10,3,384]{3,2,1,0:T(4,128)}, u32[]{:S(2)}, u32[]{:S(2)}) collective-permute-start(f32[3,10,3,384]{3,2,1,0:T(4,128)} %get-tuple-element.327), channel_id=1, source_target_pairs={{1,0},{2,1},{3,2},{5,4},{6,5},{7,6},{9,8},{10,9},{11,10},{13,12},{... | collective-permute-start | bytes 414728 | tf_op jit(solution)/shard_map/ppermute | solution.py:26
  100.9 37.7 %copy-start.45 = (f32[768]{0:T(1024)S(1)}, f32[768]{0:T(1024)}, u32[]{:S(2)}) copy-start(f32[768]{0:T(1024)} %copy-done.44) | copy-start | bytes 9220
  139.8 5.1 %collective-permute-start.8 = (f32[3,3,8,384]{3,2,1,0:T(8,128)}, f32[3,3,8,384]{3,2,1,0:T(8,128)S(1)}, u32[]{:S(2)}, u32[]{:S(2)}) collective-permute-start(f32[3,3,8,384]{3,2,1,0:T(8,128)} %get-tuple-element.328), channel_id=1, source_target_pairs={{0,4},{4,8},{8,12},{12,16},{16,20},{20,24},{24,28},{1,5},{5,9},{9,... | collective-permute-start | bytes 331784 | tf_op jit(solution)/shard_map/ppermute | solution.py:24
  142.2 6.6 %collective-permute-start.9 = (f32[3,3,8,384]{3,2,1,0:T(8,128)S(1)}, f32[3,3,8,384]{3,2,1,0:T(8,128)S(1)}, u32[]{:S(2)}, u32[]{:S(2)}) collective-permute-start(f32[3,3,8,384]{3,2,1,0:T(8,128)S(1)} %get-tuple-element.329), channel_id=1, source_target_pairs={{4,0},{8,4},{12,8},{16,12},{20,16},{24,20},{28,24},{5,1},{9,5},{13... | collective-permute-start | bytes 331784 | tf_op jit(solution)/shard_map/ppermute | solution.py:26
  149.7 3.6 %collective-permute-start.10 = (f32[3,10,3,384]{3,2,1,0:T(4,128)}, f32[3,10,3,384]{3,2,1,0:T(4,128)S(1)}, u32[]{:S(2)}, u32[]{:S(2)}) collective-permute-start(f32[3,10,3,384]{3,2,1,0:T(4,128)} %get-tuple-element.324), channel_id=1, source_target_pairs={{0,1},{1,2},{2,3},{4,5},{5,6},{6,7},{8,9},{9,10},{10,11},{12,13},{... | collective-permute-start | bytes 414728 | tf_op jit(solution)/shard_map/ppermute | solution.py:24
  151.0 4.5 %collective-permute-start.11 = (f32[3,10,3,384]{3,2,1,0:T(4,128)}, f32[3,10,3,384]{3,2,1,0:T(4,128)}, u32[]{:S(2)}, u32[]{:S(2)}) collective-permute-start(f32[3,10,3,384]{3,2,1,0:T(4,128)} %get-tuple-element.325), channel_id=1, source_target_pairs={{1,0},{2,1},{3,2},{5,4},{6,5},{7,6},{9,8},{10,9},{11,10},{13,12},{... | collective-permute-start | bytes 414728 | tf_op jit(solution)/shard_map/ppermute | solution.py:26
  (53 other events, 671.3 us)
